TPU v7x, 1024 devices: a whole 4x8x16 slice. The times are simulated.
1024 devices in a mesh: energy: 64 (over x, z), section: 16 (over y, core).
Axes of the slice: x: 4, y: 8, z: 16, core: 2. Of those that a mesh axis runs over, the one named last changes fastest.
Arguments:
- propagator: bfloat16 [64, 16, 2, 384, 384], P('energy', 'section')
- forward_source: bfloat16 [64, 16, 384, 128], P('energy', 'section'), may hold values from -6 to 6
- backward_source: bfloat16 [64, 16, 384, 128], P('energy', 'section'), may hold values from -6 to 6
- left_orbital: int32 [131072], P('section'), may hold values from 0 to 6143, as said below
- right_orbital: int32 [131072], P('section'), may hold values from 0 to 6143
- phonon_shift: int32 [8], replicated, may hold values from -6 to 6
- coupling: float32 [8, 131072], P(None, 'section'), may hold values from 0.1 to 1
Outputs:
- self_energy: float32 [2, 64, 131072], P(None, 'energy', 'section')
Inputs may be any that keep to these rules, and one draw needn't show every extreme that they name: left_orbital[p] and right_orbital[p] are orbitals of section p // 8192: both lie from (p // 8192) * 384 to that plus 1 * 384 - 1, and they differ by at most 24.
All inputs are finite; a program needn't handle non-finite values.
Results may differ from a plain program's by a relative error of at most 0.022.
Values may be sent and summed in bfloat16 or wider, within the bound.
No kernel may reach another device: no remote copies, remote signals or barrier semaphores. Data moves between devices by JAX's collectives and lax.ppermute only.
A program may use at most 64 MiB of HBM per device.

v0:
```python
import jax
import jax.numpy as jnp
from jax import lax
from jax.sharding import PartitionSpec as P


def passed_along(value, axis, steps):
    count = lax.axis_size(axis)
    leading, last = (max(0, -steps), min(count, count - steps))
    return lax.ppermute(value, axis, [(source, source + steps) for source in range(leading, last)])


def as_sent(shard):

    def short(part):
        return part.astype(jnp.bfloat16) if part.dtype == jnp.float32 else part

    return jax.tree.map(short, shard)


def complex_product(matrix, columns, adjoint):
    half = columns.shape[1] // 2
    if adjoint:
        product = jnp.einsum("cji,jn->cin", matrix, columns, preferred_element_type=jnp.float32)
        real_part = product[0, :, :half] + product[1, :, half:]
        imag_part = product[0, :, half:] - product[1, :, :half]
    else:
        product = jnp.einsum("cij,jn->cin", matrix, columns, preferred_element_type=jnp.float32)
        real_part = product[0, :, :half] - product[1, :, half:]
        imag_part = product[0, :, half:] + product[1, :, :half]
    return jnp.concatenate([real_part, imag_part], axis=1)


def as_pair(joined):
    width = joined.shape[0]
    return jnp.stack([joined[:, :width], joined[:, width:]])


def section_maps(blocks, forward_src, backward_src):
    count = blocks.shape[0]
    composite = jnp.concatenate([blocks[0, 0], blocks[0, 1]], axis=1)
    forward_part = forward_src[0]
    backward_part = backward_src[count - 1]
    return (composite, forward_part, backward_part)


def forward_pass(blocks, sources, start_state):
    current = start_state
    current = (complex_product(blocks[0], current, False) + sources[0]).astype(jnp.bfloat16)
    results = [current]
    return jnp.stack(results)


def backward_pass(blocks, sources, start_state):
    current = start_state
    results = [None] * blocks.shape[0]
    current = (complex_product(blocks[0], current, True) + sources[0]).astype(jnp.bfloat16)
    results[0] = current
    return jnp.stack(results)


def apply_forward(matrix, current, vector):
    return (complex_product(as_pair(matrix), current, False) + vector).astype(jnp.bfloat16)


def apply_backward(matrix, current, vector):
    return (complex_product(as_pair(matrix), current, True) + vector).astype(jnp.bfloat16)


def lesser(field_rows, adjoint_rows, left_index, right_index, modes):
    left_rows = jnp.take(field_rows, left_index, axis=0)
    right_rows = jnp.take(adjoint_rows, right_index, axis=0)
    first_real = jnp.einsum(
        "pr,pr->p", left_rows[:, :modes], right_rows[:, :modes], preferred_element_type=jnp.float32
    )
    first_imag = jnp.einsum(
        "pr,pr->p", left_rows[:, modes:], right_rows[:, modes:], preferred_element_type=jnp.float32
    )
    cross_one = jnp.einsum(
        "pr,pr->p", left_rows[:, modes:], right_rows[:, :modes], preferred_element_type=jnp.float32
    )
    cross_two = jnp.einsum(
        "pr,pr->p", left_rows[:, :modes], right_rows[:, modes:], preferred_element_type=jnp.float32
    )
    return jnp.stack([first_real + first_imag, cross_one - cross_two]) * modes ** (-0.5)


def shifted_sum(portion, own_energy, phonon_shift, coupling):
    count = portion.shape[1]
    positions = jnp.arange(count, dtype=jnp.int32)
    summed = jnp.zeros((portion.shape[0], own_energy.shape[0], portion.shape[2]), jnp.float32)
    for k in range(phonon_shift.shape[0]):
        selector = (positions[None, :] == (own_energy - phonon_shift[k])[:, None]).astype(
            jnp.float32
        )
        moved = jnp.einsum("ef,cfp->cep", selector, portion, precision=lax.Precision.HIGHEST)
        summed = summed + coupling[k][None, None, :] * moved
    return summed


def on_device(
    propagator, forward_source, backward_source, left_orbital, right_orbital, phonon_shift, coupling
):
    slab_count = propagator.shape[1]
    orbitals = propagator.shape[3]
    modes = forward_source.shape[3] // 2
    composite, forward_part, backward_part = jax.vmap(section_maps)(
        propagator, forward_source, backward_source
    )
    relay_turns = lax.axis_size("section") - 1

    def forward_turn(turn_index, current):
        outgoing = jax.vmap(apply_forward)(composite, current, forward_part)
        return passed_along(outgoing, "section", 1)

    def backward_turn(turn_index, current):
        outgoing = jax.vmap(apply_backward)(composite, current, backward_part)
        return passed_along(outgoing, "section", -1)

    incoming = lax.fori_loop(0, relay_turns, forward_turn, jnp.zeros_like(forward_part))
    returning = lax.fori_loop(0, relay_turns, backward_turn, jnp.zeros_like(backward_part))
    fields = jax.vmap(forward_pass)(propagator, forward_source, incoming)
    adjoints = jax.vmap(backward_pass)(propagator, backward_source, returning)
    section_base = lax.axis_index("section") * (slab_count * orbitals)
    left_local = left_orbital - section_base
    right_local = right_orbital - section_base

    def pair_values(field, adjoint_field):
        return lesser(
            field.reshape(-1, 2 * modes),
            adjoint_field.reshape(-1, 2 * modes),
            left_local,
            right_local,
            modes,
        )

    lesser_part = jnp.transpose(jax.vmap(pair_values)(fields, adjoints), (1, 0, 2))
    regrouped = lax.all_to_all(
        as_sent(lesser_part), "energy", split_axis=2, concat_axis=1, tiled=True
    ).astype(lesser_part.dtype)
    block_pairs = regrouped.shape[2]
    all_count = regrouped.shape[1]
    block_start = lax.axis_index("energy") * block_pairs
    coupling_block = lax.dynamic_slice_in_dim(coupling, block_start, block_pairs, 1)
    block_result = shifted_sum(
        regrouped, jnp.arange(all_count, dtype=jnp.int32), phonon_shift, coupling_block
    )
    self_energy = lax.all_to_all(
        as_sent(block_result), "energy", split_axis=1, concat_axis=2, tiled=True
    ).astype(block_result.dtype)
    return self_energy


def solution(mesh):
    placed = (
        P("energy", "section", None, None, None),
        P("energy", "section", None, None),
        P("energy", "section", None, None),
        P("section"),
        P("section"),
        P(),
        P(None, "section"),
    )
    return jax.shard_map(
        on_device,
        mesh=mesh,
        in_specs=placed,
        out_specs=P(None, "energy", "section"),
        check_vma=False,
    )
```

profile of v0, /device:TPU:32, one launch (start us, length us, event | category | flops | bytes accessed | tf_op | source)
XLA Modules:
  0.0 436.5 jit_solution(531175616480129732)
XLA Ops:
  3.9 109.0 %while.25 = (s32[]{:T(128)}, bf16[1,384,128]{1,2,0:T(8,128)(2,1)S(1)}, bf16[2,1,384,384]{3,2,0,1:T(8,128)(2,1)S(1)}, bf16[1,384,128]{1,2,0:T(8,128)(2,1)S(1)}, s32[]{:T(128)}) while((s32[]{:T(128)}, bf16[1,384,128]{1,2,0:T(8,128)(2,1)S(1)}, bf16[2,1,384,384]{3,2,0,1:T(8,128)(2,1)S(1)}, bf16[1,384,128]{1,2,0:T(8,128)(2,1)S(1)}, s32[]{:T(128)}) %tuple.81), condition=%wide.region_3.5_spmd, body=%wide.region_2.4_spmd.sunk | while | flops 75743232 | bytes 2457701 | solution.py:121
  6.2 2.2 collective-permute-done.1
  8.7 4.9 %collective-permute-start.1 = (bf16[1,384,128]{1,2,0:T(8,128)(2,1)S(1)}, bf16[1,384,128]{1,2,0:T(8,128)(2,1)S(1)}, u32[]{:S(2)}, u32[]{:S(2)}) collective-permute-start(bf16[1,384,128]{1,2,0:T(8,128)(2,1)S(1)} %fusion.94), channel_id=1, source_target_pairs={{1,0},{2,1},{3,2},{4,3},{5,4},{6,5},{7,6},{8,7},{9,8},{10,9},{11,1... | collective-permute-start | bytes 294920 | tf_op jit(solution)/shard_map/while/body/eval_jaxpr/ppermute | solution.py:10
  13.6 2.2 collective-permute-done.1
  16.1 4.9 %collective-permute-start.1 = (bf16[1,384,128]{1,2,0:T(8,128)(2,1)S(1)}, bf16[1,384,128]{1,2,0:T(8,128)(2,1)S(1)}, u32[]{:S(2)}, u32[]{:S(2)}) collective-permute-start(bf16[1,384,128]{1,2,0:T(8,128)(2,1)S(1)} %fusion.94), channel_id=1, source_target_pairs={{1,0},{2,1},{3,2},{4,3},{5,4},{6,5},{7,6},{8,7},{9,8},{10,9},{11,1... | collective-permute-start | bytes 294920 | tf_op jit(solution)/shard_map/while/body/eval_jaxpr/ppermute | solution.py:10
  21.1 2.2 collective-permute-done.1
  23.6 4.9 %collective-permute-start.1 = (bf16[1,384,128]{1,2,0:T(8,128)(2,1)S(1)}, bf16[1,384,128]{1,2,0:T(8,128)(2,1)S(1)}, u32[]{:S(2)}, u32[]{:S(2)}) collective-permute-start(bf16[1,384,128]{1,2,0:T(8,128)(2,1)S(1)} %fusion.94), channel_id=1, source_target_pairs={{1,0},{2,1},{3,2},{4,3},{5,4},{6,5},{7,6},{8,7},{9,8},{10,9},{11,1... | collective-permute-start | bytes 294920 | tf_op jit(solution)/shard_map/while/body/eval_jaxpr/ppermute | solution.py:10
  28.6 2.2 collective-permute-done.1
  31.1 4.9 %collective-permute-start.1 = (bf16[1,384,128]{1,2,0:T(8,128)(2,1)S(1)}, bf16[1,384,128]{1,2,0:T(8,128)(2,1)S(1)}, u32[]{:S(2)}, u32[]{:S(2)}) collective-permute-start(bf16[1,384,128]{1,2,0:T(8,128)(2,1)S(1)} %fusion.94), channel_id=1, source_target_pairs={{1,0},{2,1},{3,2},{4,3},{5,4},{6,5},{7,6},{8,7},{9,8},{10,9},{11,1... | collective-permute-start | bytes 294920 | tf_op jit(solution)/shard_map/while/body/eval_jaxpr/ppermute | solution.py:10
  36.0 2.2 collective-permute-done.1
  38.5 4.9 %collective-permute-start.1 = (bf16[1,384,128]{1,2,0:T(8,128)(2,1)S(1)}, bf16[1,384,128]{1,2,0:T(8,128)(2,1)S(1)}, u32[]{:S(2)}, u32[]{:S(2)}) collective-permute-start(bf16[1,384,128]{1,2,0:T(8,128)(2,1)S(1)} %fusion.94), channel_id=1, source_target_pairs={{1,0},{2,1},{3,2},{4,3},{5,4},{6,5},{7,6},{8,7},{9,8},{10,9},{11,1... | collective-permute-start | bytes 294920 | tf_op jit(solution)/shard_map/while/body/eval_jaxpr/ppermute | solution.py:10
  43.5 2.2 collective-permute-done.1
  46.0 5.0 %collective-permute-start.1 = (bf16[1,384,128]{1,2,0:T(8,128)(2,1)S(1)}, bf16[1,384,128]{1,2,0:T(8,128)(2,1)S(1)}, u32[]{:S(2)}, u32[]{:S(2)}) collective-permute-start(bf16[1,384,128]{1,2,0:T(8,128)(2,1)S(1)} %fusion.94), channel_id=1, source_target_pairs={{1,0},{2,1},{3,2},{4,3},{5,4},{6,5},{7,6},{8,7},{9,8},{10,9},{11,1... | collective-permute-start | bytes 294920 | tf_op jit(solution)/shard_map/while/body/eval_jaxpr/ppermute | solution.py:10
  51.0 2.2 collective-permute-done.1
  53.5 4.9 %collective-permute-start.1 = (bf16[1,384,128]{1,2,0:T(8,128)(2,1)S(1)}, bf16[1,384,128]{1,2,0:T(8,128)(2,1)S(1)}, u32[]{:S(2)}, u32[]{:S(2)}) collective-permute-start(bf16[1,384,128]{1,2,0:T(8,128)(2,1)S(1)} %fusion.94), channel_id=1, source_target_pairs={{1,0},{2,1},{3,2},{4,3},{5,4},{6,5},{7,6},{8,7},{9,8},{10,9},{11,1... | collective-permute-start | bytes 294920 | tf_op jit(solution)/shard_map/while/body/eval_jaxpr/ppermute | solution.py:10
  58.4 2.2 collective-permute-done.1
  60.9 5.0 %collective-permute-start.1 = (bf16[1,384,128]{1,2,0:T(8,128)(2,1)S(1)}, bf16[1,384,128]{1,2,0:T(8,128)(2,1)S(1)}, u32[]{:S(2)}, u32[]{:S(2)}) collective-permute-start(bf16[1,384,128]{1,2,0:T(8,128)(2,1)S(1)} %fusion.94), channel_id=1, source_target_pairs={{1,0},{2,1},{3,2},{4,3},{5,4},{6,5},{7,6},{8,7},{9,8},{10,9},{11,1... | collective-permute-start | bytes 294920 | tf_op jit(solution)/shard_map/while/body/eval_jaxpr/ppermute | solution.py:10
  65.9 2.2 collective-permute-done.1
  68.4 4.9 %collective-permute-start.1 = (bf16[1,384,128]{1,2,0:T(8,128)(2,1)S(1)}, bf16[1,384,128]{1,2,0:T(8,128)(2,1)S(1)}, u32[]{:S(2)}, u32[]{:S(2)}) collective-permute-start(bf16[1,384,128]{1,2,0:T(8,128)(2,1)S(1)} %fusion.94), channel_id=1, source_target_pairs={{1,0},{2,1},{3,2},{4,3},{5,4},{6,5},{7,6},{8,7},{9,8},{10,9},{11,1... | collective-permute-start | bytes 294920 | tf_op jit(solution)/shard_map/while/body/eval_jaxpr/ppermute | solution.py:10
  73.4 2.2 collective-permute-done.1
  75.9 5.0 %collective-permute-start.1 = (bf16[1,384,128]{1,2,0:T(8,128)(2,1)S(1)}, bf16[1,384,128]{1,2,0:T(8,128)(2,1)S(1)}, u32[]{:S(2)}, u32[]{:S(2)}) collective-permute-start(bf16[1,384,128]{1,2,0:T(8,128)(2,1)S(1)} %fusion.94), channel_id=1, source_target_pairs={{1,0},{2,1},{3,2},{4,3},{5,4},{6,5},{7,6},{8,7},{9,8},{10,9},{11,1... | collective-permute-start | bytes 294920 | tf_op jit(solution)/shard_map/while/body/eval_jaxpr/ppermute | solution.py:10
  80.8 2.2 collective-permute-done.1
  83.4 4.9 %collective-permute-start.1 = (bf16[1,384,128]{1,2,0:T(8,128)(2,1)S(1)}, bf16[1,384,128]{1,2,0:T(8,128)(2,1)S(1)}, u32[]{:S(2)}, u32[]{:S(2)}) collective-permute-start(bf16[1,384,128]{1,2,0:T(8,128)(2,1)S(1)} %fusion.94), channel_id=1, source_target_pairs={{1,0},{2,1},{3,2},{4,3},{5,4},{6,5},{7,6},{8,7},{9,8},{10,9},{11,1... | collective-permute-start | bytes 294920 | tf_op jit(solution)/shard_map/while/body/eval_jaxpr/ppermute | solution.py:10
  88.3 2.2 collective-permute-done.1
  90.8 5.0 %collective-permute-start.1 = (bf16[1,384,128]{1,2,0:T(8,128)(2,1)S(1)}, bf16[1,384,128]{1,2,0:T(8,128)(2,1)S(1)}, u32[]{:S(2)}, u32[]{:S(2)}) collective-permute-start(bf16[1,384,128]{1,2,0:T(8,128)(2,1)S(1)} %fusion.94), channel_id=1, source_target_pairs={{1,0},{2,1},{3,2},{4,3},{5,4},{6,5},{7,6},{8,7},{9,8},{10,9},{11,1... | collective-permute-start | bytes 294920 | tf_op jit(solution)/shard_map/while/body/eval_jaxpr/ppermute | solution.py:10
  95.8 2.2 collective-permute-done.1
  98.3 4.9 %collective-permute-start.1 = (bf16[1,384,128]{1,2,0:T(8,128)(2,1)S(1)}, bf16[1,384,128]{1,2,0:T(8,128)(2,1)S(1)}, u32[]{:S(2)}, u32[]{:S(2)}) collective-permute-start(bf16[1,384,128]{1,2,0:T(8,128)(2,1)S(1)} %fusion.94), channel_id=1, source_target_pairs={{1,0},{2,1},{3,2},{4,3},{5,4},{6,5},{7,6},{8,7},{9,8},{10,9},{11,1... | collective-permute-start | bytes 294920 | tf_op jit(solution)/shard_map/while/body/eval_jaxpr/ppermute | solution.py:10
  103.3 2.2 collective-permute-done.1
  105.8 5.0 %collective-permute-start.1 = (bf16[1,384,128]{1,2,0:T(8,128)(2,1)S(1)}, bf16[1,384,128]{1,2,0:T(8,128)(2,1)S(1)}, u32[]{:S(2)}, u32[]{:S(2)}) collective-permute-start(bf16[1,384,128]{1,2,0:T(8,128)(2,1)S(1)} %fusion.94), channel_id=1, source_target_pairs={{1,0},{2,1},{3,2},{4,3},{5,4},{6,5},{7,6},{8,7},{9,8},{10,9},{11,1... | collective-permute-start | bytes 294920 | tf_op jit(solution)/shard_map/while/body/eval_jaxpr/ppermute | solution.py:10
  110.7 2.2 collective-permute-done.1
  114.0 113.0 %while.24 = (s32[]{:T(128)}, bf16[1,384,128]{1,2,0:T(8,128)(2,1)S(1)}, bf16[2,1,384,384]{3,2,0,1:T(8,128)(2,1)S(1)}, bf16[1,384,128]{1,2,0:T(8,128)(2,1)S(1)}, s32[]{:T(128)}) while((s32[]{:T(128)}, bf16[1,384,128]{1,2,0:T(8,128)(2,1)S(1)}, bf16[2,1,384,384]{3,2,0,1:T(8,128)(2,1)S(1)}, bf16[1,384,128]{1,2,0:T(8,128)(2,1)S(1)}, s32[]{:T(128)}) %tuple.82), condition=%wide.region_1.0_spmd, body=%wide.region_0.0_spmd.sunk | while | flops 75743232 | bytes 2457701 | solution.py:120
  116.3 5.3 %collective-permute-done = bf16[1,384,128]{1,2,0:T(8,128)(2,1)S(1)} collective-permute-done((bf16[1,384,128]{1,2,0:T(8,128)(2,1)S(1)}, bf16[1,384,128]{1,2,0:T(8,128)(2,1)S(1)}, u32[]{:S(2)}, u32[]{:S(2)}) %collective-permute-start) | collective-permute-done | bytes 98336 | tf_op jit(solution)/shard_map/while/body/eval_jaxpr/ppermute | solution.py:10
  122.0 1.9 collective-permute-start
  123.9 5.2 %collective-permute-done = bf16[1,384,128]{1,2,0:T(8,128)(2,1)S(1)} collective-permute-done((bf16[1,384,128]{1,2,0:T(8,128)(2,1)S(1)}, bf16[1,384,128]{1,2,0:T(8,128)(2,1)S(1)}, u32[]{:S(2)}, u32[]{:S(2)}) %collective-permute-start) | collective-permute-done | bytes 98336 | tf_op jit(solution)/shard_map/while/body/eval_jaxpr/ppermute | solution.py:10
  131.4 5.2 %collective-permute-done = bf16[1,384,128]{1,2,0:T(8,128)(2,1)S(1)} collective-permute-done((bf16[1,384,128]{1,2,0:T(8,128)(2,1)S(1)}, bf16[1,384,128]{1,2,0:T(8,128)(2,1)S(1)}, u32[]{:S(2)}, u32[]{:S(2)}) %collective-permute-start) | collective-permute-done | bytes 98336 | tf_op jit(solution)/shard_map/while/body/eval_jaxpr/ppermute | solution.py:10
  138.9 5.2 %collective-permute-done = bf16[1,384,128]{1,2,0:T(8,128)(2,1)S(1)} collective-permute-done((bf16[1,384,128]{1,2,0:T(8,128)(2,1)S(1)}, bf16[1,384,128]{1,2,0:T(8,128)(2,1)S(1)}, u32[]{:S(2)}, u32[]{:S(2)}) %collective-permute-start) | collective-permute-done | bytes 98336 | tf_op jit(solution)/shard_map/while/body/eval_jaxpr/ppermute | solution.py:10
  146.5 5.2 %collective-permute-done = bf16[1,384,128]{1,2,0:T(8,128)(2,1)S(1)} collective-permute-done((bf16[1,384,128]{1,2,0:T(8,128)(2,1)S(1)}, bf16[1,384,128]{1,2,0:T(8,128)(2,1)S(1)}, u32[]{:S(2)}, u32[]{:S(2)}) %collective-permute-start) | collective-permute-done | bytes 98336 | tf_op jit(solution)/shard_map/while/body/eval_jaxpr/ppermute | solution.py:10
  154.0 5.2 %collective-permute-done = bf16[1,384,128]{1,2,0:T(8,128)(2,1)S(1)} collective-permute-done((bf16[1,384,128]{1,2,0:T(8,128)(2,1)S(1)}, bf16[1,384,128]{1,2,0:T(8,128)(2,1)S(1)}, u32[]{:S(2)}, u32[]{:S(2)}) %collective-permute-start) | collective-permute-done | bytes 98336 | tf_op jit(solution)/shard_map/while/body/eval_jaxpr/ppermute | solution.py:10
  159.6 1.9 collective-permute-start
  161.5 5.2 %collective-permute-done = bf16[1,384,128]{1,2,0:T(8,128)(2,1)S(1)} collective-permute-done((bf16[1,384,128]{1,2,0:T(8,128)(2,1)S(1)}, bf16[1,384,128]{1,2,0:T(8,128)(2,1)S(1)}, u32[]{:S(2)}, u32[]{:S(2)}) %collective-permute-start) | collective-permute-done | bytes 98336 | tf_op jit(solution)/shard_map/while/body/eval_jaxpr/ppermute | solution.py:10
  169.1 5.2 %collective-permute-done = bf16[1,384,128]{1,2,0:T(8,128)(2,1)S(1)} collective-permute-done((bf16[1,384,128]{1,2,0:T(8,128)(2,1)S(1)}, bf16[1,384,128]{1,2,0:T(8,128)(2,1)S(1)}, u32[]{:S(2)}, u32[]{:S(2)}) %collective-permute-start) | collective-permute-done | bytes 98336 | tf_op jit(solution)/shard_map/while/body/eval_jaxpr/ppermute | solution.py:10
  174.6 1.9 collective-permute-start
  176.6 5.2 %collective-permute-done = bf16[1,384,128]{1,2,0:T(8,128)(2,1)S(1)} collective-permute-done((bf16[1,384,128]{1,2,0:T(8,128)(2,1)S(1)}, bf16[1,384,128]{1,2,0:T(8,128)(2,1)S(1)}, u32[]{:S(2)}, u32[]{:S(2)}) %collective-permute-start) | collective-permute-done | bytes 98336 | tf_op jit(solution)/shard_map/while/body/eval_jaxpr/ppermute | solution.py:10
  184.1 5.2 %collective-permute-done = bf16[1,384,128]{1,2,0:T(8,128)(2,1)S(1)} collective-permute-done((bf16[1,384,128]{1,2,0:T(8,128)(2,1)S(1)}, bf16[1,384,128]{1,2,0:T(8,128)(2,1)S(1)}, u32[]{:S(2)}, u32[]{:S(2)}) %collective-permute-start) | collective-permute-done | bytes 98336 | tf_op jit(solution)/shard_map/while/body/eval_jaxpr/ppermute | solution.py:10
  191.6 5.2 %collective-permute-done = bf16[1,384,128]{1,2,0:T(8,128)(2,1)S(1)} collective-permute-done((bf16[1,384,128]{1,2,0:T(8,128)(2,1)S(1)}, bf16[1,384,128]{1,2,0:T(8,128)(2,1)S(1)}, u32[]{:S(2)}, u32[]{:S(2)}) %collective-permute-start) | collective-permute-done | bytes 98336 | tf_op jit(solution)/shard_map/while/body/eval_jaxpr/ppermute | solution.py:10
  199.2 5.2 %collective-permute-done = bf16[1,384,128]{1,2,0:T(8,128)(2,1)S(1)} collective-permute-done((bf16[1,384,128]{1,2,0:T(8,128)(2,1)S(1)}, bf16[1,384,128]{1,2,0:T(8,128)(2,1)S(1)}, u32[]{:S(2)}, u32[]{:S(2)}) %collective-permute-start) | collective-permute-done | bytes 98336 | tf_op jit(solution)/shard_map/while/body/eval_jaxpr/ppermute | solution.py:10
  204.7 1.9 collective-permute-start
  206.7 5.2 %collective-permute-done = bf16[1,384,128]{1,2,0:T(8,128)(2,1)S(1)} collective-permute-done((bf16[1,384,128]{1,2,0:T(8,128)(2,1)S(1)}, bf16[1,384,128]{1,2,0:T(8,128)(2,1)S(1)}, u32[]{:S(2)}, u32[]{:S(2)}) %collective-permute-start) | collective-permute-done | bytes 98336 | tf_op jit(solution)/shard_map/while/body/eval_jaxpr/ppermute | solution.py:10
  214.2 5.2 %collective-permute-done = bf16[1,384,128]{1,2,0:T(8,128)(2,1)S(1)} collective-permute-done((bf16[1,384,128]{1,2,0:T(8,128)(2,1)S(1)}, bf16[1,384,128]{1,2,0:T(8,128)(2,1)S(1)}, u32[]{:S(2)}, u32[]{:S(2)}) %collective-permute-start) | collective-permute-done | bytes 98336 | tf_op jit(solution)/shard_map/while/body/eval_jaxpr/ppermute | solution.py:10
  219.8 1.9 collective-permute-start
  221.7 5.2 %collective-permute-done = bf16[1,384,128]{1,2,0:T(8,128)(2,1)S(1)} collective-permute-done((bf16[1,384,128]{1,2,0:T(8,128)(2,1)S(1)}, bf16[1,384,128]{1,2,0:T(8,128)(2,1)S(1)}, u32[]{:S(2)}, u32[]{:S(2)}) %collective-permute-start) | collective-permute-done | bytes 98336 | tf_op jit(solution)/shard_map/while/body/eval_jaxpr/ppermute | solution.py:10
  227.5 29.2 %gather_fusion.1 = bf16[8192,128]{1,0:T(8,128)(2,1)} fusion(bf16[384,128]{1,0:T(8,128)(2,1)S(1)} %copy.30, s32[8192]{0:T(1024)S(1)} %get-tuple-element.173), kind=kCustom, calls=%fused_computation.1.clone | custom fusion | bytes 4227072 | tf_op jit(solution)/shard_map/vmap(jit(_take))/gather | solution.py:72
  256.7 5.8 %bitcast_select_fusion = bf16[1,8192,128]{2,1,0:T(8,128)(2,1)S(1)} fusion(bf16[8192,128]{1,0:T(8,128)(2,1)} %gather_fusion.1, pred[8192]{0:T(1024)(128)(4,1)S(1)} %get-tuple-element.170), kind=kLoop, calls=%fused_computation.32 | loop fusion | flops 1048576 | bytes 4202496 | tf_op jit(solution)/shard_map/vmap(jit(_take))/select_n | solution.py:72
  262.5 29.2 %gather_fusion = bf16[8192,128]{1,0:T(8,128)(2,1)} fusion(bf16[384,128]{1,0:T(8,128)(2,1)S(1)} %copy.28, s32[8192]{0:T(1024)S(1)} %get-tuple-element.172), kind=kCustom, calls=%fused_computation.clone | custom fusion | bytes 4227072 | tf_op jit(solution)/shard_map/vmap(jit(_take))/gather | solution.py:71
  291.7 5.8 %bitcast_select_fusion.1 = bf16[1,8192,128]{2,1,0:T(8,128)(2,1)S(1)} fusion(bf16[8192,128]{1,0:T(8,128)(2,1)} %gather_fusion, pred[8192]{0:T(1024)(128)(4,1)S(1)} %get-tuple-element.171), kind=kLoop, calls=%fused_computation.33 | loop fusion | flops 1048576 | bytes 4202496 | tf_op jit(solution)/shard_map/vmap(jit(_take))/select_n | solution.py:71
  297.6 6.1 %fusion.12 = (f32[8192]{0:T(1024)S(1)}, f32[8192]{0:T(1024)S(1)}, f32[8192]{0:T(1024)S(1)}, f32[8192]{0:T(1024)S(1)}) fusion(bf16[1,8192,128]{2,1,0:T(8,128)(2,1)S(1)} %bitcast_select_fusion.1, bf16[1,8192,128]{2,1,0:T(8,128)(2,1)S(1)} %bitcast_select_fusion), kind=kLoop, calls=%fused_computation.26 | loop fusion | flops 6258688 | bytes 4325376 | tf_op jit(solution)/shard_map/vmap(pr,pr->p)/dot_general | solution.py:76
  303.8 6.8 %copy.33 = bf16[2,1,8192]{0,1,2:T(2,128)(2,1)} copy(bf16[2,1,8192]{2,0,1:T(2,128)(2,1)S(1)} %fusion.35) | data formatting | bytes 65536 | tf_op jit(solution)/shard_map/convert_element_type | solution.py:16
  311.1 45.4 %reduce.8 = bf16[8192,2]{1,0:T(8,128)(2,1)S(1)} reduce(bf16[8192,1,2]{2,1,0:T(2,128)(2,1)} %bitcast.192, bf16[]{:T(256)} %broadcast.86), dimensions={1}, to_apply=%bitcast.174.reduce_sub_computation | reduce | bytes 65538
  356.6 3.8 reshape.584
  360.3 22.2 %all-to-all-start = ((bf16[64,2,128]{2,1,0:T(2,128)(2,1)}), bf16[64,2,128]{2,1,0:T(2,128)(2,1)S(1)}, u32[]{:S(2)}, u32[]{:S(2)}) async-start(bf16[64,2,128]{2,1,0:T(2,128)(2,1)} %reshape.584), calls=%async_computation | async-start | bytes 65536 | tf_op jit(solution)/shard_map/all_to_all | solution.py:138
  388.4 8.6 %all-to-all-done = bf16[64,2,128]{2,1,0:T(2,128)(2,1)S(1)} async-done(((bf16[64,2,128]{2,1,0:T(2,128)(2,1)}), bf16[64,2,128]{2,1,0:T(2,128)(2,1)S(1)}, u32[]{:S(2)}, u32[]{:S(2)}) %all-to-all-start) | async-done | bytes 32800 | tf_op jit(solution)/shard_map/all_to_all | solution.py:138
  396.9 8.3 %reshape.585 = bf16[8192,1,2]{2,1,0:T(2,128)(2,1)} reshape(bf16[64,2,128]{2,1,0:T(2,128)(2,1)S(1)} %all-to-all-done) | data formatting | bytes 65536
  405.2 8.1 %copy.34 = bf16[2,1,8192]{2,0,1:T(2,128)(2,1)S(1)} copy(bf16[2,1,8192]{0,1,2:T(2,128)(2,1)} %bitcast.193) | data formatting | bytes 65536 | tf_op jit(solution)/shard_map/all_to_all | solution.py:138
  415.0 20.8 %all_to_all.21 = bf16[2,64,128]{2,0,1:T(2,128)(2,1)S(1)} all-to-all(bf16[2,64,128]{2,0,1:T(2,128)(2,1)S(1)} %copy.35), channel_id=1, replica_groups=mesh['energy'=64,'section'=16] {'energy'}, dimensions={1} | all-to-all | bytes 65536 | tf_op jit(solution)/shard_map/all_to_all | solution.py:148
  (151 shorter events, 45.3 us)
Async XLA Ops:
  0.0 382.6 %copy-start = (f32[8,8192]{1,0:T(8,128)S(1)}, f32[8,8192]{1,0:T(8,128)}, u32[]{:S(2)}) copy-start(f32[8,8192]{1,0:T(8,128)} %param.19) | copy-start | bytes 786436
  3.9 109.0 %copy-start.1 = (bf16[1,1,2,384,384]{4,3,2,1,0:T(8,128)(2,1)S(1)}, bf16[1,1,2,384,384]{4,3,2,1,0:T(8,128)(2,1)}, u32[]{:S(2)}) copy-start(bf16[1,1,2,384,384]{4,3,2,1,0:T(8,128)(2,1)} %param.13) | copy-start | bytes 1769476
  4.2 4.1 collective-permute-start.1
  8.7 7.1 %collective-permute-start.1 = (bf16[1,384,128]{1,2,0:T(8,128)(2,1)S(1)}, bf16[1,384,128]{1,2,0:T(8,128)(2,1)S(1)}, u32[]{:S(2)}, u32[]{:S(2)}) collective-permute-start(bf16[1,384,128]{1,2,0:T(8,128)(2,1)S(1)} %fusion.94), channel_id=1, source_target_pairs={{1,0},{2,1},{3,2},{4,3},{5,4},{6,5},{7,6},{8,7},{9,8},{10,9},{11,1... | collective-permute-start | bytes 294920 | tf_op jit(solution)/shard_map/while/body/eval_jaxpr/ppermute | solution.py:10
  16.1 7.1 %collective-permute-start.1 = (bf16[1,384,128]{1,2,0:T(8,128)(2,1)S(1)}, bf16[1,384,128]{1,2,0:T(8,128)(2,1)S(1)}, u32[]{:S(2)}, u32[]{:S(2)}) collective-permute-start(bf16[1,384,128]{1,2,0:T(8,128)(2,1)S(1)} %fusion.94), channel_id=1, source_target_pairs={{1,0},{2,1},{3,2},{4,3},{5,4},{6,5},{7,6},{8,7},{9,8},{10,9},{11,1... | collective-permute-start | bytes 294920 | tf_op jit(solution)/shard_map/while/body/eval_jaxpr/ppermute | solution.py:10
  23.6 7.1 %collective-permute-start.1 = (bf16[1,384,128]{1,2,0:T(8,128)(2,1)S(1)}, bf16[1,384,128]{1,2,0:T(8,128)(2,1)S(1)}, u32[]{:S(2)}, u32[]{:S(2)}) collective-permute-start(bf16[1,384,128]{1,2,0:T(8,128)(2,1)S(1)} %fusion.94), channel_id=1, source_target_pairs={{1,0},{2,1},{3,2},{4,3},{5,4},{6,5},{7,6},{8,7},{9,8},{10,9},{11,1... | collective-permute-start | bytes 294920 | tf_op jit(solution)/shard_map/while/body/eval_jaxpr/ppermute | solution.py:10
  31.1 7.1 %collective-permute-start.1 = (bf16[1,384,128]{1,2,0:T(8,128)(2,1)S(1)}, bf16[1,384,128]{1,2,0:T(8,128)(2,1)S(1)}, u32[]{:S(2)}, u32[]{:S(2)}) collective-permute-start(bf16[1,384,128]{1,2,0:T(8,128)(2,1)S(1)} %fusion.94), channel_id=1, source_target_pairs={{1,0},{2,1},{3,2},{4,3},{5,4},{6,5},{7,6},{8,7},{9,8},{10,9},{11,1... | collective-permute-start | bytes 294920 | tf_op jit(solution)/shard_map/while/body/eval_jaxpr/ppermute | solution.py:10
  38.5 7.1 %collective-permute-start.1 = (bf16[1,384,128]{1,2,0:T(8,128)(2,1)S(1)}, bf16[1,384,128]{1,2,0:T(8,128)(2,1)S(1)}, u32[]{:S(2)}, u32[]{:S(2)}) collective-permute-start(bf16[1,384,128]{1,2,0:T(8,128)(2,1)S(1)} %fusion.94), channel_id=1, source_target_pairs={{1,0},{2,1},{3,2},{4,3},{5,4},{6,5},{7,6},{8,7},{9,8},{10,9},{11,1... | collective-permute-start | bytes 294920 | tf_op jit(solution)/shard_map/while/body/eval_jaxpr/ppermute | solution.py:10
  46.0 7.1 %collective-permute-start.1 = (bf16[1,384,128]{1,2,0:T(8,128)(2,1)S(1)}, bf16[1,384,128]{1,2,0:T(8,128)(2,1)S(1)}, u32[]{:S(2)}, u32[]{:S(2)}) collective-permute-start(bf16[1,384,128]{1,2,0:T(8,128)(2,1)S(1)} %fusion.94), channel_id=1, source_target_pairs={{1,0},{2,1},{3,2},{4,3},{5,4},{6,5},{7,6},{8,7},{9,8},{10,9},{11,1... | collective-permute-start | bytes 294920 | tf_op jit(solution)/shard_map/while/body/eval_jaxpr/ppermute | solution.py:10
  53.5 7.1 %collective-permute-start.1 = (bf16[1,384,128]{1,2,0:T(8,128)(2,1)S(1)}, bf16[1,384,128]{1,2,0:T(8,128)(2,1)S(1)}, u32[]{:S(2)}, u32[]{:S(2)}) collective-permute-start(bf16[1,384,128]{1,2,0:T(8,128)(2,1)S(1)} %fusion.94), channel_id=1, source_target_pairs={{1,0},{2,1},{3,2},{4,3},{5,4},{6,5},{7,6},{8,7},{9,8},{10,9},{11,1... | collective-permute-start | bytes 294920 | tf_op jit(solution)/shard_map/while/body/eval_jaxpr/ppermute | solution.py:10
  60.9 7.2 %collective-permute-start.1 = (bf16[1,384,128]{1,2,0:T(8,128)(2,1)S(1)}, bf16[1,384,128]{1,2,0:T(8,128)(2,1)S(1)}, u32[]{:S(2)}, u32[]{:S(2)}) collective-permute-start(bf16[1,384,128]{1,2,0:T(8,128)(2,1)S(1)} %fusion.94), channel_id=1, source_target_pairs={{1,0},{2,1},{3,2},{4,3},{5,4},{6,5},{7,6},{8,7},{9,8},{10,9},{11,1... | collective-permute-start | bytes 294920 | tf_op jit(solution)/shard_map/while/body/eval_jaxpr/ppermute | solution.py:10
  68.4 7.1 %collective-permute-start.1 = (bf16[1,384,128]{1,2,0:T(8,128)(2,1)S(1)}, bf16[1,384,128]{1,2,0:T(8,128)(2,1)S(1)}, u32[]{:S(2)}, u32[]{:S(2)}) collective-permute-start(bf16[1,384,128]{1,2,0:T(8,128)(2,1)S(1)} %fusion.94), channel_id=1, source_target_pairs={{1,0},{2,1},{3,2},{4,3},{5,4},{6,5},{7,6},{8,7},{9,8},{10,9},{11,1... | collective-permute-start | bytes 294920 | tf_op jit(solution)/shard_map/while/body/eval_jaxpr/ppermute | solution.py:10
  75.9 7.2 %collective-permute-start.1 = (bf16[1,384,128]{1,2,0:T(8,128)(2,1)S(1)}, bf16[1,384,128]{1,2,0:T(8,128)(2,1)S(1)}, u32[]{:S(2)}, u32[]{:S(2)}) collective-permute-start(bf16[1,384,128]{1,2,0:T(8,128)(2,1)S(1)} %fusion.94), channel_id=1, source_target_pairs={{1,0},{2,1},{3,2},{4,3},{5,4},{6,5},{7,6},{8,7},{9,8},{10,9},{11,1... | collective-permute-start | bytes 294920 | tf_op jit(solution)/shard_map/while/body/eval_jaxpr/ppermute | solution.py:10
  83.4 7.1 %collective-permute-start.1 = (bf16[1,384,128]{1,2,0:T(8,128)(2,1)S(1)}, bf16[1,384,128]{1,2,0:T(8,128)(2,1)S(1)}, u32[]{:S(2)}, u32[]{:S(2)}) collective-permute-start(bf16[1,384,128]{1,2,0:T(8,128)(2,1)S(1)} %fusion.94), channel_id=1, source_target_pairs={{1,0},{2,1},{3,2},{4,3},{5,4},{6,5},{7,6},{8,7},{9,8},{10,9},{11,1... | collective-permute-start | bytes 294920 | tf_op jit(solution)/shard_map/while/body/eval_jaxpr/ppermute | solution.py:10
  90.8 7.2 %collective-permute-start.1 = (bf16[1,384,128]{1,2,0:T(8,128)(2,1)S(1)}, bf16[1,384,128]{1,2,0:T(8,128)(2,1)S(1)}, u32[]{:S(2)}, u32[]{:S(2)}) collective-permute-start(bf16[1,384,128]{1,2,0:T(8,128)(2,1)S(1)} %fusion.94), channel_id=1, source_target_pairs={{1,0},{2,1},{3,2},{4,3},{5,4},{6,5},{7,6},{8,7},{9,8},{10,9},{11,1... | collective-permute-start | bytes 294920 | tf_op jit(solution)/shard_map/while/body/eval_jaxpr/ppermute | solution.py:10
  98.3 7.1 %collective-permute-start.1 = (bf16[1,384,128]{1,2,0:T(8,128)(2,1)S(1)}, bf16[1,384,128]{1,2,0:T(8,128)(2,1)S(1)}, u32[]{:S(2)}, u32[]{:S(2)}) collective-permute-start(bf16[1,384,128]{1,2,0:T(8,128)(2,1)S(1)} %fusion.94), channel_id=1, source_target_pairs={{1,0},{2,1},{3,2},{4,3},{5,4},{6,5},{7,6},{8,7},{9,8},{10,9},{11,1... | collective-permute-start | bytes 294920 | tf_op jit(solution)/shard_map/while/body/eval_jaxpr/ppermute | solution.py:10
  105.8 7.2 %collective-permute-start.1 = (bf16[1,384,128]{1,2,0:T(8,128)(2,1)S(1)}, bf16[1,384,128]{1,2,0:T(8,128)(2,1)S(1)}, u32[]{:S(2)}, u32[]{:S(2)}) collective-permute-start(bf16[1,384,128]{1,2,0:T(8,128)(2,1)S(1)} %fusion.94), channel_id=1, source_target_pairs={{1,0},{2,1},{3,2},{4,3},{5,4},{6,5},{7,6},{8,7},{9,8},{10,9},{11,1... | collective-permute-start | bytes 294920 | tf_op jit(solution)/shard_map/while/body/eval_jaxpr/ppermute | solution.py:10
  112.9 0.9 copy-start.2
  114.3 7.2 %collective-permute-start = (bf16[1,384,128]{1,2,0:T(8,128)(2,1)S(1)}, bf16[1,384,128]{1,2,0:T(8,128)(2,1)S(1)}, u32[]{:S(2)}, u32[]{:S(2)}) collective-permute-start(bf16[1,384,128]{1,2,0:T(8,128)(2,1)S(1)} %fusion.90), channel_id=1, source_target_pairs={{0,1},{1,2},{2,3},{3,4},{4,5},{5,6},{6,7},{7,8},{8,9},{9,10},{10,1... | collective-permute-start | bytes 294920 | tf_op jit(solution)/shard_map/while/body/eval_jaxpr/ppermute | solution.py:10
  122.0 7.1 %collective-permute-start = (bf16[1,384,128]{1,2,0:T(8,128)(2,1)S(1)}, bf16[1,384,128]{1,2,0:T(8,128)(2,1)S(1)}, u32[]{:S(2)}, u32[]{:S(2)}) collective-permute-start(bf16[1,384,128]{1,2,0:T(8,128)(2,1)S(1)} %fusion.90), channel_id=1, source_target_pairs={{0,1},{1,2},{2,3},{3,4},{4,5},{5,6},{6,7},{7,8},{8,9},{9,10},{10,1... | collective-permute-start | bytes 294920 | tf_op jit(solution)/shard_map/while/body/eval_jaxpr/ppermute | solution.py:10
  129.5 7.1 %collective-permute-start = (bf16[1,384,128]{1,2,0:T(8,128)(2,1)S(1)}, bf16[1,384,128]{1,2,0:T(8,128)(2,1)S(1)}, u32[]{:S(2)}, u32[]{:S(2)}) collective-permute-start(bf16[1,384,128]{1,2,0:T(8,128)(2,1)S(1)} %fusion.90), channel_id=1, source_target_pairs={{0,1},{1,2},{2,3},{3,4},{4,5},{5,6},{6,7},{7,8},{8,9},{9,10},{10,1... | collective-permute-start | bytes 294920 | tf_op jit(solution)/shard_map/while/body/eval_jaxpr/ppermute | solution.py:10
  137.0 7.1 %collective-permute-start = (bf16[1,384,128]{1,2,0:T(8,128)(2,1)S(1)}, bf16[1,384,128]{1,2,0:T(8,128)(2,1)S(1)}, u32[]{:S(2)}, u32[]{:S(2)}) collective-permute-start(bf16[1,384,128]{1,2,0:T(8,128)(2,1)S(1)} %fusion.90), channel_id=1, source_target_pairs={{0,1},{1,2},{2,3},{3,4},{4,5},{5,6},{6,7},{7,8},{8,9},{9,10},{10,1... | collective-permute-start | bytes 294920 | tf_op jit(solution)/shard_map/while/body/eval_jaxpr/ppermute | solution.py:10
  144.5 7.1 %collective-permute-start = (bf16[1,384,128]{1,2,0:T(8,128)(2,1)S(1)}, bf16[1,384,128]{1,2,0:T(8,128)(2,1)S(1)}, u32[]{:S(2)}, u32[]{:S(2)}) collective-permute-start(bf16[1,384,128]{1,2,0:T(8,128)(2,1)S(1)} %fusion.90), channel_id=1, source_target_pairs={{0,1},{1,2},{2,3},{3,4},{4,5},{5,6},{6,7},{7,8},{8,9},{9,10},{10,1... | collective-permute-start | bytes 294920 | tf_op jit(solution)/shard_map/while/body/eval_jaxpr/ppermute | solution.py:10
  152.1 7.1 %collective-permute-start = (bf16[1,384,128]{1,2,0:T(8,128)(2,1)S(1)}, bf16[1,384,128]{1,2,0:T(8,128)(2,1)S(1)}, u32[]{:S(2)}, u32[]{:S(2)}) collective-permute-start(bf16[1,384,128]{1,2,0:T(8,128)(2,1)S(1)} %fusion.90), channel_id=1, source_target_pairs={{0,1},{1,2},{2,3},{3,4},{4,5},{5,6},{6,7},{7,8},{8,9},{9,10},{10,1... | collective-permute-start | bytes 294920 | tf_op jit(solution)/shard_map/while/body/eval_jaxpr/ppermute | solution.py:10
  159.6 7.1 %collective-permute-start = (bf16[1,384,128]{1,2,0:T(8,128)(2,1)S(1)}, bf16[1,384,128]{1,2,0:T(8,128)(2,1)S(1)}, u32[]{:S(2)}, u32[]{:S(2)}) collective-permute-start(bf16[1,384,128]{1,2,0:T(8,128)(2,1)S(1)} %fusion.90), channel_id=1, source_target_pairs={{0,1},{1,2},{2,3},{3,4},{4,5},{5,6},{6,7},{7,8},{8,9},{9,10},{10,1... | collective-permute-start | bytes 294920 | tf_op jit(solution)/shard_map/while/body/eval_jaxpr/ppermute | solution.py:10
  167.1 7.1 %collective-permute-start = (bf16[1,384,128]{1,2,0:T(8,128)(2,1)S(1)}, bf16[1,384,128]{1,2,0:T(8,128)(2,1)S(1)}, u32[]{:S(2)}, u32[]{:S(2)}) collective-permute-start(bf16[1,384,128]{1,2,0:T(8,128)(2,1)S(1)} %fusion.90), channel_id=1, source_target_pairs={{0,1},{1,2},{2,3},{3,4},{4,5},{5,6},{6,7},{7,8},{8,9},{9,10},{10,1... | collective-permute-start | bytes 294920 | tf_op jit(solution)/shard_map/while/body/eval_jaxpr/ppermute | solution.py:10
  174.6 7.1 %collective-permute-start = (bf16[1,384,128]{1,2,0:T(8,128)(2,1)S(1)}, bf16[1,384,128]{1,2,0:T(8,128)(2,1)S(1)}, u32[]{:S(2)}, u32[]{:S(2)}) collective-permute-start(bf16[1,384,128]{1,2,0:T(8,128)(2,1)S(1)} %fusion.90), channel_id=1, source_target_pairs={{0,1},{1,2},{2,3},{3,4},{4,5},{5,6},{6,7},{7,8},{8,9},{9,10},{10,1... | collective-permute-start | bytes 294920 | tf_op jit(solution)/shard_map/while/body/eval_jaxpr/ppermute | solution.py:10
  182.2 7.1 %collective-permute-start = (bf16[1,384,128]{1,2,0:T(8,128)(2,1)S(1)}, bf16[1,384,128]{1,2,0:T(8,128)(2,1)S(1)}, u32[]{:S(2)}, u32[]{:S(2)}) collective-permute-start(bf16[1,384,128]{1,2,0:T(8,128)(2,1)S(1)} %fusion.90), channel_id=1, source_target_pairs={{0,1},{1,2},{2,3},{3,4},{4,5},{5,6},{6,7},{7,8},{8,9},{9,10},{10,1... | collective-permute-start | bytes 294920 | tf_op jit(solution)/shard_map/while/body/eval_jaxpr/ppermute | solution.py:10
  189.7 7.1 %collective-permute-start = (bf16[1,384,128]{1,2,0:T(8,128)(2,1)S(1)}, bf16[1,384,128]{1,2,0:T(8,128)(2,1)S(1)}, u32[]{:S(2)}, u32[]{:S(2)}) collective-permute-start(bf16[1,384,128]{1,2,0:T(8,128)(2,1)S(1)} %fusion.90), channel_id=1, source_target_pairs={{0,1},{1,2},{2,3},{3,4},{4,5},{5,6},{6,7},{7,8},{8,9},{9,10},{10,1... | collective-permute-start | bytes 294920 | tf_op jit(solution)/shard_map/while/body/eval_jaxpr/ppermute | solution.py:10
  197.2 7.1 %collective-permute-start = (bf16[1,384,128]{1,2,0:T(8,128)(2,1)S(1)}, bf16[1,384,128]{1,2,0:T(8,128)(2,1)S(1)}, u32[]{:S(2)}, u32[]{:S(2)}) collective-permute-start(bf16[1,384,128]{1,2,0:T(8,128)(2,1)S(1)} %fusion.90), channel_id=1, source_target_pairs={{0,1},{1,2},{2,3},{3,4},{4,5},{5,6},{6,7},{7,8},{8,9},{9,10},{10,1... | collective-permute-start | bytes 294920 | tf_op jit(solution)/shard_map/while/body/eval_jaxpr/ppermute | solution.py:10
  204.7 7.1 %collective-permute-start = (bf16[1,384,128]{1,2,0:T(8,128)(2,1)S(1)}, bf16[1,384,128]{1,2,0:T(8,128)(2,1)S(1)}, u32[]{:S(2)}, u32[]{:S(2)}) collective-permute-start(bf16[1,384,128]{1,2,0:T(8,128)(2,1)S(1)} %fusion.90), channel_id=1, source_target_pairs={{0,1},{1,2},{2,3},{3,4},{4,5},{5,6},{6,7},{7,8},{8,9},{9,10},{10,1... | collective-permute-start | bytes 294920 | tf_op jit(solution)/shard_map/while/body/eval_jaxpr/ppermute | solution.py:10
  212.3 7.1 %collective-permute-start = (bf16[1,384,128]{1,2,0:T(8,128)(2,1)S(1)}, bf16[1,384,128]{1,2,0:T(8,128)(2,1)S(1)}, u32[]{:S(2)}, u32[]{:S(2)}) collective-permute-start(bf16[1,384,128]{1,2,0:T(8,128)(2,1)S(1)} %fusion.90), channel_id=1, source_target_pairs={{0,1},{1,2},{2,3},{3,4},{4,5},{5,6},{6,7},{7,8},{8,9},{9,10},{10,1... | collective-permute-start | bytes 294920 | tf_op jit(solution)/shard_map/while/body/eval_jaxpr/ppermute | solution.py:10
  219.8 7.1 %collective-permute-start = (bf16[1,384,128]{1,2,0:T(8,128)(2,1)S(1)}, bf16[1,384,128]{1,2,0:T(8,128)(2,1)S(1)}, u32[]{:S(2)}, u32[]{:S(2)}) collective-permute-start(bf16[1,384,128]{1,2,0:T(8,128)(2,1)S(1)} %fusion.90), channel_id=1, source_target_pairs={{0,1},{1,2},{2,3},{3,4},{4,5},{5,6},{6,7},{7,8},{8,9},{9,10},{10,1... | collective-permute-start | bytes 294920 | tf_op jit(solution)/shard_map/while/body/eval_jaxpr/ppermute | solution.py:10
  356.5 26.1 %copy-start.3 = (s32[8]{0:T(128)S(1)}, s32[8]{0:T(128)}, u32[]{:S(2)}) copy-start(s32[8]{0:T(128)} %param.18) | copy-start | bytes 100
  360.3 36.6 %all-to-all-start = ((bf16[64,2,128]{2,1,0:T(2,128)(2,1)}), bf16[64,2,128]{2,1,0:T(2,128)(2,1)S(1)}, u32[]{:S(2)}, u32[]{:S(2)}) async-start(bf16[64,2,128]{2,1,0:T(2,128)(2,1)} %reshape.584), calls=%async_computation | async-start | bytes 65536 | tf_op jit(solution)/shard_map/all_to_all | solution.py:138
where the time goes:
time: 438 us; the launch traced here: 437 us
  starting transfers between devices  122 us (28%)
  waiting for transfers between devices  120 us (27%)
  local copies, waits for them, and re-layouts  90.3 us (21%)
  other arithmetic  71.7 us (16%)
  blocking collectives  20.8 us (5%)
  matrix products  10.8 us (2%)
    ppermute x30, waiting for transfers between devices, passed_along(): lax.ppermute(value, axis, [(source, source + steps) for source in range(l...  111 us
    ppermute x30, starting transfers between devices, passed_along(): lax.ppermute(value, axis, [(source, source + steps) for source in range(l...  100 us
    unnamed x1, other arithmetic  45.4 us
    gather x1, local copies, waits for them, and re-layouts, lesser(): right_rows = jnp.take(adjoint_rows, right_index, axis=0)  29.2 us
    gather x1, local copies, waits for them, and re-layouts, lesser(): left_rows = jnp.take(field_rows, left_index, axis=0)  29.2 us
    all_to_all x1, starting transfers between devices, on_device(): lax.all_to_all(as_sent(lesser_part), 'energy', split_axis=2, concat_axis=...  22.2 us
    all_to_all x1, blocking collectives, on_device(): lax.all_to_all(as_sent(block_result), 'energy', split_axis=1, concat_axis...  20.8 us
    unnamed x13, local copies, waits for them, and re-layouts  14.2 us
  transfers between devices with their start and end apart: 31, of which 31 were waited for; matrix products, arithmetic and copies ran while one was open for 1% of the time, Pallas kernels for 0%

commit v1 on v0

v1 whole, which is shorter than its diff:
```python
import jax
import jax.numpy as jnp
from jax import lax
from jax.sharding import PartitionSpec as P

MAX_SHIFT = 6


def passed_along(value, axis, steps):
    count = lax.axis_size(axis)
    leading, last = (max(0, -steps), min(count, count - steps))
    return lax.ppermute(value, axis, [(source, source + steps) for source in range(leading, last)])


def complex_product(matrix, columns, adjoint):
    half = columns.shape[1] // 2
    if adjoint:
        product = jnp.einsum("cji,jn->cin", matrix, columns, preferred_element_type=jnp.float32)
        real_part = product[0, :, :half] + product[1, :, half:]
        imag_part = product[0, :, half:] - product[1, :, :half]
    else:
        product = jnp.einsum("cij,jn->cin", matrix, columns, preferred_element_type=jnp.float32)
        real_part = product[0, :, :half] - product[1, :, half:]
        imag_part = product[0, :, half:] + product[1, :, :half]
    return jnp.concatenate([real_part, imag_part], axis=1)


def picked_rows(table, index):
    rows = table.shape[0]
    selector = (lax.broadcasted_iota(jnp.int32, (rows, index.shape[0]), 0) == index[None, :])
    return jnp.einsum(
        "ar,ap->rp", table, selector.astype(table.dtype), preferred_element_type=jnp.float32
    )


def on_device(
    propagator, forward_source, backward_source, left_orbital, right_orbital, phonon_shift, coupling
):
    orbitals = propagator.shape[3]
    modes = forward_source.shape[3] // 2
    blocks = propagator[0, 0]
    forward_src = forward_source[0, 0]
    backward_src = backward_source[0, 0]
    relay_turns = lax.axis_size("section") - 1

    def relay_turn(turn_index, state):
        fields, adjoints = state
        incoming = passed_along(fields, "section", 1)
        returning = passed_along(adjoints, "section", -1)
        fields = (complex_product(blocks, incoming, False) + forward_src).astype(jnp.bfloat16)
        adjoints = (complex_product(blocks, returning, True) + backward_src).astype(jnp.bfloat16)
        return fields, adjoints

    fields, adjoints = lax.fori_loop(0, relay_turns, relay_turn, (forward_src, backward_src))

    section_base = lax.axis_index("section") * orbitals
    left_rows = picked_rows(fields, left_orbital - section_base)
    right_rows = picked_rows(adjoints, right_orbital - section_base)
    real_part = jnp.sum(left_rows * right_rows, axis=0)
    imag_part = jnp.sum(left_rows[modes:] * right_rows[:modes], axis=0) - jnp.sum(
        left_rows[:modes] * right_rows[modes:], axis=0
    )
    lesser_part = jnp.stack([real_part, imag_part]) * modes ** (-0.5)

    sent = lesser_part.astype(jnp.bfloat16)
    self_energy = jnp.zeros_like(lesser_part)
    for offset in range(-MAX_SHIFT, MAX_SHIFT + 1):
        weight = jnp.sum(jnp.where((phonon_shift == offset)[:, None], coupling, 0.0), axis=0)
        if offset == 0:
            moved = lesser_part
        else:
            moved = passed_along(sent, "energy", offset).astype(jnp.float32)
        self_energy = self_energy + weight[None, :] * moved
    return self_energy[:, None, :]


def solution(mesh):
    placed = (
        P("energy", "section", None, None, None),
        P("energy", "section", None, None),
        P("energy", "section", None, None),
        P("section"),
        P("section"),
        P(),
        P(None, "section"),
    )
    return jax.shard_map(
        on_device,
        mesh=mesh,
        in_specs=placed,
        out_specs=P(None, "energy", "section"),
        check_vma=False,
    )
```

time: 438 us -> 246 us (0.56)
  the two profiles are of different devices: /device:TPU:32 before, /device:TPU:27 now
where the time goes in v1:
time: 246 us; the launch traced here: 243 us
  starting transfers between devices  128 us (52%)
  waiting for transfers between devices  61 us (25%)
  matrix products  46 us (19%)
  other arithmetic  4.83 us (2%)
  local copies, waits for them, and re-layouts  2.72 us (1%)
    ppermute x42, starting transfers between devices, passed_along(): lax.ppermute(value, axis, [(source, source + steps) for source in range(l...  128 us
    ppermute x42, waiting for transfers between devices, passed_along(): lax.ppermute(value, axis, [(source, source + steps) for source in range(l...  61 us
    dot_general x15, matrix products, complex_product(): jnp.einsum('cij,jn->cin', matrix, columns, preferred_element_type=jnp.flo...  20.7 us
    dot_general x15, matrix products, complex_product(): jnp.einsum('cji,jn->cin', matrix, columns, preferred_element_type=jnp.flo...  19.8 us
    dot_general x2, matrix products, picked_rows(): jnp.einsum('ar,ap->rp', table, selector.astype(table.dtype), preferred_el...  5.46 us
  transfers between devices with their start and end apart: 42, of which 18 were waited for; matrix products, arithmetic and copies ran while one was open for 9% of the time, Pallas kernels for 0%

profile of v1, /device:TPU:27, one launch (start us, length us, event | category | flops | bytes accessed | tf_op | source)
XLA Modules:
  0.0 243.3 jit_solution(5917950929685496142)
XLA Ops:
  2.9 160.6 %while.12 = (s32[]{:T(128)}, bf16[384,128]{0,1:T(8,128)(2,1)S(1)}, bf16[384,128]{0,1:T(8,128)(2,1)S(1)}, bf16[2,384,384]{2,1,0:T(8,128)(2,1)}, bf16[384,128]{0,1...) while((s32[]{:T(128)}, bf16[384,128]{0,1:T(8,128)(2,1)S(1)}, bf16[384,128]{0,1:T(8,128)(2,1)S(1)}, ...), condition=%wide.region_2.0_spmd, body=%wide.region_1.0_spmd.sunk | while | flops 151486464 | bytes 4915357 | solution.py:54
  2.9 5.0 %collective-permute-start = (bf16[384,128]{0,1:T(8,128)(2,1)S(1)}, bf16[384,128]{0,1:T(8,128)(2,1)S(1)}, u32[]{:S(2)}, u32[]{:S(2)}) collective-permute-start(bf16[384,128]{0,1:T(8,128)(2,1)S(1)} %get-tuple-element.141), channel_id=1, source_target_pairs={{0,1},{1,2},{2,3},{3,4},{4,5},{5,6},{6,7},{7,8},{8,9},{9,10},{10,1... | collective-permute-start | bytes 294920 | tf_op jit(solution)/shard_map/while/body/eval_jaxpr/ppermute | solution.py:12
  7.8 1.9 collective-permute-start.1
  11.2 3.8 %collective-permute-done.1 = bf16[384,128]{0,1:T(8,128)(2,1)S(1)} collective-permute-done((bf16[384,128]{0,1:T(8,128)(2,1)S(1)}, bf16[384,128]{0,1:T(8,128)(2,1)S(1)}, u32[]{:S(2)}, u32[]{:S(2)}) %collective-permute-start.1) | collective-permute-done | bytes 98336 | tf_op jit(solution)/shard_map/while/body/eval_jaxpr/ppermute | solution.py:12
  16.4 1.9 collective-permute-start
  18.3 2.4 collective-permute-start.1
  22.2 3.3 %collective-permute-done.1 = bf16[384,128]{0,1:T(8,128)(2,1)S(1)} collective-permute-done((bf16[384,128]{0,1:T(8,128)(2,1)S(1)}, bf16[384,128]{0,1:T(8,128)(2,1)S(1)}, u32[]{:S(2)}, u32[]{:S(2)}) %collective-permute-start.1) | collective-permute-done | bytes 98336 | tf_op jit(solution)/shard_map/while/body/eval_jaxpr/ppermute | solution.py:12
  26.9 1.9 collective-permute-start
  28.8 2.4 collective-permute-start.1
  32.7 3.3 %collective-permute-done.1 = bf16[384,128]{0,1:T(8,128)(2,1)S(1)} collective-permute-done((bf16[384,128]{0,1:T(8,128)(2,1)S(1)}, bf16[384,128]{0,1:T(8,128)(2,1)S(1)}, u32[]{:S(2)}, u32[]{:S(2)}) %collective-permute-start.1) | collective-permute-done | bytes 98336 | tf_op jit(solution)/shard_map/while/body/eval_jaxpr/ppermute | solution.py:12
  37.4 1.9 collective-permute-start
  39.3 2.4 collective-permute-start.1
  43.2 3.3 %collective-permute-done.1 = bf16[384,128]{0,1:T(8,128)(2,1)S(1)} collective-permute-done((bf16[384,128]{0,1:T(8,128)(2,1)S(1)}, bf16[384,128]{0,1:T(8,128)(2,1)S(1)}, u32[]{:S(2)}, u32[]{:S(2)}) %collective-permute-start.1) | collective-permute-done | bytes 98336 | tf_op jit(solution)/shard_map/while/body/eval_jaxpr/ppermute | solution.py:12
  47.9 1.9 collective-permute-start
  49.8 2.4 collective-permute-start.1
  53.7 3.3 %collective-permute-done.1 = bf16[384,128]{0,1:T(8,128)(2,1)S(1)} collective-permute-done((bf16[384,128]{0,1:T(8,128)(2,1)S(1)}, bf16[384,128]{0,1:T(8,128)(2,1)S(1)}, u32[]{:S(2)}, u32[]{:S(2)}) %collective-permute-start.1) | collective-permute-done | bytes 98336 | tf_op jit(solution)/shard_map/while/body/eval_jaxpr/ppermute | solution.py:12
  58.4 1.9 collective-permute-start
  60.3 2.4 collective-permute-start.1
  62.8 1.4 fusion.34
  64.2 3.3 %collective-permute-done.1 = bf16[384,128]{0,1:T(8,128)(2,1)S(1)} collective-permute-done((bf16[384,128]{0,1:T(8,128)(2,1)S(1)}, bf16[384,128]{0,1:T(8,128)(2,1)S(1)}, u32[]{:S(2)}, u32[]{:S(2)}) %collective-permute-start.1) | collective-permute-done | bytes 98336 | tf_op jit(solution)/shard_map/while/body/eval_jaxpr/ppermute | solution.py:12
  68.9 1.9 collective-permute-start
  70.8 2.4 collective-permute-start.1
  74.7 3.3 %collective-permute-done.1 = bf16[384,128]{0,1:T(8,128)(2,1)S(1)} collective-permute-done((bf16[384,128]{0,1:T(8,128)(2,1)S(1)}, bf16[384,128]{0,1:T(8,128)(2,1)S(1)}, u32[]{:S(2)}, u32[]{:S(2)}) %collective-permute-start.1) | collective-permute-done | bytes 98336 | tf_op jit(solution)/shard_map/while/body/eval_jaxpr/ppermute | solution.py:12
  79.4 1.9 collective-permute-start
  81.4 2.4 collective-permute-start.1
  83.8 1.4 fusion.34
  85.2 3.3 %collective-permute-done.1 = bf16[384,128]{0,1:T(8,128)(2,1)S(1)} collective-permute-done((bf16[384,128]{0,1:T(8,128)(2,1)S(1)}, bf16[384,128]{0,1:T(8,128)(2,1)S(1)}, u32[]{:S(2)}, u32[]{:S(2)}) %collective-permute-start.1) | collective-permute-done | bytes 98336 | tf_op jit(solution)/shard_map/while/body/eval_jaxpr/ppermute | solution.py:12
  89.9 1.9 collective-permute-start
  91.9 2.4 collective-permute-start.1
  95.7 3.3 %collective-permute-done.1 = bf16[384,128]{0,1:T(8,128)(2,1)S(1)} collective-permute-done((bf16[384,128]{0,1:T(8,128)(2,1)S(1)}, bf16[384,128]{0,1:T(8,128)(2,1)S(1)}, u32[]{:S(2)}, u32[]{:S(2)}) %collective-permute-start.1) | collective-permute-done | bytes 98336 | tf_op jit(solution)/shard_map/while/body/eval_jaxpr/ppermute | solution.py:12
  100.4 1.9 collective-permute-start
  102.4 2.4 collective-permute-start.1
  106.2 3.3 %collective-permute-done.1 = bf16[384,128]{0,1:T(8,128)(2,1)S(1)} collective-permute-done((bf16[384,128]{0,1:T(8,128)(2,1)S(1)}, bf16[384,128]{0,1:T(8,128)(2,1)S(1)}, u32[]{:S(2)}, u32[]{:S(2)}) %collective-permute-start.1) | collective-permute-done | bytes 98336 | tf_op jit(solution)/shard_map/while/body/eval_jaxpr/ppermute | solution.py:12
  110.9 1.9 collective-permute-start
  112.9 2.4 collective-permute-start.1
  116.7 3.3 %collective-permute-done.1 = bf16[384,128]{0,1:T(8,128)(2,1)S(1)} collective-permute-done((bf16[384,128]{0,1:T(8,128)(2,1)S(1)}, bf16[384,128]{0,1:T(8,128)(2,1)S(1)}, u32[]{:S(2)}, u32[]{:S(2)}) %collective-permute-start.1) | collective-permute-done | bytes 98336 | tf_op jit(solution)/shard_map/while/body/eval_jaxpr/ppermute | solution.py:12
  121.4 1.9 collective-permute-start
  123.4 2.4 collective-permute-start.1
  127.2 3.3 %collective-permute-done.1 = bf16[384,128]{0,1:T(8,128)(2,1)S(1)} collective-permute-done((bf16[384,128]{0,1:T(8,128)(2,1)S(1)}, bf16[384,128]{0,1:T(8,128)(2,1)S(1)}, u32[]{:S(2)}, u32[]{:S(2)}) %collective-permute-start.1) | collective-permute-done | bytes 98336 | tf_op jit(solution)/shard_map/while/body/eval_jaxpr/ppermute | solution.py:12
  131.9 1.9 collective-permute-start
  133.9 2.4 collective-permute-start.1
  137.7 3.3 %collective-permute-done.1 = bf16[384,128]{0,1:T(8,128)(2,1)S(1)} collective-permute-done((bf16[384,128]{0,1:T(8,128)(2,1)S(1)}, bf16[384,128]{0,1:T(8,128)(2,1)S(1)}, u32[]{:S(2)}, u32[]{:S(2)}) %collective-permute-start.1) | collective-permute-done | bytes 98336 | tf_op jit(solution)/shard_map/while/body/eval_jaxpr/ppermute | solution.py:12
  142.5 1.9 collective-permute-start
  144.4 2.4 collective-permute-start.1
  148.2 3.3 %collective-permute-done.1 = bf16[384,128]{0,1:T(8,128)(2,1)S(1)} collective-permute-done((bf16[384,128]{0,1:T(8,128)(2,1)S(1)}, bf16[384,128]{0,1:T(8,128)(2,1)S(1)}, u32[]{:S(2)}, u32[]{:S(2)}) %collective-permute-start.1) | collective-permute-done | bytes 98336 | tf_op jit(solution)/shard_map/while/body/eval_jaxpr/ppermute | solution.py:12
  153.0 1.9 collective-permute-start
  154.9 2.4 collective-permute-start.1
  158.7 3.3 %collective-permute-done.1 = bf16[384,128]{0,1:T(8,128)(2,1)S(1)} collective-permute-done((bf16[384,128]{0,1:T(8,128)(2,1)S(1)}, bf16[384,128]{0,1:T(8,128)(2,1)S(1)}, u32[]{:S(2)}, u32[]{:S(2)}) %collective-permute-start.1) | collective-permute-done | bytes 98336 | tf_op jit(solution)/shard_map/while/body/eval_jaxpr/ppermute | solution.py:12
  163.5 2.4 %fusion.11 = f32[128,8192]{1,0:T(8,128)S(1)} fusion(bf16[384,128]{0,1:T(8,128)(2,1)S(1)} %get-tuple-element.39, s32[8192]{0:T(1024)S(1)} %get-tuple-element.86), kind=kOutput, calls=%fused_computation.19 | convolution fusion | flops 808452096 | bytes 4325376 | tf_op jit(solution)/shard_map/ar,ap->rp/dot_general | solution.py:31
  165.9 3.0 %multiply_reduce_fusion = (f32[8192]{0:T(1024)S(1)}, f32[128,8192]{1,0:T(8,128)S(1)}) fusion(f32[128,8192]{1,0:T(8,128)S(1)} %fusion.11, bf16[384,128]{0,1:T(8,128)(2,1)S(1)} %get-tuple-element.38, s32[8192]{0:T(1024)S(1)} %get-tuple-element.87), kind=kOutput, calls=%fused_computation.22 | convolution fusion | flops 810541056 | bytes 8552448 | tf_op jit(solution)/shard_map/ar,ap->rp/dot_general | solution.py:31
  169.9 14.3 %collective-permute-start.13 = (bf16[2,8192]{1,0:T(2,128)(2,1)S(1)}, bf16[2,8192]{1,0:T(2,128)(2,1)S(1)}, u32[]{:S(2)}, u32[]{:S(2)}) collective-permute-start(bf16[2,8192]{1,0:T(2,128)(2,1)S(1)} %multiply_convert_fusion), channel_id=1, source_target_pairs={{0,96},{16,112},{32,128},{48,144},{64,160},{80,176},{96,192},{112,... | collective-permute-start | bytes 98312 | tf_op jit(solution)/shard_map/ppermute | solution.py:12
  184.2 9.7 %collective-permute-start.12 = (bf16[2,8192]{1,0:T(2,128)(2,1)S(1)}, bf16[2,8192]{1,0:T(2,128)(2,1)S(1)}, u32[]{:S(2)}, u32[]{:S(2)}) collective-permute-start(bf16[2,8192]{1,0:T(2,128)(2,1)S(1)} %multiply_convert_fusion), channel_id=1, source_target_pairs={{0,80},{16,96},{32,112},{48,128},{64,144},{80,160},{96,176},{112,1... | collective-permute-start | bytes 98312 | tf_op jit(solution)/shard_map/ppermute | solution.py:12
  193.9 5.8 %collective-permute-start.11 = (bf16[2,8192]{1,0:T(2,128)(2,1)S(1)}, bf16[2,8192]{1,0:T(2,128)(2,1)S(1)}, u32[]{:S(2)}, u32[]{:S(2)}) collective-permute-start(bf16[2,8192]{1,0:T(2,128)(2,1)S(1)} %multiply_convert_fusion), channel_id=1, source_target_pairs={{0,64},{16,80},{32,96},{48,112},{64,128},{80,144},{96,160},{112,17... | collective-permute-start | bytes 98312 | tf_op jit(solution)/shard_map/ppermute | solution.py:12
  199.8 1.9 collective-permute-start.10
  201.7 2.2 collective-permute-start.9
  203.9 2.2 collective-permute-start.8
  206.2 5.2 %collective-permute-start.7 = (bf16[2,8192]{1,0:T(2,128)(2,1)S(1)}, bf16[2,8192]{1,0:T(2,128)(2,1)S(1)}, u32[]{:S(2)}, u32[]{:S(2)}) collective-permute-start(bf16[2,8192]{1,0:T(2,128)(2,1)S(1)} %multiply_convert_fusion), channel_id=1, source_target_pairs={{16,0},{32,16},{48,32},{64,48},{80,64},{96,80},{112,96},{128,112},... | collective-permute-start | bytes 98312 | tf_op jit(solution)/shard_map/ppermute | solution.py:12
  212.5 4.0 %collective-permute-start.6 = (bf16[2,8192]{1,0:T(2,128)(2,1)S(1)}, bf16[2,8192]{1,0:T(2,128)(2,1)S(1)}, u32[]{:S(2)}, u32[]{:S(2)}) collective-permute-start(bf16[2,8192]{1,0:T(2,128)(2,1)S(1)} %multiply_convert_fusion), channel_id=1, source_target_pairs={{32,0},{48,16},{64,32},{80,48},{96,64},{112,80},{128,96},{144,112}... | collective-permute-start | bytes 98312 | tf_op jit(solution)/shard_map/ppermute | solution.py:12
  216.5 6.4 %collective-permute-start.5 = (bf16[2,8192]{1,0:T(2,128)(2,1)S(1)}, bf16[2,8192]{1,0:T(2,128)(2,1)S(1)}, u32[]{:S(2)}, u32[]{:S(2)}) collective-permute-start(bf16[2,8192]{1,0:T(2,128)(2,1)S(1)} %multiply_convert_fusion), channel_id=1, source_target_pairs={{48,0},{64,16},{80,32},{96,48},{112,64},{128,80},{144,96},{160,112... | collective-permute-start | bytes 98312 | tf_op jit(solution)/shard_map/ppermute | solution.py:12
  222.9 3.4 %collective-permute-start.4 = (bf16[2,8192]{1,0:T(2,128)(2,1)S(1)}, bf16[2,8192]{1,0:T(2,128)(2,1)S(1)}, u32[]{:S(2)}, u32[]{:S(2)}) collective-permute-start(bf16[2,8192]{1,0:T(2,128)(2,1)S(1)} %multiply_convert_fusion), channel_id=1, source_target_pairs={{64,0},{80,16},{96,32},{112,48},{128,64},{144,80},{160,96},{176,11... | collective-permute-start | bytes 98312 | tf_op jit(solution)/shard_map/ppermute | solution.py:12
  226.3 3.1 %collective-permute-start.3 = (bf16[2,8192]{1,0:T(2,128)(2,1)S(1)}, bf16[2,8192]{1,0:T(2,128)(2,1)S(1)}, u32[]{:S(2)}, u32[]{:S(2)}) collective-permute-start(bf16[2,8192]{1,0:T(2,128)(2,1)S(1)} %multiply_convert_fusion), channel_id=1, source_target_pairs={{80,0},{96,16},{112,32},{128,48},{144,64},{160,80},{176,96},{192,1... | collective-permute-start | bytes 98312 | tf_op jit(solution)/shard_map/ppermute | solution.py:12
  229.4 1.9 collective-permute-start.2
  232.7 3.3 %collective-permute-done.3 = bf16[2,8192]{1,0:T(2,128)(2,1)S(1)} collective-permute-done((bf16[2,8192]{1,0:T(2,128)(2,1)S(1)}, bf16[2,8192]{1,0:T(2,128)(2,1)S(1)}, u32[]{:S(2)}, u32[]{:S(2)}) %collective-permute-start.3) | collective-permute-done | bytes 32800 | tf_op jit(solution)/shard_map/ppermute | solution.py:12
  236.0 6.2 %collective-permute-done.2 = bf16[2,8192]{1,0:T(2,128)(2,1)S(1)} collective-permute-done((bf16[2,8192]{1,0:T(2,128)(2,1)S(1)}, bf16[2,8192]{1,0:T(2,128)(2,1)S(1)}, u32[]{:S(2)}, u32[]{:S(2)}) %collective-permute-start.2) | collective-permute-done | bytes 32800 | tf_op jit(solution)/shard_map/ppermute | solution.py:12
  (130 shorter events, 46.7 us)
Async XLA Ops:
  2.9 6.9 %collective-permute-start = (bf16[384,128]{0,1:T(8,128)(2,1)S(1)}, bf16[384,128]{0,1:T(8,128)(2,1)S(1)}, u32[]{:S(2)}, u32[]{:S(2)}) collective-permute-start(bf16[384,128]{0,1:T(8,128)(2,1)S(1)} %get-tuple-element.141), channel_id=1, source_target_pairs={{0,1},{1,2},{2,3},{3,4},{4,5},{5,6},{6,7},{7,8},{8,9},{9,10},{10,1... | collective-permute-start | bytes 294920 | tf_op jit(solution)/shard_map/while/body/eval_jaxpr/ppermute | solution.py:12
  7.8 7.1 %collective-permute-start.1 = (bf16[384,128]{0,1:T(8,128)(2,1)S(1)}, bf16[384,128]{0,1:T(8,128)(2,1)S(1)}, u32[]{:S(2)}, u32[]{:S(2)}) collective-permute-start(bf16[384,128]{0,1:T(8,128)(2,1)S(1)} %get-tuple-element.142), channel_id=1, source_target_pairs={{1,0},{2,1},{3,2},{4,3},{5,4},{6,5},{7,6},{8,7},{9,8},{10,9},{11,1... | collective-permute-start | bytes 294920 | tf_op jit(solution)/shard_map/while/body/eval_jaxpr/ppermute | solution.py:12
  16.4 4.3 %collective-permute-start = (bf16[384,128]{0,1:T(8,128)(2,1)S(1)}, bf16[384,128]{0,1:T(8,128)(2,1)S(1)}, u32[]{:S(2)}, u32[]{:S(2)}) collective-permute-start(bf16[384,128]{0,1:T(8,128)(2,1)S(1)} %get-tuple-element.141), channel_id=1, source_target_pairs={{0,1},{1,2},{2,3},{3,4},{4,5},{5,6},{6,7},{7,8},{8,9},{9,10},{10,1... | collective-permute-start | bytes 294920 | tf_op jit(solution)/shard_map/while/body/eval_jaxpr/ppermute | solution.py:12
  18.3 7.1 %collective-permute-start.1 = (bf16[384,128]{0,1:T(8,128)(2,1)S(1)}, bf16[384,128]{0,1:T(8,128)(2,1)S(1)}, u32[]{:S(2)}, u32[]{:S(2)}) collective-permute-start(bf16[384,128]{0,1:T(8,128)(2,1)S(1)} %get-tuple-element.142), channel_id=1, source_target_pairs={{1,0},{2,1},{3,2},{4,3},{5,4},{6,5},{7,6},{8,7},{9,8},{10,9},{11,1... | collective-permute-start | bytes 294920 | tf_op jit(solution)/shard_map/while/body/eval_jaxpr/ppermute | solution.py:12
  26.9 4.3 %collective-permute-start = (bf16[384,128]{0,1:T(8,128)(2,1)S(1)}, bf16[384,128]{0,1:T(8,128)(2,1)S(1)}, u32[]{:S(2)}, u32[]{:S(2)}) collective-permute-start(bf16[384,128]{0,1:T(8,128)(2,1)S(1)} %get-tuple-element.141), channel_id=1, source_target_pairs={{0,1},{1,2},{2,3},{3,4},{4,5},{5,6},{6,7},{7,8},{8,9},{9,10},{10,1... | collective-permute-start | bytes 294920 | tf_op jit(solution)/shard_map/while/body/eval_jaxpr/ppermute | solution.py:12
  28.8 7.1 %collective-permute-start.1 = (bf16[384,128]{0,1:T(8,128)(2,1)S(1)}, bf16[384,128]{0,1:T(8,128)(2,1)S(1)}, u32[]{:S(2)}, u32[]{:S(2)}) collective-permute-start(bf16[384,128]{0,1:T(8,128)(2,1)S(1)} %get-tuple-element.142), channel_id=1, source_target_pairs={{1,0},{2,1},{3,2},{4,3},{5,4},{6,5},{7,6},{8,7},{9,8},{10,9},{11,1... | collective-permute-start | bytes 294920 | tf_op jit(solution)/shard_map/while/body/eval_jaxpr/ppermute | solution.py:12
  37.4 4.3 %collective-permute-start = (bf16[384,128]{0,1:T(8,128)(2,1)S(1)}, bf16[384,128]{0,1:T(8,128)(2,1)S(1)}, u32[]{:S(2)}, u32[]{:S(2)}) collective-permute-start(bf16[384,128]{0,1:T(8,128)(2,1)S(1)} %get-tuple-element.141), channel_id=1, source_target_pairs={{0,1},{1,2},{2,3},{3,4},{4,5},{5,6},{6,7},{7,8},{8,9},{9,10},{10,1... | collective-permute-start | bytes 294920 | tf_op jit(solution)/shard_map/while/body/eval_jaxpr/ppermute | solution.py:12
  39.3 7.1 %collective-permute-start.1 = (bf16[384,128]{0,1:T(8,128)(2,1)S(1)}, bf16[384,128]{0,1:T(8,128)(2,1)S(1)}, u32[]{:S(2)}, u32[]{:S(2)}) collective-permute-start(bf16[384,128]{0,1:T(8,128)(2,1)S(1)} %get-tuple-element.142), channel_id=1, source_target_pairs={{1,0},{2,1},{3,2},{4,3},{5,4},{6,5},{7,6},{8,7},{9,8},{10,9},{11,1... | collective-permute-start | bytes 294920 | tf_op jit(solution)/shard_map/while/body/eval_jaxpr/ppermute | solution.py:12
  47.9 4.3 %collective-permute-start = (bf16[384,128]{0,1:T(8,128)(2,1)S(1)}, bf16[384,128]{0,1:T(8,128)(2,1)S(1)}, u32[]{:S(2)}, u32[]{:S(2)}) collective-permute-start(bf16[384,128]{0,1:T(8,128)(2,1)S(1)} %get-tuple-element.141), channel_id=1, source_target_pairs={{0,1},{1,2},{2,3},{3,4},{4,5},{5,6},{6,7},{7,8},{8,9},{9,10},{10,1... | collective-permute-start | bytes 294920 | tf_op jit(solution)/shard_map/while/body/eval_jaxpr/ppermute | solution.py:12
  49.8 7.1 %collective-permute-start.1 = (bf16[384,128]{0,1:T(8,128)(2,1)S(1)}, bf16[384,128]{0,1:T(8,128)(2,1)S(1)}, u32[]{:S(2)}, u32[]{:S(2)}) collective-permute-start(bf16[384,128]{0,1:T(8,128)(2,1)S(1)} %get-tuple-element.142), channel_id=1, source_target_pairs={{1,0},{2,1},{3,2},{4,3},{5,4},{6,5},{7,6},{8,7},{9,8},{10,9},{11,1... | collective-permute-start | bytes 294920 | tf_op jit(solution)/shard_map/while/body/eval_jaxpr/ppermute | solution.py:12
  58.4 4.3 %collective-permute-start = (bf16[384,128]{0,1:T(8,128)(2,1)S(1)}, bf16[384,128]{0,1:T(8,128)(2,1)S(1)}, u32[]{:S(2)}, u32[]{:S(2)}) collective-permute-start(bf16[384,128]{0,1:T(8,128)(2,1)S(1)} %get-tuple-element.141), channel_id=1, source_target_pairs={{0,1},{1,2},{2,3},{3,4},{4,5},{5,6},{6,7},{7,8},{8,9},{9,10},{10,1... | collective-permute-start | bytes 294920 | tf_op jit(solution)/shard_map/while/body/eval_jaxpr/ppermute | solution.py:12
  60.3 7.1 %collective-permute-start.1 = (bf16[384,128]{0,1:T(8,128)(2,1)S(1)}, bf16[384,128]{0,1:T(8,128)(2,1)S(1)}, u32[]{:S(2)}, u32[]{:S(2)}) collective-permute-start(bf16[384,128]{0,1:T(8,128)(2,1)S(1)} %get-tuple-element.142), channel_id=1, source_target_pairs={{1,0},{2,1},{3,2},{4,3},{5,4},{6,5},{7,6},{8,7},{9,8},{10,9},{11,1... | collective-permute-start | bytes 294920 | tf_op jit(solution)/shard_map/while/body/eval_jaxpr/ppermute | solution.py:12
  68.9 4.3 %collective-permute-start = (bf16[384,128]{0,1:T(8,128)(2,1)S(1)}, bf16[384,128]{0,1:T(8,128)(2,1)S(1)}, u32[]{:S(2)}, u32[]{:S(2)}) collective-permute-start(bf16[384,128]{0,1:T(8,128)(2,1)S(1)} %get-tuple-element.141), channel_id=1, source_target_pairs={{0,1},{1,2},{2,3},{3,4},{4,5},{5,6},{6,7},{7,8},{8,9},{9,10},{10,1... | collective-permute-start | bytes 294920 | tf_op jit(solution)/shard_map/while/body/eval_jaxpr/ppermute | solution.py:12
  70.8 7.1 %collective-permute-start.1 = (bf16[384,128]{0,1:T(8,128)(2,1)S(1)}, bf16[384,128]{0,1:T(8,128)(2,1)S(1)}, u32[]{:S(2)}, u32[]{:S(2)}) collective-permute-start(bf16[384,128]{0,1:T(8,128)(2,1)S(1)} %get-tuple-element.142), channel_id=1, source_target_pairs={{1,0},{2,1},{3,2},{4,3},{5,4},{6,5},{7,6},{8,7},{9,8},{10,9},{11,1... | collective-permute-start | bytes 294920 | tf_op jit(solution)/shard_map/while/body/eval_jaxpr/ppermute | solution.py:12
  79.4 4.3 %collective-permute-start = (bf16[384,128]{0,1:T(8,128)(2,1)S(1)}, bf16[384,128]{0,1:T(8,128)(2,1)S(1)}, u32[]{:S(2)}, u32[]{:S(2)}) collective-permute-start(bf16[384,128]{0,1:T(8,128)(2,1)S(1)} %get-tuple-element.141), channel_id=1, source_target_pairs={{0,1},{1,2},{2,3},{3,4},{4,5},{5,6},{6,7},{7,8},{8,9},{9,10},{10,1... | collective-permute-start | bytes 294920 | tf_op jit(solution)/shard_map/while/body/eval_jaxpr/ppermute | solution.py:12
  81.4 7.1 %collective-permute-start.1 = (bf16[384,128]{0,1:T(8,128)(2,1)S(1)}, bf16[384,128]{0,1:T(8,128)(2,1)S(1)}, u32[]{:S(2)}, u32[]{:S(2)}) collective-permute-start(bf16[384,128]{0,1:T(8,128)(2,1)S(1)} %get-tuple-element.142), channel_id=1, source_target_pairs={{1,0},{2,1},{3,2},{4,3},{5,4},{6,5},{7,6},{8,7},{9,8},{10,9},{11,1... | collective-permute-start | bytes 294920 | tf_op jit(solution)/shard_map/while/body/eval_jaxpr/ppermute | solution.py:12
  89.9 4.3 %collective-permute-start = (bf16[384,128]{0,1:T(8,128)(2,1)S(1)}, bf16[384,128]{0,1:T(8,128)(2,1)S(1)}, u32[]{:S(2)}, u32[]{:S(2)}) collective-permute-start(bf16[384,128]{0,1:T(8,128)(2,1)S(1)} %get-tuple-element.141), channel_id=1, source_target_pairs={{0,1},{1,2},{2,3},{3,4},{4,5},{5,6},{6,7},{7,8},{8,9},{9,10},{10,1... | collective-permute-start | bytes 294920 | tf_op jit(solution)/shard_map/while/body/eval_jaxpr/ppermute | solution.py:12
  91.9 7.1 %collective-permute-start.1 = (bf16[384,128]{0,1:T(8,128)(2,1)S(1)}, bf16[384,128]{0,1:T(8,128)(2,1)S(1)}, u32[]{:S(2)}, u32[]{:S(2)}) collective-permute-start(bf16[384,128]{0,1:T(8,128)(2,1)S(1)} %get-tuple-element.142), channel_id=1, source_target_pairs={{1,0},{2,1},{3,2},{4,3},{5,4},{6,5},{7,6},{8,7},{9,8},{10,9},{11,1... | collective-permute-start | bytes 294920 | tf_op jit(solution)/shard_map/while/body/eval_jaxpr/ppermute | solution.py:12
  100.4 4.3 %collective-permute-start = (bf16[384,128]{0,1:T(8,128)(2,1)S(1)}, bf16[384,128]{0,1:T(8,128)(2,1)S(1)}, u32[]{:S(2)}, u32[]{:S(2)}) collective-permute-start(bf16[384,128]{0,1:T(8,128)(2,1)S(1)} %get-tuple-element.141), channel_id=1, source_target_pairs={{0,1},{1,2},{2,3},{3,4},{4,5},{5,6},{6,7},{7,8},{8,9},{9,10},{10,1... | collective-permute-start | bytes 294920 | tf_op jit(solution)/shard_map/while/body/eval_jaxpr/ppermute | solution.py:12
  102.4 7.1 %collective-permute-start.1 = (bf16[384,128]{0,1:T(8,128)(2,1)S(1)}, bf16[384,128]{0,1:T(8,128)(2,1)S(1)}, u32[]{:S(2)}, u32[]{:S(2)}) collective-permute-start(bf16[384,128]{0,1:T(8,128)(2,1)S(1)} %get-tuple-element.142), channel_id=1, source_target_pairs={{1,0},{2,1},{3,2},{4,3},{5,4},{6,5},{7,6},{8,7},{9,8},{10,9},{11,1... | collective-permute-start | bytes 294920 | tf_op jit(solution)/shard_map/while/body/eval_jaxpr/ppermute | solution.py:12
  110.9 4.3 %collective-permute-start = (bf16[384,128]{0,1:T(8,128)(2,1)S(1)}, bf16[384,128]{0,1:T(8,128)(2,1)S(1)}, u32[]{:S(2)}, u32[]{:S(2)}) collective-permute-start(bf16[384,128]{0,1:T(8,128)(2,1)S(1)} %get-tuple-element.141), channel_id=1, source_target_pairs={{0,1},{1,2},{2,3},{3,4},{4,5},{5,6},{6,7},{7,8},{8,9},{9,10},{10,1... | collective-permute-start | bytes 294920 | tf_op jit(solution)/shard_map/while/body/eval_jaxpr/ppermute | solution.py:12
  112.9 7.1 %collective-permute-start.1 = (bf16[384,128]{0,1:T(8,128)(2,1)S(1)}, bf16[384,128]{0,1:T(8,128)(2,1)S(1)}, u32[]{:S(2)}, u32[]{:S(2)}) collective-permute-start(bf16[384,128]{0,1:T(8,128)(2,1)S(1)} %get-tuple-element.142), channel_id=1, source_target_pairs={{1,0},{2,1},{3,2},{4,3},{5,4},{6,5},{7,6},{8,7},{9,8},{10,9},{11,1... | collective-permute-start | bytes 294920 | tf_op jit(solution)/shard_map/while/body/eval_jaxpr/ppermute | solution.py:12
  121.4 4.3 %collective-permute-start = (bf16[384,128]{0,1:T(8,128)(2,1)S(1)}, bf16[384,128]{0,1:T(8,128)(2,1)S(1)}, u32[]{:S(2)}, u32[]{:S(2)}) collective-permute-start(bf16[384,128]{0,1:T(8,128)(2,1)S(1)} %get-tuple-element.141), channel_id=1, source_target_pairs={{0,1},{1,2},{2,3},{3,4},{4,5},{5,6},{6,7},{7,8},{8,9},{9,10},{10,1... | collective-permute-start | bytes 294920 | tf_op jit(solution)/shard_map/while/body/eval_jaxpr/ppermute | solution.py:12
  123.4 7.1 %collective-permute-start.1 = (bf16[384,128]{0,1:T(8,128)(2,1)S(1)}, bf16[384,128]{0,1:T(8,128)(2,1)S(1)}, u32[]{:S(2)}, u32[]{:S(2)}) collective-permute-start(bf16[384,128]{0,1:T(8,128)(2,1)S(1)} %get-tuple-element.142), channel_id=1, source_target_pairs={{1,0},{2,1},{3,2},{4,3},{5,4},{6,5},{7,6},{8,7},{9,8},{10,9},{11,1... | collective-permute-start | bytes 294920 | tf_op jit(solution)/shard_map/while/body/eval_jaxpr/ppermute | solution.py:12
  131.9 4.3 %collective-permute-start = (bf16[384,128]{0,1:T(8,128)(2,1)S(1)}, bf16[384,128]{0,1:T(8,128)(2,1)S(1)}, u32[]{:S(2)}, u32[]{:S(2)}) collective-permute-start(bf16[384,128]{0,1:T(8,128)(2,1)S(1)} %get-tuple-element.141), channel_id=1, source_target_pairs={{0,1},{1,2},{2,3},{3,4},{4,5},{5,6},{6,7},{7,8},{8,9},{9,10},{10,1... | collective-permute-start | bytes 294920 | tf_op jit(solution)/shard_map/while/body/eval_jaxpr/ppermute | solution.py:12
  133.9 7.1 %collective-permute-start.1 = (bf16[384,128]{0,1:T(8,128)(2,1)S(1)}, bf16[384,128]{0,1:T(8,128)(2,1)S(1)}, u32[]{:S(2)}, u32[]{:S(2)}) collective-permute-start(bf16[384,128]{0,1:T(8,128)(2,1)S(1)} %get-tuple-element.142), channel_id=1, source_target_pairs={{1,0},{2,1},{3,2},{4,3},{5,4},{6,5},{7,6},{8,7},{9,8},{10,9},{11,1... | collective-permute-start | bytes 294920 | tf_op jit(solution)/shard_map/while/body/eval_jaxpr/ppermute | solution.py:12
  142.5 4.3 %collective-permute-start = (bf16[384,128]{0,1:T(8,128)(2,1)S(1)}, bf16[384,128]{0,1:T(8,128)(2,1)S(1)}, u32[]{:S(2)}, u32[]{:S(2)}) collective-permute-start(bf16[384,128]{0,1:T(8,128)(2,1)S(1)} %get-tuple-element.141), channel_id=1, source_target_pairs={{0,1},{1,2},{2,3},{3,4},{4,5},{5,6},{6,7},{7,8},{8,9},{9,10},{10,1... | collective-permute-start | bytes 294920 | tf_op jit(solution)/shard_map/while/body/eval_jaxpr/ppermute | solution.py:12
  144.4 7.1 %collective-permute-start.1 = (bf16[384,128]{0,1:T(8,128)(2,1)S(1)}, bf16[384,128]{0,1:T(8,128)(2,1)S(1)}, u32[]{:S(2)}, u32[]{:S(2)}) collective-permute-start(bf16[384,128]{0,1:T(8,128)(2,1)S(1)} %get-tuple-element.142), channel_id=1, source_target_pairs={{1,0},{2,1},{3,2},{4,3},{5,4},{6,5},{7,6},{8,7},{9,8},{10,9},{11,1... | collective-permute-start | bytes 294920 | tf_op jit(solution)/shard_map/while/body/eval_jaxpr/ppermute | solution.py:12
  153.0 4.3 %collective-permute-start = (bf16[384,128]{0,1:T(8,128)(2,1)S(1)}, bf16[384,128]{0,1:T(8,128)(2,1)S(1)}, u32[]{:S(2)}, u32[]{:S(2)}) collective-permute-start(bf16[384,128]{0,1:T(8,128)(2,1)S(1)} %get-tuple-element.141), channel_id=1, source_target_pairs={{0,1},{1,2},{2,3},{3,4},{4,5},{5,6},{6,7},{7,8},{8,9},{9,10},{10,1... | collective-permute-start | bytes 294920 | tf_op jit(solution)/shard_map/while/body/eval_jaxpr/ppermute | solution.py:12
  154.9 7.1 %collective-permute-start.1 = (bf16[384,128]{0,1:T(8,128)(2,1)S(1)}, bf16[384,128]{0,1:T(8,128)(2,1)S(1)}, u32[]{:S(2)}, u32[]{:S(2)}) collective-permute-start(bf16[384,128]{0,1:T(8,128)(2,1)S(1)} %get-tuple-element.142), channel_id=1, source_target_pairs={{1,0},{2,1},{3,2},{4,3},{5,4},{6,5},{7,6},{8,7},{9,8},{10,9},{11,1... | collective-permute-start | bytes 294920 | tf_op jit(solution)/shard_map/while/body/eval_jaxpr/ppermute | solution.py:12
  168.9 35.0 %copy-start.1 = (s32[8]{0:T(128)S(1)}, s32[8]{0:T(128)}, u32[]{:S(2)}) copy-start(s32[8]{0:T(128)} %param.14) | copy-start | bytes 100
  168.9 42.4 %copy-start = (f32[8,8192]{1,0:T(8,128)S(1)}, f32[8,8192]{1,0:T(8,128)}, u32[]{:S(2)}) copy-start(f32[8,8192]{1,0:T(8,128)} %param.15) | copy-start | bytes 786436
  169.9 34.0 %collective-permute-start.13 = (bf16[2,8192]{1,0:T(2,128)(2,1)S(1)}, bf16[2,8192]{1,0:T(2,128)(2,1)S(1)}, u32[]{:S(2)}, u32[]{:S(2)}) collective-permute-start(bf16[2,8192]{1,0:T(2,128)(2,1)S(1)} %multiply_convert_fusion), channel_id=1, source_target_pairs={{0,96},{16,112},{32,128},{48,144},{64,160},{80,176},{96,192},{112,... | collective-permute-start | bytes 98312 | tf_op jit(solution)/shard_map/ppermute | solution.py:12
  184.2 22.0 %collective-permute-start.12 = (bf16[2,8192]{1,0:T(2,128)(2,1)S(1)}, bf16[2,8192]{1,0:T(2,128)(2,1)S(1)}, u32[]{:S(2)}, u32[]{:S(2)}) collective-permute-start(bf16[2,8192]{1,0:T(2,128)(2,1)S(1)} %multiply_convert_fusion), channel_id=1, source_target_pairs={{0,80},{16,96},{32,112},{48,128},{64,144},{80,160},{96,176},{112,1... | collective-permute-start | bytes 98312 | tf_op jit(solution)/shard_map/ppermute | solution.py:12
  193.9 18.6 %collective-permute-start.11 = (bf16[2,8192]{1,0:T(2,128)(2,1)S(1)}, bf16[2,8192]{1,0:T(2,128)(2,1)S(1)}, u32[]{:S(2)}, u32[]{:S(2)}) collective-permute-start(bf16[2,8192]{1,0:T(2,128)(2,1)S(1)} %multiply_convert_fusion), channel_id=1, source_target_pairs={{0,64},{16,80},{32,96},{48,112},{64,128},{80,144},{96,160},{112,17... | collective-permute-start | bytes 98312 | tf_op jit(solution)/shard_map/ppermute | solution.py:12
  199.8 16.7 %collective-permute-start.10 = (bf16[2,8192]{1,0:T(2,128)(2,1)S(1)}, bf16[2,8192]{1,0:T(2,128)(2,1)S(1)}, u32[]{:S(2)}, u32[]{:S(2)}) collective-permute-start(bf16[2,8192]{1,0:T(2,128)(2,1)S(1)} %multiply_convert_fusion), channel_id=1, source_target_pairs={{0,48},{16,64},{32,80},{48,96},{64,112},{80,128},{96,144},{112,160... | collective-permute-start | bytes 98312 | tf_op jit(solution)/shard_map/ppermute | solution.py:12
  201.7 21.2 %collective-permute-start.9 = (bf16[2,8192]{1,0:T(2,128)(2,1)S(1)}, bf16[2,8192]{1,0:T(2,128)(2,1)S(1)}, u32[]{:S(2)}, u32[]{:S(2)}) collective-permute-start(bf16[2,8192]{1,0:T(2,128)(2,1)S(1)} %multiply_convert_fusion), channel_id=1, source_target_pairs={{0,32},{16,48},{32,64},{48,80},{64,96},{80,112},{96,128},{112,144}... | collective-permute-start | bytes 98312 | tf_op jit(solution)/shard_map/ppermute | solution.py:12
  203.9 22.3 %collective-permute-start.8 = (bf16[2,8192]{1,0:T(2,128)(2,1)S(1)}, bf16[2,8192]{1,0:T(2,128)(2,1)S(1)}, u32[]{:S(2)}, u32[]{:S(2)}) collective-permute-start(bf16[2,8192]{1,0:T(2,128)(2,1)S(1)} %multiply_convert_fusion), channel_id=1, source_target_pairs={{0,16},{16,32},{32,48},{48,64},{64,80},{80,96},{96,112},{112,128},... | collective-permute-start | bytes 98312 | tf_op jit(solution)/shard_map/ppermute | solution.py:12
  206.2 23.2 %collective-permute-start.7 = (bf16[2,8192]{1,0:T(2,128)(2,1)S(1)}, bf16[2,8192]{1,0:T(2,128)(2,1)S(1)}, u32[]{:S(2)}, u32[]{:S(2)}) collective-permute-start(bf16[2,8192]{1,0:T(2,128)(2,1)S(1)} %multiply_convert_fusion), channel_id=1, source_target_pairs={{16,0},{32,16},{48,32},{64,48},{80,64},{96,80},{112,96},{128,112},... | collective-permute-start | bytes 98312 | tf_op jit(solution)/shard_map/ppermute | solution.py:12
  212.5 18.8 %collective-permute-start.6 = (bf16[2,8192]{1,0:T(2,128)(2,1)S(1)}, bf16[2,8192]{1,0:T(2,128)(2,1)S(1)}, u32[]{:S(2)}, u32[]{:S(2)}) collective-permute-start(bf16[2,8192]{1,0:T(2,128)(2,1)S(1)} %multiply_convert_fusion), channel_id=1, source_target_pairs={{32,0},{48,16},{64,32},{80,48},{96,64},{112,80},{128,96},{144,112}... | collective-permute-start | bytes 98312 | tf_op jit(solution)/shard_map/ppermute | solution.py:12
  216.5 14.8 %collective-permute-start.5 = (bf16[2,8192]{1,0:T(2,128)(2,1)S(1)}, bf16[2,8192]{1,0:T(2,128)(2,1)S(1)}, u32[]{:S(2)}, u32[]{:S(2)}) collective-permute-start(bf16[2,8192]{1,0:T(2,128)(2,1)S(1)} %multiply_convert_fusion), channel_id=1, source_target_pairs={{48,0},{64,16},{80,32},{96,48},{112,64},{128,80},{144,96},{160,112... | collective-permute-start | bytes 98312 | tf_op jit(solution)/shard_map/ppermute | solution.py:12
  222.9 9.8 %collective-permute-start.4 = (bf16[2,8192]{1,0:T(2,128)(2,1)S(1)}, bf16[2,8192]{1,0:T(2,128)(2,1)S(1)}, u32[]{:S(2)}, u32[]{:S(2)}) collective-permute-start(bf16[2,8192]{1,0:T(2,128)(2,1)S(1)} %multiply_convert_fusion), channel_id=1, source_target_pairs={{64,0},{80,16},{96,32},{112,48},{128,64},{144,80},{160,96},{176,11... | collective-permute-start | bytes 98312 | tf_op jit(solution)/shard_map/ppermute | solution.py:12
  226.3 9.7 %collective-permute-start.3 = (bf16[2,8192]{1,0:T(2,128)(2,1)S(1)}, bf16[2,8192]{1,0:T(2,128)(2,1)S(1)}, u32[]{:S(2)}, u32[]{:S(2)}) collective-permute-start(bf16[2,8192]{1,0:T(2,128)(2,1)S(1)} %multiply_convert_fusion), channel_id=1, source_target_pairs={{80,0},{96,16},{112,32},{128,48},{144,64},{160,80},{176,96},{192,1... | collective-permute-start | bytes 98312 | tf_op jit(solution)/shard_map/ppermute | solution.py:12
  229.4 12.8 %collective-permute-start.2 = (bf16[2,8192]{1,0:T(2,128)(2,1)S(1)}, bf16[2,8192]{1,0:T(2,128)(2,1)S(1)}, u32[]{:S(2)}, u32[]{:S(2)}) collective-permute-start(bf16[2,8192]{1,0:T(2,128)(2,1)S(1)} %multiply_convert_fusion), channel_id=1, source_target_pairs={{96,0},{112,16},{128,32},{144,48},{160,64},{176,80},{192,96},{208,... | collective-permute-start | bytes 98312 | tf_op jit(solution)/shard_map/ppermute | solution.py:12

commit v2 on v1

--- a/solution.py
+++ b/solution.py
@@ -25,6 +25,13 @@
     return jnp.concatenate([real_part, imag_part], axis=1)
 
 
+def matrix_product(left, right):
+    product = jnp.einsum("cij,djk->cdik", left, right, preferred_element_type=jnp.float32)
+    real_part = product[0, 0] - product[1, 1]
+    imag_part = product[0, 1] + product[1, 0]
+    return jnp.stack([real_part, imag_part]).astype(jnp.bfloat16)
+
+
 def picked_rows(table, index):
     rows = table.shape[0]
     selector = (lax.broadcasted_iota(jnp.int32, (rows, index.shape[0]), 0) == index[None, :])
@@ -33,25 +40,57 @@
     )
 
 
+def sweeps(blocks, forward_src, backward_src):
+    count = lax.axis_size("section")
+    odd = lax.axis_index("section") % 2 == 1
+    swap = [(2 * y + side, 2 * y + 1 - side) for y in range(count // 2) for side in (0, 1)]
+    other_blocks, other_src = lax.ppermute(
+        (blocks, jnp.where(odd, backward_src, forward_src)), "section", swap
+    )
+    pair_map = matrix_product(
+        jnp.where(odd, blocks, other_blocks), jnp.where(odd, other_blocks, blocks)
+    )
+    pair_forward = (complex_product(blocks, other_src, False) + forward_src).astype(jnp.bfloat16)
+    pair_backward = (complex_product(blocks, other_src, True) + backward_src).astype(jnp.bfloat16)
+    pair_adjoint = jnp.stack([pair_map[0].T, -pair_map[1].T])
+    chain_map = jnp.where(odd, pair_map, pair_adjoint)
+    chain_src = jnp.where(odd, pair_forward, pair_backward)
+    chain = [(2 * y + 1, 2 * y + 3) for y in range(count // 2 - 1)]
+    chain += [(2 * y, 2 * y - 2) for y in range(1, count // 2)]
+    state = chain_src
+    for _ in range(count // 2 - 1):
+        state = (complex_product(chain_map, lax.ppermute(state, "section", chain), False)
+                 + chain_src).astype(jnp.bfloat16)
+    hand_over = [(s, s + 1) for s in range(1, count - 1, 2)]
+    hand_over += [(s, s - 1) for s in range(2, count, 2)]
+    neighbour = lax.ppermute(state, "section", hand_over)
+    fields = jnp.where(
+        odd, state, (complex_product(blocks, neighbour, False) + forward_src).astype(jnp.bfloat16)
+    )
+    adjoints = jnp.where(
+        odd, (complex_product(blocks, neighbour, True) + backward_src).astype(jnp.bfloat16), state
+    )
+    return fields, adjoints
+
+
+def shifted_copies(sent, direction):
+    copies = []
+    step = 1
+    while len(copies) < MAX_SHIFT:
+        width = min(step, MAX_SHIFT - len(copies))
+        payload = jnp.stack(([sent] + copies)[:width])
+        arrived = passed_along(payload, "energy", direction * step)
+        copies.extend(arrived[j] for j in range(width))
+        step *= 2
+    return copies
+
+
 def on_device(
     propagator, forward_source, backward_source, left_orbital, right_orbital, phonon_shift, coupling
 ):
     orbitals = propagator.shape[3]
     modes = forward_source.shape[3] // 2
-    blocks = propagator[0, 0]
-    forward_src = forward_source[0, 0]
-    backward_src = backward_source[0, 0]
-    relay_turns = lax.axis_size("section") - 1
-
-    def relay_turn(turn_index, state):
-        fields, adjoints = state
-        incoming = passed_along(fields, "section", 1)
-        returning = passed_along(adjoints, "section", -1)
-        fields = (complex_product(blocks, incoming, False) + forward_src).astype(jnp.bfloat16)
-        adjoints = (complex_product(blocks, returning, True) + backward_src).astype(jnp.bfloat16)
-        return fields, adjoints
-
-    fields, adjoints = lax.fori_loop(0, relay_turns, relay_turn, (forward_src, backward_src))
+    fields, adjoints = sweeps(propagator[0, 0], forward_source[0, 0], backward_source[0, 0])
 
     section_base = lax.axis_index("section") * orbitals
     left_rows = picked_rows(fields, left_orbital - section_base)
@@ -63,14 +102,14 @@
     lesser_part = jnp.stack([real_part, imag_part]) * modes ** (-0.5)
 
     sent = lesser_part.astype(jnp.bfloat16)
+    moved = {0: lesser_part}
+    for direction in (1, -1):
+        for j, copy in enumerate(shifted_copies(sent, direction)):
+            moved[direction * (j + 1)] = copy.astype(jnp.float32)
     self_energy = jnp.zeros_like(lesser_part)
     for offset in range(-MAX_SHIFT, MAX_SHIFT + 1):
         weight = jnp.sum(jnp.where((phonon_shift == offset)[:, None], coupling, 0.0), axis=0)
-        if offset == 0:
-            moved = lesser_part
-        else:
-            moved = passed_along(sent, "energy", offset).astype(jnp.float32)
-        self_energy = self_energy + weight[None, :] * moved
+        self_energy = self_energy + weight[None, :] * moved[offset]
     return self_energy[:, None, :]
 
 

time: 246 us -> 153 us (0.62)
  the two profiles are of different devices: /device:TPU:27 before, /device:TPU:82 now
where the time goes in v2:
time: 153 us; the launch traced here: 152 us
  waiting for transfers between devices  69.2 us (45%)
  starting transfers between devices  44.4 us (29%)
  other arithmetic  16.4 us (11%)
  matrix products  13.2 us (9%)
  local copies, waits for them, and re-layouts  8.09 us (5%)
    ppermute x6, waiting for transfers between devices, passed_along(): lax.ppermute(value, axis, [(source, source + steps) for source in range(l...  33.1 us
    ppermute x7, waiting for transfers between devices, sweeps(): lax.ppermute(state, 'section', chain)  32.2 us
    ppermute x6, starting transfers between devices, passed_along(): lax.ppermute(value, axis, [(source, source + steps) for source in range(l...  23.4 us
    ppermute x7, starting transfers between devices, sweeps(): lax.ppermute(state, 'section', chain)  14.7 us
    convert_element_type x7, other arithmetic, sweeps(): state = (complex_product(chain_map, lax.ppermute(state, 'section', chain)...  6.47 us
    dot_general x2, matrix products, picked_rows(): jnp.einsum('ar,ap->rp', table, selector.astype(table.dtype), preferred_el...  5.93 us
    unnamed x22, local copies, waits for them, and re-layouts  5.56 us
    dot_general x9, matrix products, complex_product(): jnp.einsum('cij,jn->cin', matrix, columns, preferred_element_type=jnp.flo...  4.82 us
  transfers between devices with their start and end apart: 16, of which 12 were waited for; matrix products, arithmetic and copies ran while one was open for 11% of the time, Pallas kernels for 0%

profile of v2, /device:TPU:82, one launch (start us, length us, event | category | flops | bytes accessed | tf_op | source)
XLA Modules:
  0.0 151.8 jit_solution(10715007433640567340)
XLA Ops:
  0.0 1.1 copy.13
  1.1 1.0 copy.14
  2.2 1.9 %collective-permute-start.1 = (bf16[384,128]{0,1:T(8,128)(2,1)S(1)}, bf16[384,128]{0,1:T(8,128)(2,1)S(1)}, u32[]{:S(2)}, u32[]{:S(2)}) collective-permute-start(bf16[384,128]{0,1:T(8,128)(2,1)S(1)} %select_bitcast_fusion), channel_id=1, source_target_pairs={{0,1},{1,0},{2,3},{3,2},{4,5},{5,4},{6,7},{7,6},{8,9},{9,8},{10,11... | collective-permute-start | bytes 294920 | tf_op jit(solution)/shard_map/ppermute | solution.py:47
  4.1 2.4 %collective-permute-start = (bf16[2,384,384]{2,1,0:T(8,128)(2,1)}, bf16[2,384,384]{2,1,0:T(8,128)(2,1)S(1)}, u32[]{:S(2)}, u32[]{:S(2)}) collective-permute-start(bf16[2,384,384]{2,1,0:T(8,128)(2,1)} %bitcast.258), channel_id=1, source_target_pairs={{0,1},{1,0},{2,3},{3,2},{4,5},{5,4},{6,7},{7,6},{8,9},{9,8},{10,11... | collective-permute-start | bytes 1769480 | tf_op jit(solution)/shard_map/ppermute | solution.py:47
  6.5 1.3 convolution_bitcast_fusion.3
  7.9 1.4 convolution_bitcast_fusion.4
  9.3 0.7 fusion.28
  10.0 2.3 %collective-permute-start.2 = (bf16[384,128]{0,1:T(8,128)(2,1)}, bf16[384,128]{0,1:T(8,128)(2,1)}, u32[]{:S(2)}, u32[]{:S(2)}) collective-permute-start(bf16[384,128]{0,1:T(8,128)(2,1)} %fusion.28), channel_id=1, source_target_pairs={{1,3},{3,5},{5,7},{7,9},{9,11},{11,13},{13,15},{2,0},{4,2},{6,4},{... | collective-permute-start | bytes 294920 | tf_op jit(solution)/shard_map/ppermute | solution.py:62
  12.4 0.8 convolution_bitcast_fusion
  13.2 1.1 fusion.111
  14.3 1.3 copy.21
  15.6 2.1 %copy.22 = f32[1,1,384,384]{3,2,1,0:T(8,128)} copy(f32[1,1,384,384]{2,3,0,1:T(8,128)} %get-tuple-element.22) | data formatting | bytes 1179648
  17.7 1.8 %fusion.119 = bf16[1,384,384]{1,2,0:T(8,128)(2,1)} fusion(f32[1,1,384,384]{3,2,1,0:T(8,128)S(1)} %copy.21, f32[1,1,384,384]{3,2,1,0:T(8,128)} %copy.22), kind=kLoop, calls=%fused_computation.205 | loop fusion | flops 294912 | bytes 1474560 | tf_op jit(solution)/shard_map/stack | solution.py:55
  19.5 1.8 %fusion.120 = bf16[1,384,384]{2,1,0:T(8,128)(2,1)} fusion(f32[1,1,384,384]{3,2,1,0:T(8,128)S(1)} %copy.21, f32[1,1,384,384]{3,2,1,0:T(8,128)} %copy.22), kind=kLoop, calls=%fused_computation.206 | loop fusion | flops 294912 | bytes 1474560 | tf_op jit(solution)/shard_map/sub | solution.py:30
  21.5 1.2 copy.12
  22.6 0.2 copy.11
  22.8 1.1 maximum_select_fusion
  23.9 1.2 fusion.69
  25.2 0.9 fusion.17
  26.1 2.4 %collective-permute-start.3 = (bf16[384,128]{0,1:T(8,128)(2,1)S(1)}, bf16[384,128]{0,1:T(8,128)(2,1)S(1)}, u32[]{:S(2)}, u32[]{:S(2)}) collective-permute-start(bf16[384,128]{0,1:T(8,128)(2,1)S(1)} %fusion.17), channel_id=1, source_target_pairs={{1,3},{3,5},{5,7},{7,9},{9,11},{11,13},{13,15},{2,0},{4,2},{6,4},{... | collective-permute-start | bytes 294920 | tf_op jit(solution)/shard_map/ppermute | solution.py:62
  28.5 4.1 %collective-permute-done.3 = bf16[384,128]{0,1:T(8,128)(2,1)S(1)} collective-permute-done((bf16[384,128]{0,1:T(8,128)(2,1)S(1)}, bf16[384,128]{0,1:T(8,128)(2,1)S(1)}, u32[]{:S(2)}, u32[]{:S(2)}) %collective-permute-start.3) | collective-permute-done | bytes 98336 | tf_op jit(solution)/shard_map/ppermute | solution.py:62
  32.6 0.3 fusion.67
  33.0 0.9 fusion.18
  33.9 2.4 %collective-permute-start.4 = (bf16[384,128]{0,1:T(8,128)(2,1)S(1)}, bf16[384,128]{0,1:T(8,128)(2,1)S(1)}, u32[]{:S(2)}, u32[]{:S(2)}) collective-permute-start(bf16[384,128]{0,1:T(8,128)(2,1)S(1)} %fusion.18), channel_id=1, source_target_pairs={{1,3},{3,5},{5,7},{7,9},{9,11},{11,13},{13,15},{2,0},{4,2},{6,4},{... | collective-permute-start | bytes 294920 | tf_op jit(solution)/shard_map/ppermute | solution.py:62
  36.3 4.9 %collective-permute-done.4 = bf16[384,128]{0,1:T(8,128)(2,1)S(1)} collective-permute-done((bf16[384,128]{0,1:T(8,128)(2,1)S(1)}, bf16[384,128]{0,1:T(8,128)(2,1)S(1)}, u32[]{:S(2)}, u32[]{:S(2)}) %collective-permute-start.4) | collective-permute-done | bytes 98336 | tf_op jit(solution)/shard_map/ppermute | solution.py:62
  41.2 0.3 fusion.65
  41.5 0.9 fusion.19
  42.5 1.9 %collective-permute-start.5 = (bf16[384,128]{0,1:T(8,128)(2,1)S(1)}, bf16[384,128]{0,1:T(8,128)(2,1)S(1)}, u32[]{:S(2)}, u32[]{:S(2)}) collective-permute-start(bf16[384,128]{0,1:T(8,128)(2,1)S(1)} %fusion.19), channel_id=1, source_target_pairs={{1,3},{3,5},{5,7},{7,9},{9,11},{11,13},{13,15},{2,0},{4,2},{6,4},{... | collective-permute-start | bytes 294920 | tf_op jit(solution)/shard_map/ppermute | solution.py:62
  44.4 5.8 %collective-permute-done.5 = bf16[384,128]{0,1:T(8,128)(2,1)S(1)} collective-permute-done((bf16[384,128]{0,1:T(8,128)(2,1)S(1)}, bf16[384,128]{0,1:T(8,128)(2,1)S(1)}, u32[]{:S(2)}, u32[]{:S(2)}) %collective-permute-start.5) | collective-permute-done | bytes 98336 | tf_op jit(solution)/shard_map/ppermute | solution.py:62
  50.2 0.3 fusion.63
  50.5 0.9 fusion.20
  51.5 1.9 %collective-permute-start.6 = (bf16[384,128]{0,1:T(8,128)(2,1)S(1)}, bf16[384,128]{0,1:T(8,128)(2,1)S(1)}, u32[]{:S(2)}, u32[]{:S(2)}) collective-permute-start(bf16[384,128]{0,1:T(8,128)(2,1)S(1)} %fusion.20), channel_id=1, source_target_pairs={{1,3},{3,5},{5,7},{7,9},{9,11},{11,13},{13,15},{2,0},{4,2},{6,4},{... | collective-permute-start | bytes 294920 | tf_op jit(solution)/shard_map/ppermute | solution.py:62
  53.4 5.8 %collective-permute-done.6 = bf16[384,128]{0,1:T(8,128)(2,1)S(1)} collective-permute-done((bf16[384,128]{0,1:T(8,128)(2,1)S(1)}, bf16[384,128]{0,1:T(8,128)(2,1)S(1)}, u32[]{:S(2)}, u32[]{:S(2)}) %collective-permute-start.6) | collective-permute-done | bytes 98336 | tf_op jit(solution)/shard_map/ppermute | solution.py:62
  59.2 0.3 fusion.61
  59.5 0.9 fusion.21
  60.5 1.9 %collective-permute-start.7 = (bf16[384,128]{0,1:T(8,128)(2,1)S(1)}, bf16[384,128]{0,1:T(8,128)(2,1)S(1)}, u32[]{:S(2)}, u32[]{:S(2)}) collective-permute-start(bf16[384,128]{0,1:T(8,128)(2,1)S(1)} %fusion.21), channel_id=1, source_target_pairs={{1,3},{3,5},{5,7},{7,9},{9,11},{11,13},{13,15},{2,0},{4,2},{6,4},{... | collective-permute-start | bytes 294920 | tf_op jit(solution)/shard_map/ppermute | solution.py:62
  62.4 5.8 %collective-permute-done.7 = bf16[384,128]{0,1:T(8,128)(2,1)S(1)} collective-permute-done((bf16[384,128]{0,1:T(8,128)(2,1)S(1)}, bf16[384,128]{0,1:T(8,128)(2,1)S(1)}, u32[]{:S(2)}, u32[]{:S(2)}) %collective-permute-start.7) | collective-permute-done | bytes 98336 | tf_op jit(solution)/shard_map/ppermute | solution.py:62
  68.2 0.3 fusion.59
  68.5 0.9 fusion.22
  69.5 1.9 %collective-permute-start.8 = (bf16[384,128]{0,1:T(8,128)(2,1)S(1)}, bf16[384,128]{0,1:T(8,128)(2,1)S(1)}, u32[]{:S(2)}, u32[]{:S(2)}) collective-permute-start(bf16[384,128]{0,1:T(8,128)(2,1)S(1)} %fusion.22), channel_id=1, source_target_pairs={{1,3},{3,5},{5,7},{7,9},{9,11},{11,13},{13,15},{2,0},{4,2},{6,4},{... | collective-permute-start | bytes 294920 | tf_op jit(solution)/shard_map/ppermute | solution.py:62
  71.4 5.8 %collective-permute-done.8 = bf16[384,128]{0,1:T(8,128)(2,1)S(1)} collective-permute-done((bf16[384,128]{0,1:T(8,128)(2,1)S(1)}, bf16[384,128]{0,1:T(8,128)(2,1)S(1)}, u32[]{:S(2)}, u32[]{:S(2)}) %collective-permute-start.8) | collective-permute-done | bytes 98336 | tf_op jit(solution)/shard_map/ppermute | solution.py:62
  77.2 0.3 fusion.57
  77.6 0.9 fusion.23
  78.5 1.9 %collective-permute-start.9 = (bf16[384,128]{0,1:T(8,128)(2,1)S(1)}, bf16[384,128]{0,1:T(8,128)(2,1)S(1)}, u32[]{:S(2)}, u32[]{:S(2)}) collective-permute-start(bf16[384,128]{0,1:T(8,128)(2,1)S(1)} %fusion.23), channel_id=1, source_target_pairs={{1,2},{3,4},{5,6},{7,8},{9,10},{11,12},{13,14},{2,1},{4,3},{6,5},{... | collective-permute-start | bytes 294920 | tf_op jit(solution)/shard_map/ppermute | solution.py:66
  80.4 4.0 %collective-permute-done.9 = bf16[384,128]{0,1:T(8,128)(2,1)S(1)} collective-permute-done((bf16[384,128]{0,1:T(8,128)(2,1)S(1)}, bf16[384,128]{0,1:T(8,128)(2,1)S(1)}, u32[]{:S(2)}, u32[]{:S(2)}) %collective-permute-start.9) | collective-permute-done | bytes 98336 | tf_op jit(solution)/shard_map/ppermute | solution.py:66
  84.4 0.3 convolution_bitcast_fusion.1
  84.7 0.3 convolution_bitcast_fusion.2
  85.1 2.8 %fusion.1 = f32[128,8192]{1,0:T(8,128)S(1)} fusion(s32[8192]{0:T(1024)S(1)} %broadcast_subtract_fusion, bf16[384,128]{0,1:T(8,128)(2,1)S(1)} %fusion.23, f32[384,64]{0,1:T(8,128)S(1)} %get-tuple-element.27, f32[384,64]{0,1:T(8,128)S(1)} %get-tuple-element.26, bf16[1,1,384,128]{2,3,1,0:T(8,128)(2,1)S(1)} %copy-done.4, pred[]{:T(512)S(6)} %eq.61), kind=kOutput, calls=%fused_computation.3 | convolution fusion | flops 808697856 | bytes 4620289 | tf_op jit(solution)/shard_map/ar,ap->rp/dot_general | solution.py:38
  87.9 3.2 %multiply_reduce_fusion = (f32[8192]{0:T(1024)S(1)}, f32[128,8192]{1,0:T(8,128)S(1)}) fusion(f32[128,8192]{1,0:T(8,128)S(1)} %fusion.1, s32[8192]{0:T(1024)S(1)} %broadcast_subtract_fusion.1, bf16[384,128]{0,1:T(8,128)(2,1)S(1)} %fusion.23, f32[384,64]{0,1:T(8,128)S(1)} %get-tuple-element.25, f32[384,64]{0,1:T(8,128)S(1)} %get-tuple-element.24, ...), kind=kOutput, calls=%fused_computation.6 | convolution fusion | flops 810786816 | bytes 8847361 | tf_op jit(solution)/shard_map/ar,ap->rp/dot_general | solution.py:38
  91.1 0.9 fusion.4
  92.1 1.9 %collective-permute-start.10 = (bf16[1,2,8192]{2,0,1:T(2,128)(2,1)S(1)}, bf16[1,2,8192]{2,0,1:T(2,128)(2,1)S(1)}, u32[]{:S(2)}, u32[]{:S(2)}) collective-permute-start(bf16[1,2,8192]{2,0,1:T(2,128)(2,1)S(1)} %copy.24), channel_id=1, source_target_pairs={{16,0},{32,16},{48,32},{64,48},{80,64},{96,80},{112,96},{128,112},... | collective-permute-start | bytes 98312 | tf_op jit(solution)/shard_map/ppermute | solution.py:12
  94.0 4.5 %collective-permute-start.13 = (bf16[1,2,8192]{2,0,1:T(2,128)(2,1)S(1)}, bf16[1,2,8192]{2,0,1:T(2,128)(2,1)S(1)}, u32[]{:S(2)}, u32[]{:S(2)}) collective-permute-start(bf16[1,2,8192]{2,0,1:T(2,128)(2,1)S(1)} %copy.24), channel_id=1, source_target_pairs={{0,16},{16,32},{32,48},{48,64},{64,80},{80,96},{96,112},{112,128},... | collective-permute-start | bytes 98312 | tf_op jit(solution)/shard_map/ppermute | solution.py:12
  98.6 15.6 %collective-permute-done.13 = bf16[1,2,8192]{2,0,1:T(2,128)(2,1)S(1)} collective-permute-done((bf16[1,2,8192]{2,0,1:T(2,128)(2,1)S(1)}, bf16[1,2,8192]{2,0,1:T(2,128)(2,1)S(1)}, u32[]{:S(2)}, u32[]{:S(2)}) %collective-permute-start.13) | collective-permute-done | bytes 32800 | tf_op jit(solution)/shard_map/ppermute | solution.py:12
  114.2 0.2 pad_maximum_fusion.2
  114.4 5.4 %collective-permute-start.11 = (bf16[2,2,8192]{2,0,1:T(2,128)(2,1)S(1)}, bf16[2,2,8192]{2,0,1:T(2,128)(2,1)S(1)}, u32[]{:S(2)}, u32[]{:S(2)}) collective-permute-start(bf16[2,2,8192]{2,0,1:T(2,128)(2,1)S(1)} %get-tuple-element.48), channel_id=1, source_target_pairs={{32,0},{48,16},{64,32},{80,48},{96,64},{112,80},{128,96},{144,112}... | collective-permute-start | bytes 196616 | tf_op jit(solution)/shard_map/ppermute | solution.py:12
  119.8 1.9 %collective-permute-start.14 = (bf16[2,2,8192]{2,0,1:T(2,128)(2,1)S(1)}, bf16[2,2,8192]{2,0,1:T(2,128)(2,1)S(1)}, u32[]{:S(2)}, u32[]{:S(2)}) collective-permute-start(bf16[2,2,8192]{2,0,1:T(2,128)(2,1)S(1)} %get-tuple-element.49), channel_id=1, source_target_pairs={{0,32},{16,48},{32,64},{48,80},{64,96},{80,112},{96,128},{112,144}... | collective-permute-start | bytes 196616 | tf_op jit(solution)/shard_map/ppermute | solution.py:12
  121.7 1.1 select_reduce_fusion.12
  122.9 7.4 %collective-permute-done.14 = bf16[2,2,8192]{2,0,1:T(2,128)(2,1)S(1)} collective-permute-done((bf16[2,2,8192]{2,0,1:T(2,128)(2,1)S(1)}, bf16[2,2,8192]{2,0,1:T(2,128)(2,1)S(1)}, u32[]{:S(2)}, u32[]{:S(2)}) %collective-permute-start.14) | collective-permute-done | bytes 65568 | tf_op jit(solution)/shard_map/ppermute | solution.py:12
  130.3 0.4 fusion.24
  130.7 1.9 %collective-permute-start.12 = (bf16[3,2,8192]{2,0,1:T(4,128)(2,1)S(1)}, bf16[3,2,8192]{2,0,1:T(4,128)(2,1)S(1)}, u32[]{:S(2)}, u32[]{:S(2)}) collective-permute-start(bf16[3,2,8192]{2,0,1:T(4,128)(2,1)S(1)} %get-tuple-element.46), channel_id=1, source_target_pairs={{64,0},{80,16},{96,32},{112,48},{128,64},{144,80},{160,96},{176,11... | collective-permute-start | bytes 294920 | tf_op jit(solution)/shard_map/ppermute | solution.py:12
  132.6 7.8 %collective-permute-start.15 = (bf16[3,2,8192]{2,0,1:T(4,128)(2,1)S(1)}, bf16[3,2,8192]{2,0,1:T(4,128)(2,1)S(1)}, u32[]{:S(2)}, u32[]{:S(2)}) collective-permute-start(bf16[3,2,8192]{2,0,1:T(4,128)(2,1)S(1)} %get-tuple-element.47), channel_id=1, source_target_pairs={{0,64},{16,80},{32,96},{48,112},{64,128},{80,144},{96,160},{112,17... | collective-permute-start | bytes 294920 | tf_op jit(solution)/shard_map/ppermute | solution.py:12
  140.5 5.9 %collective-permute-done.12 = bf16[3,2,8192]{2,0,1:T(4,128)(2,1)S(1)} collective-permute-done((bf16[3,2,8192]{2,0,1:T(4,128)(2,1)S(1)}, bf16[3,2,8192]{2,0,1:T(4,128)(2,1)S(1)}, u32[]{:S(2)}, u32[]{:S(2)}) %collective-permute-start.12) | collective-permute-done | bytes 98336 | tf_op jit(solution)/shard_map/ppermute | solution.py:12
  146.4 4.0 %collective-permute-done.15 = bf16[3,2,8192]{2,0,1:T(4,128)(2,1)S(1)} collective-permute-done((bf16[3,2,8192]{2,0,1:T(4,128)(2,1)S(1)}, bf16[3,2,8192]{2,0,1:T(4,128)(2,1)S(1)}, u32[]{:S(2)}, u32[]{:S(2)}) %collective-permute-start.15) | collective-permute-done | bytes 98336 | tf_op jit(solution)/shard_map/ppermute | solution.py:12
  150.4 1.4 fusion.77
  (42 shorter events, 0.7 us)
Async XLA Ops:
  0.0 12.4 %copy-start = (bf16[1,1,2,384,384]{4,3,2,1,0:T(8,128)(2,1)S(1)}, bf16[1,1,2,384,384]{4,3,2,1,0:T(8,128)(2,1)}, u32[]{:S(2)}) copy-start(bf16[1,1,2,384,384]{4,3,2,1,0:T(8,128)(2,1)} %param.7) | copy-start | bytes 1769476
  1.1 11.3 %copy-start.3 = (bf16[1,1,384,128]{2,3,1,0:T(8,128)(2,1)}, bf16[1,1,384,128]{2,3,1,0:T(8,128)(2,1)S(1)}, u32[]{:S(2)}) copy-start(bf16[1,1,384,128]{2,3,1,0:T(8,128)(2,1)S(1)} %copy.13) | copy-start | bytes 294916
  2.1 10.2 %copy-start.1 = (bf16[1,1,384,128]{2,3,1,0:T(8,128)(2,1)}, bf16[1,1,384,128]{2,3,1,0:T(8,128)(2,1)S(1)}, u32[]{:S(2)}) copy-start(bf16[1,1,384,128]{2,3,1,0:T(8,128)(2,1)S(1)} %copy.14) | copy-start | bytes 294916
  2.2 4.3 %collective-permute-start.1 = (bf16[384,128]{0,1:T(8,128)(2,1)S(1)}, bf16[384,128]{0,1:T(8,128)(2,1)S(1)}, u32[]{:S(2)}, u32[]{:S(2)}) collective-permute-start(bf16[384,128]{0,1:T(8,128)(2,1)S(1)} %select_bitcast_fusion), channel_id=1, source_target_pairs={{0,1},{1,0},{2,3},{3,2},{4,5},{5,4},{6,7},{7,6},{8,9},{9,8},{10,11... | collective-permute-start | bytes 294920 | tf_op jit(solution)/shard_map/ppermute | solution.py:47
  4.1 8.3 %collective-permute-start = (bf16[2,384,384]{2,1,0:T(8,128)(2,1)}, bf16[2,384,384]{2,1,0:T(8,128)(2,1)S(1)}, u32[]{:S(2)}, u32[]{:S(2)}) collective-permute-start(bf16[2,384,384]{2,1,0:T(8,128)(2,1)} %bitcast.258), channel_id=1, source_target_pairs={{0,1},{1,0},{2,3},{3,2},{4,5},{5,4},{6,7},{7,6},{8,9},{9,8},{10,11... | collective-permute-start | bytes 1769480 | tf_op jit(solution)/shard_map/ppermute | solution.py:47
  10.0 13.9 %collective-permute-start.2 = (bf16[384,128]{0,1:T(8,128)(2,1)}, bf16[384,128]{0,1:T(8,128)(2,1)}, u32[]{:S(2)}, u32[]{:S(2)}) collective-permute-start(bf16[384,128]{0,1:T(8,128)(2,1)} %fusion.28), channel_id=1, source_target_pairs={{1,3},{3,5},{5,7},{7,9},{9,11},{11,13},{13,15},{2,0},{4,2},{6,4},{... | collective-permute-start | bytes 294920 | tf_op jit(solution)/shard_map/ppermute | solution.py:62
  26.1 6.5 %collective-permute-start.3 = (bf16[384,128]{0,1:T(8,128)(2,1)S(1)}, bf16[384,128]{0,1:T(8,128)(2,1)S(1)}, u32[]{:S(2)}, u32[]{:S(2)}) collective-permute-start(bf16[384,128]{0,1:T(8,128)(2,1)S(1)} %fusion.17), channel_id=1, source_target_pairs={{1,3},{3,5},{5,7},{7,9},{9,11},{11,13},{13,15},{2,0},{4,2},{6,4},{... | collective-permute-start | bytes 294920 | tf_op jit(solution)/shard_map/ppermute | solution.py:62
  33.9 7.3 %collective-permute-start.4 = (bf16[384,128]{0,1:T(8,128)(2,1)S(1)}, bf16[384,128]{0,1:T(8,128)(2,1)S(1)}, u32[]{:S(2)}, u32[]{:S(2)}) collective-permute-start(bf16[384,128]{0,1:T(8,128)(2,1)S(1)} %fusion.18), channel_id=1, source_target_pairs={{1,3},{3,5},{5,7},{7,9},{9,11},{11,13},{13,15},{2,0},{4,2},{6,4},{... | collective-permute-start | bytes 294920 | tf_op jit(solution)/shard_map/ppermute | solution.py:62
  42.4 29.0 %copy-start.6 = (s32[8192]{0:T(1024)S(1)}, s32[8192]{0:T(1024)}, u32[]{:S(2)}) copy-start(s32[8192]{0:T(1024)} %param.11) | copy-start | bytes 98308
  42.5 7.7 %collective-permute-start.5 = (bf16[384,128]{0,1:T(8,128)(2,1)S(1)}, bf16[384,128]{0,1:T(8,128)(2,1)S(1)}, u32[]{:S(2)}, u32[]{:S(2)}) collective-permute-start(bf16[384,128]{0,1:T(8,128)(2,1)S(1)} %fusion.19), channel_id=1, source_target_pairs={{1,3},{3,5},{5,7},{7,9},{9,11},{11,13},{13,15},{2,0},{4,2},{6,4},{... | collective-permute-start | bytes 294920 | tf_op jit(solution)/shard_map/ppermute | solution.py:62
  51.5 29.0 %copy-start.7 = (s32[8192]{0:T(1024)S(1)}, s32[8192]{0:T(1024)}, u32[]{:S(2)}) copy-start(s32[8192]{0:T(1024)} %param.10) | copy-start | bytes 98308
  51.5 7.7 %collective-permute-start.6 = (bf16[384,128]{0,1:T(8,128)(2,1)S(1)}, bf16[384,128]{0,1:T(8,128)(2,1)S(1)}, u32[]{:S(2)}, u32[]{:S(2)}) collective-permute-start(bf16[384,128]{0,1:T(8,128)(2,1)S(1)} %fusion.20), channel_id=1, source_target_pairs={{1,3},{3,5},{5,7},{7,9},{9,11},{11,13},{13,15},{2,0},{4,2},{6,4},{... | collective-permute-start | bytes 294920 | tf_op jit(solution)/shard_map/ppermute | solution.py:62
  60.5 7.7 %collective-permute-start.7 = (bf16[384,128]{0,1:T(8,128)(2,1)S(1)}, bf16[384,128]{0,1:T(8,128)(2,1)S(1)}, u32[]{:S(2)}, u32[]{:S(2)}) collective-permute-start(bf16[384,128]{0,1:T(8,128)(2,1)S(1)} %fusion.21), channel_id=1, source_target_pairs={{1,3},{3,5},{5,7},{7,9},{9,11},{11,13},{13,15},{2,0},{4,2},{6,4},{... | collective-permute-start | bytes 294920 | tf_op jit(solution)/shard_map/ppermute | solution.py:62
  68.5 16.6 %copy-start.4 = (bf16[1,1,384,128]{2,3,1,0:T(8,128)(2,1)S(1)}, bf16[1,1,384,128]{2,3,1,0:T(8,128)(2,1)}, u32[]{:S(2)}) copy-start(bf16[1,1,384,128]{2,3,1,0:T(8,128)(2,1)} %copy-done.3) | copy-start | bytes 294916
  69.5 7.7 %collective-permute-start.8 = (bf16[384,128]{0,1:T(8,128)(2,1)S(1)}, bf16[384,128]{0,1:T(8,128)(2,1)S(1)}, u32[]{:S(2)}, u32[]{:S(2)}) collective-permute-start(bf16[384,128]{0,1:T(8,128)(2,1)S(1)} %fusion.22), channel_id=1, source_target_pairs={{1,3},{3,5},{5,7},{7,9},{9,11},{11,13},{13,15},{2,0},{4,2},{6,4},{... | collective-permute-start | bytes 294920 | tf_op jit(solution)/shard_map/ppermute | solution.py:62
  78.5 5.9 %collective-permute-start.9 = (bf16[384,128]{0,1:T(8,128)(2,1)S(1)}, bf16[384,128]{0,1:T(8,128)(2,1)S(1)}, u32[]{:S(2)}, u32[]{:S(2)}) collective-permute-start(bf16[384,128]{0,1:T(8,128)(2,1)S(1)} %fusion.23), channel_id=1, source_target_pairs={{1,2},{3,4},{5,6},{7,8},{9,10},{11,12},{13,14},{2,1},{4,3},{6,5},{... | collective-permute-start | bytes 294920 | tf_op jit(solution)/shard_map/ppermute | solution.py:66
  85.0 2.8 %copy-start.2 = (bf16[1,1,384,128]{2,3,1,0:T(8,128)(2,1)S(1)}, bf16[1,1,384,128]{2,3,1,0:T(8,128)(2,1)}, u32[]{:S(2)}) copy-start(bf16[1,1,384,128]{2,3,1,0:T(8,128)(2,1)} %copy-done.1) | copy-start | bytes 294916
  91.0 7.4 %copy-start.8 = (s32[8]{0:T(128)S(1)}, s32[8]{0:T(128)}, u32[]{:S(2)}) copy-start(s32[8]{0:T(128)} %param.12) | copy-start | bytes 100
  91.1 30.7 %copy-start.5 = (f32[8,8192]{1,0:T(8,128)S(1)}, f32[8,8192]{1,0:T(8,128)}, u32[]{:S(2)}) copy-start(f32[8,8192]{1,0:T(8,128)} %param.13) | copy-start | bytes 786436
  92.1 6.5 %collective-permute-start.10 = (bf16[1,2,8192]{2,0,1:T(2,128)(2,1)S(1)}, bf16[1,2,8192]{2,0,1:T(2,128)(2,1)S(1)}, u32[]{:S(2)}, u32[]{:S(2)}) collective-permute-start(bf16[1,2,8192]{2,0,1:T(2,128)(2,1)S(1)} %copy.24), channel_id=1, source_target_pairs={{16,0},{32,16},{48,32},{64,48},{80,64},{96,80},{112,96},{128,112},... | collective-permute-start | bytes 98312 | tf_op jit(solution)/shard_map/ppermute | solution.py:12
  94.0 20.2 %collective-permute-start.13 = (bf16[1,2,8192]{2,0,1:T(2,128)(2,1)S(1)}, bf16[1,2,8192]{2,0,1:T(2,128)(2,1)S(1)}, u32[]{:S(2)}, u32[]{:S(2)}) collective-permute-start(bf16[1,2,8192]{2,0,1:T(2,128)(2,1)S(1)} %copy.24), channel_id=1, source_target_pairs={{0,16},{16,32},{32,48},{48,64},{64,80},{80,96},{96,112},{112,128},... | collective-permute-start | bytes 98312 | tf_op jit(solution)/shard_map/ppermute | solution.py:12
  114.4 8.4 %collective-permute-start.11 = (bf16[2,2,8192]{2,0,1:T(2,128)(2,1)S(1)}, bf16[2,2,8192]{2,0,1:T(2,128)(2,1)S(1)}, u32[]{:S(2)}, u32[]{:S(2)}) collective-permute-start(bf16[2,2,8192]{2,0,1:T(2,128)(2,1)S(1)} %get-tuple-element.48), channel_id=1, source_target_pairs={{32,0},{48,16},{64,32},{80,48},{96,64},{112,80},{128,96},{144,112}... | collective-permute-start | bytes 196616 | tf_op jit(solution)/shard_map/ppermute | solution.py:12
  119.8 10.5 %collective-permute-start.14 = (bf16[2,2,8192]{2,0,1:T(2,128)(2,1)S(1)}, bf16[2,2,8192]{2,0,1:T(2,128)(2,1)S(1)}, u32[]{:S(2)}, u32[]{:S(2)}) collective-permute-start(bf16[2,2,8192]{2,0,1:T(2,128)(2,1)S(1)} %get-tuple-element.49), channel_id=1, source_target_pairs={{0,32},{16,48},{32,64},{48,80},{64,96},{80,112},{96,128},{112,144}... | collective-permute-start | bytes 196616 | tf_op jit(solution)/shard_map/ppermute | solution.py:12
  130.7 15.7 %collective-permute-start.12 = (bf16[3,2,8192]{2,0,1:T(4,128)(2,1)S(1)}, bf16[3,2,8192]{2,0,1:T(4,128)(2,1)S(1)}, u32[]{:S(2)}, u32[]{:S(2)}) collective-permute-start(bf16[3,2,8192]{2,0,1:T(4,128)(2,1)S(1)} %get-tuple-element.46), channel_id=1, source_target_pairs={{64,0},{80,16},{96,32},{112,48},{128,64},{144,80},{160,96},{176,11... | collective-permute-start | bytes 294920 | tf_op jit(solution)/shard_map/ppermute | solution.py:12
  132.6 17.8 %collective-permute-start.15 = (bf16[3,2,8192]{2,0,1:T(4,128)(2,1)S(1)}, bf16[3,2,8192]{2,0,1:T(4,128)(2,1)S(1)}, u32[]{:S(2)}, u32[]{:S(2)}) collective-permute-start(bf16[3,2,8192]{2,0,1:T(4,128)(2,1)S(1)} %get-tuple-element.47), channel_id=1, source_target_pairs={{0,64},{16,80},{32,96},{48,112},{64,128},{80,144},{96,160},{112,17... | collective-permute-start | bytes 294920 | tf_op jit(solution)/shard_map/ppermute | solution.py:12

commit v3 on v2

--- a/solution.py
+++ b/solution.py
@@ -29,7 +29,24 @@
     product = jnp.einsum("cij,djk->cdik", left, right, preferred_element_type=jnp.float32)
     real_part = product[0, 0] - product[1, 1]
     imag_part = product[0, 1] + product[1, 0]
-    return jnp.stack([real_part, imag_part]).astype(jnp.bfloat16)
+    return real_part, imag_part
+
+
+def adjoint_product(left, right):
+    product = jnp.einsum("ckj,dji->cdik", left, right, preferred_element_type=jnp.float32)
+    real_part = product[0, 0] - product[1, 1]
+    imag_part = -(product[0, 1] + product[1, 0])
+    return real_part, imag_part
+
+
+def stacked(columns):
+    half = columns.shape[1] // 2
+    return jnp.concatenate([columns[:, :half], columns[:, half:]], axis=0)
+
+
+def joined(rows):
+    half = rows.shape[0] // 2
+    return jnp.concatenate([rows[:half], rows[half:]], axis=1)
 
 
 def picked_rows(table, index):
@@ -47,20 +64,30 @@
     other_blocks, other_src = lax.ppermute(
         (blocks, jnp.where(odd, backward_src, forward_src)), "section", swap
     )
-    pair_map = matrix_product(
-        jnp.where(odd, blocks, other_blocks), jnp.where(odd, other_blocks, blocks)
+    left = jnp.where(odd, blocks, other_blocks)
+    right = jnp.where(odd, other_blocks, blocks)
+    forward_real, forward_imag = matrix_product(left, right)
+    backward_real, backward_imag = adjoint_product(left, right)
+    real_part = jnp.where(odd, forward_real, backward_real).astype(jnp.bfloat16)
+    imag_part = jnp.where(odd, forward_imag, backward_imag).astype(jnp.bfloat16)
+    chain_map = jnp.concatenate(
+        [
+            jnp.concatenate([real_part, -imag_part], axis=1),
+            jnp.concatenate([imag_part, real_part], axis=1),
+        ],
+        axis=0,
     )
     pair_forward = (complex_product(blocks, other_src, False) + forward_src).astype(jnp.bfloat16)
     pair_backward = (complex_product(blocks, other_src, True) + backward_src).astype(jnp.bfloat16)
-    pair_adjoint = jnp.stack([pair_map[0].T, -pair_map[1].T])
-    chain_map = jnp.where(odd, pair_map, pair_adjoint)
-    chain_src = jnp.where(odd, pair_forward, pair_backward)
+    chain_src = stacked(jnp.where(odd, pair_forward, pair_backward))
     chain = [(2 * y + 1, 2 * y + 3) for y in range(count // 2 - 1)]
     chain += [(2 * y, 2 * y - 2) for y in range(1, count // 2)]
     state = chain_src
     for _ in range(count // 2 - 1):
-        state = (complex_product(chain_map, lax.ppermute(state, "section", chain), False)
+        arrived = lax.ppermute(state, "section", chain)
+        state = (jnp.dot(chain_map, arrived, preferred_element_type=jnp.float32)
                  + chain_src).astype(jnp.bfloat16)
+    state = joined(state)
     hand_over = [(s, s + 1) for s in range(1, count - 1, 2)]
     hand_over += [(s, s - 1) for s in range(2, count, 2)]
     neighbour = lax.ppermute(state, "section", hand_over)

time: 153 us -> 143 us (0.935)
  the two profiles are of different devices: /device:TPU:82 before, /device:TPU:83 now
where the time goes in v3:
time: 143 us; the launch traced here: 142 us
  starting transfers between devices  70.1 us (49%)
  waiting for transfers between devices  45 us (31%)
  matrix products  15.7 us (11%)
  other arithmetic  6.6 us (5%)
  local copies, waits for them, and re-layouts  4.6 us (3%)
    ppermute x6, waiting for transfers between devices, passed_along(): lax.ppermute(value, axis, [(source, source + steps) for source in range(l...  33.1 us
    ppermute x7, starting transfers between devices, sweeps(): arrived = lax.ppermute(state, 'section', chain)  29.8 us
    ppermute x6, starting transfers between devices, passed_along(): lax.ppermute(value, axis, [(source, source + steps) for source in range(l...  22.2 us
    ppermute x1, starting transfers between devices, sweeps(): neighbour = lax.ppermute(state, 'section', hand_over)  13.4 us
    ppermute x7, waiting for transfers between devices, sweeps(): arrived = lax.ppermute(state, 'section', chain)  9.65 us
    dot_general x2, matrix products, picked_rows(): jnp.einsum('ar,ap->rp', table, selector.astype(table.dtype), preferred_el...  5.93 us
    dot_general x7, matrix products, sweeps(): jnp.dot(chain_map, arrived, preferred_element_type=jnp.float32) + chain_src  5.62 us
    ppermute x2, starting transfers between devices, sweeps(): lax.ppermute((blocks, jnp.where(odd, backward_src, forward_src)), 'sectio...  4.64 us
  transfers between devices with their start and end apart: 16, of which 11 were waited for; matrix products, arithmetic and copies ran while one was open for 6% of the time, Pallas kernels for 0%

profile of v3, /device:TPU:83, one launch (start us, length us, event | category | flops | bytes accessed | tf_op | source)
XLA Modules:
  0.0 142.4 jit_solution(5359418431101061582)
XLA Ops:
  0.0 1.0 copy.14
  1.0 1.0 copy.15
  2.0 0.0 copy-start
  2.1 2.7 %collective-permute-start.1 = (bf16[384,128]{0,1:T(8,128)(2,1)S(1)}, bf16[384,128]{0,1:T(8,128)(2,1)S(1)}, u32[]{:S(2)}, u32[]{:S(2)}) collective-permute-start(bf16[384,128]{0,1:T(8,128)(2,1)S(1)} %select_bitcast_fusion), channel_id=1, source_target_pairs={{0,1},{1,0},{2,3},{3,2},{4,5},{5,4},{6,7},{7,6},{8,9},{9,8},{10,11... | collective-permute-start | bytes 294920 | tf_op jit(solution)/shard_map/ppermute | solution.py:64
  4.8 1.9 %collective-permute-start = (bf16[2,384,384]{2,1,0:T(8,128)(2,1)}, bf16[2,384,384]{2,1,0:T(8,128)(2,1)S(1)}, u32[]{:S(2)}, u32[]{:S(2)}) collective-permute-start(bf16[2,384,384]{2,1,0:T(8,128)(2,1)} %bitcast.223), channel_id=1, source_target_pairs={{0,1},{1,0},{2,3},{3,2},{4,5},{5,4},{6,7},{7,6},{8,9},{9,8},{10,11... | collective-permute-start | bytes 1769480 | tf_op jit(solution)/shard_map/ppermute | solution.py:64
  6.7 0.0 collective-permute-done.1
  6.7 1.3 convolution_bitcast_fusion.2
  8.1 1.4 convolution_bitcast_fusion.3
  9.5 0.1 fusion.36
  9.6 0.6 pad_maximum_fusion.2
  10.2 3.2 %collective-permute-start.2 = (bf16[768,64]{0,1:T(8,128)(2,1)}, bf16[768,64]{0,1:T(8,128)(2,1)}, u32[]{:S(2)}, u32[]{:S(2)}) collective-permute-start(bf16[768,64]{0,1:T(8,128)(2,1)} %pad_maximum_fusion.2), channel_id=1, source_target_pairs={{1,3},{3,5},{5,7},{7,9},{9,11},{11,13},{13,15},{2,0},{4,2},{6,4},{... | collective-permute-start | bytes 294920 | tf_op jit(solution)/shard_map/ppermute | solution.py:87
  13.4 0.0 collective-permute-done
  13.4 0.8 fusion.20
  14.3 2.0 %copy.9 = f32[2,384,2,384]{1,3,0,2:T(8,128)} copy(f32[2,384,2,384]{3,1,2,0:T(8,128)S(1)} %fusion.20) | data formatting | bytes 4718592 | tf_op jit(solution)/shard_map/cij,djk->cdik/dot_general | solution.py:29
  16.3 1.5 %fusion.90 = (bf16[384,384]{1,0:T(8,128)(2,1)S(1)}, bf16[384,384]{1,0:T(8,128)(2,1)S(1)}) fusion(f32[2,2,384,384]{3,2,0,1:T(8,128)S(1)} %bitcast.221, f32[2,2,384,384]{3,2,1,0:T(8,128)} %bitcast.224, pred[]{:T(512)S(6)} %eq.61), kind=kLoop, calls=%fused_computation.173 | loop fusion | flops 884736 | bytes 2949121 | tf_op jit(solution)/shard_map/neg | solution.py:75
  17.8 0.5 copy-done.1
  18.3 0.1 fusion.26
  18.4 0.0 collective-permute-done.2
  18.4 1.5 %fusion.6 = bf16[768,64]{0,1:T(8,128)(2,1)S(1)} fusion(bf16[768,64]{0,1:T(8,128)(2,1)} %collective-permute-done.2, bf16[384,64]{0,1:T(8,128)(2,1)S(1)} %get-tuple-element.33, bf16[384,64]{0,1:T(8,128)(2,1)S(1)} %get-tuple-element.32, bf16[384,384]{1,0:T(8,128)(2,1)S(1)} %fusion.26, bf16[384,384]{1,0:T(8,128)(2,1)S(1)} %get-tuple-element.21, ...), kind=kOutput, calls=%fused_computation.23 | convolution fusion | flops 80510976 | bytes 1179648 | tf_op jit(solution)/shard_map/dot_general | solution.py:88
  19.9 4.4 %collective-permute-start.3 = (bf16[768,64]{0,1:T(8,128)(2,1)S(1)}, bf16[768,64]{0,1:T(8,128)(2,1)S(1)}, u32[]{:S(2)}, u32[]{:S(2)}) collective-permute-start(bf16[768,64]{0,1:T(8,128)(2,1)S(1)} %fusion.6), channel_id=1, source_target_pairs={{1,3},{3,5},{5,7},{7,9},{9,11},{11,13},{13,15},{2,0},{4,2},{6,4},{... | collective-permute-start | bytes 294920 | tf_op jit(solution)/shard_map/ppermute | solution.py:87
  24.3 1.6 %collective-permute-done.3 = bf16[768,64]{0,1:T(8,128)(2,1)S(1)} collective-permute-done((bf16[768,64]{0,1:T(8,128)(2,1)S(1)}, bf16[768,64]{0,1:T(8,128)(2,1)S(1)}, u32[]{:S(2)}, u32[]{:S(2)}) %collective-permute-start.3) | collective-permute-done | bytes 98336 | tf_op jit(solution)/shard_map/ppermute | solution.py:87
  25.9 0.5 fusion.7
  26.4 4.0 %collective-permute-start.4 = (bf16[768,64]{0,1:T(8,128)(2,1)S(1)}, bf16[768,64]{0,1:T(8,128)(2,1)S(1)}, u32[]{:S(2)}, u32[]{:S(2)}) collective-permute-start(bf16[768,64]{0,1:T(8,128)(2,1)S(1)} %fusion.7), channel_id=1, source_target_pairs={{1,3},{3,5},{5,7},{7,9},{9,11},{11,13},{13,15},{2,0},{4,2},{6,4},{... | collective-permute-start | bytes 294920 | tf_op jit(solution)/shard_map/ppermute | solution.py:87
  30.5 1.6 %collective-permute-done.4 = bf16[768,64]{0,1:T(8,128)(2,1)S(1)} collective-permute-done((bf16[768,64]{0,1:T(8,128)(2,1)S(1)}, bf16[768,64]{0,1:T(8,128)(2,1)S(1)}, u32[]{:S(2)}, u32[]{:S(2)}) %collective-permute-start.4) | collective-permute-done | bytes 98336 | tf_op jit(solution)/shard_map/ppermute | solution.py:87
  32.1 0.5 fusion.8
  32.6 3.7 %collective-permute-start.5 = (bf16[768,64]{0,1:T(8,128)(2,1)S(1)}, bf16[768,64]{0,1:T(8,128)(2,1)S(1)}, u32[]{:S(2)}, u32[]{:S(2)}) collective-permute-start(bf16[768,64]{0,1:T(8,128)(2,1)S(1)} %fusion.8), channel_id=1, source_target_pairs={{1,3},{3,5},{5,7},{7,9},{9,11},{11,13},{13,15},{2,0},{4,2},{6,4},{... | collective-permute-start | bytes 294920 | tf_op jit(solution)/shard_map/ppermute | solution.py:87
  36.3 1.6 %collective-permute-done.5 = bf16[768,64]{0,1:T(8,128)(2,1)S(1)} collective-permute-done((bf16[768,64]{0,1:T(8,128)(2,1)S(1)}, bf16[768,64]{0,1:T(8,128)(2,1)S(1)}, u32[]{:S(2)}, u32[]{:S(2)}) %collective-permute-start.5) | collective-permute-done | bytes 98336 | tf_op jit(solution)/shard_map/ppermute | solution.py:87
  38.0 0.5 fusion.9
  38.5 4.4 %collective-permute-start.6 = (bf16[768,64]{0,1:T(8,128)(2,1)S(1)}, bf16[768,64]{0,1:T(8,128)(2,1)S(1)}, u32[]{:S(2)}, u32[]{:S(2)}) collective-permute-start(bf16[768,64]{0,1:T(8,128)(2,1)S(1)} %fusion.9), channel_id=1, source_target_pairs={{1,3},{3,5},{5,7},{7,9},{9,11},{11,13},{13,15},{2,0},{4,2},{6,4},{... | collective-permute-start | bytes 294920 | tf_op jit(solution)/shard_map/ppermute | solution.py:87
  42.9 1.6 %collective-permute-done.6 = bf16[768,64]{0,1:T(8,128)(2,1)S(1)} collective-permute-done((bf16[768,64]{0,1:T(8,128)(2,1)S(1)}, bf16[768,64]{0,1:T(8,128)(2,1)S(1)}, u32[]{:S(2)}, u32[]{:S(2)}) %collective-permute-start.6) | collective-permute-done | bytes 98336 | tf_op jit(solution)/shard_map/ppermute | solution.py:87
  44.5 0.5 fusion.10
  45.0 5.1 %collective-permute-start.7 = (bf16[768,64]{0,1:T(8,128)(2,1)S(1)}, bf16[768,64]{0,1:T(8,128)(2,1)S(1)}, u32[]{:S(2)}, u32[]{:S(2)}) collective-permute-start(bf16[768,64]{0,1:T(8,128)(2,1)S(1)} %fusion.10), channel_id=1, source_target_pairs={{1,3},{3,5},{5,7},{7,9},{9,11},{11,13},{13,15},{2,0},{4,2},{6,4},{... | collective-permute-start | bytes 294920 | tf_op jit(solution)/shard_map/ppermute | solution.py:87
  50.1 1.6 %collective-permute-done.7 = bf16[768,64]{0,1:T(8,128)(2,1)S(1)} collective-permute-done((bf16[768,64]{0,1:T(8,128)(2,1)S(1)}, bf16[768,64]{0,1:T(8,128)(2,1)S(1)}, u32[]{:S(2)}, u32[]{:S(2)}) %collective-permute-start.7) | collective-permute-done | bytes 98336 | tf_op jit(solution)/shard_map/ppermute | solution.py:87
  51.7 1.6 %fusion.11 = bf16[768,64]{0,1:T(8,128)(2,1)S(1)} fusion(bf16[768,64]{0,1:T(8,128)(2,1)S(1)} %collective-permute-done.7, bf16[384,64]{0,1:T(8,128)(2,1)S(1)} %get-tuple-element.33, bf16[384,64]{0,1:T(8,128)(2,1)S(1)} %get-tuple-element.32, bf16[384,384]{1,0:T(8,128)(2,1)} %copy-done.4, bf16[384,384]{1,0:T(8,128)(2,1)} %copy-done.2, ...), kind=kOutput, calls=%fused_computation.28 | convolution fusion | flops 80510976 | bytes 1179648 | tf_op jit(solution)/shard_map/dot_general | solution.py:88
  53.4 4.9 %collective-permute-start.8 = (bf16[768,64]{0,1:T(8,128)(2,1)S(1)}, bf16[768,64]{0,1:T(8,128)(2,1)S(1)}, u32[]{:S(2)}, u32[]{:S(2)}) collective-permute-start(bf16[768,64]{0,1:T(8,128)(2,1)S(1)} %fusion.11), channel_id=1, source_target_pairs={{1,3},{3,5},{5,7},{7,9},{9,11},{11,13},{13,15},{2,0},{4,2},{6,4},{... | collective-permute-start | bytes 294920 | tf_op jit(solution)/shard_map/ppermute | solution.py:87
  58.3 0.0 copy-start.8
  58.4 1.6 %collective-permute-done.8 = bf16[768,64]{0,1:T(8,128)(2,1)S(1)} collective-permute-done((bf16[768,64]{0,1:T(8,128)(2,1)S(1)}, bf16[768,64]{0,1:T(8,128)(2,1)S(1)}, u32[]{:S(2)}, u32[]{:S(2)}) %collective-permute-start.8) | collective-permute-done | bytes 98336 | tf_op jit(solution)/shard_map/ppermute | solution.py:87
  59.9 0.5 fusion.12
  60.5 13.4 %collective-permute-start.9 = (bf16[384,128]{0,1:T(8,128)(2,1)S(1)}, bf16[384,128]{0,1:T(8,128)(2,1)S(1)}, u32[]{:S(2)}, u32[]{:S(2)}) collective-permute-start(bf16[384,128]{0,1:T(8,128)(2,1)S(1)} %pad_maximum_fusion.3), channel_id=1, source_target_pairs={{1,2},{3,4},{5,6},{7,8},{9,10},{11,12},{13,14},{2,1},{4,3},{6,5},{... | collective-permute-start | bytes 294920 | tf_op jit(solution)/shard_map/ppermute | solution.py:93
  73.9 2.3 %collective-permute-done.9 = bf16[384,128]{0,1:T(8,128)(2,1)S(1)} collective-permute-done((bf16[384,128]{0,1:T(8,128)(2,1)S(1)}, bf16[384,128]{0,1:T(8,128)(2,1)S(1)}, u32[]{:S(2)}, u32[]{:S(2)}) %collective-permute-start.9) | collective-permute-done | bytes 98336 | tf_op jit(solution)/shard_map/ppermute | solution.py:93
  76.2 0.3 convolution_bitcast_fusion
  76.5 0.3 convolution_bitcast_fusion.1
  76.8 2.8 %fusion.1 = f32[128,8192]{1,0:T(8,128)S(1)} fusion(s32[8192]{0:T(1024)S(1)} %broadcast_subtract_fusion, f32[384,64]{0,1:T(8,128)S(1)} %get-tuple-element.25, f32[384,64]{0,1:T(8,128)S(1)} %get-tuple-element.24, bf16[1,1,384,128]{2,3,1,0:T(8,128)(2,1)S(1)} %copy.14, pred[]{:T(512)S(6)} %eq.61, bf16[384,64]{0,1:T(8,128)(2,1)S(1)} %get-tuple-element.31, ...), kind=kOutput, calls=%fused_computation.3 | convolution fusion | flops 808894464 | bytes 4620289 | tf_op jit(solution)/shard_map/ar,ap->rp/dot_general | solution.py:55
  79.6 3.2 %multiply_reduce_fusion = (f32[8192]{0:T(1024)S(1)}, f32[128,8192]{1,0:T(8,128)S(1)}) fusion(f32[128,8192]{1,0:T(8,128)S(1)} %fusion.1, s32[8192]{0:T(1024)S(1)} %broadcast_subtract_fusion.1, f32[384,64]{0,1:T(8,128)S(1)} %get-tuple-element.23, f32[384,64]{0,1:T(8,128)S(1)} %get-tuple-element.22, bf16[1,1,384,128]{2,3,1,0:T(8,128)(2,1)S(1)} %copy.15, ...), kind=kOutput, calls=%fused_computation.6 | convolution fusion | flops 810983424 | bytes 8847361 | tf_op jit(solution)/shard_map/ar,ap->rp/dot_general | solution.py:55
  82.7 0.0 copy-start.9
  82.8 0.0 copy-start.6
  82.8 0.9 fusion.4
  83.7 0.1 maximum_multiply_fusion
  83.7 0.1 copy.25
  83.8 1.9 %collective-permute-start.10 = (bf16[1,2,8192]{2,0,1:T(2,128)(2,1)S(1)}, bf16[1,2,8192]{2,0,1:T(2,128)(2,1)S(1)}, u32[]{:S(2)}, u32[]{:S(2)}) collective-permute-start(bf16[1,2,8192]{2,0,1:T(2,128)(2,1)S(1)} %copy.25), channel_id=1, source_target_pairs={{16,0},{32,16},{48,32},{64,48},{80,64},{96,80},{112,96},{128,112},... | collective-permute-start | bytes 98312 | tf_op jit(solution)/shard_map/ppermute | solution.py:12
  85.7 4.0 %collective-permute-start.13 = (bf16[1,2,8192]{2,0,1:T(2,128)(2,1)S(1)}, bf16[1,2,8192]{2,0,1:T(2,128)(2,1)S(1)}, u32[]{:S(2)}, u32[]{:S(2)}) collective-permute-start(bf16[1,2,8192]{2,0,1:T(2,128)(2,1)S(1)} %copy.25), channel_id=1, source_target_pairs={{0,16},{16,32},{32,48},{48,64},{64,80},{80,96},{96,112},{112,128},... | collective-permute-start | bytes 98312 | tf_op jit(solution)/shard_map/ppermute | solution.py:12
  89.8 14.9 %collective-permute-done.13 = bf16[1,2,8192]{2,0,1:T(2,128)(2,1)S(1)} collective-permute-done((bf16[1,2,8192]{2,0,1:T(2,128)(2,1)S(1)}, bf16[1,2,8192]{2,0,1:T(2,128)(2,1)S(1)}, u32[]{:S(2)}, u32[]{:S(2)}) %collective-permute-start.13) | collective-permute-done | bytes 32800 | tf_op jit(solution)/shard_map/ppermute | solution.py:12
  104.7 0.2 pad_maximum_fusion.4
  105.0 5.0 %collective-permute-start.11 = (bf16[2,2,8192]{2,0,1:T(2,128)(2,1)S(1)}, bf16[2,2,8192]{2,0,1:T(2,128)(2,1)S(1)}, u32[]{:S(2)}, u32[]{:S(2)}) collective-permute-start(bf16[2,2,8192]{2,0,1:T(2,128)(2,1)S(1)} %get-tuple-element.36), channel_id=1, source_target_pairs={{32,0},{48,16},{64,32},{80,48},{96,64},{112,80},{128,96},{144,112}... | collective-permute-start | bytes 196616 | tf_op jit(solution)/shard_map/ppermute | solution.py:12
  110.0 2.1 %collective-permute-start.14 = (bf16[2,2,8192]{2,0,1:T(2,128)(2,1)S(1)}, bf16[2,2,8192]{2,0,1:T(2,128)(2,1)S(1)}, u32[]{:S(2)}, u32[]{:S(2)}) collective-permute-start(bf16[2,2,8192]{2,0,1:T(2,128)(2,1)S(1)} %get-tuple-element.37), channel_id=1, source_target_pairs={{0,32},{16,48},{32,64},{48,80},{64,96},{80,112},{96,128},{112,144}... | collective-permute-start | bytes 196616 | tf_op jit(solution)/shard_map/ppermute | solution.py:12
  112.1 1.1 select_reduce_fusion.12
  113.2 0.0 collective-permute-done.11
  113.2 6.6 %collective-permute-done.14 = bf16[2,2,8192]{2,0,1:T(2,128)(2,1)S(1)} collective-permute-done((bf16[2,2,8192]{2,0,1:T(2,128)(2,1)S(1)}, bf16[2,2,8192]{2,0,1:T(2,128)(2,1)S(1)}, u32[]{:S(2)}, u32[]{:S(2)}) %collective-permute-start.14) | collective-permute-done | bytes 65568 | tf_op jit(solution)/shard_map/ppermute | solution.py:12
  119.9 0.4 fusion.32
  120.3 1.9 %collective-permute-start.12 = (bf16[3,2,8192]{2,0,1:T(4,128)(2,1)S(1)}, bf16[3,2,8192]{2,0,1:T(4,128)(2,1)S(1)}, u32[]{:S(2)}, u32[]{:S(2)}) collective-permute-start(bf16[3,2,8192]{2,0,1:T(4,128)(2,1)S(1)} %get-tuple-element.34), channel_id=1, source_target_pairs={{64,0},{80,16},{96,32},{112,48},{128,64},{144,80},{160,96},{176,11... | collective-permute-start | bytes 294920 | tf_op jit(solution)/shard_map/ppermute | solution.py:12
  122.2 7.3 %collective-permute-start.15 = (bf16[3,2,8192]{2,0,1:T(4,128)(2,1)S(1)}, bf16[3,2,8192]{2,0,1:T(4,128)(2,1)S(1)}, u32[]{:S(2)}, u32[]{:S(2)}) collective-permute-start(bf16[3,2,8192]{2,0,1:T(4,128)(2,1)S(1)} %get-tuple-element.35), channel_id=1, source_target_pairs={{0,64},{16,80},{32,96},{48,112},{64,128},{80,144},{96,160},{112,17... | collective-permute-start | bytes 294920 | tf_op jit(solution)/shard_map/ppermute | solution.py:12
  129.5 2.5 %collective-permute-done.12 = bf16[3,2,8192]{2,0,1:T(4,128)(2,1)S(1)} collective-permute-done((bf16[3,2,8192]{2,0,1:T(4,128)(2,1)S(1)}, bf16[3,2,8192]{2,0,1:T(4,128)(2,1)S(1)}, u32[]{:S(2)}, u32[]{:S(2)}) %collective-permute-start.12) | collective-permute-done | bytes 98336 | tf_op jit(solution)/shard_map/ppermute | solution.py:12
  132.0 9.1 %collective-permute-done.15 = bf16[3,2,8192]{2,0,1:T(4,128)(2,1)S(1)} collective-permute-done((bf16[3,2,8192]{2,0,1:T(4,128)(2,1)S(1)}, bf16[3,2,8192]{2,0,1:T(4,128)(2,1)S(1)}, u32[]{:S(2)}, u32[]{:S(2)}) %collective-permute-start.15) | collective-permute-done | bytes 98336 | tf_op jit(solution)/shard_map/ppermute | solution.py:12
  141.1 1.4 fusion.57
  (28 shorter events, 0.2 us)
Async XLA Ops:
  2.0 11.4 %copy-start = (bf16[1,1,2,384,384]{4,3,2,1,0:T(8,128)(2,1)S(1)}, bf16[1,1,2,384,384]{4,3,2,1,0:T(8,128)(2,1)}, u32[]{:S(2)}) copy-start(bf16[1,1,2,384,384]{4,3,2,1,0:T(8,128)(2,1)} %param.7) | copy-start | bytes 1769476
  2.1 4.7 %collective-permute-start.1 = (bf16[384,128]{0,1:T(8,128)(2,1)S(1)}, bf16[384,128]{0,1:T(8,128)(2,1)S(1)}, u32[]{:S(2)}, u32[]{:S(2)}) collective-permute-start(bf16[384,128]{0,1:T(8,128)(2,1)S(1)} %select_bitcast_fusion), channel_id=1, source_target_pairs={{0,1},{1,0},{2,3},{3,2},{4,5},{5,4},{6,7},{7,6},{8,9},{9,8},{10,11... | collective-permute-start | bytes 294920 | tf_op jit(solution)/shard_map/ppermute | solution.py:64
  4.8 8.6 %collective-permute-start = (bf16[2,384,384]{2,1,0:T(8,128)(2,1)}, bf16[2,384,384]{2,1,0:T(8,128)(2,1)S(1)}, u32[]{:S(2)}, u32[]{:S(2)}) collective-permute-start(bf16[2,384,384]{2,1,0:T(8,128)(2,1)} %bitcast.223), channel_id=1, source_target_pairs={{0,1},{1,0},{2,3},{3,2},{4,5},{5,4},{6,7},{7,6},{8,9},{9,8},{10,11... | collective-permute-start | bytes 1769480 | tf_op jit(solution)/shard_map/ppermute | solution.py:64
  10.2 8.2 %collective-permute-start.2 = (bf16[768,64]{0,1:T(8,128)(2,1)}, bf16[768,64]{0,1:T(8,128)(2,1)}, u32[]{:S(2)}, u32[]{:S(2)}) collective-permute-start(bf16[768,64]{0,1:T(8,128)(2,1)} %pad_maximum_fusion.2), channel_id=1, source_target_pairs={{1,3},{3,5},{5,7},{7,9},{9,11},{11,13},{13,15},{2,0},{4,2},{6,4},{... | collective-permute-start | bytes 294920 | tf_op jit(solution)/shard_map/ppermute | solution.py:87
  16.3 2.0 %copy-start.1 = (f32[2,384,2,384]{1,3,0,2:T(8,128)S(1)}, f32[2,384,2,384]{1,3,0,2:T(8,128)}, u32[]{:S(2)}) copy-start(f32[2,384,2,384]{1,3,0,2:T(8,128)} %copy.9) | copy-start | bytes 7077892
  18.3 26.2 %copy-start.2 = (bf16[384,384]{1,0:T(8,128)(2,1)}, bf16[384,384]{1,0:T(8,128)(2,1)S(1)}, u32[]{:S(2)}) copy-start(bf16[384,384]{1,0:T(8,128)(2,1)S(1)} %get-tuple-element.21) | copy-start | bytes 884740
  18.4 26.1 %copy-start.4 = (bf16[384,384]{1,0:T(8,128)(2,1)}, bf16[384,384]{1,0:T(8,128)(2,1)S(1)}, u32[]{:S(2)}) copy-start(bf16[384,384]{1,0:T(8,128)(2,1)S(1)} %fusion.26) | copy-start | bytes 884740
  19.9 6.0 %collective-permute-start.3 = (bf16[768,64]{0,1:T(8,128)(2,1)S(1)}, bf16[768,64]{0,1:T(8,128)(2,1)S(1)}, u32[]{:S(2)}, u32[]{:S(2)}) collective-permute-start(bf16[768,64]{0,1:T(8,128)(2,1)S(1)} %fusion.6), channel_id=1, source_target_pairs={{1,3},{3,5},{5,7},{7,9},{9,11},{11,13},{13,15},{2,0},{4,2},{6,4},{... | collective-permute-start | bytes 294920 | tf_op jit(solution)/shard_map/ppermute | solution.py:87
  26.4 5.7 %collective-permute-start.4 = (bf16[768,64]{0,1:T(8,128)(2,1)S(1)}, bf16[768,64]{0,1:T(8,128)(2,1)S(1)}, u32[]{:S(2)}, u32[]{:S(2)}) collective-permute-start(bf16[768,64]{0,1:T(8,128)(2,1)S(1)} %fusion.7), channel_id=1, source_target_pairs={{1,3},{3,5},{5,7},{7,9},{9,11},{11,13},{13,15},{2,0},{4,2},{6,4},{... | collective-permute-start | bytes 294920 | tf_op jit(solution)/shard_map/ppermute | solution.py:87
  32.6 5.4 %collective-permute-start.5 = (bf16[768,64]{0,1:T(8,128)(2,1)S(1)}, bf16[768,64]{0,1:T(8,128)(2,1)S(1)}, u32[]{:S(2)}, u32[]{:S(2)}) collective-permute-start(bf16[768,64]{0,1:T(8,128)(2,1)S(1)} %fusion.8), channel_id=1, source_target_pairs={{1,3},{3,5},{5,7},{7,9},{9,11},{11,13},{13,15},{2,0},{4,2},{6,4},{... | collective-permute-start | bytes 294920 | tf_op jit(solution)/shard_map/ppermute | solution.py:87
  38.5 6.1 %collective-permute-start.6 = (bf16[768,64]{0,1:T(8,128)(2,1)S(1)}, bf16[768,64]{0,1:T(8,128)(2,1)S(1)}, u32[]{:S(2)}, u32[]{:S(2)}) collective-permute-start(bf16[768,64]{0,1:T(8,128)(2,1)S(1)} %fusion.9), channel_id=1, source_target_pairs={{1,3},{3,5},{5,7},{7,9},{9,11},{11,13},{13,15},{2,0},{4,2},{6,4},{... | collective-permute-start | bytes 294920 | tf_op jit(solution)/shard_map/ppermute | solution.py:87
  45.0 13.3 %copy-start.7 = (s32[8192]{0:T(1024)S(1)}, s32[8192]{0:T(1024)}, u32[]{:S(2)}) copy-start(s32[8192]{0:T(1024)} %param.11) | copy-start | bytes 98308
  45.0 6.7 %collective-permute-start.7 = (bf16[768,64]{0,1:T(8,128)(2,1)S(1)}, bf16[768,64]{0,1:T(8,128)(2,1)S(1)}, u32[]{:S(2)}, u32[]{:S(2)}) collective-permute-start(bf16[768,64]{0,1:T(8,128)(2,1)S(1)} %fusion.10), channel_id=1, source_target_pairs={{1,3},{3,5},{5,7},{7,9},{9,11},{11,13},{13,15},{2,0},{4,2},{6,4},{... | collective-permute-start | bytes 294920 | tf_op jit(solution)/shard_map/ppermute | solution.py:87
  50.1 9.8 %copy-start.3 = (bf16[384,384]{1,0:T(8,128)(2,1)S(1)}, bf16[384,384]{1,0:T(8,128)(2,1)}, u32[]{:S(2)}) copy-start(bf16[384,384]{1,0:T(8,128)(2,1)} %copy-done.2) | copy-start | bytes 884740
  50.1 9.8 %copy-start.5 = (bf16[384,384]{1,0:T(8,128)(2,1)S(1)}, bf16[384,384]{1,0:T(8,128)(2,1)}, u32[]{:S(2)}) copy-start(bf16[384,384]{1,0:T(8,128)(2,1)} %copy-done.4) | copy-start | bytes 884740
  53.4 6.6 %collective-permute-start.8 = (bf16[768,64]{0,1:T(8,128)(2,1)S(1)}, bf16[768,64]{0,1:T(8,128)(2,1)S(1)}, u32[]{:S(2)}, u32[]{:S(2)}) collective-permute-start(bf16[768,64]{0,1:T(8,128)(2,1)S(1)} %fusion.11), channel_id=1, source_target_pairs={{1,3},{3,5},{5,7},{7,9},{9,11},{11,13},{13,15},{2,0},{4,2},{6,4},{... | collective-permute-start | bytes 294920 | tf_op jit(solution)/shard_map/ppermute | solution.py:87
  58.3 15.5 %copy-start.8 = (s32[8192]{0:T(1024)S(1)}, s32[8192]{0:T(1024)}, u32[]{:S(2)}) copy-start(s32[8192]{0:T(1024)} %param.10) | copy-start | bytes 98308
  60.5 15.7 %collective-permute-start.9 = (bf16[384,128]{0,1:T(8,128)(2,1)S(1)}, bf16[384,128]{0,1:T(8,128)(2,1)S(1)}, u32[]{:S(2)}, u32[]{:S(2)}) collective-permute-start(bf16[384,128]{0,1:T(8,128)(2,1)S(1)} %pad_maximum_fusion.3), channel_id=1, source_target_pairs={{1,2},{3,4},{5,6},{7,8},{9,10},{11,12},{13,14},{2,1},{4,3},{6,5},{... | collective-permute-start | bytes 294920 | tf_op jit(solution)/shard_map/ppermute | solution.py:93
  82.7 7.0 %copy-start.9 = (s32[8]{0:T(128)S(1)}, s32[8]{0:T(128)}, u32[]{:S(2)}) copy-start(s32[8]{0:T(128)} %param.12) | copy-start | bytes 100
  82.8 29.3 %copy-start.6 = (f32[8,8192]{1,0:T(8,128)S(1)}, f32[8,8192]{1,0:T(8,128)}, u32[]{:S(2)}) copy-start(f32[8,8192]{1,0:T(8,128)} %param.13) | copy-start | bytes 786436
  83.8 6.0 %collective-permute-start.10 = (bf16[1,2,8192]{2,0,1:T(2,128)(2,1)S(1)}, bf16[1,2,8192]{2,0,1:T(2,128)(2,1)S(1)}, u32[]{:S(2)}, u32[]{:S(2)}) collective-permute-start(bf16[1,2,8192]{2,0,1:T(2,128)(2,1)S(1)} %copy.25), channel_id=1, source_target_pairs={{16,0},{32,16},{48,32},{64,48},{80,64},{96,80},{112,96},{128,112},... | collective-permute-start | bytes 98312 | tf_op jit(solution)/shard_map/ppermute | solution.py:12
  85.7 19.0 %collective-permute-start.13 = (bf16[1,2,8192]{2,0,1:T(2,128)(2,1)S(1)}, bf16[1,2,8192]{2,0,1:T(2,128)(2,1)S(1)}, u32[]{:S(2)}, u32[]{:S(2)}) collective-permute-start(bf16[1,2,8192]{2,0,1:T(2,128)(2,1)S(1)} %copy.25), channel_id=1, source_target_pairs={{0,16},{16,32},{32,48},{48,64},{64,80},{80,96},{96,112},{112,128},... | collective-permute-start | bytes 98312 | tf_op jit(solution)/shard_map/ppermute | solution.py:12
  105.0 8.3 %collective-permute-start.11 = (bf16[2,2,8192]{2,0,1:T(2,128)(2,1)S(1)}, bf16[2,2,8192]{2,0,1:T(2,128)(2,1)S(1)}, u32[]{:S(2)}, u32[]{:S(2)}) collective-permute-start(bf16[2,2,8192]{2,0,1:T(2,128)(2,1)S(1)} %get-tuple-element.36), channel_id=1, source_target_pairs={{32,0},{48,16},{64,32},{80,48},{96,64},{112,80},{128,96},{144,112}... | collective-permute-start | bytes 196616 | tf_op jit(solution)/shard_map/ppermute | solution.py:12
  110.0 9.9 %collective-permute-start.14 = (bf16[2,2,8192]{2,0,1:T(2,128)(2,1)S(1)}, bf16[2,2,8192]{2,0,1:T(2,128)(2,1)S(1)}, u32[]{:S(2)}, u32[]{:S(2)}) collective-permute-start(bf16[2,2,8192]{2,0,1:T(2,128)(2,1)S(1)} %get-tuple-element.37), channel_id=1, source_target_pairs={{0,32},{16,48},{32,64},{48,80},{64,96},{80,112},{96,128},{112,144}... | collective-permute-start | bytes 196616 | tf_op jit(solution)/shard_map/ppermute | solution.py:12
  120.3 11.7 %collective-permute-start.12 = (bf16[3,2,8192]{2,0,1:T(4,128)(2,1)S(1)}, bf16[3,2,8192]{2,0,1:T(4,128)(2,1)S(1)}, u32[]{:S(2)}, u32[]{:S(2)}) collective-permute-start(bf16[3,2,8192]{2,0,1:T(4,128)(2,1)S(1)} %get-tuple-element.34), channel_id=1, source_target_pairs={{64,0},{80,16},{96,32},{112,48},{128,64},{144,80},{160,96},{176,11... | collective-permute-start | bytes 294920 | tf_op jit(solution)/shard_map/ppermute | solution.py:12
  122.2 18.9 %collective-permute-start.15 = (bf16[3,2,8192]{2,0,1:T(4,128)(2,1)S(1)}, bf16[3,2,8192]{2,0,1:T(4,128)(2,1)S(1)}, u32[]{:S(2)}, u32[]{:S(2)}) collective-permute-start(bf16[3,2,8192]{2,0,1:T(4,128)(2,1)S(1)} %get-tuple-element.35), channel_id=1, source_target_pairs={{0,64},{16,80},{32,96},{48,112},{64,128},{80,144},{96,160},{112,17... | collective-permute-start | bytes 294920 | tf_op jit(solution)/shard_map/ppermute | solution.py:12

commit v4 on v3

--- a/solution.py
+++ b/solution.py
@@ -80,13 +80,32 @@
     pair_forward = (complex_product(blocks, other_src, False) + forward_src).astype(jnp.bfloat16)
     pair_backward = (complex_product(blocks, other_src, True) + backward_src).astype(jnp.bfloat16)
     chain_src = stacked(jnp.where(odd, pair_forward, pair_backward))
-    chain = [(2 * y + 1, 2 * y + 3) for y in range(count // 2 - 1)]
-    chain += [(2 * y, 2 * y - 2) for y in range(1, count // 2)]
-    state = chain_src
-    for _ in range(count // 2 - 1):
-        arrived = lax.ppermute(state, "section", chain)
-        state = (jnp.dot(chain_map, arrived, preferred_element_type=jnp.float32)
+    chips = count // 2
+    chip = lax.axis_index("section") // 2
+    chain = [(2 * y + 1, 2 * y + 3) for y in range(chips - 1)]
+    chain += [(2 * y, 2 * y - 2) for y in range(1, chips)]
+    own_map = jnp.stack([real_part, imag_part])
+    upstream_map, upstream_src = lax.ppermute((own_map, chain_src), "section", chain)
+    has_upstream = jnp.where(odd, chip >= 1, chip <= chips - 2)
+    joint_real, joint_imag = matrix_product(own_map, upstream_map)
+    joint_real = jnp.where(has_upstream, joint_real, real_part).astype(jnp.bfloat16)
+    joint_imag = jnp.where(has_upstream, joint_imag, imag_part).astype(jnp.bfloat16)
+    joint_src = (jnp.dot(chain_map, upstream_src, preferred_element_type=jnp.float32)
                  + chain_src).astype(jnp.bfloat16)
+    joint_map = jnp.concatenate(
+        [
+            jnp.concatenate([joint_real, -joint_imag], axis=1),
+            jnp.concatenate([joint_imag, joint_real], axis=1),
+        ],
+        axis=0,
+    )
+    stride = [(2 * y + 1, 2 * y + 5) for y in range(chips - 2)]
+    stride += [(2 * y, 2 * y - 4) for y in range(2, chips)]
+    state = joint_src
+    for _ in range((chips - 1) // 2):
+        arrived = lax.ppermute(state, "section", stride)
+        state = (jnp.dot(joint_map, arrived, preferred_element_type=jnp.float32)
+                 + joint_src).astype(jnp.bfloat16)
     state = joined(state)
     hand_over = [(s, s + 1) for s in range(1, count - 1, 2)]
     hand_over += [(s, s - 1) for s in range(2, count, 2)]

time: 143 us -> 133 us (0.930)
  the two profiles are of different devices: /device:TPU:83 before, /device:TPU:18 now
where the time goes in v4:
time: 133 us; the launch traced here: 132 us
  starting transfers between devices  54.9 us (41%)
  waiting for transfers between devices  51.1 us (38%)
  matrix products  13.8 us (10%)
  other arithmetic  7.57 us (6%)
  local copies, waits for them, and re-layouts  4.22 us (3%)
    ppermute x6, starting transfers between devices, passed_along(): lax.ppermute(value, axis, [(source, source + steps) for source in range(l...  37.7 us
    ppermute x6, waiting for transfers between devices, passed_along(): lax.ppermute(value, axis, [(source, source + steps) for source in range(l...  20.3 us
    ppermute x3, waiting for transfers between devices, sweeps(): arrived = lax.ppermute(state, 'section', stride)  18.8 us
    ppermute x2, waiting for transfers between devices, sweeps(): lax.ppermute((own_map, chain_src), 'section', chain)  8.03 us
    ppermute x3, starting transfers between devices, sweeps(): arrived = lax.ppermute(state, 'section', stride)  6.21 us
    dot_general x2, matrix products, picked_rows(): jnp.einsum('ar,ap->rp', table, selector.astype(table.dtype), preferred_el...  5.93 us
    ppermute x2, starting transfers between devices, sweeps(): lax.ppermute((own_map, chain_src), 'section', chain)  4.71 us
    ppermute x2, starting transfers between devices, sweeps(): lax.ppermute((blocks, jnp.where(odd, backward_src, forward_src)), 'sectio...  4.33 us
  transfers between devices with their start and end apart: 14, of which 10 were waited for; matrix products, arithmetic and copies ran while one was open for 5% of the time, Pallas kernels for 0%

profile of v4, /device:TPU:18, one launch (start us, length us, event | category | flops | bytes accessed | tf_op | source)
XLA Modules:
  0.0 132.1 jit_solution(13063526774390812200)
XLA Ops:
  0.0 1.1 copy.16
  1.1 0.0 copy-start.4
  1.1 1.0 copy.17
  2.1 0.0 copy-start.2
  2.2 1.9 %collective-permute-start.2 = (bf16[384,128]{0,1:T(8,128)(2,1)S(1)}, bf16[384,128]{0,1:T(8,128)(2,1)S(1)}, u32[]{:S(2)}, u32[]{:S(2)}) collective-permute-start(bf16[384,128]{0,1:T(8,128)(2,1)S(1)} %select_bitcast_fusion), channel_id=1, source_target_pairs={{0,1},{1,0},{2,3},{3,2},{4,5},{5,4},{6,7},{7,6},{8,9},{9,8},{10,11... | collective-permute-start | bytes 294920 | tf_op jit(solution)/shard_map/ppermute | solution.py:64
  4.1 2.4 %collective-permute-start = (bf16[2,384,384]{2,1,0:T(8,128)(2,1)}, bf16[2,384,384]{2,1,0:T(8,128)(2,1)S(1)}, u32[]{:S(2)}, u32[]{:S(2)}) collective-permute-start(bf16[2,384,384]{2,1,0:T(8,128)(2,1)} %bitcast.240), channel_id=1, source_target_pairs={{0,1},{1,0},{2,3},{3,2},{4,5},{5,4},{6,7},{7,6},{8,9},{9,8},{10,11... | collective-permute-start | bytes 1769480 | tf_op jit(solution)/shard_map/ppermute | solution.py:64
  6.5 0.0 collective-permute-done.2
  6.5 1.3 %convolution_bitcast_fusion.3 = f32[2,384,128]{1,2,0:T(8,128)S(1)} fusion(bf16[384,128]{0,1:T(8,128)(2,1)S(1)} %collective-permute-done.2, bf16[1,1,2,384,384]{4,3,2,1,0:T(8,128)(2,1)} %param.7), kind=kOutput, calls=%fused_computation.14 | convolution fusion | flops 75497472 | bytes 1081344 | tf_op jit(solution)/shard_map/cji,jn->cin/dot_general | solution.py:18
  7.9 1.4 %convolution_bitcast_fusion.4 = f32[2,384,128]{1,2,0:T(8,128)S(1)} fusion(bf16[384,128]{0,1:T(8,128)(2,1)S(1)} %collective-permute-done.2, bf16[1,1,2,384,384]{4,3,2,1,0:T(8,128)(2,1)} %param.7), kind=kOutput, calls=%fused_computation.15 | convolution fusion | flops 75497472 | bytes 1081344 | tf_op jit(solution)/shard_map/cij,jn->cin/dot_general | solution.py:22
  9.3 0.7 fusion.52
  10.0 0.0 copy-done.4
  10.0 0.0 copy-done.2
  10.0 0.0 collective-permute-done
  10.0 0.8 fusion.36
  10.8 2.0 %copy.9 = f32[2,384,2,384]{1,3,0,2:T(8,128)} copy(f32[2,384,2,384]{3,1,2,0:T(8,128)S(1)} %fusion.36) | data formatting | bytes 4718592 | tf_op jit(solution)/shard_map/cij,djk->cdik/dot_general | solution.py:29
  12.8 2.3 %bitcast_negate_fusion = (bf16[384,384]{1,0:T(8,128)(2,1)}, bf16[1,1,384,384]{3,2,0,1:T(8,128)(2,1)S(1)}) fusion(f32[2,2,384,384]{3,2,0,1:T(8,128)S(1)} %bitcast.238, f32[2,2,384,384]{3,2,1,0:T(8,128)} %bitcast.241, pred[]{:T(512)S(6)} %eq.61), kind=kLoop, calls=%fused_computation.181 | loop fusion | flops 884736 | bytes 2949121 | tf_op jit(solution)/shard_map/neg | solution.py:75
  15.1 0.1 fusion.35
  15.2 0.1 pad_maximum_fusion
  15.3 2.4 %collective-permute-start.1 = (bf16[2,384,384]{2,1,0:T(8,128)(2,1)S(1)}, bf16[2,384,384]{2,1,0:T(8,128)(2,1)S(1)}, u32[]{:S(2)}, u32[]{:S(2)}) collective-permute-start(bf16[2,384,384]{2,1,0:T(8,128)(2,1)S(1)} %pad_maximum_fusion), channel_id=1, source_target_pairs={{1,3},{3,5},{5,7},{7,9},{9,11},{11,13},{13,15},{2,0},{4,2},{6,4},{... | collective-permute-start | bytes 1769480 | tf_op jit(solution)/shard_map/ppermute | solution.py:88
  17.7 2.4 %collective-permute-start.3 = (bf16[768,64]{0,1:T(8,128)(2,1)S(1)}, bf16[768,64]{0,1:T(8,128)(2,1)S(1)}, u32[]{:S(2)}, u32[]{:S(2)}) collective-permute-start(bf16[768,64]{0,1:T(8,128)(2,1)S(1)} %pad_maximum_fusion.3), channel_id=1, source_target_pairs={{1,3},{3,5},{5,7},{7,9},{9,11},{11,13},{13,15},{2,0},{4,2},{6,4},{... | collective-permute-start | bytes 294920 | tf_op jit(solution)/shard_map/ppermute | solution.py:88
  20.1 8.0 %collective-permute-done.3 = bf16[768,64]{0,1:T(8,128)(2,1)S(1)} collective-permute-done((bf16[768,64]{0,1:T(8,128)(2,1)S(1)}, bf16[768,64]{0,1:T(8,128)(2,1)S(1)}, u32[]{:S(2)}, u32[]{:S(2)}) %collective-permute-start.3) | collective-permute-done | bytes 98336 | tf_op jit(solution)/shard_map/ppermute | solution.py:88
  28.1 1.5 %fusion.20 = bf16[768,64]{0,1:T(8,128)(2,1)S(1)} fusion(bf16[768,64]{0,1:T(8,128)(2,1)S(1)} %collective-permute-done.3, bf16[384,384]{1,0:T(8,128)(2,1)S(1)} %bitcast.247, bf16[384,384]{1,0:T(8,128)(2,1)S(1)} %bitcast.244, bf16[384,384]{1,0:T(8,128)(2,1)} %get-tuple-element.22, bf16[384,64]{0,1:T(8,128)(2,1)S(1)} %get-tuple-element.35, ...), kind=kOutput, calls=%fused_computation.32 | convolution fusion | flops 80510976 | bytes 1179648 | tf_op jit(solution)/shard_map/dot_general | solution.py:93
  29.6 2.2 %collective-permute-start.4 = (bf16[768,64]{0,1:T(8,128)(2,1)S(1)}, bf16[768,64]{0,1:T(8,128)(2,1)S(1)}, u32[]{:S(2)}, u32[]{:S(2)}) collective-permute-start(bf16[768,64]{0,1:T(8,128)(2,1)S(1)} %fusion.20), channel_id=1, source_target_pairs={{1,5},{3,7},{5,9},{7,11},{9,13},{11,15},{4,0},{6,2},{8,4},{10,6},{... | collective-permute-start | bytes 294920 | tf_op jit(solution)/shard_map/ppermute | solution.py:106
  31.8 0.0 collective-permute-done.1
  31.8 0.8 convolution_bitcast_fusion
  32.6 0.1 fusion.107
  32.7 0.1 fusion.28
  32.8 5.4 %collective-permute-done.4 = bf16[768,64]{0,1:T(8,128)(2,1)S(1)} collective-permute-done((bf16[768,64]{0,1:T(8,128)(2,1)S(1)}, bf16[768,64]{0,1:T(8,128)(2,1)S(1)}, u32[]{:S(2)}, u32[]{:S(2)}) %collective-permute-start.4) | collective-permute-done | bytes 98336 | tf_op jit(solution)/shard_map/ppermute | solution.py:106
  38.2 0.5 fusion.17
  38.7 2.1 %collective-permute-start.5 = (bf16[768,64]{0,1:T(8,128)(2,1)S(1)}, bf16[768,64]{0,1:T(8,128)(2,1)S(1)}, u32[]{:S(2)}, u32[]{:S(2)}) collective-permute-start(bf16[768,64]{0,1:T(8,128)(2,1)S(1)} %fusion.17), channel_id=1, source_target_pairs={{1,5},{3,7},{5,9},{7,11},{9,13},{11,15},{4,0},{6,2},{8,4},{10,6},{... | collective-permute-start | bytes 294920 | tf_op jit(solution)/shard_map/ppermute | solution.py:106
  40.8 6.7 %collective-permute-done.5 = bf16[768,64]{0,1:T(8,128)(2,1)S(1)} collective-permute-done((bf16[768,64]{0,1:T(8,128)(2,1)S(1)}, bf16[768,64]{0,1:T(8,128)(2,1)S(1)}, u32[]{:S(2)}, u32[]{:S(2)}) %collective-permute-start.5) | collective-permute-done | bytes 98336 | tf_op jit(solution)/shard_map/ppermute | solution.py:106
  47.4 0.5 fusion.18
  47.9 1.9 %collective-permute-start.6 = (bf16[768,64]{0,1:T(8,128)(2,1)S(1)}, bf16[768,64]{0,1:T(8,128)(2,1)S(1)}, u32[]{:S(2)}, u32[]{:S(2)}) collective-permute-start(bf16[768,64]{0,1:T(8,128)(2,1)S(1)} %fusion.18), channel_id=1, source_target_pairs={{1,5},{3,7},{5,9},{7,11},{9,13},{11,15},{4,0},{6,2},{8,4},{10,6},{... | collective-permute-start | bytes 294920 | tf_op jit(solution)/shard_map/ppermute | solution.py:106
  49.9 0.0 copy-start.9
  49.9 6.8 %collective-permute-done.6 = bf16[768,64]{0,1:T(8,128)(2,1)S(1)} collective-permute-done((bf16[768,64]{0,1:T(8,128)(2,1)S(1)}, bf16[768,64]{0,1:T(8,128)(2,1)S(1)}, u32[]{:S(2)}, u32[]{:S(2)}) %collective-permute-start.6) | collective-permute-done | bytes 98336 | tf_op jit(solution)/shard_map/ppermute | solution.py:106
  56.7 0.5 fusion.19
  57.2 1.9 %collective-permute-start.7 = (bf16[384,128]{0,1:T(8,128)(2,1)S(1)}, bf16[384,128]{0,1:T(8,128)(2,1)S(1)}, u32[]{:S(2)}, u32[]{:S(2)}) collective-permute-start(bf16[384,128]{0,1:T(8,128)(2,1)S(1)} %pad_maximum_fusion.4), channel_id=1, source_target_pairs={{1,2},{3,4},{5,6},{7,8},{9,10},{11,12},{13,14},{2,1},{4,3},{6,5},{... | collective-permute-start | bytes 294920 | tf_op jit(solution)/shard_map/ppermute | solution.py:112
  59.2 4.0 %collective-permute-done.7 = bf16[384,128]{0,1:T(8,128)(2,1)S(1)} collective-permute-done((bf16[384,128]{0,1:T(8,128)(2,1)S(1)}, bf16[384,128]{0,1:T(8,128)(2,1)S(1)}, u32[]{:S(2)}, u32[]{:S(2)}) %collective-permute-start.7) | collective-permute-done | bytes 98336 | tf_op jit(solution)/shard_map/ppermute | solution.py:112
  63.1 0.3 convolution_bitcast_fusion.1
  63.4 0.3 convolution_bitcast_fusion.2
  63.8 2.8 %fusion.1 = f32[128,8192]{1,0:T(8,128)S(1)} fusion(s32[8192]{0:T(1024)S(1)} %broadcast_subtract_fusion, f32[384,64]{0,1:T(8,128)S(1)} %get-tuple-element.27, f32[384,64]{0,1:T(8,128)S(1)} %get-tuple-element.26, bf16[1,1,384,128]{2,3,1,0:T(8,128)(2,1)S(1)} %copy-done.5, pred[]{:T(512)S(6)} %eq.61, bf16[384,64]{0,1:T(8,128)(2,1)S(1)} %get-tuple-element.33, ...), kind=kOutput, calls=%fused_computation.3 | convolution fusion | flops 808894464 | bytes 4620289 | tf_op jit(solution)/shard_map/ar,ap->rp/dot_general | solution.py:55
  66.6 3.2 %multiply_reduce_fusion = (f32[8192]{0:T(1024)S(1)}, f32[128,8192]{1,0:T(8,128)S(1)}) fusion(f32[128,8192]{1,0:T(8,128)S(1)} %fusion.1, s32[8192]{0:T(1024)S(1)} %broadcast_subtract_fusion.1, f32[384,64]{0,1:T(8,128)S(1)} %get-tuple-element.25, f32[384,64]{0,1:T(8,128)S(1)} %get-tuple-element.24, bf16[1,1,384,128]{2,3,1,0:T(8,128)(2,1)S(1)} %copy-done.3, ...), kind=kOutput, calls=%fused_computation.6 | convolution fusion | flops 810983424 | bytes 8847361 | tf_op jit(solution)/shard_map/ar,ap->rp/dot_general | solution.py:55
  69.8 0.0 copy-start.10
  69.8 0.0 copy-start.7
  69.8 0.9 fusion.4
  70.7 0.1 maximum_multiply_fusion
  70.7 0.1 copy.31
  70.8 4.3 %collective-permute-start.11 = (bf16[1,2,8192]{2,0,1:T(2,128)(2,1)S(1)}, bf16[1,2,8192]{2,0,1:T(2,128)(2,1)S(1)}, u32[]{:S(2)}, u32[]{:S(2)}) collective-permute-start(bf16[1,2,8192]{2,0,1:T(2,128)(2,1)S(1)} %copy.31), channel_id=1, source_target_pairs={{0,16},{16,32},{32,48},{48,64},{64,80},{80,96},{96,112},{112,128},... | collective-permute-start | bytes 98312 | tf_op jit(solution)/shard_map/ppermute | solution.py:12
  75.1 15.8 %collective-permute-start.8 = (bf16[1,2,8192]{2,0,1:T(2,128)(2,1)S(1)}, bf16[1,2,8192]{2,0,1:T(2,128)(2,1)S(1)}, u32[]{:S(2)}, u32[]{:S(2)}) collective-permute-start(bf16[1,2,8192]{2,0,1:T(2,128)(2,1)S(1)} %copy.31), channel_id=1, source_target_pairs={{16,0},{32,16},{48,32},{64,48},{80,64},{96,80},{112,96},{128,112},... | collective-permute-start | bytes 98312 | tf_op jit(solution)/shard_map/ppermute | solution.py:12
  90.9 0.0 copy-done.10
  91.0 0.3 collective-permute-done.11
  91.2 1.6 %collective-permute-done.8 = bf16[1,2,8192]{2,0,1:T(2,128)(2,1)S(1)} collective-permute-done((bf16[1,2,8192]{2,0,1:T(2,128)(2,1)S(1)}, bf16[1,2,8192]{2,0,1:T(2,128)(2,1)S(1)}, u32[]{:S(2)}, u32[]{:S(2)}) %collective-permute-start.8) | collective-permute-done | bytes 32800 | tf_op jit(solution)/shard_map/ppermute | solution.py:12
  92.8 0.2 pad_maximum_fusion.5
  93.1 5.7 %collective-permute-start.9 = (bf16[2,2,8192]{2,0,1:T(2,128)(2,1)S(1)}, bf16[2,2,8192]{2,0,1:T(2,128)(2,1)S(1)}, u32[]{:S(2)}, u32[]{:S(2)}) collective-permute-start(bf16[2,2,8192]{2,0,1:T(2,128)(2,1)S(1)} %get-tuple-element.38), channel_id=1, source_target_pairs={{32,0},{48,16},{64,32},{80,48},{96,64},{112,80},{128,96},{144,112}... | collective-permute-start | bytes 196616 | tf_op jit(solution)/shard_map/ppermute | solution.py:12
  98.8 2.1 %collective-permute-start.12 = (bf16[2,2,8192]{2,0,1:T(2,128)(2,1)S(1)}, bf16[2,2,8192]{2,0,1:T(2,128)(2,1)S(1)}, u32[]{:S(2)}, u32[]{:S(2)}) collective-permute-start(bf16[2,2,8192]{2,0,1:T(2,128)(2,1)S(1)} %get-tuple-element.39), channel_id=1, source_target_pairs={{0,32},{16,48},{32,64},{48,80},{64,96},{80,112},{96,128},{112,144}... | collective-permute-start | bytes 196616 | tf_op jit(solution)/shard_map/ppermute | solution.py:12
  100.9 1.1 select_reduce_fusion.12
  102.0 0.0 collective-permute-done.9
  102.0 6.7 %collective-permute-done.12 = bf16[2,2,8192]{2,0,1:T(2,128)(2,1)S(1)} collective-permute-done((bf16[2,2,8192]{2,0,1:T(2,128)(2,1)S(1)}, bf16[2,2,8192]{2,0,1:T(2,128)(2,1)S(1)}, u32[]{:S(2)}, u32[]{:S(2)}) %collective-permute-start.12) | collective-permute-done | bytes 65568 | tf_op jit(solution)/shard_map/ppermute | solution.py:12
  108.7 0.4 fusion.48
  109.1 3.5 %collective-permute-start.10 = (bf16[3,2,8192]{2,0,1:T(4,128)(2,1)S(1)}, bf16[3,2,8192]{2,0,1:T(4,128)(2,1)S(1)}, u32[]{:S(2)}, u32[]{:S(2)}) collective-permute-start(bf16[3,2,8192]{2,0,1:T(4,128)(2,1)S(1)} %get-tuple-element.36), channel_id=1, source_target_pairs={{64,0},{80,16},{96,32},{112,48},{128,64},{144,80},{160,96},{176,11... | collective-permute-start | bytes 294920 | tf_op jit(solution)/shard_map/ppermute | solution.py:12
  112.6 6.3 %collective-permute-start.13 = (bf16[3,2,8192]{2,0,1:T(4,128)(2,1)S(1)}, bf16[3,2,8192]{2,0,1:T(4,128)(2,1)S(1)}, u32[]{:S(2)}, u32[]{:S(2)}) collective-permute-start(bf16[3,2,8192]{2,0,1:T(4,128)(2,1)S(1)} %get-tuple-element.37), channel_id=1, source_target_pairs={{0,64},{16,80},{32,96},{48,112},{64,128},{80,144},{96,160},{112,17... | collective-permute-start | bytes 294920 | tf_op jit(solution)/shard_map/ppermute | solution.py:12
  118.9 6.7 %collective-permute-done.10 = bf16[3,2,8192]{2,0,1:T(4,128)(2,1)S(1)} collective-permute-done((bf16[3,2,8192]{2,0,1:T(4,128)(2,1)S(1)}, bf16[3,2,8192]{2,0,1:T(4,128)(2,1)S(1)}, u32[]{:S(2)}, u32[]{:S(2)}) %collective-permute-start.10) | collective-permute-done | bytes 98336 | tf_op jit(solution)/shard_map/ppermute | solution.py:12
  125.7 5.0 %collective-permute-done.13 = bf16[3,2,8192]{2,0,1:T(4,128)(2,1)S(1)} collective-permute-done((bf16[3,2,8192]{2,0,1:T(4,128)(2,1)S(1)}, bf16[3,2,8192]{2,0,1:T(4,128)(2,1)S(1)}, u32[]{:S(2)}, u32[]{:S(2)}) %collective-permute-start.13) | collective-permute-done | bytes 98336 | tf_op jit(solution)/shard_map/ppermute | solution.py:12
  130.7 1.4 %fusion.73 = f32[2,1,8192]{2,1,0:T(1,128)} fusion(bf16[3,2,8192]{2,0,1:T(4,128)(2,1)S(1)} %collective-permute-done.13, bf16[2,2,8192]{2,0,1:T(2,128)(2,1)S(1)} %collective-permute-done.12, f32[1,1,8192]{2,1,0:T(1,128)S(1)} %bitcast.254, f32[1,1,8192]{2,1,0:T(1,128)S(1)} %bitcast.252, bf16[1,2,8192]{2,0,1:T(2,128)(2,1)S(1)} %collective-permute-done.11, ...), kind=kLoop, calls=%fused_computation.120 | loop fusion | flops 622592 | bytes 950272 | tf_op jit(solution)/shard_map/add | solution.py:158
  (27 shorter events, 0.2 us)
Async XLA Ops:
  0.0 10.0 %copy-start = (bf16[1,1,2,384,384]{4,3,2,1,0:T(8,128)(2,1)S(1)}, bf16[1,1,2,384,384]{4,3,2,1,0:T(8,128)(2,1)}, u32[]{:S(2)}) copy-start(bf16[1,1,2,384,384]{4,3,2,1,0:T(8,128)(2,1)} %param.7) | copy-start | bytes 1769476
  1.1 8.9 %copy-start.4 = (bf16[1,1,384,128]{2,3,1,0:T(8,128)(2,1)}, bf16[1,1,384,128]{2,3,1,0:T(8,128)(2,1)S(1)}, u32[]{:S(2)}) copy-start(bf16[1,1,384,128]{2,3,1,0:T(8,128)(2,1)S(1)} %copy.16) | copy-start | bytes 294916
  2.1 7.8 %copy-start.2 = (bf16[1,1,384,128]{2,3,1,0:T(8,128)(2,1)}, bf16[1,1,384,128]{2,3,1,0:T(8,128)(2,1)S(1)}, u32[]{:S(2)}) copy-start(bf16[1,1,384,128]{2,3,1,0:T(8,128)(2,1)S(1)} %copy.17) | copy-start | bytes 294916
  2.2 4.3 %collective-permute-start.2 = (bf16[384,128]{0,1:T(8,128)(2,1)S(1)}, bf16[384,128]{0,1:T(8,128)(2,1)S(1)}, u32[]{:S(2)}, u32[]{:S(2)}) collective-permute-start(bf16[384,128]{0,1:T(8,128)(2,1)S(1)} %select_bitcast_fusion), channel_id=1, source_target_pairs={{0,1},{1,0},{2,3},{3,2},{4,5},{5,4},{6,7},{7,6},{8,9},{9,8},{10,11... | collective-permute-start | bytes 294920 | tf_op jit(solution)/shard_map/ppermute | solution.py:64
  4.1 5.9 %collective-permute-start = (bf16[2,384,384]{2,1,0:T(8,128)(2,1)}, bf16[2,384,384]{2,1,0:T(8,128)(2,1)S(1)}, u32[]{:S(2)}, u32[]{:S(2)}) collective-permute-start(bf16[2,384,384]{2,1,0:T(8,128)(2,1)} %bitcast.240), channel_id=1, source_target_pairs={{0,1},{1,0},{2,3},{3,2},{4,5},{5,4},{6,7},{7,6},{8,9},{9,8},{10,11... | collective-permute-start | bytes 1769480 | tf_op jit(solution)/shard_map/ppermute | solution.py:64
  12.8 2.3 %copy-start.1 = (f32[2,384,2,384]{1,3,0,2:T(8,128)S(1)}, f32[2,384,2,384]{1,3,0,2:T(8,128)}, u32[]{:S(2)}) copy-start(f32[2,384,2,384]{1,3,0,2:T(8,128)} %copy.9) | copy-start | bytes 7077892
  15.1 2.6 %copy-start.6 = (bf16[384,128]{0,1:T(8,128)(2,1)S(1)}, bf16[384,128]{0,1:T(8,128)(2,1)}, u32[]{:S(2)}) copy-start(bf16[384,128]{0,1:T(8,128)(2,1)} %fusion.52) | copy-start | bytes 294916
  15.3 16.6 %collective-permute-start.1 = (bf16[2,384,384]{2,1,0:T(8,128)(2,1)S(1)}, bf16[2,384,384]{2,1,0:T(8,128)(2,1)S(1)}, u32[]{:S(2)}, u32[]{:S(2)}) collective-permute-start(bf16[2,384,384]{2,1,0:T(8,128)(2,1)S(1)} %pad_maximum_fusion), channel_id=1, source_target_pairs={{1,3},{3,5},{5,7},{7,9},{9,11},{11,13},{13,15},{2,0},{4,2},{6,4},{... | collective-permute-start | bytes 1769480 | tf_op jit(solution)/shard_map/ppermute | solution.py:88
  17.7 10.4 %collective-permute-start.3 = (bf16[768,64]{0,1:T(8,128)(2,1)S(1)}, bf16[768,64]{0,1:T(8,128)(2,1)S(1)}, u32[]{:S(2)}, u32[]{:S(2)}) collective-permute-start(bf16[768,64]{0,1:T(8,128)(2,1)S(1)} %pad_maximum_fusion.3), channel_id=1, source_target_pairs={{1,3},{3,5},{5,7},{7,9},{9,11},{11,13},{13,15},{2,0},{4,2},{6,4},{... | collective-permute-start | bytes 294920 | tf_op jit(solution)/shard_map/ppermute | solution.py:88
  29.6 8.6 %collective-permute-start.4 = (bf16[768,64]{0,1:T(8,128)(2,1)S(1)}, bf16[768,64]{0,1:T(8,128)(2,1)S(1)}, u32[]{:S(2)}, u32[]{:S(2)}) collective-permute-start(bf16[768,64]{0,1:T(8,128)(2,1)S(1)} %fusion.20), channel_id=1, source_target_pairs={{1,5},{3,7},{5,9},{7,11},{9,13},{11,15},{4,0},{6,2},{8,4},{10,6},{... | collective-permute-start | bytes 294920 | tf_op jit(solution)/shard_map/ppermute | solution.py:106
  38.7 11.2 %copy-start.8 = (s32[8192]{0:T(1024)S(1)}, s32[8192]{0:T(1024)}, u32[]{:S(2)}) copy-start(s32[8192]{0:T(1024)} %param.11) | copy-start | bytes 98308
  38.7 8.8 %collective-permute-start.5 = (bf16[768,64]{0,1:T(8,128)(2,1)S(1)}, bf16[768,64]{0,1:T(8,128)(2,1)S(1)}, u32[]{:S(2)}, u32[]{:S(2)}) collective-permute-start(bf16[768,64]{0,1:T(8,128)(2,1)S(1)} %fusion.17), channel_id=1, source_target_pairs={{1,5},{3,7},{5,9},{7,11},{9,13},{11,15},{4,0},{6,2},{8,4},{10,6},{... | collective-permute-start | bytes 294920 | tf_op jit(solution)/shard_map/ppermute | solution.py:106
  47.9 8.7 %collective-permute-start.6 = (bf16[768,64]{0,1:T(8,128)(2,1)S(1)}, bf16[768,64]{0,1:T(8,128)(2,1)S(1)}, u32[]{:S(2)}, u32[]{:S(2)}) collective-permute-start(bf16[768,64]{0,1:T(8,128)(2,1)S(1)} %fusion.18), channel_id=1, source_target_pairs={{1,5},{3,7},{5,9},{7,11},{9,13},{11,15},{4,0},{6,2},{8,4},{10,6},{... | collective-permute-start | bytes 294920 | tf_op jit(solution)/shard_map/ppermute | solution.py:106
  49.9 9.2 %copy-start.9 = (s32[8192]{0:T(1024)S(1)}, s32[8192]{0:T(1024)}, u32[]{:S(2)}) copy-start(s32[8192]{0:T(1024)} %param.10) | copy-start | bytes 98308
  57.2 6.6 %copy-start.5 = (bf16[1,1,384,128]{2,3,1,0:T(8,128)(2,1)S(1)}, bf16[1,1,384,128]{2,3,1,0:T(8,128)(2,1)}, u32[]{:S(2)}) copy-start(bf16[1,1,384,128]{2,3,1,0:T(8,128)(2,1)} %copy-done.4) | copy-start | bytes 294916
  57.2 5.9 %collective-permute-start.7 = (bf16[384,128]{0,1:T(8,128)(2,1)S(1)}, bf16[384,128]{0,1:T(8,128)(2,1)S(1)}, u32[]{:S(2)}, u32[]{:S(2)}) collective-permute-start(bf16[384,128]{0,1:T(8,128)(2,1)S(1)} %pad_maximum_fusion.4), channel_id=1, source_target_pairs={{1,2},{3,4},{5,6},{7,8},{9,10},{11,12},{13,14},{2,1},{4,3},{6,5},{... | collective-permute-start | bytes 294920 | tf_op jit(solution)/shard_map/ppermute | solution.py:112
  63.8 2.8 %copy-start.3 = (bf16[1,1,384,128]{2,3,1,0:T(8,128)(2,1)S(1)}, bf16[1,1,384,128]{2,3,1,0:T(8,128)(2,1)}, u32[]{:S(2)}) copy-start(bf16[1,1,384,128]{2,3,1,0:T(8,128)(2,1)} %copy-done.2) | copy-start | bytes 294916
  69.8 21.2 %copy-start.10 = (s32[8]{0:T(128)S(1)}, s32[8]{0:T(128)}, u32[]{:S(2)}) copy-start(s32[8]{0:T(128)} %param.12) | copy-start | bytes 100
  69.8 31.1 %copy-start.7 = (f32[8,8192]{1,0:T(8,128)S(1)}, f32[8,8192]{1,0:T(8,128)}, u32[]{:S(2)}) copy-start(f32[8,8192]{1,0:T(8,128)} %param.13) | copy-start | bytes 786436
  70.8 20.4 %collective-permute-start.11 = (bf16[1,2,8192]{2,0,1:T(2,128)(2,1)S(1)}, bf16[1,2,8192]{2,0,1:T(2,128)(2,1)S(1)}, u32[]{:S(2)}, u32[]{:S(2)}) collective-permute-start(bf16[1,2,8192]{2,0,1:T(2,128)(2,1)S(1)} %copy.31), channel_id=1, source_target_pairs={{0,16},{16,32},{32,48},{48,64},{64,80},{80,96},{96,112},{112,128},... | collective-permute-start | bytes 98312 | tf_op jit(solution)/shard_map/ppermute | solution.py:12
  75.1 17.7 %collective-permute-start.8 = (bf16[1,2,8192]{2,0,1:T(2,128)(2,1)S(1)}, bf16[1,2,8192]{2,0,1:T(2,128)(2,1)S(1)}, u32[]{:S(2)}, u32[]{:S(2)}) collective-permute-start(bf16[1,2,8192]{2,0,1:T(2,128)(2,1)S(1)} %copy.31), channel_id=1, source_target_pairs={{16,0},{32,16},{48,32},{64,48},{80,64},{96,80},{112,96},{128,112},... | collective-permute-start | bytes 98312 | tf_op jit(solution)/shard_map/ppermute | solution.py:12
  93.1 9.0 %collective-permute-start.9 = (bf16[2,2,8192]{2,0,1:T(2,128)(2,1)S(1)}, bf16[2,2,8192]{2,0,1:T(2,128)(2,1)S(1)}, u32[]{:S(2)}, u32[]{:S(2)}) collective-permute-start(bf16[2,2,8192]{2,0,1:T(2,128)(2,1)S(1)} %get-tuple-element.38), channel_id=1, source_target_pairs={{32,0},{48,16},{64,32},{80,48},{96,64},{112,80},{128,96},{144,112}... | collective-permute-start | bytes 196616 | tf_op jit(solution)/shard_map/ppermute | solution.py:12
  98.8 9.9 %collective-permute-start.12 = (bf16[2,2,8192]{2,0,1:T(2,128)(2,1)S(1)}, bf16[2,2,8192]{2,0,1:T(2,128)(2,1)S(1)}, u32[]{:S(2)}, u32[]{:S(2)}) collective-permute-start(bf16[2,2,8192]{2,0,1:T(2,128)(2,1)S(1)} %get-tuple-element.39), channel_id=1, source_target_pairs={{0,32},{16,48},{32,64},{48,80},{64,96},{80,112},{96,128},{112,144}... | collective-permute-start | bytes 196616 | tf_op jit(solution)/shard_map/ppermute | solution.py:12
  109.1 16.5 %collective-permute-start.10 = (bf16[3,2,8192]{2,0,1:T(4,128)(2,1)S(1)}, bf16[3,2,8192]{2,0,1:T(4,128)(2,1)S(1)}, u32[]{:S(2)}, u32[]{:S(2)}) collective-permute-start(bf16[3,2,8192]{2,0,1:T(4,128)(2,1)S(1)} %get-tuple-element.36), channel_id=1, source_target_pairs={{64,0},{80,16},{96,32},{112,48},{128,64},{144,80},{160,96},{176,11... | collective-permute-start | bytes 294920 | tf_op jit(solution)/shard_map/ppermute | solution.py:12
  112.6 18.1 %collective-permute-start.13 = (bf16[3,2,8192]{2,0,1:T(4,128)(2,1)S(1)}, bf16[3,2,8192]{2,0,1:T(4,128)(2,1)S(1)}, u32[]{:S(2)}, u32[]{:S(2)}) collective-permute-start(bf16[3,2,8192]{2,0,1:T(4,128)(2,1)S(1)} %get-tuple-element.37), channel_id=1, source_target_pairs={{0,64},{16,80},{32,96},{48,112},{64,128},{80,144},{96,160},{112,17... | collective-permute-start | bytes 294920 | tf_op jit(solution)/shard_map/ppermute | solution.py:12

commit v5 on v4

--- a/solution.py
+++ b/solution.py
@@ -148,10 +148,16 @@
     lesser_part = jnp.stack([real_part, imag_part]) * modes ** (-0.5)
 
     sent = lesser_part.astype(jnp.bfloat16)
+    gathered = lax.all_gather(sent, "energy")
+    energy = lax.axis_index("energy")
+    last = gathered.shape[0] - 1
     moved = {0: lesser_part}
-    for direction in (1, -1):
-        for j, copy in enumerate(shifted_copies(sent, direction)):
-            moved[direction * (j + 1)] = copy.astype(jnp.float32)
+    for offset in range(-MAX_SHIFT, MAX_SHIFT + 1):
+        if offset != 0:
+            source = energy - offset
+            picked = lax.dynamic_index_in_dim(gathered, jnp.clip(source, 0, last), 0, False)
+            inside = (source >= 0) & (source <= last)
+            moved[offset] = jnp.where(inside, picked.astype(jnp.float32), 0.0)
     self_energy = jnp.zeros_like(lesser_part)
     for offset in range(-MAX_SHIFT, MAX_SHIFT + 1):
         weight = jnp.sum(jnp.where((phonon_shift == offset)[:, None], coupling, 0.0), axis=0)

time: 133 us -> 244 us (1.83)
  the two profiles are of different devices: /device:TPU:18 before, /device:TPU:8 now
where the time goes in v5:
time: 244 us; the launch traced here: 243 us
  waiting for transfers between devices  175 us (72%)
  starting transfers between devices  27.4 us (11%)
  between operations  13.9 us (6%)
  matrix products  13.8 us (6%)
  other arithmetic  7.63 us (3%)
  local copies, waits for them, and re-layouts  5.48 us (2%)
    all_gather x1, waiting for transfers between devices, on_device(): gathered = lax.all_gather(sent, 'energy')  148 us
    ppermute x3, waiting for transfers between devices, sweeps(): arrived = lax.ppermute(state, 'section', stride)  17.3 us
    ppermute x2, starting transfers between devices, sweeps(): lax.ppermute((own_map, chain_src), 'section', chain)  16.9 us
    ppermute x2, waiting for transfers between devices, sweeps(): lax.ppermute((own_map, chain_src), 'section', chain)  6.43 us
    dot_general x2, matrix products, picked_rows(): jnp.einsum('ar,ap->rp', table, selector.astype(table.dtype), preferred_el...  5.92 us
  transfers between devices with their start and end apart: 9, of which 6 were waited for; matrix products, arithmetic and copies ran while one was open for 3% of the time, Pallas kernels for 0%

profile of v5, /device:TPU:8, one launch (start us, length us, event | category | flops | bytes accessed | tf_op | source)
XLA Modules:
  0.0 243.4 jit_solution(5770972788359637097)
XLA Ops:
  6.5 0.0 all-gather.2.cloned.1.call-start
  6.5 0.0 copy-start
  6.5 1.1 copy.29
  7.6 0.0 copy-start.4
  7.6 1.0 copy.30
  8.7 0.0 copy-start.2
  8.7 1.9 collective-permute-start.2
  10.6 2.4 collective-permute-start
  13.0 0.0 collective-permute-done.2
  13.1 1.3 convolution_bitcast_fusion.3
  14.4 1.4 convolution_bitcast_fusion.4
  15.8 0.7 fusion.50
  16.5 0.0 copy-done.4
  16.5 0.0 copy-done.2
  16.5 0.0 collective-permute-done
  16.5 0.0 copy-done
  16.5 0.8 fusion.36
  17.4 2.0 copy.22
  19.3 0.0 copy-start.1
  19.4 2.3 bitcast_negate_fusion
  21.6 0.0 copy-done.1
  21.6 0.1 fusion.35
  21.7 0.1 pad_maximum_fusion
  21.8 15.0 %collective-permute-start.1 = (bf16[2,384,384]{2,1,0:T(8,128)(2,1)S(1)}, bf16[2,384,384]{2,1,0:T(8,128)(2,1)S(1)}, u32[]{:S(2)}, u32[]{:S(2)}) collective-permute-start(bf16[2,384,384]{2,1,0:T(8,128)(2,1)S(1)} %pad_maximum_fusion), channel_id=1, source_target_pairs={{1,3},{3,5},{5,7},{7,9},{9,11},{11,13},{13,15},{2,0},{4,2},{6,4},{... | collective-permute-start | bytes 1769480 | tf_op jit(solution)/shard_map/ppermute | solution.py:88
  36.8 0.0 copy-done.6
  36.9 1.9 collective-permute-start.3
  38.8 6.4 %collective-permute-done.3 = bf16[768,64]{0,1:T(8,128)(2,1)S(1)} collective-permute-done((bf16[768,64]{0,1:T(8,128)(2,1)S(1)}, bf16[768,64]{0,1:T(8,128)(2,1)S(1)}, u32[]{:S(2)}, u32[]{:S(2)}) %collective-permute-start.3) | collective-permute-done | bytes 98336 | tf_op jit(solution)/shard_map/ppermute | solution.py:88
  45.3 1.5 fusion.20
  46.7 1.3 collective-permute-start.4
  48.0 0.0 collective-permute-done.1
  48.0 0.8 convolution_bitcast_fusion
  48.8 0.1 fusion.114
  48.9 0.1 fusion.28
  49.0 5.1 %collective-permute-done.4 = bf16[768,64]{0,1:T(8,128)(2,1)S(1)} collective-permute-done((bf16[768,64]{0,1:T(8,128)(2,1)S(1)}, bf16[768,64]{0,1:T(8,128)(2,1)S(1)}, u32[]{:S(2)}, u32[]{:S(2)}) %collective-permute-start.4) | collective-permute-done | bytes 98336 | tf_op jit(solution)/shard_map/ppermute | solution.py:106
  54.1 0.5 fusion.17
  54.6 1.4 collective-permute-start.5
  56.1 6.1 %collective-permute-done.5 = bf16[768,64]{0,1:T(8,128)(2,1)S(1)} collective-permute-done((bf16[768,64]{0,1:T(8,128)(2,1)S(1)}, bf16[768,64]{0,1:T(8,128)(2,1)S(1)}, u32[]{:S(2)}, u32[]{:S(2)}) %collective-permute-start.5) | collective-permute-done | bytes 98336 | tf_op jit(solution)/shard_map/ppermute | solution.py:106
  62.2 0.5 fusion.18
  62.7 1.3 collective-permute-start.6
  64.0 0.0 copy-done.8
  64.0 0.0 copy-start.9
  64.0 6.1 %collective-permute-done.6 = bf16[768,64]{0,1:T(8,128)(2,1)S(1)} collective-permute-done((bf16[768,64]{0,1:T(8,128)(2,1)S(1)}, bf16[768,64]{0,1:T(8,128)(2,1)S(1)}, u32[]{:S(2)}, u32[]{:S(2)}) %collective-permute-start.6) | collective-permute-done | bytes 98336 | tf_op jit(solution)/shard_map/ppermute | solution.py:106
  70.1 0.5 fusion.19
  70.6 2.1 collective-permute-start.7
  72.7 0.0 copy-done.9
  72.8 3.8 %collective-permute-done.7 = bf16[384,128]{0,1:T(8,128)(2,1)S(1)} collective-permute-done((bf16[384,128]{0,1:T(8,128)(2,1)S(1)}, bf16[384,128]{0,1:T(8,128)(2,1)S(1)}, u32[]{:S(2)}, u32[]{:S(2)}) %collective-permute-start.7) | collective-permute-done | bytes 98336 | tf_op jit(solution)/shard_map/ppermute | solution.py:112
  76.6 0.3 convolution_bitcast_fusion.1
  76.9 0.3 convolution_bitcast_fusion.2
  77.2 0.0 copy-done.5
  77.2 0.0 copy-start.3
  77.2 2.8 %fusion.1 = f32[128,8192]{1,0:T(8,128)S(1)} fusion(s32[8192]{0:T(1024)S(1)} %broadcast_subtract_fusion, f32[384,64]{0,1:T(8,128)S(1)} %get-tuple-element.39, f32[384,64]{0,1:T(8,128)S(1)} %get-tuple-element.38, bf16[1,1,384,128]{2,3,1,0:T(8,128)(2,1)S(1)} %copy-done.5, pred[]{:T(512)S(6)} %eq.61, bf16[384,64]{0,1:T(8,128)(2,1)S(1)} %get-tuple-element.45, ...), kind=kOutput, calls=%fused_computation.3 | convolution fusion | flops 808894464 | bytes 4620289 | tf_op jit(solution)/shard_map/ar,ap->rp/dot_general | solution.py:55
  80.0 0.0 copy-done.3
  80.0 3.2 %multiply_reduce_fusion = (f32[8192]{0:T(1024)S(1)}, f32[128,8192]{1,0:T(8,128)S(1)}) fusion(f32[128,8192]{1,0:T(8,128)S(1)} %fusion.1, s32[8192]{0:T(1024)S(1)} %broadcast_subtract_fusion.1, f32[384,64]{0,1:T(8,128)S(1)} %get-tuple-element.37, f32[384,64]{0,1:T(8,128)S(1)} %get-tuple-element.36, bf16[1,1,384,128]{2,3,1,0:T(8,128)(2,1)S(1)} %copy-done.3, ...), kind=kOutput, calls=%fused_computation.6 | convolution fusion | flops 810983424 | bytes 8847361 | tf_op jit(solution)/shard_map/ar,ap->rp/dot_general | solution.py:55
  83.2 0.0 copy-start.10
  83.2 0.0 copy-start.7
  83.2 0.9 fusion.4
  84.1 0.7 fusion.105
  84.8 0.0 all-gather.2.cloned.1.call-update
  84.9 0.0 copy-done.10
  84.9 0.0 copy-done.7
  84.9 1.1 select_reduce_fusion.12
  86.0 147.7 %all-gather.2.cloned.1.call-done = bf16[64,2,8192]{2,1,0:T(2,128)(2,1)} async-done(((bf16[1,2,8192]{2,1,0:T(2,128)(2,1)}), bf16[64,2,8192]{2,1,0:T(2,128)(2,1)}) %all-gather.2.cloned.1.call-update) | async-done | bytes 2097168 | tf_op jit(solution)/shard_map/all_gather | solution.py:151
  233.8 1.3 constant_dynamic-slice_fusion.11
  235.1 1.5 fusion.102
  (16 shorter events, 0.2 us)
Async XLA Ops:
  6.5 227.2 %all-gather.2.cloned.1.call-start = ((), (), s32[]{:S(2)}) async-start(), calls=%async_computation | async-start | bytes 2129920 | tf_op jit(solution)/shard_map/all_gather | solution.py:151
  6.5 10.0 %copy-start = (bf16[1,1,2,384,384]{4,3,2,1,0:T(8,128)(2,1)S(1)}, bf16[1,1,2,384,384]{4,3,2,1,0:T(8,128)(2,1)}, u32[]{:S(2)}) copy-start(bf16[1,1,2,384,384]{4,3,2,1,0:T(8,128)(2,1)} %param.7) | copy-start | bytes 1769476
  7.6 8.9 %copy-start.4 = (bf16[1,1,384,128]{2,3,1,0:T(8,128)(2,1)}, bf16[1,1,384,128]{2,3,1,0:T(8,128)(2,1)S(1)}, u32[]{:S(2)}) copy-start(bf16[1,1,384,128]{2,3,1,0:T(8,128)(2,1)S(1)} %copy.29) | copy-start | bytes 294916
  8.7 7.8 %copy-start.2 = (bf16[1,1,384,128]{2,3,1,0:T(8,128)(2,1)}, bf16[1,1,384,128]{2,3,1,0:T(8,128)(2,1)S(1)}, u32[]{:S(2)}) copy-start(bf16[1,1,384,128]{2,3,1,0:T(8,128)(2,1)S(1)} %copy.30) | copy-start | bytes 294916
  8.7 4.3 %collective-permute-start.2 = (bf16[384,128]{0,1:T(8,128)(2,1)S(1)}, bf16[384,128]{0,1:T(8,128)(2,1)S(1)}, u32[]{:S(2)}, u32[]{:S(2)}) collective-permute-start(bf16[384,128]{0,1:T(8,128)(2,1)S(1)} %select_bitcast_fusion), channel_id=1, source_target_pairs={{0,1},{1,0},{2,3},{3,2},{4,5},{5,4},{6,7},{7,6},{8,9},{9,8},{10,11... | collective-permute-start | bytes 294920 | tf_op jit(solution)/shard_map/ppermute | solution.py:64
  10.6 5.9 %collective-permute-start = (bf16[2,384,384]{2,1,0:T(8,128)(2,1)}, bf16[2,384,384]{2,1,0:T(8,128)(2,1)S(1)}, u32[]{:S(2)}, u32[]{:S(2)}) collective-permute-start(bf16[2,384,384]{2,1,0:T(8,128)(2,1)} %bitcast.250), channel_id=1, source_target_pairs={{0,1},{1,0},{2,3},{3,2},{4,5},{5,4},{6,7},{7,6},{8,9},{9,8},{10,11... | collective-permute-start | bytes 1769480 | tf_op jit(solution)/shard_map/ppermute | solution.py:64
  19.3 2.3 copy-start.1
  21.6 15.2 %copy-start.6 = (bf16[384,128]{0,1:T(8,128)(2,1)S(1)}, bf16[384,128]{0,1:T(8,128)(2,1)}, u32[]{:S(2)}) copy-start(bf16[384,128]{0,1:T(8,128)(2,1)} %fusion.50) | copy-start | bytes 294916
  21.8 26.2 %collective-permute-start.1 = (bf16[2,384,384]{2,1,0:T(8,128)(2,1)S(1)}, bf16[2,384,384]{2,1,0:T(8,128)(2,1)S(1)}, u32[]{:S(2)}, u32[]{:S(2)}) collective-permute-start(bf16[2,384,384]{2,1,0:T(8,128)(2,1)S(1)} %pad_maximum_fusion), channel_id=1, source_target_pairs={{1,3},{3,5},{5,7},{7,9},{9,11},{11,13},{13,15},{2,0},{4,2},{6,4},{... | collective-permute-start | bytes 1769480 | tf_op jit(solution)/shard_map/ppermute | solution.py:88
  36.9 8.4 %collective-permute-start.3 = (bf16[768,64]{0,1:T(8,128)(2,1)S(1)}, bf16[768,64]{0,1:T(8,128)(2,1)S(1)}, u32[]{:S(2)}, u32[]{:S(2)}) collective-permute-start(bf16[768,64]{0,1:T(8,128)(2,1)S(1)} %pad_maximum_fusion.1), channel_id=1, source_target_pairs={{1,3},{3,5},{5,7},{7,9},{9,11},{11,13},{13,15},{2,0},{4,2},{6,4},{... | collective-permute-start | bytes 294920 | tf_op jit(solution)/shard_map/ppermute | solution.py:88
  46.7 7.4 %collective-permute-start.4 = (bf16[768,64]{0,1:T(8,128)(2,1)S(1)}, bf16[768,64]{0,1:T(8,128)(2,1)S(1)}, u32[]{:S(2)}, u32[]{:S(2)}) collective-permute-start(bf16[768,64]{0,1:T(8,128)(2,1)S(1)} %fusion.20), channel_id=1, source_target_pairs={{1,5},{3,7},{5,9},{7,11},{9,13},{11,15},{4,0},{6,2},{8,4},{10,6},{... | collective-permute-start | bytes 294920 | tf_op jit(solution)/shard_map/ppermute | solution.py:106
  54.6 9.3 %copy-start.8 = (s32[8192]{0:T(1024)S(1)}, s32[8192]{0:T(1024)}, u32[]{:S(2)}) copy-start(s32[8192]{0:T(1024)} %param.11) | copy-start | bytes 98308
  54.6 7.5 %collective-permute-start.5 = (bf16[768,64]{0,1:T(8,128)(2,1)S(1)}, bf16[768,64]{0,1:T(8,128)(2,1)S(1)}, u32[]{:S(2)}, u32[]{:S(2)}) collective-permute-start(bf16[768,64]{0,1:T(8,128)(2,1)S(1)} %fusion.17), channel_id=1, source_target_pairs={{1,5},{3,7},{5,9},{7,11},{9,13},{11,15},{4,0},{6,2},{8,4},{10,6},{... | collective-permute-start | bytes 294920 | tf_op jit(solution)/shard_map/ppermute | solution.py:106
  62.7 7.4 %collective-permute-start.6 = (bf16[768,64]{0,1:T(8,128)(2,1)S(1)}, bf16[768,64]{0,1:T(8,128)(2,1)S(1)}, u32[]{:S(2)}, u32[]{:S(2)}) collective-permute-start(bf16[768,64]{0,1:T(8,128)(2,1)S(1)} %fusion.18), channel_id=1, source_target_pairs={{1,5},{3,7},{5,9},{7,11},{9,13},{11,15},{4,0},{6,2},{8,4},{10,6},{... | collective-permute-start | bytes 294920 | tf_op jit(solution)/shard_map/ppermute | solution.py:106
  64.0 8.7 %copy-start.9 = (s32[8192]{0:T(1024)S(1)}, s32[8192]{0:T(1024)}, u32[]{:S(2)}) copy-start(s32[8192]{0:T(1024)} %param.10) | copy-start | bytes 98308
  70.6 6.6 %copy-start.5 = (bf16[1,1,384,128]{2,3,1,0:T(8,128)(2,1)S(1)}, bf16[1,1,384,128]{2,3,1,0:T(8,128)(2,1)}, u32[]{:S(2)}) copy-start(bf16[1,1,384,128]{2,3,1,0:T(8,128)(2,1)} %copy-done.4) | copy-start | bytes 294916
  70.6 5.9 %collective-permute-start.7 = (bf16[384,128]{0,1:T(8,128)(2,1)S(1)}, bf16[384,128]{0,1:T(8,128)(2,1)S(1)}, u32[]{:S(2)}, u32[]{:S(2)}) collective-permute-start(bf16[384,128]{0,1:T(8,128)(2,1)S(1)} %pad_maximum_fusion.2), channel_id=1, source_target_pairs={{1,2},{3,4},{5,6},{7,8},{9,10},{11,12},{13,14},{2,1},{4,3},{6,5},{... | collective-permute-start | bytes 294920 | tf_op jit(solution)/shard_map/ppermute | solution.py:112
  77.2 2.8 %copy-start.3 = (bf16[1,1,384,128]{2,3,1,0:T(8,128)(2,1)S(1)}, bf16[1,1,384,128]{2,3,1,0:T(8,128)(2,1)}, u32[]{:S(2)}) copy-start(bf16[1,1,384,128]{2,3,1,0:T(8,128)(2,1)} %copy-done.2) | copy-start | bytes 294916
  83.2 1.7 copy-start.10
  83.2 1.7 copy-start.7
Sparse Core Ops, SparseCore 0:
  84.9 148.7 all-gather.1

commit v6 on v4

--- a/solution.py
+++ b/solution.py
@@ -70,13 +70,6 @@
     backward_real, backward_imag = adjoint_product(left, right)
     real_part = jnp.where(odd, forward_real, backward_real).astype(jnp.bfloat16)
     imag_part = jnp.where(odd, forward_imag, backward_imag).astype(jnp.bfloat16)
-    chain_map = jnp.concatenate(
-        [
-            jnp.concatenate([real_part, -imag_part], axis=1),
-            jnp.concatenate([imag_part, real_part], axis=1),
-        ],
-        axis=0,
-    )
     pair_forward = (complex_product(blocks, other_src, False) + forward_src).astype(jnp.bfloat16)
     pair_backward = (complex_product(blocks, other_src, True) + backward_src).astype(jnp.bfloat16)
     chain_src = stacked(jnp.where(odd, pair_forward, pair_backward))
@@ -90,7 +83,7 @@
     joint_real, joint_imag = matrix_product(own_map, upstream_map)
     joint_real = jnp.where(has_upstream, joint_real, real_part).astype(jnp.bfloat16)
     joint_imag = jnp.where(has_upstream, joint_imag, imag_part).astype(jnp.bfloat16)
-    joint_src = (jnp.dot(chain_map, upstream_src, preferred_element_type=jnp.float32)
+    joint_src = (stacked(complex_product(own_map, joined(upstream_src), False))
                  + chain_src).astype(jnp.bfloat16)
     joint_map = jnp.concatenate(
         [
@@ -119,15 +112,19 @@
     return fields, adjoints
 
 
+SHIFT_ROUNDS = (((1, (0,)), (2, (0,))), ((3, (0, 1)), (4, (1, 2))))
+
+
 def shifted_copies(sent, direction):
-    copies = []
-    step = 1
-    while len(copies) < MAX_SHIFT:
-        width = min(step, MAX_SHIFT - len(copies))
-        payload = jnp.stack(([sent] + copies)[:width])
-        arrived = passed_along(payload, "energy", direction * step)
-        copies.extend(arrived[j] for j in range(width))
-        step *= 2
+    copies = {0: sent}
+    for rounds in SHIFT_ROUNDS:
+        arrived = {}
+        for step, held in rounds:
+            payload = jnp.stack([copies[k] for k in held])
+            moved = passed_along(payload, "energy", direction * step)
+            for j, k in enumerate(held):
+                arrived[k + step] = moved[j]
+        copies.update(arrived)
     return copies
 
 
@@ -150,8 +147,9 @@
     sent = lesser_part.astype(jnp.bfloat16)
     moved = {0: lesser_part}
     for direction in (1, -1):
-        for j, copy in enumerate(shifted_copies(sent, direction)):
-            moved[direction * (j + 1)] = copy.astype(jnp.float32)
+        for k, copy in shifted_copies(sent, direction).items():
+            if k != 0:
+                moved[direction * k] = copy.astype(jnp.float32)
     self_energy = jnp.zeros_like(lesser_part)
     for offset in range(-MAX_SHIFT, MAX_SHIFT + 1):
         weight = jnp.sum(jnp.where((phonon_shift == offset)[:, None], coupling, 0.0), axis=0)

time: 133 us -> 127 us (0.955)
  waiting for transfers between devices: 51.1 us -> 38.8 us
  starting transfers between devices: 54.9 us -> 61.5 us
    ppermute x6 -> x8, waiting for transfers between devices: 20.3 us -> 13 us  [passed_along(): lax.ppermute(value, axis, [(source, source + steps) for source in range(l...]
    ppermute x6 -> x8, starting transfers between devices: 37.7 us -> 44.6 us  [passed_along(): lax.ppermute(value, axis, [(source, source + steps) for source in range(l...]
    ppermute x3, waiting for transfers between devices: 18.8 us -> 15.6 us  [sweeps(): arrived = lax.ppermute(state, 'section', stride)]
    neg x1 -> x0, other arithmetic: 2.25 us -> none  [sweeps(): -imag_part]
    ppermute x2, waiting for transfers between devices: 8.03 us -> 6.23 us  [sweeps(): lax.ppermute((own_map, chain_src), 'section', chain)]
    dot_general x1 -> x0, matrix products: 1.46 us -> none  [sweeps(): jnp.dot(chain_map, upstream_src, preferred_element_type=jnp.float32)]
    convert_element_type x1, other arithmetic: 0.11 us -> 1.5 us  [sweeps(): real_part = jnp.where(odd, forward_real, backward_real).astype(jnp.bfloat16)]
  transfers between devices with their start and end apart: 14 -> 16, of which waited for: 10 -> 8; matrix products, arithmetic and copies ran while one was open for 5% -> 9% of each run, Pallas kernels for 0% -> 0%
where the time goes in v6:
time: 127 us; the launch traced here: 126 us
  starting transfers between devices  61.5 us (48%)
  waiting for transfers between devices  38.8 us (31%)
  matrix products  12.6 us (10%)
  other arithmetic  6.72 us (5%)
  local copies, waits for them, and re-layouts  5.52 us (4%)
    ppermute x8, starting transfers between devices, passed_along(): lax.ppermute(value, axis, [(source, source + steps) for source in range(l...  44.6 us
    ppermute x3, waiting for transfers between devices, sweeps(): arrived = lax.ppermute(state, 'section', stride)  15.6 us
    ppermute x8, waiting for transfers between devices, passed_along(): lax.ppermute(value, axis, [(source, source + steps) for source in range(l...  13 us
    ppermute x2, waiting for transfers between devices, sweeps(): lax.ppermute((own_map, chain_src), 'section', chain)  6.23 us
    dot_general x2, matrix products, picked_rows(): jnp.einsum('ar,ap->rp', table, selector.astype(table.dtype), preferred_el...  5.92 us
    ppermute x3, starting transfers between devices, sweeps(): arrived = lax.ppermute(state, 'section', stride)  5.89 us
    ppermute x2, starting transfers between devices, sweeps(): lax.ppermute((own_map, chain_src), 'section', chain)  4.7 us
    ppermute x2, starting transfers between devices, sweeps(): lax.ppermute((blocks, jnp.where(odd, backward_src, forward_src)), 'sectio...  4.46 us
  transfers between devices with their start and end apart: 16, of which 8 were waited for; matrix products, arithmetic and copies ran while one was open for 9% of the time, Pallas kernels for 0%

profile of v6, /device:TPU:18, one launch (start us, length us, event | category | flops | bytes accessed | tf_op | source)
XLA Modules:
  0.0 125.9 jit_solution(12705125058726738538)
XLA Ops:
  0.0 1.0 copy.18
  1.0 1.0 copy.19
  2.1 0.0 copy-start
  2.1 2.1 %collective-permute-start.2 = (bf16[384,128]{0,1:T(8,128)(2,1)S(1)}, bf16[384,128]{0,1:T(8,128)(2,1)S(1)}, u32[]{:S(2)}, u32[]{:S(2)}) collective-permute-start(bf16[384,128]{0,1:T(8,128)(2,1)S(1)} %select_bitcast_fusion), channel_id=1, source_target_pairs={{0,1},{1,0},{2,3},{3,2},{4,5},{5,4},{6,7},{7,6},{8,9},{9,8},{10,11... | collective-permute-start | bytes 294920 | tf_op jit(solution)/shard_map/ppermute | solution.py:64
  4.2 2.4 %collective-permute-start = (bf16[2,384,384]{2,1,0:T(8,128)(2,1)}, bf16[2,384,384]{2,1,0:T(8,128)(2,1)S(1)}, u32[]{:S(2)}, u32[]{:S(2)}) collective-permute-start(bf16[2,384,384]{2,1,0:T(8,128)(2,1)} %bitcast.239), channel_id=1, source_target_pairs={{0,1},{1,0},{2,3},{3,2},{4,5},{5,4},{6,7},{7,6},{8,9},{9,8},{10,11... | collective-permute-start | bytes 1769480 | tf_op jit(solution)/shard_map/ppermute | solution.py:64
  6.6 0.0 collective-permute-done.2
  6.6 1.3 %convolution_bitcast_fusion.3 = f32[2,384,128]{1,2,0:T(8,128)S(1)} fusion(bf16[384,128]{0,1:T(8,128)(2,1)S(1)} %collective-permute-done.2, bf16[1,1,2,384,384]{4,3,2,1,0:T(8,128)(2,1)} %param.7), kind=kOutput, calls=%fused_computation.14 | convolution fusion | flops 75497472 | bytes 1081344 | tf_op jit(solution)/shard_map/cji,jn->cin/dot_general | solution.py:18
  8.0 1.4 %convolution_bitcast_fusion.4 = f32[2,384,128]{1,2,0:T(8,128)S(1)} fusion(bf16[384,128]{0,1:T(8,128)(2,1)S(1)} %collective-permute-done.2, bf16[1,1,2,384,384]{4,3,2,1,0:T(8,128)(2,1)} %param.7), kind=kOutput, calls=%fused_computation.15 | convolution fusion | flops 75497472 | bytes 1081344 | tf_op jit(solution)/shard_map/cij,jn->cin/dot_general | solution.py:22
  9.5 0.0 copy-start.8
  9.5 0.7 pad_maximum_fusion.1
  10.1 2.3 %collective-permute-start.3 = (bf16[768,64]{0,1:T(8,128)(2,1)}, bf16[768,64]{0,1:T(8,128)(2,1)}, u32[]{:S(2)}, u32[]{:S(2)}) collective-permute-start(bf16[768,64]{0,1:T(8,128)(2,1)} %pad_maximum_fusion.1), channel_id=1, source_target_pairs={{1,3},{3,5},{5,7},{7,9},{9,11},{11,13},{13,15},{2,0},{4,2},{6,4},{... | collective-permute-start | bytes 294920 | tf_op jit(solution)/shard_map/ppermute | solution.py:81
  12.5 0.0 collective-permute-done
  12.5 0.8 fusion.21
  13.4 2.0 %copy.9 = f32[2,384,2,384]{1,3,0,2:T(8,128)} copy(f32[2,384,2,384]{3,1,2,0:T(8,128)S(1)} %fusion.21) | data formatting | bytes 4718592 | tf_op jit(solution)/shard_map/cij,djk->cdik/dot_general | solution.py:29
  15.4 1.5 %fusion.20 = bf16[1,1,384,384]{3,2,1,0:T(8,128)(2,1)S(1)} fusion(f32[2,2,384,384]{3,2,0,1:T(8,128)S(1)} %bitcast.237, f32[2,2,384,384]{3,2,1,0:T(8,128)} %bitcast.240, pred[]{:T(512)S(6)} %eq.61), kind=kLoop, calls=%fused_computation.39 | loop fusion | flops 589824 | bytes 2654209 | tf_op jit(solution)/shard_map/convert_element_type | solution.py:71
  16.9 0.5 copy-done.1
  17.4 0.1 fusion.16
  17.5 0.1 pad_maximum_fusion
  17.6 2.4 %collective-permute-start.1 = (bf16[2,384,384]{2,1,0:T(8,128)(2,1)S(1)}, bf16[2,384,384]{2,1,0:T(8,128)(2,1)S(1)}, u32[]{:S(2)}, u32[]{:S(2)}) collective-permute-start(bf16[2,384,384]{2,1,0:T(8,128)(2,1)S(1)} %pad_maximum_fusion), channel_id=1, source_target_pairs={{1,3},{3,5},{5,7},{7,9},{9,11},{11,13},{13,15},{2,0},{4,2},{6,4},{... | collective-permute-start | bytes 1769480 | tf_op jit(solution)/shard_map/ppermute | solution.py:81
  19.9 0.0 collective-permute-done.3
  20.0 0.8 fusion.101
  20.8 0.3 fusion.51
  21.2 1.9 %collective-permute-start.4 = (bf16[768,64]{0,1:T(8,128)(2,1)S(1)}, bf16[768,64]{0,1:T(8,128)(2,1)S(1)}, u32[]{:S(2)}, u32[]{:S(2)}) collective-permute-start(bf16[768,64]{0,1:T(8,128)(2,1)S(1)} %fusion.35), channel_id=1, source_target_pairs={{1,5},{3,7},{5,9},{7,11},{9,13},{11,15},{4,0},{6,2},{8,4},{10,6},{... | collective-permute-start | bytes 294920 | tf_op jit(solution)/shard_map/ppermute | solution.py:99
  23.1 6.2 %collective-permute-done.1 = bf16[2,384,384]{2,1,0:T(8,128)(2,1)S(1)} collective-permute-done((bf16[2,384,384]{2,1,0:T(8,128)(2,1)S(1)}, bf16[2,384,384]{2,1,0:T(8,128)(2,1)S(1)}, u32[]{:S(2)}, u32[]{:S(2)}) %collective-permute-start.1) | collective-permute-done | bytes 589856 | tf_op jit(solution)/shard_map/ppermute | solution.py:81
  29.4 0.8 convolution_bitcast_fusion
  30.1 0.1 fusion.98
  30.3 0.1 fusion.29
  30.3 0.0 copy-start.11
  30.4 2.3 %collective-permute-done.4 = bf16[768,64]{0,1:T(8,128)(2,1)S(1)} collective-permute-done((bf16[768,64]{0,1:T(8,128)(2,1)S(1)}, bf16[768,64]{0,1:T(8,128)(2,1)S(1)}, u32[]{:S(2)}, u32[]{:S(2)}) %collective-permute-start.4) | collective-permute-done | bytes 98336 | tf_op jit(solution)/shard_map/ppermute | solution.py:99
  32.6 0.5 fusion.6
  33.2 2.1 %collective-permute-start.5 = (bf16[768,64]{0,1:T(8,128)(2,1)S(1)}, bf16[768,64]{0,1:T(8,128)(2,1)S(1)}, u32[]{:S(2)}, u32[]{:S(2)}) collective-permute-start(bf16[768,64]{0,1:T(8,128)(2,1)S(1)} %fusion.6), channel_id=1, source_target_pairs={{1,5},{3,7},{5,9},{7,11},{9,13},{11,15},{4,0},{6,2},{8,4},{10,6},{... | collective-permute-start | bytes 294920 | tf_op jit(solution)/shard_map/ppermute | solution.py:99
  35.2 6.7 %collective-permute-done.5 = bf16[768,64]{0,1:T(8,128)(2,1)S(1)} collective-permute-done((bf16[768,64]{0,1:T(8,128)(2,1)S(1)}, bf16[768,64]{0,1:T(8,128)(2,1)S(1)}, u32[]{:S(2)}, u32[]{:S(2)}) %collective-permute-start.5) | collective-permute-done | bytes 98336 | tf_op jit(solution)/shard_map/ppermute | solution.py:99
  41.9 0.5 fusion.7
  42.4 1.9 %collective-permute-start.6 = (bf16[768,64]{0,1:T(8,128)(2,1)S(1)}, bf16[768,64]{0,1:T(8,128)(2,1)S(1)}, u32[]{:S(2)}, u32[]{:S(2)}) collective-permute-start(bf16[768,64]{0,1:T(8,128)(2,1)S(1)} %fusion.7), channel_id=1, source_target_pairs={{1,5},{3,7},{5,9},{7,11},{9,13},{11,15},{4,0},{6,2},{8,4},{10,6},{... | collective-permute-start | bytes 294920 | tf_op jit(solution)/shard_map/ppermute | solution.py:99
  44.4 0.0 copy-start.13
  44.4 6.7 %collective-permute-done.6 = bf16[768,64]{0,1:T(8,128)(2,1)S(1)} collective-permute-done((bf16[768,64]{0,1:T(8,128)(2,1)S(1)}, bf16[768,64]{0,1:T(8,128)(2,1)S(1)}, u32[]{:S(2)}, u32[]{:S(2)}) %collective-permute-start.6) | collective-permute-done | bytes 98336 | tf_op jit(solution)/shard_map/ppermute | solution.py:99
  51.0 0.5 fusion.8
  51.6 1.9 %collective-permute-start.7 = (bf16[384,128]{0,1:T(8,128)(2,1)S(1)}, bf16[384,128]{0,1:T(8,128)(2,1)S(1)}, u32[]{:S(2)}, u32[]{:S(2)}) collective-permute-start(bf16[384,128]{0,1:T(8,128)(2,1)S(1)} %pad_maximum_fusion.2), channel_id=1, source_target_pairs={{1,2},{3,4},{5,6},{7,8},{9,10},{11,12},{13,14},{2,1},{4,3},{6,5},{... | collective-permute-start | bytes 294920 | tf_op jit(solution)/shard_map/ppermute | solution.py:105
  53.5 4.0 %collective-permute-done.7 = bf16[384,128]{0,1:T(8,128)(2,1)S(1)} collective-permute-done((bf16[384,128]{0,1:T(8,128)(2,1)S(1)}, bf16[384,128]{0,1:T(8,128)(2,1)S(1)}, u32[]{:S(2)}, u32[]{:S(2)}) %collective-permute-start.7) | collective-permute-done | bytes 98336 | tf_op jit(solution)/shard_map/ppermute | solution.py:105
  57.5 0.3 convolution_bitcast_fusion.1
  57.8 0.3 convolution_bitcast_fusion.2
  58.2 2.8 %fusion.1 = f32[128,8192]{1,0:T(8,128)S(1)} fusion(s32[8192]{0:T(1024)S(1)} %broadcast_subtract_fusion, f32[384,64]{0,1:T(8,128)S(1)} %get-tuple-element.25, f32[384,64]{0,1:T(8,128)S(1)} %get-tuple-element.24, bf16[1,1,384,128]{2,3,1,0:T(8,128)(2,1)S(1)} %copy-done.5, pred[]{:T(512)S(6)} %eq.61, bf16[384,64]{0,1:T(8,128)(2,1)S(1)} %get-tuple-element.33, ...), kind=kOutput, calls=%fused_computation.3 | convolution fusion | flops 808894464 | bytes 4620289 | tf_op jit(solution)/shard_map/ar,ap->rp/dot_general | solution.py:55
  61.0 3.2 %multiply_reduce_fusion = (f32[8192]{0:T(1024)S(1)}, f32[128,8192]{1,0:T(8,128)S(1)}) fusion(f32[128,8192]{1,0:T(8,128)S(1)} %fusion.1, s32[8192]{0:T(1024)S(1)} %broadcast_subtract_fusion.1, f32[384,64]{0,1:T(8,128)S(1)} %get-tuple-element.23, f32[384,64]{0,1:T(8,128)S(1)} %get-tuple-element.22, bf16[1,1,384,128]{2,3,1,0:T(8,128)(2,1)S(1)} %copy-done.3, ...), kind=kOutput, calls=%fused_computation.6 | convolution fusion | flops 810983424 | bytes 8847361 | tf_op jit(solution)/shard_map/ar,ap->rp/dot_general | solution.py:55
  64.1 0.0 copy-start.10
  64.1 0.9 fusion.4
  65.0 0.1 maximum_multiply_fusion
  65.1 0.1 copy.33
  65.2 4.3 %collective-permute-start.12 = (bf16[1,2,8192]{2,0,1:T(2,128)(2,1)S(1)}, bf16[1,2,8192]{2,0,1:T(2,128)(2,1)S(1)}, u32[]{:S(2)}, u32[]{:S(2)}) collective-permute-start(bf16[1,2,8192]{2,0,1:T(2,128)(2,1)S(1)} %copy.33), channel_id=1, source_target_pairs={{0,16},{16,32},{32,48},{48,64},{64,80},{80,96},{96,112},{112,128},... | collective-permute-start | bytes 98312 | tf_op jit(solution)/shard_map/ppermute | solution.py:12
  69.5 6.1 %collective-permute-start.13 = (bf16[1,2,8192]{2,0,1:T(2,128)(2,1)S(1)}, bf16[1,2,8192]{2,0,1:T(2,128)(2,1)S(1)}, u32[]{:S(2)}, u32[]{:S(2)}) collective-permute-start(bf16[1,2,8192]{2,0,1:T(2,128)(2,1)S(1)} %copy.33), channel_id=1, source_target_pairs={{0,32},{16,48},{32,64},{48,80},{64,96},{80,112},{96,128},{112,144}... | collective-permute-start | bytes 98312 | tf_op jit(solution)/shard_map/ppermute | solution.py:12
  75.5 11.7 %collective-permute-start.8 = (bf16[1,2,8192]{2,0,1:T(2,128)(2,1)S(1)}, bf16[1,2,8192]{2,0,1:T(2,128)(2,1)S(1)}, u32[]{:S(2)}, u32[]{:S(2)}) collective-permute-start(bf16[1,2,8192]{2,0,1:T(2,128)(2,1)S(1)} %copy.33), channel_id=1, source_target_pairs={{16,0},{32,16},{48,32},{64,48},{80,64},{96,80},{112,96},{128,112},... | collective-permute-start | bytes 98312 | tf_op jit(solution)/shard_map/ppermute | solution.py:12
  87.2 5.0 %collective-permute-start.9 = (bf16[1,2,8192]{2,0,1:T(2,128)(2,1)S(1)}, bf16[1,2,8192]{2,0,1:T(2,128)(2,1)S(1)}, u32[]{:S(2)}, u32[]{:S(2)}) collective-permute-start(bf16[1,2,8192]{2,0,1:T(2,128)(2,1)S(1)} %copy.33), channel_id=1, source_target_pairs={{32,0},{48,16},{64,32},{80,48},{96,64},{112,80},{128,96},{144,112}... | collective-permute-start | bytes 98312 | tf_op jit(solution)/shard_map/ppermute | solution.py:12
  92.2 1.1 select_reduce_fusion.12
  93.4 0.0 collective-permute-done.12
  93.4 0.0 collective-permute-done.8
  93.4 1.3 %collective-permute-done.9 = bf16[1,2,8192]{2,0,1:T(2,128)(2,1)S(1)} collective-permute-done((bf16[1,2,8192]{2,0,1:T(2,128)(2,1)S(1)}, bf16[1,2,8192]{2,0,1:T(2,128)(2,1)S(1)}, u32[]{:S(2)}, u32[]{:S(2)}) %collective-permute-start.9) | collective-permute-done | bytes 32800 | tf_op jit(solution)/shard_map/ppermute | solution.py:12
  94.7 0.5 pad_maximum_fusion.3
  95.2 7.9 %collective-permute-start.10 = (bf16[2,2,8192]{2,0,1:T(2,128)(2,1)S(1)}, bf16[2,2,8192]{2,0,1:T(2,128)(2,1)S(1)}, u32[]{:S(2)}, u32[]{:S(2)}) collective-permute-start(bf16[2,2,8192]{2,0,1:T(2,128)(2,1)S(1)} %get-tuple-element.38), channel_id=1, source_target_pairs={{64,0},{80,16},{96,32},{112,48},{128,64},{144,80},{160,96},{176,11... | collective-permute-start | bytes 196616 | tf_op jit(solution)/shard_map/ppermute | solution.py:12
  103.2 1.9 %collective-permute-start.11 = (bf16[2,2,8192]{2,0,1:T(2,128)(2,1)S(1)}, bf16[2,2,8192]{2,0,1:T(2,128)(2,1)S(1)}, u32[]{:S(2)}, u32[]{:S(2)}) collective-permute-start(bf16[2,2,8192]{2,0,1:T(2,128)(2,1)S(1)} %get-tuple-element.39), channel_id=1, source_target_pairs={{48,0},{64,16},{80,32},{96,48},{112,64},{128,80},{144,96},{160,112... | collective-permute-start | bytes 196616 | tf_op jit(solution)/shard_map/ppermute | solution.py:12
  105.1 5.7 %collective-permute-start.14 = (bf16[2,2,8192]{2,0,1:T(2,128)(2,1)S(1)}, bf16[2,2,8192]{2,0,1:T(2,128)(2,1)S(1)}, u32[]{:S(2)}, u32[]{:S(2)}) collective-permute-start(bf16[2,2,8192]{2,0,1:T(2,128)(2,1)S(1)} %get-tuple-element.40), channel_id=1, source_target_pairs={{0,48},{16,64},{32,80},{48,96},{64,112},{80,128},{96,144},{112,160... | collective-permute-start | bytes 196616 | tf_op jit(solution)/shard_map/ppermute | solution.py:12
  110.8 2.0 %collective-permute-start.15 = (bf16[2,2,8192]{2,0,1:T(2,128)(2,1)S(1)}, bf16[2,2,8192]{2,0,1:T(2,128)(2,1)S(1)}, u32[]{:S(2)}, u32[]{:S(2)}) collective-permute-start(bf16[2,2,8192]{2,0,1:T(2,128)(2,1)S(1)} %get-tuple-element.41), channel_id=1, source_target_pairs={{0,64},{16,80},{32,96},{48,112},{64,128},{80,144},{96,160},{112,17... | collective-permute-start | bytes 196616 | tf_op jit(solution)/shard_map/ppermute | solution.py:12
  112.8 0.0 collective-permute-done.11
  112.8 3.3 %collective-permute-done.14 = bf16[2,2,8192]{2,0,1:T(2,128)(2,1)S(1)} collective-permute-done((bf16[2,2,8192]{2,0,1:T(2,128)(2,1)S(1)}, bf16[2,2,8192]{2,0,1:T(2,128)(2,1)S(1)}, u32[]{:S(2)}, u32[]{:S(2)}) %collective-permute-start.14) | collective-permute-done | bytes 65568 | tf_op jit(solution)/shard_map/ppermute | solution.py:12
  116.1 8.4 %collective-permute-done.15 = bf16[2,2,8192]{2,0,1:T(2,128)(2,1)S(1)} collective-permute-done((bf16[2,2,8192]{2,0,1:T(2,128)(2,1)S(1)}, bf16[2,2,8192]{2,0,1:T(2,128)(2,1)S(1)}, u32[]{:S(2)}, u32[]{:S(2)}) %collective-permute-start.15) | collective-permute-done | bytes 65568 | tf_op jit(solution)/shard_map/ppermute | solution.py:12
  124.5 1.3 %fusion.64 = f32[2,1,8192]{2,1,0:T(1,128)} fusion(bf16[2,2,8192]{2,0,1:T(2,128)(2,1)S(1)} %collective-permute-done.15, bf16[2,2,8192]{2,0,1:T(2,128)(2,1)S(1)} %collective-permute-done.14, bf16[1,2,8192]{2,0,1:T(2,128)(2,1)S(1)} %collective-permute-done.13, f32[1,1,8192]{2,1,0:T(1,128)S(1)} %bitcast.251, f32[1,1,8192]{2,1,0:T(1,128)S(1)} %bitcast.249, ...), kind=kLoop, calls=%fused_computation.117 | loop fusion | flops 622592 | bytes 950272 | tf_op jit(solution)/shard_map/add | solution.py:156
  (39 shorter events, 0.3 us)
Async XLA Ops:
  1.0 8.4 %copy-start.4 = (bf16[1,1,384,128]{2,3,1,0:T(8,128)(2,1)}, bf16[1,1,384,128]{2,3,1,0:T(8,128)(2,1)S(1)}, u32[]{:S(2)}) copy-start(bf16[1,1,384,128]{2,3,1,0:T(8,128)(2,1)S(1)} %copy.18) | copy-start | bytes 294916
  2.1 8.1 %copy-start.2 = (bf16[1,1,384,128]{2,3,1,0:T(8,128)(2,1)}, bf16[1,1,384,128]{2,3,1,0:T(8,128)(2,1)S(1)}, u32[]{:S(2)}) copy-start(bf16[1,1,384,128]{2,3,1,0:T(8,128)(2,1)S(1)} %copy.19) | copy-start | bytes 294916
  2.1 10.5 %copy-start = (bf16[1,1,2,384,384]{4,3,2,1,0:T(8,128)(2,1)S(1)}, bf16[1,1,2,384,384]{4,3,2,1,0:T(8,128)(2,1)}, u32[]{:S(2)}) copy-start(bf16[1,1,2,384,384]{4,3,2,1,0:T(8,128)(2,1)} %param.7) | copy-start | bytes 1769476
  2.1 4.5 %collective-permute-start.2 = (bf16[384,128]{0,1:T(8,128)(2,1)S(1)}, bf16[384,128]{0,1:T(8,128)(2,1)S(1)}, u32[]{:S(2)}, u32[]{:S(2)}) collective-permute-start(bf16[384,128]{0,1:T(8,128)(2,1)S(1)} %select_bitcast_fusion), channel_id=1, source_target_pairs={{0,1},{1,0},{2,3},{3,2},{4,5},{5,4},{6,7},{7,6},{8,9},{9,8},{10,11... | collective-permute-start | bytes 294920 | tf_op jit(solution)/shard_map/ppermute | solution.py:64
  4.2 8.4 %collective-permute-start = (bf16[2,384,384]{2,1,0:T(8,128)(2,1)}, bf16[2,384,384]{2,1,0:T(8,128)(2,1)S(1)}, u32[]{:S(2)}, u32[]{:S(2)}) collective-permute-start(bf16[2,384,384]{2,1,0:T(8,128)(2,1)} %bitcast.239), channel_id=1, source_target_pairs={{0,1},{1,0},{2,3},{3,2},{4,5},{5,4},{6,7},{7,6},{8,9},{9,8},{10,11... | collective-permute-start | bytes 1769480 | tf_op jit(solution)/shard_map/ppermute | solution.py:64
  9.5 3.0 %copy-start.6 = (bf16[384,64]{0,1:T(8,128)(2,1)}, bf16[384,64]{0,1:T(8,128)(2,1)S(1)}, u32[]{:S(2)}) copy-start(bf16[384,64]{0,1:T(8,128)(2,1)S(1)} %get-tuple-element.36) | copy-start | bytes 147460
  9.5 3.0 %copy-start.8 = (bf16[384,64]{0,1:T(8,128)(2,1)}, bf16[384,64]{0,1:T(8,128)(2,1)S(1)}, u32[]{:S(2)}) copy-start(bf16[384,64]{0,1:T(8,128)(2,1)S(1)} %get-tuple-element.37) | copy-start | bytes 147460
  10.1 9.8 %collective-permute-start.3 = (bf16[768,64]{0,1:T(8,128)(2,1)}, bf16[768,64]{0,1:T(8,128)(2,1)}, u32[]{:S(2)}, u32[]{:S(2)}) collective-permute-start(bf16[768,64]{0,1:T(8,128)(2,1)} %pad_maximum_fusion.1), channel_id=1, source_target_pairs={{1,3},{3,5},{5,7},{7,9},{9,11},{11,13},{13,15},{2,0},{4,2},{6,4},{... | collective-permute-start | bytes 294920 | tf_op jit(solution)/shard_map/ppermute | solution.py:81
  15.4 2.0 %copy-start.1 = (f32[2,384,2,384]{1,3,0,2:T(8,128)S(1)}, f32[2,384,2,384]{1,3,0,2:T(8,128)}, u32[]{:S(2)}) copy-start(f32[2,384,2,384]{1,3,0,2:T(8,128)} %copy.9) | copy-start | bytes 7077892
  17.4 3.8 %copy-start.7 = (bf16[384,64]{0,1:T(8,128)(2,1)S(1)}, bf16[384,64]{0,1:T(8,128)(2,1)}, u32[]{:S(2)}) copy-start(bf16[384,64]{0,1:T(8,128)(2,1)} %copy-done.6) | copy-start | bytes 147460
  17.4 3.8 %copy-start.9 = (bf16[384,64]{0,1:T(8,128)(2,1)S(1)}, bf16[384,64]{0,1:T(8,128)(2,1)}, u32[]{:S(2)}) copy-start(bf16[384,64]{0,1:T(8,128)(2,1)} %copy-done.8) | copy-start | bytes 147460
  17.6 11.8 %collective-permute-start.1 = (bf16[2,384,384]{2,1,0:T(8,128)(2,1)S(1)}, bf16[2,384,384]{2,1,0:T(8,128)(2,1)S(1)}, u32[]{:S(2)}, u32[]{:S(2)}) collective-permute-start(bf16[2,384,384]{2,1,0:T(8,128)(2,1)S(1)} %pad_maximum_fusion), channel_id=1, source_target_pairs={{1,3},{3,5},{5,7},{7,9},{9,11},{11,13},{13,15},{2,0},{4,2},{6,4},{... | collective-permute-start | bytes 1769480 | tf_op jit(solution)/shard_map/ppermute | solution.py:81
  21.2 11.4 %collective-permute-start.4 = (bf16[768,64]{0,1:T(8,128)(2,1)S(1)}, bf16[768,64]{0,1:T(8,128)(2,1)S(1)}, u32[]{:S(2)}, u32[]{:S(2)}) collective-permute-start(bf16[768,64]{0,1:T(8,128)(2,1)S(1)} %fusion.35), channel_id=1, source_target_pairs={{1,5},{3,7},{5,9},{7,11},{9,13},{11,15},{4,0},{6,2},{8,4},{10,6},{... | collective-permute-start | bytes 294920 | tf_op jit(solution)/shard_map/ppermute | solution.py:99
  30.3 4.9 %copy-start.11 = (s32[8192]{0:T(1024)S(1)}, s32[8192]{0:T(1024)}, u32[]{:S(2)}) copy-start(s32[8192]{0:T(1024)} %param.11) | copy-start | bytes 98308
  33.1 11.2 %copy-start.12 = (s32[8192]{0:T(1024)S(1)}, s32[8192]{0:T(1024)}, u32[]{:S(2)}) copy-start(s32[8192]{0:T(1024)} %param.10) | copy-start | bytes 98308
  33.2 8.8 %collective-permute-start.5 = (bf16[768,64]{0,1:T(8,128)(2,1)S(1)}, bf16[768,64]{0,1:T(8,128)(2,1)S(1)}, u32[]{:S(2)}, u32[]{:S(2)}) collective-permute-start(bf16[768,64]{0,1:T(8,128)(2,1)S(1)} %fusion.6), channel_id=1, source_target_pairs={{1,5},{3,7},{5,9},{7,11},{9,13},{11,15},{4,0},{6,2},{8,4},{10,6},{... | collective-permute-start | bytes 294920 | tf_op jit(solution)/shard_map/ppermute | solution.py:99
  42.4 8.6 %collective-permute-start.6 = (bf16[768,64]{0,1:T(8,128)(2,1)S(1)}, bf16[768,64]{0,1:T(8,128)(2,1)S(1)}, u32[]{:S(2)}, u32[]{:S(2)}) collective-permute-start(bf16[768,64]{0,1:T(8,128)(2,1)S(1)} %fusion.7), channel_id=1, source_target_pairs={{1,5},{3,7},{5,9},{7,11},{9,13},{11,15},{4,0},{6,2},{8,4},{10,6},{... | collective-permute-start | bytes 294920 | tf_op jit(solution)/shard_map/ppermute | solution.py:99
  44.4 9.1 %copy-start.13 = (s32[8]{0:T(128)S(1)}, s32[8]{0:T(128)}, u32[]{:S(2)}) copy-start(s32[8]{0:T(128)} %param.12) | copy-start | bytes 100
  51.5 6.6 %copy-start.5 = (bf16[1,1,384,128]{2,3,1,0:T(8,128)(2,1)S(1)}, bf16[1,1,384,128]{2,3,1,0:T(8,128)(2,1)}, u32[]{:S(2)}) copy-start(bf16[1,1,384,128]{2,3,1,0:T(8,128)(2,1)} %copy-done.4) | copy-start | bytes 294916
  51.6 5.9 %collective-permute-start.7 = (bf16[384,128]{0,1:T(8,128)(2,1)S(1)}, bf16[384,128]{0,1:T(8,128)(2,1)S(1)}, u32[]{:S(2)}, u32[]{:S(2)}) collective-permute-start(bf16[384,128]{0,1:T(8,128)(2,1)S(1)} %pad_maximum_fusion.2), channel_id=1, source_target_pairs={{1,2},{3,4},{5,6},{7,8},{9,10},{11,12},{13,14},{2,1},{4,3},{6,5},{... | collective-permute-start | bytes 294920 | tf_op jit(solution)/shard_map/ppermute | solution.py:105
  58.2 2.8 %copy-start.3 = (bf16[1,1,384,128]{2,3,1,0:T(8,128)(2,1)S(1)}, bf16[1,1,384,128]{2,3,1,0:T(8,128)(2,1)}, u32[]{:S(2)}) copy-start(bf16[1,1,384,128]{2,3,1,0:T(8,128)(2,1)} %copy-done.2) | copy-start | bytes 294916
  64.1 28.1 %copy-start.10 = (f32[8,8192]{1,0:T(8,128)S(1)}, f32[8,8192]{1,0:T(8,128)}, u32[]{:S(2)}) copy-start(f32[8,8192]{1,0:T(8,128)} %param.13) | copy-start | bytes 786436
  65.2 28.2 %collective-permute-start.12 = (bf16[1,2,8192]{2,0,1:T(2,128)(2,1)S(1)}, bf16[1,2,8192]{2,0,1:T(2,128)(2,1)S(1)}, u32[]{:S(2)}, u32[]{:S(2)}) collective-permute-start(bf16[1,2,8192]{2,0,1:T(2,128)(2,1)S(1)} %copy.33), channel_id=1, source_target_pairs={{0,16},{16,32},{32,48},{48,64},{64,80},{80,96},{96,112},{112,128},... | collective-permute-start | bytes 98312 | tf_op jit(solution)/shard_map/ppermute | solution.py:12
  69.5 23.9 %collective-permute-start.13 = (bf16[1,2,8192]{2,0,1:T(2,128)(2,1)S(1)}, bf16[1,2,8192]{2,0,1:T(2,128)(2,1)S(1)}, u32[]{:S(2)}, u32[]{:S(2)}) collective-permute-start(bf16[1,2,8192]{2,0,1:T(2,128)(2,1)S(1)} %copy.33), channel_id=1, source_target_pairs={{0,32},{16,48},{32,64},{48,80},{64,96},{80,112},{96,128},{112,144}... | collective-permute-start | bytes 98312 | tf_op jit(solution)/shard_map/ppermute | solution.py:12
  75.5 17.8 %collective-permute-start.8 = (bf16[1,2,8192]{2,0,1:T(2,128)(2,1)S(1)}, bf16[1,2,8192]{2,0,1:T(2,128)(2,1)S(1)}, u32[]{:S(2)}, u32[]{:S(2)}) collective-permute-start(bf16[1,2,8192]{2,0,1:T(2,128)(2,1)S(1)} %copy.33), channel_id=1, source_target_pairs={{16,0},{32,16},{48,32},{64,48},{80,64},{96,80},{112,96},{128,112},... | collective-permute-start | bytes 98312 | tf_op jit(solution)/shard_map/ppermute | solution.py:12
  87.2 7.5 %collective-permute-start.9 = (bf16[1,2,8192]{2,0,1:T(2,128)(2,1)S(1)}, bf16[1,2,8192]{2,0,1:T(2,128)(2,1)S(1)}, u32[]{:S(2)}, u32[]{:S(2)}) collective-permute-start(bf16[1,2,8192]{2,0,1:T(2,128)(2,1)S(1)} %copy.33), channel_id=1, source_target_pairs={{32,0},{48,16},{64,32},{80,48},{96,64},{112,80},{128,96},{144,112}... | collective-permute-start | bytes 98312 | tf_op jit(solution)/shard_map/ppermute | solution.py:12
  95.2 17.6 %collective-permute-start.10 = (bf16[2,2,8192]{2,0,1:T(2,128)(2,1)S(1)}, bf16[2,2,8192]{2,0,1:T(2,128)(2,1)S(1)}, u32[]{:S(2)}, u32[]{:S(2)}) collective-permute-start(bf16[2,2,8192]{2,0,1:T(2,128)(2,1)S(1)} %get-tuple-element.38), channel_id=1, source_target_pairs={{64,0},{80,16},{96,32},{112,48},{128,64},{144,80},{160,96},{176,11... | collective-permute-start | bytes 196616 | tf_op jit(solution)/shard_map/ppermute | solution.py:12
  103.2 9.7 %collective-permute-start.11 = (bf16[2,2,8192]{2,0,1:T(2,128)(2,1)S(1)}, bf16[2,2,8192]{2,0,1:T(2,128)(2,1)S(1)}, u32[]{:S(2)}, u32[]{:S(2)}) collective-permute-start(bf16[2,2,8192]{2,0,1:T(2,128)(2,1)S(1)} %get-tuple-element.39), channel_id=1, source_target_pairs={{48,0},{64,16},{80,32},{96,48},{112,64},{128,80},{144,96},{160,112... | collective-permute-start | bytes 196616 | tf_op jit(solution)/shard_map/ppermute | solution.py:12
  105.1 11.0 %collective-permute-start.14 = (bf16[2,2,8192]{2,0,1:T(2,128)(2,1)S(1)}, bf16[2,2,8192]{2,0,1:T(2,128)(2,1)S(1)}, u32[]{:S(2)}, u32[]{:S(2)}) collective-permute-start(bf16[2,2,8192]{2,0,1:T(2,128)(2,1)S(1)} %get-tuple-element.40), channel_id=1, source_target_pairs={{0,48},{16,64},{32,80},{48,96},{64,112},{80,128},{96,144},{112,160... | collective-permute-start | bytes 196616 | tf_op jit(solution)/shard_map/ppermute | solution.py:12
  110.8 13.7 %collective-permute-start.15 = (bf16[2,2,8192]{2,0,1:T(2,128)(2,1)S(1)}, bf16[2,2,8192]{2,0,1:T(2,128)(2,1)S(1)}, u32[]{:S(2)}, u32[]{:S(2)}) collective-permute-start(bf16[2,2,8192]{2,0,1:T(2,128)(2,1)S(1)} %get-tuple-element.41), channel_id=1, source_target_pairs={{0,64},{16,80},{32,96},{48,112},{64,128},{80,144},{96,160},{112,17... | collective-permute-start | bytes 196616 | tf_op jit(solution)/shard_map/ppermute | solution.py:12

commit v7 on v6

--- a/solution.py
+++ b/solution.py
@@ -112,7 +112,7 @@
     return fields, adjoints
 
 
-SHIFT_ROUNDS = (((1, (0,)), (2, (0,))), ((3, (0, 1)), (4, (1, 2))))
+SHIFT_ROUNDS = (tuple((step, (0,)) for step in range(1, MAX_SHIFT + 1)),)
 
 
 def shifted_copies(sent, direction):

time: 127 us -> 148 us (1.17)
  starting transfers between devices: 61.5 us -> 86.7 us
  waiting for transfers between devices: 38.8 us -> 35.2 us
    ppermute x8 -> x12, starting transfers between devices: 44.6 us -> 69.8 us  [passed_along(): lax.ppermute(value, axis, [(source, source + steps) for source in range(l...]
    ppermute x8 -> x12, waiting for transfers between devices: 13 us -> 9.29 us  [passed_along(): lax.ppermute(value, axis, [(source, source + steps) for source in range(l...]
  transfers between devices with their start and end apart: 16 -> 20, of which waited for: 8 -> 8; matrix products, arithmetic and copies ran while one was open for 9% -> 8% of each run, Pallas kernels for 0% -> 0%
where the time goes in v7:
time: 148 us; the launch traced here: 147 us
  starting transfers between devices  86.7 us (59%)
  waiting for transfers between devices  35.2 us (24%)
  matrix products  12.6 us (9%)
  other arithmetic  6.18 us (4%)
  local copies, waits for them, and re-layouts  5.52 us (4%)
    ppermute x12, starting transfers between devices, passed_along(): lax.ppermute(value, axis, [(source, source + steps) for source in range(l...  69.8 us
    ppermute x3, waiting for transfers between devices, sweeps(): arrived = lax.ppermute(state, 'section', stride)  15.7 us
    ppermute x12, waiting for transfers between devices, passed_along(): lax.ppermute(value, axis, [(source, source + steps) for source in range(l...  9.29 us
    ppermute x2, waiting for transfers between devices, sweeps(): lax.ppermute((own_map, chain_src), 'section', chain)  6.23 us
    dot_general x2, matrix products, picked_rows(): jnp.einsum('ar,ap->rp', table, selector.astype(table.dtype), preferred_el...  5.92 us
    ppermute x3, starting transfers between devices, sweeps(): arrived = lax.ppermute(state, 'section', stride)  5.89 us
    ppermute x2, starting transfers between devices, sweeps(): lax.ppermute((own_map, chain_src), 'section', chain)  4.71 us
    ppermute x2, starting transfers between devices, sweeps(): lax.ppermute((blocks, jnp.where(odd, backward_src, forward_src)), 'sectio...  4.46 us
  transfers between devices with their start and end apart: 20, of which 8 were waited for; matrix products, arithmetic and copies ran while one was open for 8% of the time, Pallas kernels for 0%

profile of v7, /device:TPU:18, one launch (start us, length us, event | category | flops | bytes accessed | tf_op | source)
XLA Modules:
  0.0 146.9 jit_solution(3910568274915403373)
XLA Ops:
  0.0 1.0 copy.18
  1.0 1.0 copy.19
  2.1 0.0 copy-start
  2.1 2.1 %collective-permute-start.2 = (bf16[384,128]{0,1:T(8,128)(2,1)S(1)}, bf16[384,128]{0,1:T(8,128)(2,1)S(1)}, u32[]{:S(2)}, u32[]{:S(2)}) collective-permute-start(bf16[384,128]{0,1:T(8,128)(2,1)S(1)} %select_bitcast_fusion), channel_id=1, source_target_pairs={{0,1},{1,0},{2,3},{3,2},{4,5},{5,4},{6,7},{7,6},{8,9},{9,8},{10,11... | collective-permute-start | bytes 294920 | tf_op jit(solution)/shard_map/ppermute | solution.py:64
  4.2 2.4 %collective-permute-start = (bf16[2,384,384]{2,1,0:T(8,128)(2,1)}, bf16[2,384,384]{2,1,0:T(8,128)(2,1)S(1)}, u32[]{:S(2)}, u32[]{:S(2)}) collective-permute-start(bf16[2,384,384]{2,1,0:T(8,128)(2,1)} %bitcast.171), channel_id=1, source_target_pairs={{0,1},{1,0},{2,3},{3,2},{4,5},{5,4},{6,7},{7,6},{8,9},{9,8},{10,11... | collective-permute-start | bytes 1769480 | tf_op jit(solution)/shard_map/ppermute | solution.py:64
  6.6 0.0 collective-permute-done.2
  6.6 1.3 convolution_bitcast_fusion.3
  8.0 1.4 convolution_bitcast_fusion.4
  9.5 0.0 copy-start.8
  9.5 0.7 pad_maximum_fusion.1
  10.2 2.3 %collective-permute-start.3 = (bf16[768,64]{0,1:T(8,128)(2,1)}, bf16[768,64]{0,1:T(8,128)(2,1)}, u32[]{:S(2)}, u32[]{:S(2)}) collective-permute-start(bf16[768,64]{0,1:T(8,128)(2,1)} %pad_maximum_fusion.1), channel_id=1, source_target_pairs={{1,3},{3,5},{5,7},{7,9},{9,11},{11,13},{13,15},{2,0},{4,2},{6,4},{... | collective-permute-start | bytes 294920 | tf_op jit(solution)/shard_map/ppermute | solution.py:81
  12.5 0.0 collective-permute-done
  12.5 0.8 fusion.21
  13.4 2.0 %copy.9 = f32[2,384,2,384]{1,3,0,2:T(8,128)} copy(f32[2,384,2,384]{3,1,2,0:T(8,128)S(1)} %fusion.21) | data formatting | bytes 4718592 | tf_op jit(solution)/shard_map/cij,djk->cdik/dot_general | solution.py:29
  15.4 1.5 %fusion.20 = bf16[1,1,384,384]{3,2,1,0:T(8,128)(2,1)S(1)} fusion(f32[2,2,384,384]{3,2,0,1:T(8,128)S(1)} %bitcast.169, f32[2,2,384,384]{3,2,1,0:T(8,128)} %bitcast.172, pred[]{:T(512)S(6)} %eq.61), kind=kLoop, calls=%fused_computation.39 | loop fusion | flops 589824 | bytes 2654209 | tf_op jit(solution)/shard_map/convert_element_type | solution.py:71
  16.9 0.5 copy-done.1
  17.4 0.1 fusion.16
  17.5 0.1 pad_maximum_fusion
  17.6 2.4 %collective-permute-start.1 = (bf16[2,384,384]{2,1,0:T(8,128)(2,1)S(1)}, bf16[2,384,384]{2,1,0:T(8,128)(2,1)S(1)}, u32[]{:S(2)}, u32[]{:S(2)}) collective-permute-start(bf16[2,384,384]{2,1,0:T(8,128)(2,1)S(1)} %pad_maximum_fusion), channel_id=1, source_target_pairs={{1,3},{3,5},{5,7},{7,9},{9,11},{11,13},{13,15},{2,0},{4,2},{6,4},{... | collective-permute-start | bytes 1769480 | tf_op jit(solution)/shard_map/ppermute | solution.py:81
  20.0 0.8 fusion.85
  20.8 0.3 fusion.51
  21.2 1.9 %collective-permute-start.4 = (bf16[768,64]{0,1:T(8,128)(2,1)S(1)}, bf16[768,64]{0,1:T(8,128)(2,1)S(1)}, u32[]{:S(2)}, u32[]{:S(2)}) collective-permute-start(bf16[768,64]{0,1:T(8,128)(2,1)S(1)} %fusion.35), channel_id=1, source_target_pairs={{1,5},{3,7},{5,9},{7,11},{9,13},{11,15},{4,0},{6,2},{8,4},{10,6},{... | collective-permute-start | bytes 294920 | tf_op jit(solution)/shard_map/ppermute | solution.py:99
  23.1 6.2 %collective-permute-done.1 = bf16[2,384,384]{2,1,0:T(8,128)(2,1)S(1)} collective-permute-done((bf16[2,384,384]{2,1,0:T(8,128)(2,1)S(1)}, bf16[2,384,384]{2,1,0:T(8,128)(2,1)S(1)}, u32[]{:S(2)}, u32[]{:S(2)}) %collective-permute-start.1) | collective-permute-done | bytes 589856 | tf_op jit(solution)/shard_map/ppermute | solution.py:81
  29.4 0.8 convolution_bitcast_fusion
  30.1 0.1 fusion.82
  30.3 0.1 fusion.29
  30.4 2.3 %collective-permute-done.4 = bf16[768,64]{0,1:T(8,128)(2,1)S(1)} collective-permute-done((bf16[768,64]{0,1:T(8,128)(2,1)S(1)}, bf16[768,64]{0,1:T(8,128)(2,1)S(1)}, u32[]{:S(2)}, u32[]{:S(2)}) %collective-permute-start.4) | collective-permute-done | bytes 98336 | tf_op jit(solution)/shard_map/ppermute | solution.py:99
  32.6 0.5 fusion.6
  33.2 2.1 %collective-permute-start.5 = (bf16[768,64]{0,1:T(8,128)(2,1)S(1)}, bf16[768,64]{0,1:T(8,128)(2,1)S(1)}, u32[]{:S(2)}, u32[]{:S(2)}) collective-permute-start(bf16[768,64]{0,1:T(8,128)(2,1)S(1)} %fusion.6), channel_id=1, source_target_pairs={{1,5},{3,7},{5,9},{7,11},{9,13},{11,15},{4,0},{6,2},{8,4},{10,6},{... | collective-permute-start | bytes 294920 | tf_op jit(solution)/shard_map/ppermute | solution.py:99
  35.2 6.7 %collective-permute-done.5 = bf16[768,64]{0,1:T(8,128)(2,1)S(1)} collective-permute-done((bf16[768,64]{0,1:T(8,128)(2,1)S(1)}, bf16[768,64]{0,1:T(8,128)(2,1)S(1)}, u32[]{:S(2)}, u32[]{:S(2)}) %collective-permute-start.5) | collective-permute-done | bytes 98336 | tf_op jit(solution)/shard_map/ppermute | solution.py:99
  41.9 0.5 fusion.7
  42.4 1.9 %collective-permute-start.6 = (bf16[768,64]{0,1:T(8,128)(2,1)S(1)}, bf16[768,64]{0,1:T(8,128)(2,1)S(1)}, u32[]{:S(2)}, u32[]{:S(2)}) collective-permute-start(bf16[768,64]{0,1:T(8,128)(2,1)S(1)} %fusion.7), channel_id=1, source_target_pairs={{1,5},{3,7},{5,9},{7,11},{9,13},{11,15},{4,0},{6,2},{8,4},{10,6},{... | collective-permute-start | bytes 294920 | tf_op jit(solution)/shard_map/ppermute | solution.py:99
  44.4 0.0 copy-start.12
  44.4 6.7 %collective-permute-done.6 = bf16[768,64]{0,1:T(8,128)(2,1)S(1)} collective-permute-done((bf16[768,64]{0,1:T(8,128)(2,1)S(1)}, bf16[768,64]{0,1:T(8,128)(2,1)S(1)}, u32[]{:S(2)}, u32[]{:S(2)}) %collective-permute-start.6) | collective-permute-done | bytes 98336 | tf_op jit(solution)/shard_map/ppermute | solution.py:99
  51.0 0.5 fusion.8
  51.6 1.9 %collective-permute-start.7 = (bf16[384,128]{0,1:T(8,128)(2,1)S(1)}, bf16[384,128]{0,1:T(8,128)(2,1)S(1)}, u32[]{:S(2)}, u32[]{:S(2)}) collective-permute-start(bf16[384,128]{0,1:T(8,128)(2,1)S(1)} %pad_maximum_fusion.2), channel_id=1, source_target_pairs={{1,2},{3,4},{5,6},{7,8},{9,10},{11,12},{13,14},{2,1},{4,3},{6,5},{... | collective-permute-start | bytes 294920 | tf_op jit(solution)/shard_map/ppermute | solution.py:105
  53.5 4.0 %collective-permute-done.7 = bf16[384,128]{0,1:T(8,128)(2,1)S(1)} collective-permute-done((bf16[384,128]{0,1:T(8,128)(2,1)S(1)}, bf16[384,128]{0,1:T(8,128)(2,1)S(1)}, u32[]{:S(2)}, u32[]{:S(2)}) %collective-permute-start.7) | collective-permute-done | bytes 98336 | tf_op jit(solution)/shard_map/ppermute | solution.py:105
  57.5 0.3 convolution_bitcast_fusion.1
  57.8 0.3 convolution_bitcast_fusion.2
  58.2 2.8 %fusion.1 = f32[128,8192]{1,0:T(8,128)S(1)} fusion(s32[8192]{0:T(1024)S(1)} %broadcast_subtract_fusion, f32[384,64]{0,1:T(8,128)S(1)} %get-tuple-element.25, f32[384,64]{0,1:T(8,128)S(1)} %get-tuple-element.24, bf16[1,1,384,128]{2,3,1,0:T(8,128)(2,1)S(1)} %copy-done.5, pred[]{:T(512)S(6)} %eq.61, bf16[384,64]{0,1:T(8,128)(2,1)S(1)} %get-tuple-element.33, ...), kind=kOutput, calls=%fused_computation.3 | convolution fusion | flops 808894464 | bytes 4620289 | tf_op jit(solution)/shard_map/ar,ap->rp/dot_general | solution.py:55
  61.0 3.2 %multiply_reduce_fusion = (f32[8192]{0:T(1024)S(1)}, f32[128,8192]{1,0:T(8,128)S(1)}) fusion(f32[128,8192]{1,0:T(8,128)S(1)} %fusion.1, s32[8192]{0:T(1024)S(1)} %broadcast_subtract_fusion.1, f32[384,64]{0,1:T(8,128)S(1)} %get-tuple-element.23, f32[384,64]{0,1:T(8,128)S(1)} %get-tuple-element.22, bf16[1,1,384,128]{2,3,1,0:T(8,128)(2,1)S(1)} %copy-done.3, ...), kind=kOutput, calls=%fused_computation.6 | convolution fusion | flops 810983424 | bytes 8847361 | tf_op jit(solution)/shard_map/ar,ap->rp/dot_general | solution.py:55
  64.1 0.0 copy-start.13
  64.1 0.0 copy-start.10
  64.2 0.9 fusion.4
  65.0 0.1 maximum_multiply_fusion
  65.1 0.1 copy.33
  65.2 18.2 %collective-permute-start.10 = (bf16[1,2,8192]{2,0,1:T(2,128)(2,1)S(1)}, bf16[1,2,8192]{2,0,1:T(2,128)(2,1)S(1)}, u32[]{:S(2)}, u32[]{:S(2)}) collective-permute-start(bf16[1,2,8192]{2,0,1:T(2,128)(2,1)S(1)} %copy.33), channel_id=1, source_target_pairs={{64,0},{80,16},{96,32},{112,48},{128,64},{144,80},{160,96},{176,11... | collective-permute-start | bytes 98312 | tf_op jit(solution)/shard_map/ppermute | solution.py:12
  83.3 3.7 %collective-permute-start.11 = (bf16[1,2,8192]{2,0,1:T(2,128)(2,1)S(1)}, bf16[1,2,8192]{2,0,1:T(2,128)(2,1)S(1)}, u32[]{:S(2)}, u32[]{:S(2)}) collective-permute-start(bf16[1,2,8192]{2,0,1:T(2,128)(2,1)S(1)} %copy.33), channel_id=1, source_target_pairs={{48,0},{64,16},{80,32},{96,48},{112,64},{128,80},{144,96},{160,112... | collective-permute-start | bytes 98312 | tf_op jit(solution)/shard_map/ppermute | solution.py:12
  87.0 1.9 %collective-permute-start.12 = (bf16[1,2,8192]{2,0,1:T(2,128)(2,1)S(1)}, bf16[1,2,8192]{2,0,1:T(2,128)(2,1)S(1)}, u32[]{:S(2)}, u32[]{:S(2)}) collective-permute-start(bf16[1,2,8192]{2,0,1:T(2,128)(2,1)S(1)} %copy.33), channel_id=1, source_target_pairs={{32,0},{48,16},{64,32},{80,48},{96,64},{112,80},{128,96},{144,112}... | collective-permute-start | bytes 98312 | tf_op jit(solution)/shard_map/ppermute | solution.py:12
  89.0 2.5 %collective-permute-start.13 = (bf16[1,2,8192]{2,0,1:T(2,128)(2,1)S(1)}, bf16[1,2,8192]{2,0,1:T(2,128)(2,1)S(1)}, u32[]{:S(2)}, u32[]{:S(2)}) collective-permute-start(bf16[1,2,8192]{2,0,1:T(2,128)(2,1)S(1)} %copy.33), channel_id=1, source_target_pairs={{16,0},{32,16},{48,32},{64,48},{80,64},{96,80},{112,96},{128,112},... | collective-permute-start | bytes 98312 | tf_op jit(solution)/shard_map/ppermute | solution.py:12
  91.5 3.4 %collective-permute-start.14 = (bf16[1,2,8192]{2,0,1:T(2,128)(2,1)S(1)}, bf16[1,2,8192]{2,0,1:T(2,128)(2,1)S(1)}, u32[]{:S(2)}, u32[]{:S(2)}) collective-permute-start(bf16[1,2,8192]{2,0,1:T(2,128)(2,1)S(1)} %copy.33), channel_id=1, source_target_pairs={{0,16},{16,32},{32,48},{48,64},{64,80},{80,96},{96,112},{112,128},... | collective-permute-start | bytes 98312 | tf_op jit(solution)/shard_map/ppermute | solution.py:12
  94.8 4.8 %collective-permute-start.15 = (bf16[1,2,8192]{2,0,1:T(2,128)(2,1)S(1)}, bf16[1,2,8192]{2,0,1:T(2,128)(2,1)S(1)}, u32[]{:S(2)}, u32[]{:S(2)}) collective-permute-start(bf16[1,2,8192]{2,0,1:T(2,128)(2,1)S(1)} %copy.33), channel_id=1, source_target_pairs={{0,32},{16,48},{32,64},{48,80},{64,96},{80,112},{96,128},{112,144}... | collective-permute-start | bytes 98312 | tf_op jit(solution)/shard_map/ppermute | solution.py:12
  99.7 0.0 collective-permute-done.11
  99.7 5.2 %collective-permute-start.16 = (bf16[1,2,8192]{2,0,1:T(2,128)(2,1)S(1)}, bf16[1,2,8192]{2,0,1:T(2,128)(2,1)S(1)}, u32[]{:S(2)}, u32[]{:S(2)}) collective-permute-start(bf16[1,2,8192]{2,0,1:T(2,128)(2,1)S(1)} %copy.33), channel_id=1, source_target_pairs={{0,48},{16,64},{32,80},{48,96},{64,112},{80,128},{96,144},{112,160... | collective-permute-start | bytes 98312 | tf_op jit(solution)/shard_map/ppermute | solution.py:12
  104.9 1.1 select_reduce_fusion.12
  106.0 5.9 %collective-permute-start.17 = (bf16[1,2,8192]{2,0,1:T(2,128)(2,1)S(1)}, bf16[1,2,8192]{2,0,1:T(2,128)(2,1)S(1)}, u32[]{:S(2)}, u32[]{:S(2)}) collective-permute-start(bf16[1,2,8192]{2,0,1:T(2,128)(2,1)S(1)} %copy.33), channel_id=1, source_target_pairs={{0,64},{16,80},{32,96},{48,112},{64,128},{80,144},{96,160},{112,17... | collective-permute-start | bytes 98312 | tf_op jit(solution)/shard_map/ppermute | solution.py:12
  111.9 1.9 %collective-permute-start.18 = (bf16[1,2,8192]{2,0,1:T(2,128)(2,1)S(1)}, bf16[1,2,8192]{2,0,1:T(2,128)(2,1)S(1)}, u32[]{:S(2)}, u32[]{:S(2)}) collective-permute-start(bf16[1,2,8192]{2,0,1:T(2,128)(2,1)S(1)} %copy.33), channel_id=1, source_target_pairs={{0,80},{16,96},{32,112},{48,128},{64,144},{80,160},{96,176},{112,1... | collective-permute-start | bytes 98312 | tf_op jit(solution)/shard_map/ppermute | solution.py:12
  113.8 10.5 %collective-permute-start.19 = (bf16[1,2,8192]{2,0,1:T(2,128)(2,1)S(1)}, bf16[1,2,8192]{2,0,1:T(2,128)(2,1)S(1)}, u32[]{:S(2)}, u32[]{:S(2)}) collective-permute-start(bf16[1,2,8192]{2,0,1:T(2,128)(2,1)S(1)} %copy.33), channel_id=1, source_target_pairs={{0,96},{16,112},{32,128},{48,144},{64,160},{80,176},{96,192},{112,... | collective-permute-start | bytes 98312 | tf_op jit(solution)/shard_map/ppermute | solution.py:12
  124.3 3.7 %collective-permute-start.8 = (bf16[1,2,8192]{2,0,1:T(2,128)(2,1)S(1)}, bf16[1,2,8192]{2,0,1:T(2,128)(2,1)S(1)}, u32[]{:S(2)}, u32[]{:S(2)}) collective-permute-start(bf16[1,2,8192]{2,0,1:T(2,128)(2,1)S(1)} %copy.33), channel_id=1, source_target_pairs={{96,0},{112,16},{128,32},{144,48},{160,64},{176,80},{192,96},{208,... | collective-permute-start | bytes 98312 | tf_op jit(solution)/shard_map/ppermute | solution.py:12
  128.1 8.2 %collective-permute-start.9 = (bf16[1,2,8192]{2,0,1:T(2,128)(2,1)S(1)}, bf16[1,2,8192]{2,0,1:T(2,128)(2,1)S(1)}, u32[]{:S(2)}, u32[]{:S(2)}) collective-permute-start(bf16[1,2,8192]{2,0,1:T(2,128)(2,1)S(1)} %copy.33), channel_id=1, source_target_pairs={{80,0},{96,16},{112,32},{128,48},{144,64},{160,80},{176,96},{192,1... | collective-permute-start | bytes 98312 | tf_op jit(solution)/shard_map/ppermute | solution.py:12
  136.3 0.5 collective-permute-done.19
  136.8 2.0 %collective-permute-done.8 = bf16[1,2,8192]{2,0,1:T(2,128)(2,1)S(1)} collective-permute-done((bf16[1,2,8192]{2,0,1:T(2,128)(2,1)S(1)}, bf16[1,2,8192]{2,0,1:T(2,128)(2,1)S(1)}, u32[]{:S(2)}, u32[]{:S(2)}) %collective-permute-start.8) | collective-permute-done | bytes 32800 | tf_op jit(solution)/shard_map/ppermute | solution.py:12
  138.8 6.7 %collective-permute-done.9 = bf16[1,2,8192]{2,0,1:T(2,128)(2,1)S(1)} collective-permute-done((bf16[1,2,8192]{2,0,1:T(2,128)(2,1)S(1)}, bf16[1,2,8192]{2,0,1:T(2,128)(2,1)S(1)}, u32[]{:S(2)}, u32[]{:S(2)}) %collective-permute-start.9) | collective-permute-done | bytes 32800 | tf_op jit(solution)/shard_map/ppermute | solution.py:12
  145.6 1.3 fusion.64
  (46 shorter events, 0.4 us)
Async XLA Ops:
  1.0 8.4 %copy-start.4 = (bf16[1,1,384,128]{2,3,1,0:T(8,128)(2,1)}, bf16[1,1,384,128]{2,3,1,0:T(8,128)(2,1)S(1)}, u32[]{:S(2)}) copy-start(bf16[1,1,384,128]{2,3,1,0:T(8,128)(2,1)S(1)} %copy.18) | copy-start | bytes 294916
  2.1 8.1 %copy-start.2 = (bf16[1,1,384,128]{2,3,1,0:T(8,128)(2,1)}, bf16[1,1,384,128]{2,3,1,0:T(8,128)(2,1)S(1)}, u32[]{:S(2)}) copy-start(bf16[1,1,384,128]{2,3,1,0:T(8,128)(2,1)S(1)} %copy.19) | copy-start | bytes 294916
  2.1 10.5 %copy-start = (bf16[1,1,2,384,384]{4,3,2,1,0:T(8,128)(2,1)S(1)}, bf16[1,1,2,384,384]{4,3,2,1,0:T(8,128)(2,1)}, u32[]{:S(2)}) copy-start(bf16[1,1,2,384,384]{4,3,2,1,0:T(8,128)(2,1)} %param.7) | copy-start | bytes 1769476
  2.1 4.5 %collective-permute-start.2 = (bf16[384,128]{0,1:T(8,128)(2,1)S(1)}, bf16[384,128]{0,1:T(8,128)(2,1)S(1)}, u32[]{:S(2)}, u32[]{:S(2)}) collective-permute-start(bf16[384,128]{0,1:T(8,128)(2,1)S(1)} %select_bitcast_fusion), channel_id=1, source_target_pairs={{0,1},{1,0},{2,3},{3,2},{4,5},{5,4},{6,7},{7,6},{8,9},{9,8},{10,11... | collective-permute-start | bytes 294920 | tf_op jit(solution)/shard_map/ppermute | solution.py:64
  4.2 8.4 %collective-permute-start = (bf16[2,384,384]{2,1,0:T(8,128)(2,1)}, bf16[2,384,384]{2,1,0:T(8,128)(2,1)S(1)}, u32[]{:S(2)}, u32[]{:S(2)}) collective-permute-start(bf16[2,384,384]{2,1,0:T(8,128)(2,1)} %bitcast.171), channel_id=1, source_target_pairs={{0,1},{1,0},{2,3},{3,2},{4,5},{5,4},{6,7},{7,6},{8,9},{9,8},{10,11... | collective-permute-start | bytes 1769480 | tf_op jit(solution)/shard_map/ppermute | solution.py:64
  9.5 3.0 %copy-start.6 = (bf16[384,64]{0,1:T(8,128)(2,1)}, bf16[384,64]{0,1:T(8,128)(2,1)S(1)}, u32[]{:S(2)}) copy-start(bf16[384,64]{0,1:T(8,128)(2,1)S(1)} %get-tuple-element.36) | copy-start | bytes 147460
  9.5 3.0 %copy-start.8 = (bf16[384,64]{0,1:T(8,128)(2,1)}, bf16[384,64]{0,1:T(8,128)(2,1)S(1)}, u32[]{:S(2)}) copy-start(bf16[384,64]{0,1:T(8,128)(2,1)S(1)} %get-tuple-element.37) | copy-start | bytes 147460
  10.2 9.8 %collective-permute-start.3 = (bf16[768,64]{0,1:T(8,128)(2,1)}, bf16[768,64]{0,1:T(8,128)(2,1)}, u32[]{:S(2)}, u32[]{:S(2)}) collective-permute-start(bf16[768,64]{0,1:T(8,128)(2,1)} %pad_maximum_fusion.1), channel_id=1, source_target_pairs={{1,3},{3,5},{5,7},{7,9},{9,11},{11,13},{13,15},{2,0},{4,2},{6,4},{... | collective-permute-start | bytes 294920 | tf_op jit(solution)/shard_map/ppermute | solution.py:81
  15.4 2.0 %copy-start.1 = (f32[2,384,2,384]{1,3,0,2:T(8,128)S(1)}, f32[2,384,2,384]{1,3,0,2:T(8,128)}, u32[]{:S(2)}) copy-start(f32[2,384,2,384]{1,3,0,2:T(8,128)} %copy.9) | copy-start | bytes 7077892
  17.4 3.8 %copy-start.7 = (bf16[384,64]{0,1:T(8,128)(2,1)S(1)}, bf16[384,64]{0,1:T(8,128)(2,1)}, u32[]{:S(2)}) copy-start(bf16[384,64]{0,1:T(8,128)(2,1)} %copy-done.6) | copy-start | bytes 147460
  17.4 3.8 %copy-start.9 = (bf16[384,64]{0,1:T(8,128)(2,1)S(1)}, bf16[384,64]{0,1:T(8,128)(2,1)}, u32[]{:S(2)}) copy-start(bf16[384,64]{0,1:T(8,128)(2,1)} %copy-done.8) | copy-start | bytes 147460
  17.6 11.8 %collective-permute-start.1 = (bf16[2,384,384]{2,1,0:T(8,128)(2,1)S(1)}, bf16[2,384,384]{2,1,0:T(8,128)(2,1)S(1)}, u32[]{:S(2)}, u32[]{:S(2)}) collective-permute-start(bf16[2,384,384]{2,1,0:T(8,128)(2,1)S(1)} %pad_maximum_fusion), channel_id=1, source_target_pairs={{1,3},{3,5},{5,7},{7,9},{9,11},{11,13},{13,15},{2,0},{4,2},{6,4},{... | collective-permute-start | bytes 1769480 | tf_op jit(solution)/shard_map/ppermute | solution.py:81
  21.2 11.4 %collective-permute-start.4 = (bf16[768,64]{0,1:T(8,128)(2,1)S(1)}, bf16[768,64]{0,1:T(8,128)(2,1)S(1)}, u32[]{:S(2)}, u32[]{:S(2)}) collective-permute-start(bf16[768,64]{0,1:T(8,128)(2,1)S(1)} %fusion.35), channel_id=1, source_target_pairs={{1,5},{3,7},{5,9},{7,11},{9,13},{11,15},{4,0},{6,2},{8,4},{10,6},{... | collective-permute-start | bytes 294920 | tf_op jit(solution)/shard_map/ppermute | solution.py:99
  33.1 11.2 %copy-start.11 = (s32[8192]{0:T(1024)S(1)}, s32[8192]{0:T(1024)}, u32[]{:S(2)}) copy-start(s32[8192]{0:T(1024)} %param.11) | copy-start | bytes 98308
  33.2 8.8 %collective-permute-start.5 = (bf16[768,64]{0,1:T(8,128)(2,1)S(1)}, bf16[768,64]{0,1:T(8,128)(2,1)S(1)}, u32[]{:S(2)}, u32[]{:S(2)}) collective-permute-start(bf16[768,64]{0,1:T(8,128)(2,1)S(1)} %fusion.6), channel_id=1, source_target_pairs={{1,5},{3,7},{5,9},{7,11},{9,13},{11,15},{4,0},{6,2},{8,4},{10,6},{... | collective-permute-start | bytes 294920 | tf_op jit(solution)/shard_map/ppermute | solution.py:99
  42.4 8.6 %collective-permute-start.6 = (bf16[768,64]{0,1:T(8,128)(2,1)S(1)}, bf16[768,64]{0,1:T(8,128)(2,1)S(1)}, u32[]{:S(2)}, u32[]{:S(2)}) collective-permute-start(bf16[768,64]{0,1:T(8,128)(2,1)S(1)} %fusion.7), channel_id=1, source_target_pairs={{1,5},{3,7},{5,9},{7,11},{9,13},{11,15},{4,0},{6,2},{8,4},{10,6},{... | collective-permute-start | bytes 294920 | tf_op jit(solution)/shard_map/ppermute | solution.py:99
  44.4 9.1 %copy-start.12 = (s32[8192]{0:T(1024)S(1)}, s32[8192]{0:T(1024)}, u32[]{:S(2)}) copy-start(s32[8192]{0:T(1024)} %param.10) | copy-start | bytes 98308
  51.5 6.6 %copy-start.5 = (bf16[1,1,384,128]{2,3,1,0:T(8,128)(2,1)S(1)}, bf16[1,1,384,128]{2,3,1,0:T(8,128)(2,1)}, u32[]{:S(2)}) copy-start(bf16[1,1,384,128]{2,3,1,0:T(8,128)(2,1)} %copy-done.4) | copy-start | bytes 294916
  51.6 5.9 %collective-permute-start.7 = (bf16[384,128]{0,1:T(8,128)(2,1)S(1)}, bf16[384,128]{0,1:T(8,128)(2,1)S(1)}, u32[]{:S(2)}, u32[]{:S(2)}) collective-permute-start(bf16[384,128]{0,1:T(8,128)(2,1)S(1)} %pad_maximum_fusion.2), channel_id=1, source_target_pairs={{1,2},{3,4},{5,6},{7,8},{9,10},{11,12},{13,14},{2,1},{4,3},{6,5},{... | collective-permute-start | bytes 294920 | tf_op jit(solution)/shard_map/ppermute | solution.py:105
  58.2 2.8 %copy-start.3 = (bf16[1,1,384,128]{2,3,1,0:T(8,128)(2,1)S(1)}, bf16[1,1,384,128]{2,3,1,0:T(8,128)(2,1)}, u32[]{:S(2)}) copy-start(bf16[1,1,384,128]{2,3,1,0:T(8,128)(2,1)} %copy-done.2) | copy-start | bytes 294916
  64.1 22.9 %copy-start.13 = (s32[8]{0:T(128)S(1)}, s32[8]{0:T(128)}, u32[]{:S(2)}) copy-start(s32[8]{0:T(128)} %param.12) | copy-start | bytes 100
  64.1 40.7 %copy-start.10 = (f32[8,8192]{1,0:T(8,128)S(1)}, f32[8,8192]{1,0:T(8,128)}, u32[]{:S(2)}) copy-start(f32[8,8192]{1,0:T(8,128)} %param.13) | copy-start | bytes 786436
  65.2 29.7 %collective-permute-start.10 = (bf16[1,2,8192]{2,0,1:T(2,128)(2,1)S(1)}, bf16[1,2,8192]{2,0,1:T(2,128)(2,1)S(1)}, u32[]{:S(2)}, u32[]{:S(2)}) collective-permute-start(bf16[1,2,8192]{2,0,1:T(2,128)(2,1)S(1)} %copy.33), channel_id=1, source_target_pairs={{64,0},{80,16},{96,32},{112,48},{128,64},{144,80},{160,96},{176,11... | collective-permute-start | bytes 98312 | tf_op jit(solution)/shard_map/ppermute | solution.py:12
  83.3 16.3 %collective-permute-start.11 = (bf16[1,2,8192]{2,0,1:T(2,128)(2,1)S(1)}, bf16[1,2,8192]{2,0,1:T(2,128)(2,1)S(1)}, u32[]{:S(2)}, u32[]{:S(2)}) collective-permute-start(bf16[1,2,8192]{2,0,1:T(2,128)(2,1)S(1)} %copy.33), channel_id=1, source_target_pairs={{48,0},{64,16},{80,32},{96,48},{112,64},{128,80},{144,96},{160,112... | collective-permute-start | bytes 98312 | tf_op jit(solution)/shard_map/ppermute | solution.py:12
  87.0 19.0 %collective-permute-start.12 = (bf16[1,2,8192]{2,0,1:T(2,128)(2,1)S(1)}, bf16[1,2,8192]{2,0,1:T(2,128)(2,1)S(1)}, u32[]{:S(2)}, u32[]{:S(2)}) collective-permute-start(bf16[1,2,8192]{2,0,1:T(2,128)(2,1)S(1)} %copy.33), channel_id=1, source_target_pairs={{32,0},{48,16},{64,32},{80,48},{96,64},{112,80},{128,96},{144,112}... | collective-permute-start | bytes 98312 | tf_op jit(solution)/shard_map/ppermute | solution.py:12
  89.0 22.9 %collective-permute-start.13 = (bf16[1,2,8192]{2,0,1:T(2,128)(2,1)S(1)}, bf16[1,2,8192]{2,0,1:T(2,128)(2,1)S(1)}, u32[]{:S(2)}, u32[]{:S(2)}) collective-permute-start(bf16[1,2,8192]{2,0,1:T(2,128)(2,1)S(1)} %copy.33), channel_id=1, source_target_pairs={{16,0},{32,16},{48,32},{64,48},{80,64},{96,80},{112,96},{128,112},... | collective-permute-start | bytes 98312 | tf_op jit(solution)/shard_map/ppermute | solution.py:12
  91.5 22.4 %collective-permute-start.14 = (bf16[1,2,8192]{2,0,1:T(2,128)(2,1)S(1)}, bf16[1,2,8192]{2,0,1:T(2,128)(2,1)S(1)}, u32[]{:S(2)}, u32[]{:S(2)}) collective-permute-start(bf16[1,2,8192]{2,0,1:T(2,128)(2,1)S(1)} %copy.33), channel_id=1, source_target_pairs={{0,16},{16,32},{32,48},{48,64},{64,80},{80,96},{96,112},{112,128},... | collective-permute-start | bytes 98312 | tf_op jit(solution)/shard_map/ppermute | solution.py:12
  94.8 29.5 %collective-permute-start.15 = (bf16[1,2,8192]{2,0,1:T(2,128)(2,1)S(1)}, bf16[1,2,8192]{2,0,1:T(2,128)(2,1)S(1)}, u32[]{:S(2)}, u32[]{:S(2)}) collective-permute-start(bf16[1,2,8192]{2,0,1:T(2,128)(2,1)S(1)} %copy.33), channel_id=1, source_target_pairs={{0,32},{16,48},{32,64},{48,80},{64,96},{80,112},{96,128},{112,144}... | collective-permute-start | bytes 98312 | tf_op jit(solution)/shard_map/ppermute | solution.py:12
  99.7 28.4 %collective-permute-start.16 = (bf16[1,2,8192]{2,0,1:T(2,128)(2,1)S(1)}, bf16[1,2,8192]{2,0,1:T(2,128)(2,1)S(1)}, u32[]{:S(2)}, u32[]{:S(2)}) collective-permute-start(bf16[1,2,8192]{2,0,1:T(2,128)(2,1)S(1)} %copy.33), channel_id=1, source_target_pairs={{0,48},{16,64},{32,80},{48,96},{64,112},{80,128},{96,144},{112,160... | collective-permute-start | bytes 98312 | tf_op jit(solution)/shard_map/ppermute | solution.py:12
  106.0 30.3 %collective-permute-start.17 = (bf16[1,2,8192]{2,0,1:T(2,128)(2,1)S(1)}, bf16[1,2,8192]{2,0,1:T(2,128)(2,1)S(1)}, u32[]{:S(2)}, u32[]{:S(2)}) collective-permute-start(bf16[1,2,8192]{2,0,1:T(2,128)(2,1)S(1)} %copy.33), channel_id=1, source_target_pairs={{0,64},{16,80},{32,96},{48,112},{64,128},{80,144},{96,160},{112,17... | collective-permute-start | bytes 98312 | tf_op jit(solution)/shard_map/ppermute | solution.py:12
  111.9 24.4 %collective-permute-start.18 = (bf16[1,2,8192]{2,0,1:T(2,128)(2,1)S(1)}, bf16[1,2,8192]{2,0,1:T(2,128)(2,1)S(1)}, u32[]{:S(2)}, u32[]{:S(2)}) collective-permute-start(bf16[1,2,8192]{2,0,1:T(2,128)(2,1)S(1)} %copy.33), channel_id=1, source_target_pairs={{0,80},{16,96},{32,112},{48,128},{64,144},{80,160},{96,176},{112,1... | collective-permute-start | bytes 98312 | tf_op jit(solution)/shard_map/ppermute | solution.py:12
  113.8 22.9 %collective-permute-start.19 = (bf16[1,2,8192]{2,0,1:T(2,128)(2,1)S(1)}, bf16[1,2,8192]{2,0,1:T(2,128)(2,1)S(1)}, u32[]{:S(2)}, u32[]{:S(2)}) collective-permute-start(bf16[1,2,8192]{2,0,1:T(2,128)(2,1)S(1)} %copy.33), channel_id=1, source_target_pairs={{0,96},{16,112},{32,128},{48,144},{64,160},{80,176},{96,192},{112,... | collective-permute-start | bytes 98312 | tf_op jit(solution)/shard_map/ppermute | solution.py:12
  124.3 14.5 %collective-permute-start.8 = (bf16[1,2,8192]{2,0,1:T(2,128)(2,1)S(1)}, bf16[1,2,8192]{2,0,1:T(2,128)(2,1)S(1)}, u32[]{:S(2)}, u32[]{:S(2)}) collective-permute-start(bf16[1,2,8192]{2,0,1:T(2,128)(2,1)S(1)} %copy.33), channel_id=1, source_target_pairs={{96,0},{112,16},{128,32},{144,48},{160,64},{176,80},{192,96},{208,... | collective-permute-start | bytes 98312 | tf_op jit(solution)/shard_map/ppermute | solution.py:12
  128.1 17.5 %collective-permute-start.9 = (bf16[1,2,8192]{2,0,1:T(2,128)(2,1)S(1)}, bf16[1,2,8192]{2,0,1:T(2,128)(2,1)S(1)}, u32[]{:S(2)}, u32[]{:S(2)}) collective-permute-start(bf16[1,2,8192]{2,0,1:T(2,128)(2,1)S(1)} %copy.33), channel_id=1, source_target_pairs={{80,0},{96,16},{112,32},{128,48},{144,64},{160,80},{176,96},{192,1... | collective-permute-start | bytes 98312 | tf_op jit(solution)/shard_map/ppermute | solution.py:12

commit v8 on v6

--- a/solution.py
+++ b/solution.py
@@ -57,12 +57,22 @@
     )
 
 
+def packed(pair, columns):
+    return jnp.concatenate([pair[0], pair[1], columns], axis=1)
+
+
+def unpacked(joined_array):
+    width = joined_array.shape[0]
+    pair = jnp.stack([joined_array[:, :width], joined_array[:, width:2 * width]])
+    return pair, joined_array[:, 2 * width:]
+
+
 def sweeps(blocks, forward_src, backward_src):
     count = lax.axis_size("section")
     odd = lax.axis_index("section") % 2 == 1
     swap = [(2 * y + side, 2 * y + 1 - side) for y in range(count // 2) for side in (0, 1)]
-    other_blocks, other_src = lax.ppermute(
-        (blocks, jnp.where(odd, backward_src, forward_src)), "section", swap
+    other_blocks, other_src = unpacked(
+        lax.ppermute(packed(blocks, jnp.where(odd, backward_src, forward_src)), "section", swap)
     )
     left = jnp.where(odd, blocks, other_blocks)
     right = jnp.where(odd, other_blocks, blocks)
@@ -72,19 +82,22 @@
     imag_part = jnp.where(odd, forward_imag, backward_imag).astype(jnp.bfloat16)
     pair_forward = (complex_product(blocks, other_src, False) + forward_src).astype(jnp.bfloat16)
     pair_backward = (complex_product(blocks, other_src, True) + backward_src).astype(jnp.bfloat16)
-    chain_src = stacked(jnp.where(odd, pair_forward, pair_backward))
+    chain_src = jnp.where(odd, pair_forward, pair_backward)
     chips = count // 2
     chip = lax.axis_index("section") // 2
     chain = [(2 * y + 1, 2 * y + 3) for y in range(chips - 1)]
     chain += [(2 * y, 2 * y - 2) for y in range(1, chips)]
     own_map = jnp.stack([real_part, imag_part])
-    upstream_map, upstream_src = lax.ppermute((own_map, chain_src), "section", chain)
+    upstream_map, upstream_src = unpacked(
+        lax.ppermute(packed(own_map, chain_src), "section", chain)
+    )
     has_upstream = jnp.where(odd, chip >= 1, chip <= chips - 2)
     joint_real, joint_imag = matrix_product(own_map, upstream_map)
     joint_real = jnp.where(has_upstream, joint_real, real_part).astype(jnp.bfloat16)
     joint_imag = jnp.where(has_upstream, joint_imag, imag_part).astype(jnp.bfloat16)
-    joint_src = (stacked(complex_product(own_map, joined(upstream_src), False))
-                 + chain_src).astype(jnp.bfloat16)
+    joint_src = stacked(
+        (complex_product(own_map, upstream_src, False) + chain_src).astype(jnp.bfloat16)
+    )
     joint_map = jnp.concatenate(
         [
             jnp.concatenate([joint_real, -joint_imag], axis=1),

time: 127 us -> 138 us (1.087)
  the two profiles are of different devices: /device:TPU:18 before, /device:TPU:23 now
where the time goes in v8:
time: 138 us; the launch traced here: 137 us
  starting transfers between devices  77.9 us (56%)
  waiting for transfers between devices  31.8 us (23%)
  matrix products  12.4 us (9%)
  other arithmetic  7.15 us (5%)
  local copies, waits for them, and re-layouts  7.05 us (5%)
    ppermute x8, starting transfers between devices, passed_along(): lax.ppermute(value, axis, [(source, source + steps) for source in range(l...  44.6 us
    ppermute x3, starting transfers between devices, sweeps(): arrived = lax.ppermute(state, 'section', stride)  18.2 us
    ppermute x3, waiting for transfers between devices, sweeps(): arrived = lax.ppermute(state, 'section', stride)  10.2 us
    ppermute x1, starting transfers between devices, sweeps(): neighbour = lax.ppermute(state, 'section', hand_over)  9.22 us
    ppermute x8, waiting for transfers between devices, passed_along(): lax.ppermute(value, axis, [(source, source + steps) for source in range(l...  9.07 us
    ppermute x1, waiting for transfers between devices, sweeps(): lax.ppermute(packed(own_map, chain_src), 'section', chain)  8.73 us
    dot_general x2, matrix products, picked_rows(): jnp.einsum('ar,ap->rp', table, selector.astype(table.dtype), preferred_el...  5.92 us
    unnamed x21, local copies, waits for them, and re-layouts  4.72 us
  transfers between devices with their start and end apart: 14, of which 9 were waited for; matrix products, arithmetic and copies ran while one was open for 2% of the time, Pallas kernels for 0%

profile of v8, /device:TPU:23, one launch (start us, length us, event | category | flops | bytes accessed | tf_op | source)
XLA Modules:
  0.0 136.9 jit_solution(6225030177828765391)
XLA Ops:
  0.0 1.0 copy.10
  1.0 1.0 copy.11
  2.0 1.4 %copy.8 = bf16[1,1,2,384,384]{3,4,2,1,0:T(8,128)(2,1)S(1)} copy(bf16[1,1,2,384,384]{4,3,2,1,0:T(8,128)(2,1)} %param.7) | data formatting | bytes 1179648 | tf_op args[0]
  3.4 0.1 slice_bitcast_fusion.7
  3.5 0.1 pad_maximum_fusion
  3.6 2.6 %collective-permute-start = (bf16[384,896]{0,1:T(8,128)(2,1)S(1)}, bf16[384,896]{0,1:T(8,128)(2,1)S(1)}, u32[]{:S(2)}, u32[]{:S(2)}) collective-permute-start(bf16[384,896]{0,1:T(8,128)(2,1)S(1)} %pad_maximum_fusion), channel_id=1, source_target_pairs={{0,1},{1,0},{2,3},{3,2},{4,5},{5,4},{6,7},{7,6},{8,9},{9,8},{10,11... | collective-permute-start | bytes 2064392 | tf_op jit(solution)/shard_map/ppermute | solution.py:75
  6.2 1.7 %collective-permute-done = bf16[384,896]{0,1:T(8,128)(2,1)S(1)} collective-permute-done((bf16[384,896]{0,1:T(8,128)(2,1)S(1)}, bf16[384,896]{0,1:T(8,128)(2,1)S(1)}, u32[]{:S(2)}, u32[]{:S(2)}) %collective-permute-start) | collective-permute-done | bytes 688160 | tf_op jit(solution)/shard_map/ppermute | solution.py:75
  7.9 0.1 slice_bitcast_fusion.5
  8.0 0.8 copy-done.2
  8.8 0.8 fusion.25
  9.6 2.0 %copy.15 = f32[2,384,2,384]{1,3,0,2:T(8,128)} copy(f32[2,384,2,384]{3,1,2,0:T(8,128)S(1)} %fusion.25) | data formatting | bytes 4718592 | tf_op jit(solution)/shard_map/cij,djk->cdik/dot_general | solution.py:29
  11.5 1.5 %fusion.21 = bf16[1,1,384,384]{3,2,1,0:T(8,128)(2,1)S(1)} fusion(f32[2,2,384,384]{3,2,0,1:T(8,128)S(1)} %bitcast.250, f32[2,2,384,384]{3,2,1,0:T(8,128)} %bitcast.252, pred[]{:T(512)S(6)} %eq.61), kind=kLoop, calls=%fused_computation.42 | loop fusion | flops 589824 | bytes 2654209 | tf_op jit(solution)/shard_map/convert_element_type | solution.py:81
  13.0 0.5 copy-done.1
  13.6 0.1 fusion.17
  13.7 1.3 convolution_bitcast_fusion.3
  15.0 1.2 convolution_bitcast_fusion.4
  16.2 0.3 fusion.47
  16.5 0.2 fusion.53
  16.7 0.1 pad_maximum_fusion.1
  16.8 3.2 %collective-permute-start.1 = (bf16[384,896]{1,0:T(8,128)(2,1)S(1)}, bf16[384,896]{1,0:T(8,128)(2,1)S(1)}, u32[]{:S(2)}, u32[]{:S(2)}) collective-permute-start(bf16[384,896]{1,0:T(8,128)(2,1)S(1)} %pad_maximum_fusion.1), channel_id=1, source_target_pairs={{1,3},{3,5},{5,7},{7,9},{9,11},{11,13},{13,15},{2,0},{4,2},{6,4},{... | collective-permute-start | bytes 2064392 | tf_op jit(solution)/shard_map/ppermute | solution.py:92
  20.0 8.7 %collective-permute-done.1 = bf16[384,896]{1,0:T(8,128)(2,1)S(1)} collective-permute-done((bf16[384,896]{1,0:T(8,128)(2,1)S(1)}, bf16[384,896]{1,0:T(8,128)(2,1)S(1)}, u32[]{:S(2)}, u32[]{:S(2)}) %collective-permute-start.1) | collective-permute-done | bytes 688160 | tf_op jit(solution)/shard_map/ppermute | solution.py:92
  28.8 0.3 fusion.35
  29.1 0.2 fusion.45
  29.2 0.1 fusion.50
  29.4 0.1 fusion.98
  29.5 6.4 %collective-permute-start.2 = (bf16[768,64]{1,0:T(8,128)(2,1)S(1)}, bf16[768,64]{1,0:T(8,128)(2,1)S(1)}, u32[]{:S(2)}, u32[]{:S(2)}) collective-permute-start(bf16[768,64]{1,0:T(8,128)(2,1)S(1)} %pad_maximum_fusion.7), channel_id=1, source_target_pairs={{1,5},{3,7},{5,9},{7,11},{9,13},{11,15},{4,0},{6,2},{8,4},{10,6},{... | collective-permute-start | bytes 294920 | tf_op jit(solution)/shard_map/ppermute | solution.py:112
  35.9 0.1 slice_bitcast_fusion.3
  36.0 0.8 convolution_bitcast_fusion
  36.8 0.1 fusion.95
  36.9 0.1 fusion.14
  37.0 3.4 %collective-permute-done.2 = bf16[768,64]{1,0:T(8,128)(2,1)S(1)} collective-permute-done((bf16[768,64]{1,0:T(8,128)(2,1)S(1)}, bf16[768,64]{1,0:T(8,128)(2,1)S(1)}, u32[]{:S(2)}, u32[]{:S(2)}) %collective-permute-start.2) | collective-permute-done | bytes 98336 | tf_op jit(solution)/shard_map/ppermute | solution.py:112
  40.3 0.5 fusion.6
  40.8 5.9 %collective-permute-start.3 = (bf16[768,64]{1,0:T(8,128)(2,1)S(1)}, bf16[768,64]{1,0:T(8,128)(2,1)S(1)}, u32[]{:S(2)}, u32[]{:S(2)}) collective-permute-start(bf16[768,64]{1,0:T(8,128)(2,1)S(1)} %fusion.6), channel_id=1, source_target_pairs={{1,5},{3,7},{5,9},{7,11},{9,13},{11,15},{4,0},{6,2},{8,4},{10,6},{... | collective-permute-start | bytes 294920 | tf_op jit(solution)/shard_map/ppermute | solution.py:112
  46.8 3.3 %collective-permute-done.3 = bf16[768,64]{1,0:T(8,128)(2,1)S(1)} collective-permute-done((bf16[768,64]{1,0:T(8,128)(2,1)S(1)}, bf16[768,64]{1,0:T(8,128)(2,1)S(1)}, u32[]{:S(2)}, u32[]{:S(2)}) %collective-permute-start.3) | collective-permute-done | bytes 98336 | tf_op jit(solution)/shard_map/ppermute | solution.py:112
  50.0 0.5 fusion.7
  50.5 5.9 %collective-permute-start.4 = (bf16[768,64]{1,0:T(8,128)(2,1)S(1)}, bf16[768,64]{1,0:T(8,128)(2,1)S(1)}, u32[]{:S(2)}, u32[]{:S(2)}) collective-permute-start(bf16[768,64]{1,0:T(8,128)(2,1)S(1)} %fusion.7), channel_id=1, source_target_pairs={{1,5},{3,7},{5,9},{7,11},{9,13},{11,15},{4,0},{6,2},{8,4},{10,6},{... | collective-permute-start | bytes 294920 | tf_op jit(solution)/shard_map/ppermute | solution.py:112
  56.5 3.6 %collective-permute-done.4 = bf16[768,64]{1,0:T(8,128)(2,1)S(1)} collective-permute-done((bf16[768,64]{1,0:T(8,128)(2,1)S(1)}, bf16[768,64]{1,0:T(8,128)(2,1)S(1)}, u32[]{:S(2)}, u32[]{:S(2)}) %collective-permute-start.4) | collective-permute-done | bytes 98336 | tf_op jit(solution)/shard_map/ppermute | solution.py:112
  60.1 0.5 fusion.8
  60.6 0.1 pad_maximum_fusion.8
  60.7 9.2 %collective-permute-start.5 = (bf16[384,128]{1,0:T(8,128)(2,1)S(1)}, bf16[384,128]{1,0:T(8,128)(2,1)S(1)}, u32[]{:S(2)}, u32[]{:S(2)}) collective-permute-start(bf16[384,128]{1,0:T(8,128)(2,1)S(1)} %pad_maximum_fusion.8), channel_id=1, source_target_pairs={{1,2},{3,4},{5,6},{7,8},{9,10},{11,12},{13,14},{2,1},{4,3},{6,5},{... | collective-permute-start | bytes 294920 | tf_op jit(solution)/shard_map/ppermute | solution.py:118
  69.9 2.1 %collective-permute-done.5 = bf16[384,128]{1,0:T(8,128)(2,1)S(1)} collective-permute-done((bf16[384,128]{1,0:T(8,128)(2,1)S(1)}, bf16[384,128]{1,0:T(8,128)(2,1)S(1)}, u32[]{:S(2)}, u32[]{:S(2)}) %collective-permute-start.5) | collective-permute-done | bytes 98336 | tf_op jit(solution)/shard_map/ppermute | solution.py:118
  72.0 0.4 convolution_bitcast_fusion.1
  72.4 0.2 fusion.41
  72.5 0.3 convolution_bitcast_fusion.2
  72.9 0.2 fusion.43
  73.0 2.7 %fusion.1 = f32[128,8192]{1,0:T(8,128)S(1)} fusion(s32[8192]{0:T(1024)S(1)} %broadcast_subtract_fusion, bf16[384,128]{1,0:T(8,128)(2,1)S(1)} %pad_maximum_fusion.8, f32[384,64]{1,0:T(8,128)S(1)} %get-tuple-element.31, f32[384,64]{1,0:T(8,128)S(1)} %get-tuple-element.30, bf16[1,1,384,128]{3,2,1,0:T(8,128)(2,1)S(1)} %copy-done.4, pred[]{:T(512)S(6)} %eq.61), kind=kOutput, calls=%fused_computation.3 | convolution fusion | flops 808697856 | bytes 4620289 | tf_op jit(solution)/shard_map/ar,ap->rp/dot_general | solution.py:55
  75.8 3.2 %multiply_reduce_fusion = (f32[8192]{0:T(1024)S(1)}, f32[128,8192]{1,0:T(8,128)S(1)}) fusion(f32[128,8192]{1,0:T(8,128)S(1)} %fusion.1, s32[8192]{0:T(1024)S(1)} %broadcast_subtract_fusion.1, bf16[384,128]{1,0:T(8,128)(2,1)S(1)} %pad_maximum_fusion.8, f32[384,64]{1,0:T(8,128)S(1)} %get-tuple-element.29, f32[384,64]{1,0:T(8,128)S(1)} %get-tuple-element.28, ...), kind=kOutput, calls=%fused_computation.6 | convolution fusion | flops 810786816 | bytes 8847361 | tf_op jit(solution)/shard_map/ar,ap->rp/dot_general | solution.py:55
  79.0 0.9 fusion.4
  79.9 0.1 maximum_multiply_fusion
  79.9 0.1 copy.57
  80.0 4.0 %collective-permute-start.10 = (bf16[1,2,8192]{2,0,1:T(2,128)(2,1)S(1)}, bf16[1,2,8192]{2,0,1:T(2,128)(2,1)S(1)}, u32[]{:S(2)}, u32[]{:S(2)}) collective-permute-start(bf16[1,2,8192]{2,0,1:T(2,128)(2,1)S(1)} %copy.57), channel_id=1, source_target_pairs={{0,16},{16,32},{32,48},{48,64},{64,80},{80,96},{96,112},{112,128},... | collective-permute-start | bytes 98312 | tf_op jit(solution)/shard_map/ppermute | solution.py:12
  84.0 5.8 %collective-permute-start.11 = (bf16[1,2,8192]{2,0,1:T(2,128)(2,1)S(1)}, bf16[1,2,8192]{2,0,1:T(2,128)(2,1)S(1)}, u32[]{:S(2)}, u32[]{:S(2)}) collective-permute-start(bf16[1,2,8192]{2,0,1:T(2,128)(2,1)S(1)} %copy.57), channel_id=1, source_target_pairs={{0,32},{16,48},{32,64},{48,80},{64,96},{80,112},{96,128},{112,144}... | collective-permute-start | bytes 98312 | tf_op jit(solution)/shard_map/ppermute | solution.py:12
  89.8 12.2 %collective-permute-start.6 = (bf16[1,2,8192]{2,0,1:T(2,128)(2,1)S(1)}, bf16[1,2,8192]{2,0,1:T(2,128)(2,1)S(1)}, u32[]{:S(2)}, u32[]{:S(2)}) collective-permute-start(bf16[1,2,8192]{2,0,1:T(2,128)(2,1)S(1)} %copy.57), channel_id=1, source_target_pairs={{16,0},{32,16},{48,32},{64,48},{80,64},{96,80},{112,96},{128,112},... | collective-permute-start | bytes 98312 | tf_op jit(solution)/shard_map/ppermute | solution.py:12
  102.0 4.3 %collective-permute-start.7 = (bf16[1,2,8192]{2,0,1:T(2,128)(2,1)S(1)}, bf16[1,2,8192]{2,0,1:T(2,128)(2,1)S(1)}, u32[]{:S(2)}, u32[]{:S(2)}) collective-permute-start(bf16[1,2,8192]{2,0,1:T(2,128)(2,1)S(1)} %copy.57), channel_id=1, source_target_pairs={{32,0},{48,16},{64,32},{80,48},{96,64},{112,80},{128,96},{144,112}... | collective-permute-start | bytes 98312 | tf_op jit(solution)/shard_map/ppermute | solution.py:12
  106.3 1.1 select_reduce_fusion.12
  107.5 0.7 collective-permute-done.7
  108.2 0.5 pad_maximum_fusion.9
  108.7 1.9 %collective-permute-start.12 = (bf16[2,2,8192]{2,0,1:T(2,128)(2,1)S(1)}, bf16[2,2,8192]{2,0,1:T(2,128)(2,1)S(1)}, u32[]{:S(2)}, u32[]{:S(2)}) collective-permute-start(bf16[2,2,8192]{2,0,1:T(2,128)(2,1)S(1)} %get-tuple-element.44), channel_id=1, source_target_pairs={{0,48},{16,64},{32,80},{48,96},{64,112},{80,128},{96,144},{112,160... | collective-permute-start | bytes 196616 | tf_op jit(solution)/shard_map/ppermute | solution.py:12
  110.7 7.2 %collective-permute-start.13 = (bf16[2,2,8192]{2,0,1:T(2,128)(2,1)S(1)}, bf16[2,2,8192]{2,0,1:T(2,128)(2,1)S(1)}, u32[]{:S(2)}, u32[]{:S(2)}) collective-permute-start(bf16[2,2,8192]{2,0,1:T(2,128)(2,1)S(1)} %get-tuple-element.45), channel_id=1, source_target_pairs={{0,64},{16,80},{32,96},{48,112},{64,128},{80,144},{96,160},{112,17... | collective-permute-start | bytes 196616 | tf_op jit(solution)/shard_map/ppermute | solution.py:12
  117.9 3.3 %collective-permute-start.8 = (bf16[2,2,8192]{2,0,1:T(2,128)(2,1)S(1)}, bf16[2,2,8192]{2,0,1:T(2,128)(2,1)S(1)}, u32[]{:S(2)}, u32[]{:S(2)}) collective-permute-start(bf16[2,2,8192]{2,0,1:T(2,128)(2,1)S(1)} %get-tuple-element.42), channel_id=1, source_target_pairs={{64,0},{80,16},{96,32},{112,48},{128,64},{144,80},{160,96},{176,11... | collective-permute-start | bytes 196616 | tf_op jit(solution)/shard_map/ppermute | solution.py:12
  121.2 5.9 %collective-permute-start.9 = (bf16[2,2,8192]{2,0,1:T(2,128)(2,1)S(1)}, bf16[2,2,8192]{2,0,1:T(2,128)(2,1)S(1)}, u32[]{:S(2)}, u32[]{:S(2)}) collective-permute-start(bf16[2,2,8192]{2,0,1:T(2,128)(2,1)S(1)} %get-tuple-element.43), channel_id=1, source_target_pairs={{48,0},{64,16},{80,32},{96,48},{112,64},{128,80},{144,96},{160,112... | collective-permute-start | bytes 196616 | tf_op jit(solution)/shard_map/ppermute | solution.py:12
  127.2 5.1 %collective-permute-done.8 = bf16[2,2,8192]{2,0,1:T(2,128)(2,1)S(1)} collective-permute-done((bf16[2,2,8192]{2,0,1:T(2,128)(2,1)S(1)}, bf16[2,2,8192]{2,0,1:T(2,128)(2,1)S(1)}, u32[]{:S(2)}, u32[]{:S(2)}) %collective-permute-start.8) | collective-permute-done | bytes 65568 | tf_op jit(solution)/shard_map/ppermute | solution.py:12
  132.3 3.2 %collective-permute-done.9 = bf16[2,2,8192]{2,0,1:T(2,128)(2,1)S(1)} collective-permute-done((bf16[2,2,8192]{2,0,1:T(2,128)(2,1)S(1)}, bf16[2,2,8192]{2,0,1:T(2,128)(2,1)S(1)}, u32[]{:S(2)}, u32[]{:S(2)}) %collective-permute-start.9) | collective-permute-done | bytes 65568 | tf_op jit(solution)/shard_map/ppermute | solution.py:12
  135.5 1.3 fusion.64
  (29 shorter events, 0.2 us)
Async XLA Ops:
  3.6 4.3 %collective-permute-start = (bf16[384,896]{0,1:T(8,128)(2,1)S(1)}, bf16[384,896]{0,1:T(8,128)(2,1)S(1)}, u32[]{:S(2)}, u32[]{:S(2)}) collective-permute-start(bf16[384,896]{0,1:T(8,128)(2,1)S(1)} %pad_maximum_fusion), channel_id=1, source_target_pairs={{0,1},{1,0},{2,3},{3,2},{4,5},{5,4},{6,7},{7,6},{8,9},{9,8},{10,11... | collective-permute-start | bytes 2064392 | tf_op jit(solution)/shard_map/ppermute | solution.py:75
  7.9 0.8 copy-start.2
  11.5 2.0 %copy-start.1 = (f32[2,384,2,384]{1,3,0,2:T(8,128)S(1)}, f32[2,384,2,384]{1,3,0,2:T(8,128)}, u32[]{:S(2)}) copy-start(f32[2,384,2,384]{1,3,0,2:T(8,128)} %copy.15) | copy-start | bytes 7077892
  11.5 2.1 %copy-start = (bf16[1,1,2,384,384]{4,3,2,1,0:T(8,128)(2,1)S(1)}, bf16[1,1,2,384,384]{4,3,2,1,0:T(8,128)(2,1)}, u32[]{:S(2)}) copy-start(bf16[1,1,2,384,384]{4,3,2,1,0:T(8,128)(2,1)} %param.7) | copy-start | bytes 1769476
  13.7 2.8 %copy-start.3 = (bf16[1,1,384,128]{3,2,1,0:T(8,128)(2,1)S(1)}, bf16[1,1,384,128]{3,2,1,0:T(8,128)(2,1)}, u32[]{:S(2)}) copy-start(bf16[1,1,384,128]{3,2,1,0:T(8,128)(2,1)} %param.8) | copy-start | bytes 294916
  13.7 2.8 %copy-start.4 = (bf16[1,1,384,128]{3,2,1,0:T(8,128)(2,1)S(1)}, bf16[1,1,384,128]{3,2,1,0:T(8,128)(2,1)}, u32[]{:S(2)}) copy-start(bf16[1,1,384,128]{3,2,1,0:T(8,128)(2,1)} %param.9) | copy-start | bytes 294916
  16.8 12.0 %collective-permute-start.1 = (bf16[384,896]{1,0:T(8,128)(2,1)S(1)}, bf16[384,896]{1,0:T(8,128)(2,1)S(1)}, u32[]{:S(2)}, u32[]{:S(2)}) collective-permute-start(bf16[384,896]{1,0:T(8,128)(2,1)S(1)} %pad_maximum_fusion.1), channel_id=1, source_target_pairs={{1,3},{3,5},{5,7},{7,9},{9,11},{11,13},{13,15},{2,0},{4,2},{6,4},{... | collective-permute-start | bytes 2064392 | tf_op jit(solution)/shard_map/ppermute | solution.py:92
  29.5 10.8 %collective-permute-start.2 = (bf16[768,64]{1,0:T(8,128)(2,1)S(1)}, bf16[768,64]{1,0:T(8,128)(2,1)S(1)}, u32[]{:S(2)}, u32[]{:S(2)}) collective-permute-start(bf16[768,64]{1,0:T(8,128)(2,1)S(1)} %pad_maximum_fusion.7), channel_id=1, source_target_pairs={{1,5},{3,7},{5,9},{7,11},{9,13},{11,15},{4,0},{6,2},{8,4},{10,6},{... | collective-permute-start | bytes 294920 | tf_op jit(solution)/shard_map/ppermute | solution.py:112
  40.3 6.4 %copy-start.6 = (s32[8192]{0:T(1024)S(1)}, s32[8192]{0:T(1024)}, u32[]{:S(2)}) copy-start(s32[8192]{0:T(1024)} %param.11) | copy-start | bytes 98308
  40.8 9.2 %collective-permute-start.3 = (bf16[768,64]{1,0:T(8,128)(2,1)S(1)}, bf16[768,64]{1,0:T(8,128)(2,1)S(1)}, u32[]{:S(2)}, u32[]{:S(2)}) collective-permute-start(bf16[768,64]{1,0:T(8,128)(2,1)S(1)} %fusion.6), channel_id=1, source_target_pairs={{1,5},{3,7},{5,9},{7,11},{9,13},{11,15},{4,0},{6,2},{8,4},{10,6},{... | collective-permute-start | bytes 294920 | tf_op jit(solution)/shard_map/ppermute | solution.py:112
  46.8 9.7 %copy-start.7 = (s32[8192]{0:T(1024)S(1)}, s32[8192]{0:T(1024)}, u32[]{:S(2)}) copy-start(s32[8192]{0:T(1024)} %param.10) | copy-start | bytes 98308
  50.5 9.5 %collective-permute-start.4 = (bf16[768,64]{1,0:T(8,128)(2,1)S(1)}, bf16[768,64]{1,0:T(8,128)(2,1)S(1)}, u32[]{:S(2)}, u32[]{:S(2)}) collective-permute-start(bf16[768,64]{1,0:T(8,128)(2,1)S(1)} %fusion.7), channel_id=1, source_target_pairs={{1,5},{3,7},{5,9},{7,11},{9,13},{11,15},{4,0},{6,2},{8,4},{10,6},{... | collective-permute-start | bytes 294920 | tf_op jit(solution)/shard_map/ppermute | solution.py:112
  56.5 13.4 %copy-start.8 = (s32[8]{0:T(128)S(1)}, s32[8]{0:T(128)}, u32[]{:S(2)}) copy-start(s32[8]{0:T(128)} %param.12) | copy-start | bytes 100
  60.7 11.3 %collective-permute-start.5 = (bf16[384,128]{1,0:T(8,128)(2,1)S(1)}, bf16[384,128]{1,0:T(8,128)(2,1)S(1)}, u32[]{:S(2)}, u32[]{:S(2)}) collective-permute-start(bf16[384,128]{1,0:T(8,128)(2,1)S(1)} %pad_maximum_fusion.8), channel_id=1, source_target_pairs={{1,2},{3,4},{5,6},{7,8},{9,10},{11,12},{13,14},{2,1},{4,3},{6,5},{... | collective-permute-start | bytes 294920 | tf_op jit(solution)/shard_map/ppermute | solution.py:118
  79.0 27.3 %copy-start.5 = (f32[8,8192]{1,0:T(8,128)S(1)}, f32[8,8192]{1,0:T(8,128)}, u32[]{:S(2)}) copy-start(f32[8,8192]{1,0:T(8,128)} %param.13) | copy-start | bytes 786436
  80.0 27.4 %collective-permute-start.10 = (bf16[1,2,8192]{2,0,1:T(2,128)(2,1)S(1)}, bf16[1,2,8192]{2,0,1:T(2,128)(2,1)S(1)}, u32[]{:S(2)}, u32[]{:S(2)}) collective-permute-start(bf16[1,2,8192]{2,0,1:T(2,128)(2,1)S(1)} %copy.57), channel_id=1, source_target_pairs={{0,16},{16,32},{32,48},{48,64},{64,80},{80,96},{96,112},{112,128},... | collective-permute-start | bytes 98312 | tf_op jit(solution)/shard_map/ppermute | solution.py:12
  84.0 23.5 %collective-permute-start.11 = (bf16[1,2,8192]{2,0,1:T(2,128)(2,1)S(1)}, bf16[1,2,8192]{2,0,1:T(2,128)(2,1)S(1)}, u32[]{:S(2)}, u32[]{:S(2)}) collective-permute-start(bf16[1,2,8192]{2,0,1:T(2,128)(2,1)S(1)} %copy.57), channel_id=1, source_target_pairs={{0,32},{16,48},{32,64},{48,80},{64,96},{80,112},{96,128},{112,144}... | collective-permute-start | bytes 98312 | tf_op jit(solution)/shard_map/ppermute | solution.py:12
  89.8 17.7 %collective-permute-start.6 = (bf16[1,2,8192]{2,0,1:T(2,128)(2,1)S(1)}, bf16[1,2,8192]{2,0,1:T(2,128)(2,1)S(1)}, u32[]{:S(2)}, u32[]{:S(2)}) collective-permute-start(bf16[1,2,8192]{2,0,1:T(2,128)(2,1)S(1)} %copy.57), channel_id=1, source_target_pairs={{16,0},{32,16},{48,32},{64,48},{80,64},{96,80},{112,96},{128,112},... | collective-permute-start | bytes 98312 | tf_op jit(solution)/shard_map/ppermute | solution.py:12
  102.0 6.2 %collective-permute-start.7 = (bf16[1,2,8192]{2,0,1:T(2,128)(2,1)S(1)}, bf16[1,2,8192]{2,0,1:T(2,128)(2,1)S(1)}, u32[]{:S(2)}, u32[]{:S(2)}) collective-permute-start(bf16[1,2,8192]{2,0,1:T(2,128)(2,1)S(1)} %copy.57), channel_id=1, source_target_pairs={{32,0},{48,16},{64,32},{80,48},{96,64},{112,80},{128,96},{144,112}... | collective-permute-start | bytes 98312 | tf_op jit(solution)/shard_map/ppermute | solution.py:12
  108.7 18.4 %collective-permute-start.12 = (bf16[2,2,8192]{2,0,1:T(2,128)(2,1)S(1)}, bf16[2,2,8192]{2,0,1:T(2,128)(2,1)S(1)}, u32[]{:S(2)}, u32[]{:S(2)}) collective-permute-start(bf16[2,2,8192]{2,0,1:T(2,128)(2,1)S(1)} %get-tuple-element.44), channel_id=1, source_target_pairs={{0,48},{16,64},{32,80},{48,96},{64,112},{80,128},{96,144},{112,160... | collective-permute-start | bytes 196616 | tf_op jit(solution)/shard_map/ppermute | solution.py:12
  110.7 16.5 %collective-permute-start.13 = (bf16[2,2,8192]{2,0,1:T(2,128)(2,1)S(1)}, bf16[2,2,8192]{2,0,1:T(2,128)(2,1)S(1)}, u32[]{:S(2)}, u32[]{:S(2)}) collective-permute-start(bf16[2,2,8192]{2,0,1:T(2,128)(2,1)S(1)} %get-tuple-element.45), channel_id=1, source_target_pairs={{0,64},{16,80},{32,96},{48,112},{64,128},{80,144},{96,160},{112,17... | collective-permute-start | bytes 196616 | tf_op jit(solution)/shard_map/ppermute | solution.py:12
  117.9 14.5 %collective-permute-start.8 = (bf16[2,2,8192]{2,0,1:T(2,128)(2,1)S(1)}, bf16[2,2,8192]{2,0,1:T(2,128)(2,1)S(1)}, u32[]{:S(2)}, u32[]{:S(2)}) collective-permute-start(bf16[2,2,8192]{2,0,1:T(2,128)(2,1)S(1)} %get-tuple-element.42), channel_id=1, source_target_pairs={{64,0},{80,16},{96,32},{112,48},{128,64},{144,80},{160,96},{176,11... | collective-permute-start | bytes 196616 | tf_op jit(solution)/shard_map/ppermute | solution.py:12
  121.2 14.3 %collective-permute-start.9 = (bf16[2,2,8192]{2,0,1:T(2,128)(2,1)S(1)}, bf16[2,2,8192]{2,0,1:T(2,128)(2,1)S(1)}, u32[]{:S(2)}, u32[]{:S(2)}) collective-permute-start(bf16[2,2,8192]{2,0,1:T(2,128)(2,1)S(1)} %get-tuple-element.43), channel_id=1, source_target_pairs={{48,0},{64,16},{80,32},{96,48},{112,64},{128,80},{144,96},{160,112... | collective-permute-start | bytes 196616 | tf_op jit(solution)/shard_map/ppermute | solution.py:12

commit v9 on v6

--- a/solution.py
+++ b/solution.py
@@ -103,13 +103,12 @@
     hand_over = [(s, s + 1) for s in range(1, count - 1, 2)]
     hand_over += [(s, s - 1) for s in range(2, count, 2)]
     neighbour = lax.ppermute(state, "section", hand_over)
-    fields = jnp.where(
-        odd, state, (complex_product(blocks, neighbour, False) + forward_src).astype(jnp.bfloat16)
+    other = jnp.where(
+        odd,
+        (complex_product(blocks, neighbour, True) + backward_src).astype(jnp.bfloat16),
+        (complex_product(blocks, neighbour, False) + forward_src).astype(jnp.bfloat16),
     )
-    adjoints = jnp.where(
-        odd, (complex_product(blocks, neighbour, True) + backward_src).astype(jnp.bfloat16), state
-    )
-    return fields, adjoints
+    return state, other
 
 
 SHIFT_ROUNDS = (((1, (0,)), (2, (0,))), ((3, (0, 1)), (4, (1, 2))))
@@ -133,15 +132,18 @@
 ):
     orbitals = propagator.shape[3]
     modes = forward_source.shape[3] // 2
-    fields, adjoints = sweeps(propagator[0, 0], forward_source[0, 0], backward_source[0, 0])
-
+    own, other = sweeps(propagator[0, 0], forward_source[0, 0], backward_source[0, 0])
+    odd = lax.axis_index("section") % 2 == 1
     section_base = lax.axis_index("section") * orbitals
-    left_rows = picked_rows(fields, left_orbital - section_base)
-    right_rows = picked_rows(adjoints, right_orbital - section_base)
-    real_part = jnp.sum(left_rows * right_rows, axis=0)
-    imag_part = jnp.sum(left_rows[modes:] * right_rows[:modes], axis=0) - jnp.sum(
-        left_rows[:modes] * right_rows[modes:], axis=0
+    left_local = left_orbital - section_base
+    right_local = right_orbital - section_base
+    own_rows = picked_rows(own, jnp.where(odd, left_local, right_local))
+    other_rows = picked_rows(other, jnp.where(odd, right_local, left_local))
+    real_part = jnp.sum(own_rows * other_rows, axis=0)
+    swapped_imag = jnp.sum(own_rows[modes:] * other_rows[:modes], axis=0) - jnp.sum(
+        own_rows[:modes] * other_rows[modes:], axis=0
     )
+    imag_part = jnp.where(odd, swapped_imag, -swapped_imag)
     lesser_part = jnp.stack([real_part, imag_part]) * modes ** (-0.5)
 
     sent = lesser_part.astype(jnp.bfloat16)

time: 127 us -> 127 us (level)
  no operation moved by 1% of the time
where the time goes in v9:
time: 127 us; the launch traced here: 126 us
  starting transfers between devices  61.7 us (49%)
  waiting for transfers between devices  38.9 us (31%)
  matrix products  12.5 us (10%)
  other arithmetic  6.75 us (5%)
  local copies, waits for them, and re-layouts  5.52 us (4%)
    ppermute x8, starting transfers between devices, passed_along(): lax.ppermute(value, axis, [(source, source + steps) for source in range(l...  44.6 us
    ppermute x3, waiting for transfers between devices, sweeps(): arrived = lax.ppermute(state, 'section', stride)  15.6 us
    ppermute x8, waiting for transfers between devices, passed_along(): lax.ppermute(value, axis, [(source, source + steps) for source in range(l...  13 us
    ppermute x2, waiting for transfers between devices, sweeps(): lax.ppermute((own_map, chain_src), 'section', chain)  6.23 us
    ppermute x3, starting transfers between devices, sweeps(): arrived = lax.ppermute(state, 'section', stride)  5.89 us
    dot_general x2, matrix products, picked_rows(): jnp.einsum('ar,ap->rp', table, selector.astype(table.dtype), preferred_el...  5.76 us
    ppermute x2, starting transfers between devices, sweeps(): lax.ppermute((own_map, chain_src), 'section', chain)  4.7 us
    ppermute x2, starting transfers between devices, sweeps(): lax.ppermute((blocks, jnp.where(odd, backward_src, forward_src)), 'sectio...  4.46 us
  transfers between devices with their start and end apart: 16, of which 8 were waited for; matrix products, arithmetic and copies ran while one was open for 9% of the time, Pallas kernels for 0%

profile of v9, /device:TPU:18, one launch (start us, length us, event | category | flops | bytes accessed | tf_op | source)
XLA Modules:
  0.0 125.9 jit_solution(5390149762138560503)
XLA Ops:
  0.0 1.0 copy.18
  1.0 1.0 copy.19
  2.1 0.0 copy-start
  2.1 2.1 %collective-permute-start.2 = (bf16[384,128]{0,1:T(8,128)(2,1)S(1)}, bf16[384,128]{0,1:T(8,128)(2,1)S(1)}, u32[]{:S(2)}, u32[]{:S(2)}) collective-permute-start(bf16[384,128]{0,1:T(8,128)(2,1)S(1)} %select_bitcast_fusion), channel_id=1, source_target_pairs={{0,1},{1,0},{2,3},{3,2},{4,5},{5,4},{6,7},{7,6},{8,9},{9,8},{10,11... | collective-permute-start | bytes 294920 | tf_op jit(solution)/shard_map/ppermute | solution.py:64
  4.2 2.4 %collective-permute-start = (bf16[2,384,384]{2,1,0:T(8,128)(2,1)}, bf16[2,384,384]{2,1,0:T(8,128)(2,1)S(1)}, u32[]{:S(2)}, u32[]{:S(2)}) collective-permute-start(bf16[2,384,384]{2,1,0:T(8,128)(2,1)} %bitcast.239), channel_id=1, source_target_pairs={{0,1},{1,0},{2,3},{3,2},{4,5},{5,4},{6,7},{7,6},{8,9},{9,8},{10,11... | collective-permute-start | bytes 1769480 | tf_op jit(solution)/shard_map/ppermute | solution.py:64
  6.6 0.0 collective-permute-done.2
  6.6 1.3 %convolution_bitcast_fusion.3 = f32[2,384,128]{1,2,0:T(8,128)S(1)} fusion(bf16[384,128]{0,1:T(8,128)(2,1)S(1)} %collective-permute-done.2, bf16[1,1,2,384,384]{4,3,2,1,0:T(8,128)(2,1)} %param.7), kind=kOutput, calls=%fused_computation.14 | convolution fusion | flops 75497472 | bytes 1081344 | tf_op jit(solution)/shard_map/cji,jn->cin/dot_general | solution.py:18
  8.0 1.4 %convolution_bitcast_fusion.4 = f32[2,384,128]{1,2,0:T(8,128)S(1)} fusion(bf16[384,128]{0,1:T(8,128)(2,1)S(1)} %collective-permute-done.2, bf16[1,1,2,384,384]{4,3,2,1,0:T(8,128)(2,1)} %param.7), kind=kOutput, calls=%fused_computation.15 | convolution fusion | flops 75497472 | bytes 1081344 | tf_op jit(solution)/shard_map/cij,jn->cin/dot_general | solution.py:22
  9.5 0.0 copy-start.8
  9.5 0.7 pad_maximum_fusion.1
  10.1 2.3 %collective-permute-start.3 = (bf16[768,64]{0,1:T(8,128)(2,1)}, bf16[768,64]{0,1:T(8,128)(2,1)}, u32[]{:S(2)}, u32[]{:S(2)}) collective-permute-start(bf16[768,64]{0,1:T(8,128)(2,1)} %pad_maximum_fusion.1), channel_id=1, source_target_pairs={{1,3},{3,5},{5,7},{7,9},{9,11},{11,13},{13,15},{2,0},{4,2},{6,4},{... | collective-permute-start | bytes 294920 | tf_op jit(solution)/shard_map/ppermute | solution.py:81
  12.5 0.0 collective-permute-done
  12.5 0.8 fusion.21
  13.4 2.0 %copy.9 = f32[2,384,2,384]{1,3,0,2:T(8,128)} copy(f32[2,384,2,384]{3,1,2,0:T(8,128)S(1)} %fusion.21) | data formatting | bytes 4718592 | tf_op jit(solution)/shard_map/cij,djk->cdik/dot_general | solution.py:29
  15.4 1.5 %fusion.20 = bf16[1,1,384,384]{3,2,1,0:T(8,128)(2,1)S(1)} fusion(f32[2,2,384,384]{3,2,0,1:T(8,128)S(1)} %bitcast.237, f32[2,2,384,384]{3,2,1,0:T(8,128)} %bitcast.240, pred[]{:T(512)S(6)} %eq.63), kind=kLoop, calls=%fused_computation.39 | loop fusion | flops 589824 | bytes 2654209 | tf_op jit(solution)/shard_map/convert_element_type | solution.py:71
  16.9 0.5 copy-done.1
  17.4 0.1 fusion.16
  17.5 0.1 pad_maximum_fusion
  17.6 2.4 %collective-permute-start.1 = (bf16[2,384,384]{2,1,0:T(8,128)(2,1)S(1)}, bf16[2,384,384]{2,1,0:T(8,128)(2,1)S(1)}, u32[]{:S(2)}, u32[]{:S(2)}) collective-permute-start(bf16[2,384,384]{2,1,0:T(8,128)(2,1)S(1)} %pad_maximum_fusion), channel_id=1, source_target_pairs={{1,3},{3,5},{5,7},{7,9},{9,11},{11,13},{13,15},{2,0},{4,2},{6,4},{... | collective-permute-start | bytes 1769480 | tf_op jit(solution)/shard_map/ppermute | solution.py:81
  19.9 0.0 collective-permute-done.3
  20.0 0.8 fusion.99
  20.8 0.3 fusion.50
  21.2 1.9 %collective-permute-start.4 = (bf16[768,64]{0,1:T(8,128)(2,1)S(1)}, bf16[768,64]{0,1:T(8,128)(2,1)S(1)}, u32[]{:S(2)}, u32[]{:S(2)}) collective-permute-start(bf16[768,64]{0,1:T(8,128)(2,1)S(1)} %fusion.35), channel_id=1, source_target_pairs={{1,5},{3,7},{5,9},{7,11},{9,13},{11,15},{4,0},{6,2},{8,4},{10,6},{... | collective-permute-start | bytes 294920 | tf_op jit(solution)/shard_map/ppermute | solution.py:99
  23.1 6.2 %collective-permute-done.1 = bf16[2,384,384]{2,1,0:T(8,128)(2,1)S(1)} collective-permute-done((bf16[2,384,384]{2,1,0:T(8,128)(2,1)S(1)}, bf16[2,384,384]{2,1,0:T(8,128)(2,1)S(1)}, u32[]{:S(2)}, u32[]{:S(2)}) %collective-permute-start.1) | collective-permute-done | bytes 589856 | tf_op jit(solution)/shard_map/ppermute | solution.py:81
  29.4 0.8 convolution_bitcast_fusion
  30.1 0.1 fusion.96
  30.3 0.1 fusion.29
  30.3 2.3 %collective-permute-done.4 = bf16[768,64]{0,1:T(8,128)(2,1)S(1)} collective-permute-done((bf16[768,64]{0,1:T(8,128)(2,1)S(1)}, bf16[768,64]{0,1:T(8,128)(2,1)S(1)}, u32[]{:S(2)}, u32[]{:S(2)}) %collective-permute-start.4) | collective-permute-done | bytes 98336 | tf_op jit(solution)/shard_map/ppermute | solution.py:99
  32.6 0.5 fusion.6
  33.2 0.0 copy-start.12
  33.2 2.1 %collective-permute-start.5 = (bf16[768,64]{0,1:T(8,128)(2,1)S(1)}, bf16[768,64]{0,1:T(8,128)(2,1)S(1)}, u32[]{:S(2)}, u32[]{:S(2)}) collective-permute-start(bf16[768,64]{0,1:T(8,128)(2,1)S(1)} %fusion.6), channel_id=1, source_target_pairs={{1,5},{3,7},{5,9},{7,11},{9,13},{11,15},{4,0},{6,2},{8,4},{10,6},{... | collective-permute-start | bytes 294920 | tf_op jit(solution)/shard_map/ppermute | solution.py:99
  35.2 6.7 %collective-permute-done.5 = bf16[768,64]{0,1:T(8,128)(2,1)S(1)} collective-permute-done((bf16[768,64]{0,1:T(8,128)(2,1)S(1)}, bf16[768,64]{0,1:T(8,128)(2,1)S(1)}, u32[]{:S(2)}, u32[]{:S(2)}) %collective-permute-start.5) | collective-permute-done | bytes 98336 | tf_op jit(solution)/shard_map/ppermute | solution.py:99
  41.9 0.5 fusion.7
  42.4 1.9 %collective-permute-start.6 = (bf16[768,64]{0,1:T(8,128)(2,1)S(1)}, bf16[768,64]{0,1:T(8,128)(2,1)S(1)}, u32[]{:S(2)}, u32[]{:S(2)}) collective-permute-start(bf16[768,64]{0,1:T(8,128)(2,1)S(1)} %fusion.7), channel_id=1, source_target_pairs={{1,5},{3,7},{5,9},{7,11},{9,13},{11,15},{4,0},{6,2},{8,4},{10,6},{... | collective-permute-start | bytes 294920 | tf_op jit(solution)/shard_map/ppermute | solution.py:99
  44.4 0.0 copy-start.13
  44.4 6.6 %collective-permute-done.6 = bf16[768,64]{0,1:T(8,128)(2,1)S(1)} collective-permute-done((bf16[768,64]{0,1:T(8,128)(2,1)S(1)}, bf16[768,64]{0,1:T(8,128)(2,1)S(1)}, u32[]{:S(2)}, u32[]{:S(2)}) %collective-permute-start.6) | collective-permute-done | bytes 98336 | tf_op jit(solution)/shard_map/ppermute | solution.py:99
  51.0 0.5 fusion.8
  51.6 2.1 %collective-permute-start.7 = (bf16[384,128]{0,1:T(8,128)(2,1)S(1)}, bf16[384,128]{0,1:T(8,128)(2,1)S(1)}, u32[]{:S(2)}, u32[]{:S(2)}) collective-permute-start(bf16[384,128]{0,1:T(8,128)(2,1)S(1)} %pad_maximum_fusion.2), channel_id=1, source_target_pairs={{1,2},{3,4},{5,6},{7,8},{9,10},{11,12},{13,14},{2,1},{4,3},{6,5},{... | collective-permute-start | bytes 294920 | tf_op jit(solution)/shard_map/ppermute | solution.py:105
  53.7 4.0 %collective-permute-done.7 = bf16[384,128]{0,1:T(8,128)(2,1)S(1)} collective-permute-done((bf16[384,128]{0,1:T(8,128)(2,1)S(1)}, bf16[384,128]{0,1:T(8,128)(2,1)S(1)}, u32[]{:S(2)}, u32[]{:S(2)}) %collective-permute-start.7) | collective-permute-done | bytes 98336 | tf_op jit(solution)/shard_map/ppermute | solution.py:105
  57.7 0.3 convolution_bitcast_fusion.2
  58.0 0.3 convolution_bitcast_fusion.1
  58.3 2.8 %fusion.1 = f32[128,8192]{1,0:T(8,128)S(1)} fusion(s32[8192]{0:T(1024)S(1)} %get-tuple-element.43, f32[384,64]{0,1:T(8,128)S(1)} %get-tuple-element.25, f32[384,64]{0,1:T(8,128)S(1)} %get-tuple-element.24, f32[384,64]{0,1:T(8,128)S(1)} %get-tuple-element.23, f32[384,64]{0,1:T(8,128)S(1)} %get-tuple-element.22, bf16[1,1,384,128]{2,3,1,0:T(8,128)(2,1)S(1)} %copy-done.5, ...), kind=kOutput, calls=%fused_computation.3 | convolution fusion | flops 808894464 | bytes 4816897 | tf_op jit(solution)/shard_map/ar,ap->rp/dot_general | solution.py:55
  61.1 3.0 %multiply_reduce_fusion = (f32[8192]{0:T(1024)S(1)}, f32[128,8192]{1,0:T(8,128)S(1)}) fusion(f32[128,8192]{1,0:T(8,128)S(1)} %fusion.1, s32[8192]{0:T(1024)S(1)} %get-tuple-element.42, bf16[384,64]{0,1:T(8,128)(2,1)S(1)} %get-tuple-element.33, bf16[384,64]{0,1:T(8,128)(2,1)S(1)} %get-tuple-element.32), kind=kOutput, calls=%fused_computation.6 | convolution fusion | flops 810737664 | bytes 8552448 | tf_op jit(solution)/shard_map/ar,ap->rp/dot_general | solution.py:55
  64.1 0.0 copy-start.10
  64.1 0.9 fusion.4
  65.0 0.1 maximum_multiply_fusion
  65.1 0.1 copy.33
  65.2 4.3 %collective-permute-start.12 = (bf16[1,2,8192]{2,0,1:T(2,128)(2,1)S(1)}, bf16[1,2,8192]{2,0,1:T(2,128)(2,1)S(1)}, u32[]{:S(2)}, u32[]{:S(2)}) collective-permute-start(bf16[1,2,8192]{2,0,1:T(2,128)(2,1)S(1)} %copy.33), channel_id=1, source_target_pairs={{0,16},{16,32},{32,48},{48,64},{64,80},{80,96},{96,112},{112,128},... | collective-permute-start | bytes 98312 | tf_op jit(solution)/shard_map/ppermute | solution.py:12
  69.5 6.1 %collective-permute-start.13 = (bf16[1,2,8192]{2,0,1:T(2,128)(2,1)S(1)}, bf16[1,2,8192]{2,0,1:T(2,128)(2,1)S(1)}, u32[]{:S(2)}, u32[]{:S(2)}) collective-permute-start(bf16[1,2,8192]{2,0,1:T(2,128)(2,1)S(1)} %copy.33), channel_id=1, source_target_pairs={{0,32},{16,48},{32,64},{48,80},{64,96},{80,112},{96,128},{112,144}... | collective-permute-start | bytes 98312 | tf_op jit(solution)/shard_map/ppermute | solution.py:12
  75.6 11.7 %collective-permute-start.8 = (bf16[1,2,8192]{2,0,1:T(2,128)(2,1)S(1)}, bf16[1,2,8192]{2,0,1:T(2,128)(2,1)S(1)}, u32[]{:S(2)}, u32[]{:S(2)}) collective-permute-start(bf16[1,2,8192]{2,0,1:T(2,128)(2,1)S(1)} %copy.33), channel_id=1, source_target_pairs={{16,0},{32,16},{48,32},{64,48},{80,64},{96,80},{112,96},{128,112},... | collective-permute-start | bytes 98312 | tf_op jit(solution)/shard_map/ppermute | solution.py:12
  87.2 5.0 %collective-permute-start.9 = (bf16[1,2,8192]{2,0,1:T(2,128)(2,1)S(1)}, bf16[1,2,8192]{2,0,1:T(2,128)(2,1)S(1)}, u32[]{:S(2)}, u32[]{:S(2)}) collective-permute-start(bf16[1,2,8192]{2,0,1:T(2,128)(2,1)S(1)} %copy.33), channel_id=1, source_target_pairs={{32,0},{48,16},{64,32},{80,48},{96,64},{112,80},{128,96},{144,112}... | collective-permute-start | bytes 98312 | tf_op jit(solution)/shard_map/ppermute | solution.py:12
  92.3 1.1 select_reduce_fusion.12
  93.4 0.0 collective-permute-done.12
  93.4 0.0 collective-permute-done.8
  93.4 1.3 %collective-permute-done.9 = bf16[1,2,8192]{2,0,1:T(2,128)(2,1)S(1)} collective-permute-done((bf16[1,2,8192]{2,0,1:T(2,128)(2,1)S(1)}, bf16[1,2,8192]{2,0,1:T(2,128)(2,1)S(1)}, u32[]{:S(2)}, u32[]{:S(2)}) %collective-permute-start.9) | collective-permute-done | bytes 32800 | tf_op jit(solution)/shard_map/ppermute | solution.py:12
  94.7 0.5 pad_maximum_fusion.3
  95.3 7.9 %collective-permute-start.10 = (bf16[2,2,8192]{2,0,1:T(2,128)(2,1)S(1)}, bf16[2,2,8192]{2,0,1:T(2,128)(2,1)S(1)}, u32[]{:S(2)}, u32[]{:S(2)}) collective-permute-start(bf16[2,2,8192]{2,0,1:T(2,128)(2,1)S(1)} %get-tuple-element.38), channel_id=1, source_target_pairs={{64,0},{80,16},{96,32},{112,48},{128,64},{144,80},{160,96},{176,11... | collective-permute-start | bytes 196616 | tf_op jit(solution)/shard_map/ppermute | solution.py:12
  103.2 1.9 %collective-permute-start.11 = (bf16[2,2,8192]{2,0,1:T(2,128)(2,1)S(1)}, bf16[2,2,8192]{2,0,1:T(2,128)(2,1)S(1)}, u32[]{:S(2)}, u32[]{:S(2)}) collective-permute-start(bf16[2,2,8192]{2,0,1:T(2,128)(2,1)S(1)} %get-tuple-element.39), channel_id=1, source_target_pairs={{48,0},{64,16},{80,32},{96,48},{112,64},{128,80},{144,96},{160,112... | collective-permute-start | bytes 196616 | tf_op jit(solution)/shard_map/ppermute | solution.py:12
  105.1 5.7 %collective-permute-start.14 = (bf16[2,2,8192]{2,0,1:T(2,128)(2,1)S(1)}, bf16[2,2,8192]{2,0,1:T(2,128)(2,1)S(1)}, u32[]{:S(2)}, u32[]{:S(2)}) collective-permute-start(bf16[2,2,8192]{2,0,1:T(2,128)(2,1)S(1)} %get-tuple-element.40), channel_id=1, source_target_pairs={{0,48},{16,64},{32,80},{48,96},{64,112},{80,128},{96,144},{112,160... | collective-permute-start | bytes 196616 | tf_op jit(solution)/shard_map/ppermute | solution.py:12
  110.8 2.0 %collective-permute-start.15 = (bf16[2,2,8192]{2,0,1:T(2,128)(2,1)S(1)}, bf16[2,2,8192]{2,0,1:T(2,128)(2,1)S(1)}, u32[]{:S(2)}, u32[]{:S(2)}) collective-permute-start(bf16[2,2,8192]{2,0,1:T(2,128)(2,1)S(1)} %get-tuple-element.41), channel_id=1, source_target_pairs={{0,64},{16,80},{32,96},{48,112},{64,128},{80,144},{96,160},{112,17... | collective-permute-start | bytes 196616 | tf_op jit(solution)/shard_map/ppermute | solution.py:12
  112.8 0.0 collective-permute-done.11
  112.8 3.3 %collective-permute-done.14 = bf16[2,2,8192]{2,0,1:T(2,128)(2,1)S(1)} collective-permute-done((bf16[2,2,8192]{2,0,1:T(2,128)(2,1)S(1)}, bf16[2,2,8192]{2,0,1:T(2,128)(2,1)S(1)}, u32[]{:S(2)}, u32[]{:S(2)}) %collective-permute-start.14) | collective-permute-done | bytes 65568 | tf_op jit(solution)/shard_map/ppermute | solution.py:12
  116.1 8.4 %collective-permute-done.15 = bf16[2,2,8192]{2,0,1:T(2,128)(2,1)S(1)} collective-permute-done((bf16[2,2,8192]{2,0,1:T(2,128)(2,1)S(1)}, bf16[2,2,8192]{2,0,1:T(2,128)(2,1)S(1)}, u32[]{:S(2)}, u32[]{:S(2)}) %collective-permute-start.15) | collective-permute-done | bytes 65568 | tf_op jit(solution)/shard_map/ppermute | solution.py:12
  124.5 1.3 %fusion.62 = f32[2,1,8192]{2,1,0:T(1,128)} fusion(bf16[2,2,8192]{2,0,1:T(2,128)(2,1)S(1)} %collective-permute-done.15, bf16[2,2,8192]{2,0,1:T(2,128)(2,1)S(1)} %collective-permute-done.14, bf16[1,2,8192]{2,0,1:T(2,128)(2,1)S(1)} %collective-permute-done.13, f32[1,1,8192]{2,1,0:T(1,128)S(1)} %fusion.88, f32[1,1,8192]{2,1,0:T(1,128)S(1)} %bitcast.249, ...), kind=kLoop, calls=%fused_computation.115 | loop fusion | flops 622592 | bytes 950272 | tf_op jit(solution)/shard_map/add | solution.py:158
  (39 shorter events, 0.4 us)
Async XLA Ops:
  1.0 8.4 %copy-start.2 = (bf16[1,1,384,128]{2,3,1,0:T(8,128)(2,1)}, bf16[1,1,384,128]{2,3,1,0:T(8,128)(2,1)S(1)}, u32[]{:S(2)}) copy-start(bf16[1,1,384,128]{2,3,1,0:T(8,128)(2,1)S(1)} %copy.18) | copy-start | bytes 294916
  2.1 8.1 %copy-start.4 = (bf16[1,1,384,128]{2,3,1,0:T(8,128)(2,1)}, bf16[1,1,384,128]{2,3,1,0:T(8,128)(2,1)S(1)}, u32[]{:S(2)}) copy-start(bf16[1,1,384,128]{2,3,1,0:T(8,128)(2,1)S(1)} %copy.19) | copy-start | bytes 294916
  2.1 10.5 %copy-start = (bf16[1,1,2,384,384]{4,3,2,1,0:T(8,128)(2,1)S(1)}, bf16[1,1,2,384,384]{4,3,2,1,0:T(8,128)(2,1)}, u32[]{:S(2)}) copy-start(bf16[1,1,2,384,384]{4,3,2,1,0:T(8,128)(2,1)} %param.7) | copy-start | bytes 1769476
  2.1 4.5 %collective-permute-start.2 = (bf16[384,128]{0,1:T(8,128)(2,1)S(1)}, bf16[384,128]{0,1:T(8,128)(2,1)S(1)}, u32[]{:S(2)}, u32[]{:S(2)}) collective-permute-start(bf16[384,128]{0,1:T(8,128)(2,1)S(1)} %select_bitcast_fusion), channel_id=1, source_target_pairs={{0,1},{1,0},{2,3},{3,2},{4,5},{5,4},{6,7},{7,6},{8,9},{9,8},{10,11... | collective-permute-start | bytes 294920 | tf_op jit(solution)/shard_map/ppermute | solution.py:64
  4.2 8.4 %collective-permute-start = (bf16[2,384,384]{2,1,0:T(8,128)(2,1)}, bf16[2,384,384]{2,1,0:T(8,128)(2,1)S(1)}, u32[]{:S(2)}, u32[]{:S(2)}) collective-permute-start(bf16[2,384,384]{2,1,0:T(8,128)(2,1)} %bitcast.239), channel_id=1, source_target_pairs={{0,1},{1,0},{2,3},{3,2},{4,5},{5,4},{6,7},{7,6},{8,9},{9,8},{10,11... | collective-permute-start | bytes 1769480 | tf_op jit(solution)/shard_map/ppermute | solution.py:64
  9.5 3.0 %copy-start.6 = (bf16[384,64]{0,1:T(8,128)(2,1)}, bf16[384,64]{0,1:T(8,128)(2,1)S(1)}, u32[]{:S(2)}) copy-start(bf16[384,64]{0,1:T(8,128)(2,1)S(1)} %get-tuple-element.36) | copy-start | bytes 147460
  9.5 3.0 %copy-start.8 = (bf16[384,64]{0,1:T(8,128)(2,1)}, bf16[384,64]{0,1:T(8,128)(2,1)S(1)}, u32[]{:S(2)}) copy-start(bf16[384,64]{0,1:T(8,128)(2,1)S(1)} %get-tuple-element.37) | copy-start | bytes 147460
  10.1 9.8 %collective-permute-start.3 = (bf16[768,64]{0,1:T(8,128)(2,1)}, bf16[768,64]{0,1:T(8,128)(2,1)}, u32[]{:S(2)}, u32[]{:S(2)}) collective-permute-start(bf16[768,64]{0,1:T(8,128)(2,1)} %pad_maximum_fusion.1), channel_id=1, source_target_pairs={{1,3},{3,5},{5,7},{7,9},{9,11},{11,13},{13,15},{2,0},{4,2},{6,4},{... | collective-permute-start | bytes 294920 | tf_op jit(solution)/shard_map/ppermute | solution.py:81
  15.4 2.0 %copy-start.1 = (f32[2,384,2,384]{1,3,0,2:T(8,128)S(1)}, f32[2,384,2,384]{1,3,0,2:T(8,128)}, u32[]{:S(2)}) copy-start(f32[2,384,2,384]{1,3,0,2:T(8,128)} %copy.9) | copy-start | bytes 7077892
  17.4 3.8 %copy-start.7 = (bf16[384,64]{0,1:T(8,128)(2,1)S(1)}, bf16[384,64]{0,1:T(8,128)(2,1)}, u32[]{:S(2)}) copy-start(bf16[384,64]{0,1:T(8,128)(2,1)} %copy-done.6) | copy-start | bytes 147460
  17.4 3.8 %copy-start.9 = (bf16[384,64]{0,1:T(8,128)(2,1)S(1)}, bf16[384,64]{0,1:T(8,128)(2,1)}, u32[]{:S(2)}) copy-start(bf16[384,64]{0,1:T(8,128)(2,1)} %copy-done.8) | copy-start | bytes 147460
  17.6 11.8 %collective-permute-start.1 = (bf16[2,384,384]{2,1,0:T(8,128)(2,1)S(1)}, bf16[2,384,384]{2,1,0:T(8,128)(2,1)S(1)}, u32[]{:S(2)}, u32[]{:S(2)}) collective-permute-start(bf16[2,384,384]{2,1,0:T(8,128)(2,1)S(1)} %pad_maximum_fusion), channel_id=1, source_target_pairs={{1,3},{3,5},{5,7},{7,9},{9,11},{11,13},{13,15},{2,0},{4,2},{6,4},{... | collective-permute-start | bytes 1769480 | tf_op jit(solution)/shard_map/ppermute | solution.py:81
  21.2 11.4 %collective-permute-start.4 = (bf16[768,64]{0,1:T(8,128)(2,1)S(1)}, bf16[768,64]{0,1:T(8,128)(2,1)S(1)}, u32[]{:S(2)}, u32[]{:S(2)}) collective-permute-start(bf16[768,64]{0,1:T(8,128)(2,1)S(1)} %fusion.35), channel_id=1, source_target_pairs={{1,5},{3,7},{5,9},{7,11},{9,13},{11,15},{4,0},{6,2},{8,4},{10,6},{... | collective-permute-start | bytes 294920 | tf_op jit(solution)/shard_map/ppermute | solution.py:99
  33.1 11.2 %copy-start.11 = (s32[8192]{0:T(1024)S(1)}, s32[8192]{0:T(1024)}, u32[]{:S(2)}) copy-start(s32[8192]{0:T(1024)} %param.11) | copy-start | bytes 98308
  33.2 11.2 %copy-start.12 = (s32[8192]{0:T(1024)S(1)}, s32[8192]{0:T(1024)}, u32[]{:S(2)}) copy-start(s32[8192]{0:T(1024)} %param.10) | copy-start | bytes 98308
  33.2 8.8 %collective-permute-start.5 = (bf16[768,64]{0,1:T(8,128)(2,1)S(1)}, bf16[768,64]{0,1:T(8,128)(2,1)S(1)}, u32[]{:S(2)}, u32[]{:S(2)}) collective-permute-start(bf16[768,64]{0,1:T(8,128)(2,1)S(1)} %fusion.6), channel_id=1, source_target_pairs={{1,5},{3,7},{5,9},{7,11},{9,13},{11,15},{4,0},{6,2},{8,4},{10,6},{... | collective-permute-start | bytes 294920 | tf_op jit(solution)/shard_map/ppermute | solution.py:99
  42.4 8.6 %collective-permute-start.6 = (bf16[768,64]{0,1:T(8,128)(2,1)S(1)}, bf16[768,64]{0,1:T(8,128)(2,1)S(1)}, u32[]{:S(2)}, u32[]{:S(2)}) collective-permute-start(bf16[768,64]{0,1:T(8,128)(2,1)S(1)} %fusion.7), channel_id=1, source_target_pairs={{1,5},{3,7},{5,9},{7,11},{9,13},{11,15},{4,0},{6,2},{8,4},{10,6},{... | collective-permute-start | bytes 294920 | tf_op jit(solution)/shard_map/ppermute | solution.py:99
  44.4 9.3 %copy-start.13 = (s32[8]{0:T(128)S(1)}, s32[8]{0:T(128)}, u32[]{:S(2)}) copy-start(s32[8]{0:T(128)} %param.12) | copy-start | bytes 100
  51.5 6.8 %copy-start.3 = (bf16[1,1,384,128]{2,3,1,0:T(8,128)(2,1)S(1)}, bf16[1,1,384,128]{2,3,1,0:T(8,128)(2,1)}, u32[]{:S(2)}) copy-start(bf16[1,1,384,128]{2,3,1,0:T(8,128)(2,1)} %copy-done.2) | copy-start | bytes 294916
  51.6 6.8 %copy-start.5 = (bf16[1,1,384,128]{2,3,1,0:T(8,128)(2,1)S(1)}, bf16[1,1,384,128]{2,3,1,0:T(8,128)(2,1)}, u32[]{:S(2)}) copy-start(bf16[1,1,384,128]{2,3,1,0:T(8,128)(2,1)} %copy-done.4) | copy-start | bytes 294916
  51.6 6.1 %collective-permute-start.7 = (bf16[384,128]{0,1:T(8,128)(2,1)S(1)}, bf16[384,128]{0,1:T(8,128)(2,1)S(1)}, u32[]{:S(2)}, u32[]{:S(2)}) collective-permute-start(bf16[384,128]{0,1:T(8,128)(2,1)S(1)} %pad_maximum_fusion.2), channel_id=1, source_target_pairs={{1,2},{3,4},{5,6},{7,8},{9,10},{11,12},{13,14},{2,1},{4,3},{6,5},{... | collective-permute-start | bytes 294920 | tf_op jit(solution)/shard_map/ppermute | solution.py:105
  64.1 28.1 %copy-start.10 = (f32[8,8192]{1,0:T(8,128)S(1)}, f32[8,8192]{1,0:T(8,128)}, u32[]{:S(2)}) copy-start(f32[8,8192]{1,0:T(8,128)} %param.13) | copy-start | bytes 786436
  65.2 28.2 %collective-permute-start.12 = (bf16[1,2,8192]{2,0,1:T(2,128)(2,1)S(1)}, bf16[1,2,8192]{2,0,1:T(2,128)(2,1)S(1)}, u32[]{:S(2)}, u32[]{:S(2)}) collective-permute-start(bf16[1,2,8192]{2,0,1:T(2,128)(2,1)S(1)} %copy.33), channel_id=1, source_target_pairs={{0,16},{16,32},{32,48},{48,64},{64,80},{80,96},{96,112},{112,128},... | collective-permute-start | bytes 98312 | tf_op jit(solution)/shard_map/ppermute | solution.py:12
  69.5 23.9 %collective-permute-start.13 = (bf16[1,2,8192]{2,0,1:T(2,128)(2,1)S(1)}, bf16[1,2,8192]{2,0,1:T(2,128)(2,1)S(1)}, u32[]{:S(2)}, u32[]{:S(2)}) collective-permute-start(bf16[1,2,8192]{2,0,1:T(2,128)(2,1)S(1)} %copy.33), channel_id=1, source_target_pairs={{0,32},{16,48},{32,64},{48,80},{64,96},{80,112},{96,128},{112,144}... | collective-permute-start | bytes 98312 | tf_op jit(solution)/shard_map/ppermute | solution.py:12
  75.6 17.8 %collective-permute-start.8 = (bf16[1,2,8192]{2,0,1:T(2,128)(2,1)S(1)}, bf16[1,2,8192]{2,0,1:T(2,128)(2,1)S(1)}, u32[]{:S(2)}, u32[]{:S(2)}) collective-permute-start(bf16[1,2,8192]{2,0,1:T(2,128)(2,1)S(1)} %copy.33), channel_id=1, source_target_pairs={{16,0},{32,16},{48,32},{64,48},{80,64},{96,80},{112,96},{128,112},... | collective-permute-start | bytes 98312 | tf_op jit(solution)/shard_map/ppermute | solution.py:12
  87.2 7.5 %collective-permute-start.9 = (bf16[1,2,8192]{2,0,1:T(2,128)(2,1)S(1)}, bf16[1,2,8192]{2,0,1:T(2,128)(2,1)S(1)}, u32[]{:S(2)}, u32[]{:S(2)}) collective-permute-start(bf16[1,2,8192]{2,0,1:T(2,128)(2,1)S(1)} %copy.33), channel_id=1, source_target_pairs={{32,0},{48,16},{64,32},{80,48},{96,64},{112,80},{128,96},{144,112}... | collective-permute-start | bytes 98312 | tf_op jit(solution)/shard_map/ppermute | solution.py:12
  95.3 17.6 %collective-permute-start.10 = (bf16[2,2,8192]{2,0,1:T(2,128)(2,1)S(1)}, bf16[2,2,8192]{2,0,1:T(2,128)(2,1)S(1)}, u32[]{:S(2)}, u32[]{:S(2)}) collective-permute-start(bf16[2,2,8192]{2,0,1:T(2,128)(2,1)S(1)} %get-tuple-element.38), channel_id=1, source_target_pairs={{64,0},{80,16},{96,32},{112,48},{128,64},{144,80},{160,96},{176,11... | collective-permute-start | bytes 196616 | tf_op jit(solution)/shard_map/ppermute | solution.py:12
  103.2 9.7 %collective-permute-start.11 = (bf16[2,2,8192]{2,0,1:T(2,128)(2,1)S(1)}, bf16[2,2,8192]{2,0,1:T(2,128)(2,1)S(1)}, u32[]{:S(2)}, u32[]{:S(2)}) collective-permute-start(bf16[2,2,8192]{2,0,1:T(2,128)(2,1)S(1)} %get-tuple-element.39), channel_id=1, source_target_pairs={{48,0},{64,16},{80,32},{96,48},{112,64},{128,80},{144,96},{160,112... | collective-permute-start | bytes 196616 | tf_op jit(solution)/shard_map/ppermute | solution.py:12
  105.1 11.0 %collective-permute-start.14 = (bf16[2,2,8192]{2,0,1:T(2,128)(2,1)S(1)}, bf16[2,2,8192]{2,0,1:T(2,128)(2,1)S(1)}, u32[]{:S(2)}, u32[]{:S(2)}) collective-permute-start(bf16[2,2,8192]{2,0,1:T(2,128)(2,1)S(1)} %get-tuple-element.40), channel_id=1, source_target_pairs={{0,48},{16,64},{32,80},{48,96},{64,112},{80,128},{96,144},{112,160... | collective-permute-start | bytes 196616 | tf_op jit(solution)/shard_map/ppermute | solution.py:12
  110.8 13.7 %collective-permute-start.15 = (bf16[2,2,8192]{2,0,1:T(2,128)(2,1)S(1)}, bf16[2,2,8192]{2,0,1:T(2,128)(2,1)S(1)}, u32[]{:S(2)}, u32[]{:S(2)}) collective-permute-start(bf16[2,2,8192]{2,0,1:T(2,128)(2,1)S(1)} %get-tuple-element.41), channel_id=1, source_target_pairs={{0,64},{16,80},{32,96},{48,112},{64,128},{80,144},{96,160},{112,17... | collective-permute-start | bytes 196616 | tf_op jit(solution)/shard_map/ppermute | solution.py:12

commit v10 on v9

--- a/solution.py
+++ b/solution.py
@@ -64,15 +64,23 @@
     other_blocks, other_src = lax.ppermute(
         (blocks, jnp.where(odd, backward_src, forward_src)), "section", swap
     )
-    left = jnp.where(odd, blocks, other_blocks)
-    right = jnp.where(odd, other_blocks, blocks)
-    forward_real, forward_imag = matrix_product(left, right)
-    backward_real, backward_imag = adjoint_product(left, right)
-    real_part = jnp.where(odd, forward_real, backward_real).astype(jnp.bfloat16)
-    imag_part = jnp.where(odd, forward_imag, backward_imag).astype(jnp.bfloat16)
-    pair_forward = (complex_product(blocks, other_src, False) + forward_src).astype(jnp.bfloat16)
-    pair_backward = (complex_product(blocks, other_src, True) + backward_src).astype(jnp.bfloat16)
-    chain_src = stacked(jnp.where(odd, pair_forward, pair_backward))
+
+    def forward_pair():
+        real_part, imag_part = matrix_product(blocks, other_blocks)
+        source = complex_product(blocks, other_src, False) + forward_src
+        return real_part.astype(jnp.bfloat16), imag_part.astype(jnp.bfloat16), source.astype(
+            jnp.bfloat16
+        )
+
+    def backward_pair():
+        real_part, imag_part = adjoint_product(other_blocks, blocks)
+        source = complex_product(blocks, other_src, True) + backward_src
+        return real_part.astype(jnp.bfloat16), imag_part.astype(jnp.bfloat16), source.astype(
+            jnp.bfloat16
+        )
+
+    real_part, imag_part, pair_src = lax.cond(odd, forward_pair, backward_pair)
+    chain_src = stacked(pair_src)
     chips = count // 2
     chip = lax.axis_index("section") // 2
     chain = [(2 * y + 1, 2 * y + 3) for y in range(chips - 1)]

time: 127 us -> 124 us (0.976)
  the two profiles are of different devices: /device:TPU:18 before, /device:TPU:22 now
where the time goes in v10:
time: 124 us
  starting transfers between devices  62.6 us (50%)
  waiting for transfers between devices  39.3 us (32%)
  matrix products  10.7 us (9%)
  other arithmetic  6.46 us (5%)
  local copies, waits for them, and re-layouts  4 us (3%)
    ppermute x8, starting transfers between devices, passed_along(): lax.ppermute(value, axis, [(source, source + steps) for source in range(l...  45.3 us
    ppermute x8, waiting for transfers between devices, passed_along(): lax.ppermute(value, axis, [(source, source + steps) for source in range(l...  14.1 us
    ppermute x3, waiting for transfers between devices, sweeps(): arrived = lax.ppermute(state, 'section', stride)  13.8 us
    ppermute x2, waiting for transfers between devices, sweeps(): lax.ppermute((own_map, chain_src), 'section', chain)  6.76 us
    ppermute x3, starting transfers between devices, sweeps(): arrived = lax.ppermute(state, 'section', stride)  6.21 us
    dot_general x2, matrix products, picked_rows(): jnp.einsum('ar,ap->rp', table, selector.astype(table.dtype), preferred_el...  5.77 us
    ppermute x2, starting transfers between devices, sweeps(): lax.ppermute((own_map, chain_src), 'section', chain)  4.72 us
    ppermute x2, starting transfers between devices, sweeps(): lax.ppermute((blocks, jnp.where(odd, backward_src, forward_src)), 'sectio...  4.32 us
  transfers between devices with their start and end apart: 16, of which 10 were waited for; matrix products, arithmetic and copies ran while one was open for 5% of the time, Pallas kernels for 0%

profile of v10, /device:TPU:22, one launch (start us, length us, event | category | flops | bytes accessed | tf_op | source)
XLA Modules:
  0.0 123.6 jit_solution(4240600778771610274)
XLA Ops:
  0.0 1.9 %collective-permute-start = (bf16[2,384,384]{2,1,0:T(8,128)(2,1)}, bf16[2,384,384]{2,1,0:T(8,128)(2,1)S(1)}, u32[]{:S(2)}, u32[]{:S(2)}) collective-permute-start(bf16[2,384,384]{2,1,0:T(8,128)(2,1)} %bitcast.234), channel_id=1, source_target_pairs={{0,1},{1,0},{2,3},{3,2},{4,5},{5,4},{6,7},{7,6},{8,9},{9,8},{10,11... | collective-permute-start | bytes 1769480 | tf_op jit(solution)/shard_map/ppermute | solution.py:64
  1.9 1.0 copy.13
  2.9 1.0 copy.14
  4.0 2.4 %collective-permute-start.1 = (bf16[384,128]{0,1:T(8,128)(2,1)S(1)}, bf16[384,128]{0,1:T(8,128)(2,1)S(1)}, u32[]{:S(2)}, u32[]{:S(2)}) collective-permute-start(bf16[384,128]{0,1:T(8,128)(2,1)S(1)} %broadcast_select_fusion), channel_id=1, source_target_pairs={{0,1},{1,0},{2,3},{3,2},{4,5},{5,4},{6,7},{7,6},{8,9},{9,8},{10,11... | collective-permute-start | bytes 294920 | tf_op jit(solution)/shard_map/ppermute | solution.py:64
  6.4 0.9 collective-permute-done.1
  7.3 0.0 collective-permute-done
  7.3 4.2 %conditional.3 = (bf16[1,384,384]{2,1,0:T(8,128)(2,1)S(1)}, bf16[1,384,384]{2,1,0:T(8,128)(2,1)S(1)}, f32[384,128]{0,1:T(8,128)S(1)}, bf16[384,128]{0,1:T(8,128)...) conditional(s32[]{:T(128)} %convert_element_type.304, (bf16[2,384,384]{2,1,0:T(8,128)(2,1)}, ...), branch_computations={%region_1.2_spmd, %region_2.3_spmd} | conditional | flops 529317888 | bytes 12288076
  7.3 1.4 %fusion.7 = f32[2,384,128]{1,2,0:T(8,128)S(1)} fusion(bf16[2,384,384]{2,1,0:T(8,128)(2,1)} %get-tuple-element.59, bf16[384,128]{0,1:T(8,128)(2,1)S(1)} %get-tuple-element.61), kind=kOutput, calls=%fused_computation.13 | convolution fusion | flops 75497472 | bytes 1081344 | tf_op jit(solution)/shard_map/cond/branch_0_fun/cji,jn->cin/dot_general | solution.py:18
  8.8 0.0 copy-done.1
  8.8 0.8 convolution_bitcast_fusion
  9.6 0.2 fusion.1
  9.8 0.9 copy.36
  10.6 0.9 copy.38
  11.7 2.4 %collective-permute-start.3 = (bf16[768,64]{0,1:T(8,128)(2,1)S(1)}, bf16[768,64]{0,1:T(8,128)(2,1)S(1)}, u32[]{:S(2)}, u32[]{:S(2)}) collective-permute-start(bf16[768,64]{0,1:T(8,128)(2,1)S(1)} %pad_maximum_fusion.2), channel_id=1, source_target_pairs={{1,3},{3,5},{5,7},{7,9},{9,11},{11,13},{13,15},{2,0},{4,2},{6,4},{... | collective-permute-start | bytes 294920 | tf_op jit(solution)/shard_map/ppermute | solution.py:89
  14.1 2.4 %collective-permute-start.2 = (bf16[2,384,384]{2,1,0:T(8,128)(2,1)S(1)}, bf16[2,384,384]{2,1,0:T(8,128)(2,1)S(1)}, u32[]{:S(2)}, u32[]{:S(2)}) collective-permute-start(bf16[2,384,384]{2,1,0:T(8,128)(2,1)S(1)} %constant_dynamic-update-slice_fusion), channel_id=1, source_target_pairs={{1,3},{3,5},{5,7},{7,9},{9,11},{11,13},{13,15},{2,0},{4,2},{6,4},{... | collective-permute-start | bytes 1769480 | tf_op jit(solution)/shard_map/ppermute | solution.py:89
  16.5 1.7 %collective-permute-done.3 = bf16[768,64]{0,1:T(8,128)(2,1)S(1)} collective-permute-done((bf16[768,64]{0,1:T(8,128)(2,1)S(1)}, bf16[768,64]{0,1:T(8,128)(2,1)S(1)}, u32[]{:S(2)}, u32[]{:S(2)}) %collective-permute-start.3) | collective-permute-done | bytes 98336 | tf_op jit(solution)/shard_map/ppermute | solution.py:89
  18.2 0.3 fusion.47
  18.6 2.2 %collective-permute-start.4 = (bf16[768,64]{0,1:T(8,128)(2,1)S(1)}, bf16[768,64]{0,1:T(8,128)(2,1)S(1)}, u32[]{:S(2)}, u32[]{:S(2)}) collective-permute-start(bf16[768,64]{0,1:T(8,128)(2,1)S(1)} %fusion.35), channel_id=1, source_target_pairs={{1,5},{3,7},{5,9},{7,11},{9,13},{11,15},{4,0},{6,2},{8,4},{10,6},{... | collective-permute-start | bytes 294920 | tf_op jit(solution)/shard_map/ppermute | solution.py:107
  20.8 5.0 %collective-permute-done.2 = bf16[2,384,384]{2,1,0:T(8,128)(2,1)S(1)} collective-permute-done((bf16[2,384,384]{2,1,0:T(8,128)(2,1)S(1)}, bf16[2,384,384]{2,1,0:T(8,128)(2,1)S(1)}, u32[]{:S(2)}, u32[]{:S(2)}) %collective-permute-start.2) | collective-permute-done | bytes 589856 | tf_op jit(solution)/shard_map/ppermute | solution.py:89
  25.9 0.8 convolution_bitcast_fusion.2
  26.7 1.1 fusion.88
  27.8 1.0 fusion.32
  28.8 0.3 collective-permute-done.4
  29.2 0.3 fusion.23
  29.5 0.0 copy-start.5
  29.5 2.1 %collective-permute-start.5 = (bf16[768,64]{0,1:T(8,128)(2,1)S(1)}, bf16[768,64]{0,1:T(8,128)(2,1)S(1)}, u32[]{:S(2)}, u32[]{:S(2)}) collective-permute-start(bf16[768,64]{0,1:T(8,128)(2,1)S(1)} %fusion.23), channel_id=1, source_target_pairs={{1,5},{3,7},{5,9},{7,11},{9,13},{11,15},{4,0},{6,2},{8,4},{10,6},{... | collective-permute-start | bytes 294920 | tf_op jit(solution)/shard_map/ppermute | solution.py:107
  31.6 6.7 %collective-permute-done.5 = bf16[768,64]{0,1:T(8,128)(2,1)S(1)} collective-permute-done((bf16[768,64]{0,1:T(8,128)(2,1)S(1)}, bf16[768,64]{0,1:T(8,128)(2,1)S(1)}, u32[]{:S(2)}, u32[]{:S(2)}) %collective-permute-start.5) | collective-permute-done | bytes 98336 | tf_op jit(solution)/shard_map/ppermute | solution.py:107
  38.3 0.3 fusion.24
  38.6 1.9 %collective-permute-start.6 = (bf16[768,64]{0,1:T(8,128)(2,1)S(1)}, bf16[768,64]{0,1:T(8,128)(2,1)S(1)}, u32[]{:S(2)}, u32[]{:S(2)}) collective-permute-start(bf16[768,64]{0,1:T(8,128)(2,1)S(1)} %fusion.24), channel_id=1, source_target_pairs={{1,5},{3,7},{5,9},{7,11},{9,13},{11,15},{4,0},{6,2},{8,4},{10,6},{... | collective-permute-start | bytes 294920 | tf_op jit(solution)/shard_map/ppermute | solution.py:107
  40.5 0.0 copy-done.4
  40.5 0.0 copy-done.5
  40.6 0.0 copy-start.6
  40.6 0.0 copy-start
  40.6 6.7 %collective-permute-done.6 = bf16[768,64]{0,1:T(8,128)(2,1)S(1)} collective-permute-done((bf16[768,64]{0,1:T(8,128)(2,1)S(1)}, bf16[768,64]{0,1:T(8,128)(2,1)S(1)}, u32[]{:S(2)}, u32[]{:S(2)}) %collective-permute-start.6) | collective-permute-done | bytes 98336 | tf_op jit(solution)/shard_map/ppermute | solution.py:107
  47.3 0.3 fusion.25
  47.7 2.1 %collective-permute-start.7 = (bf16[384,128]{0,1:T(8,128)(2,1)S(1)}, bf16[384,128]{0,1:T(8,128)(2,1)S(1)}, u32[]{:S(2)}, u32[]{:S(2)}) collective-permute-start(bf16[384,128]{0,1:T(8,128)(2,1)S(1)} %pad_maximum_fusion.3), channel_id=1, source_target_pairs={{1,2},{3,4},{5,6},{7,8},{9,10},{11,12},{13,14},{2,1},{4,3},{6,5},{... | collective-permute-start | bytes 294920 | tf_op jit(solution)/shard_map/ppermute | solution.py:113
  49.8 3.8 %collective-permute-done.7 = bf16[384,128]{0,1:T(8,128)(2,1)S(1)} collective-permute-done((bf16[384,128]{0,1:T(8,128)(2,1)S(1)}, bf16[384,128]{0,1:T(8,128)(2,1)S(1)}, u32[]{:S(2)}, u32[]{:S(2)}) %collective-permute-start.7) | collective-permute-done | bytes 98336 | tf_op jit(solution)/shard_map/ppermute | solution.py:113
  53.6 0.3 convolution_bitcast_fusion.3
  53.9 0.3 convolution_bitcast_fusion.4
  54.3 2.8 %fusion.18 = f32[128,8192]{1,0:T(8,128)S(1)} fusion(s32[8192]{0:T(1024)S(1)} %get-tuple-element.146, f32[384,64]{0,1:T(8,128)S(1)} %get-tuple-element.132, f32[384,64]{0,1:T(8,128)S(1)} %get-tuple-element.131, f32[384,64]{0,1:T(8,128)S(1)} %get-tuple-element.162, f32[384,64]{0,1:T(8,128)S(1)} %get-tuple-element.163, pred[]{:T(512)S(6)} %eq.63, ...), kind=kOutput, calls=%fused_computation.32 | convolution fusion | flops 808894464 | bytes 4816897 | tf_op jit(solution)/shard_map/ar,ap->rp/dot_general | solution.py:55
  57.1 3.0 %multiply_reduce_fusion = (f32[8192]{0:T(1024)S(1)}, f32[128,8192]{1,0:T(8,128)S(1)}) fusion(f32[128,8192]{1,0:T(8,128)S(1)} %fusion.18, s32[8192]{0:T(1024)S(1)} %get-tuple-element.145, bf16[384,64]{0,1:T(8,128)(2,1)S(1)} %get-tuple-element.136, bf16[384,64]{0,1:T(8,128)(2,1)S(1)} %get-tuple-element.135), kind=kOutput, calls=%fused_computation.35 | convolution fusion | flops 810737664 | bytes 8552448 | tf_op jit(solution)/shard_map/ar,ap->rp/dot_general | solution.py:55
  60.0 0.0 copy-start.3
  60.1 0.9 fusion.21
  61.0 0.1 maximum_multiply_fusion
  61.1 0.1 copy.43
  61.1 4.3 %collective-permute-start.12 = (bf16[1,2,8192]{2,0,1:T(2,128)(2,1)S(1)}, bf16[1,2,8192]{2,0,1:T(2,128)(2,1)S(1)}, u32[]{:S(2)}, u32[]{:S(2)}) collective-permute-start(bf16[1,2,8192]{2,0,1:T(2,128)(2,1)S(1)} %copy.43), channel_id=1, source_target_pairs={{0,16},{16,32},{32,48},{48,64},{64,80},{80,96},{96,112},{112,128},... | collective-permute-start | bytes 98312 | tf_op jit(solution)/shard_map/ppermute | solution.py:12
  65.4 6.1 %collective-permute-start.13 = (bf16[1,2,8192]{2,0,1:T(2,128)(2,1)S(1)}, bf16[1,2,8192]{2,0,1:T(2,128)(2,1)S(1)}, u32[]{:S(2)}, u32[]{:S(2)}) collective-permute-start(bf16[1,2,8192]{2,0,1:T(2,128)(2,1)S(1)} %copy.43), channel_id=1, source_target_pairs={{0,32},{16,48},{32,64},{48,80},{64,96},{80,112},{96,128},{112,144}... | collective-permute-start | bytes 98312 | tf_op jit(solution)/shard_map/ppermute | solution.py:12
  71.5 12.0 %collective-permute-start.8 = (bf16[1,2,8192]{2,0,1:T(2,128)(2,1)S(1)}, bf16[1,2,8192]{2,0,1:T(2,128)(2,1)S(1)}, u32[]{:S(2)}, u32[]{:S(2)}) collective-permute-start(bf16[1,2,8192]{2,0,1:T(2,128)(2,1)S(1)} %copy.43), channel_id=1, source_target_pairs={{16,0},{32,16},{48,32},{64,48},{80,64},{96,80},{112,96},{128,112},... | collective-permute-start | bytes 98312 | tf_op jit(solution)/shard_map/ppermute | solution.py:12
  83.5 4.8 %collective-permute-start.9 = (bf16[1,2,8192]{2,0,1:T(2,128)(2,1)S(1)}, bf16[1,2,8192]{2,0,1:T(2,128)(2,1)S(1)}, u32[]{:S(2)}, u32[]{:S(2)}) collective-permute-start(bf16[1,2,8192]{2,0,1:T(2,128)(2,1)S(1)} %copy.43), channel_id=1, source_target_pairs={{32,0},{48,16},{64,32},{80,48},{96,64},{112,80},{128,96},{144,112}... | collective-permute-start | bytes 98312 | tf_op jit(solution)/shard_map/ppermute | solution.py:12
  88.3 1.1 select_reduce_fusion.12
  89.4 0.0 collective-permute-done.12
  89.4 0.0 collective-permute-done.13
  89.5 0.0 collective-permute-done.8
  89.5 1.5 %collective-permute-done.9 = bf16[1,2,8192]{2,0,1:T(2,128)(2,1)S(1)} collective-permute-done((bf16[1,2,8192]{2,0,1:T(2,128)(2,1)S(1)}, bf16[1,2,8192]{2,0,1:T(2,128)(2,1)S(1)}, u32[]{:S(2)}, u32[]{:S(2)}) %collective-permute-start.9) | collective-permute-done | bytes 32800 | tf_op jit(solution)/shard_map/ppermute | solution.py:12
  91.0 0.5 pad_maximum_fusion.4
  91.5 8.6 %collective-permute-start.10 = (bf16[2,2,8192]{2,0,1:T(2,128)(2,1)S(1)}, bf16[2,2,8192]{2,0,1:T(2,128)(2,1)S(1)}, u32[]{:S(2)}, u32[]{:S(2)}) collective-permute-start(bf16[2,2,8192]{2,0,1:T(2,128)(2,1)S(1)} %get-tuple-element.141), channel_id=1, source_target_pairs={{64,0},{80,16},{96,32},{112,48},{128,64},{144,80},{160,96},{176,11... | collective-permute-start | bytes 196616 | tf_op jit(solution)/shard_map/ppermute | solution.py:12
  100.1 1.9 %collective-permute-start.11 = (bf16[2,2,8192]{2,0,1:T(2,128)(2,1)S(1)}, bf16[2,2,8192]{2,0,1:T(2,128)(2,1)S(1)}, u32[]{:S(2)}, u32[]{:S(2)}) collective-permute-start(bf16[2,2,8192]{2,0,1:T(2,128)(2,1)S(1)} %get-tuple-element.142), channel_id=1, source_target_pairs={{48,0},{64,16},{80,32},{96,48},{112,64},{128,80},{144,96},{160,112... | collective-permute-start | bytes 196616 | tf_op jit(solution)/shard_map/ppermute | solution.py:12
  102.0 5.7 %collective-permute-start.14 = (bf16[2,2,8192]{2,0,1:T(2,128)(2,1)S(1)}, bf16[2,2,8192]{2,0,1:T(2,128)(2,1)S(1)}, u32[]{:S(2)}, u32[]{:S(2)}) collective-permute-start(bf16[2,2,8192]{2,0,1:T(2,128)(2,1)S(1)} %get-tuple-element.143), channel_id=1, source_target_pairs={{0,48},{16,64},{32,80},{48,96},{64,112},{80,128},{96,144},{112,160... | collective-permute-start | bytes 196616 | tf_op jit(solution)/shard_map/ppermute | solution.py:12
  107.7 1.9 %collective-permute-start.15 = (bf16[2,2,8192]{2,0,1:T(2,128)(2,1)S(1)}, bf16[2,2,8192]{2,0,1:T(2,128)(2,1)S(1)}, u32[]{:S(2)}, u32[]{:S(2)}) collective-permute-start(bf16[2,2,8192]{2,0,1:T(2,128)(2,1)S(1)} %get-tuple-element.144), channel_id=1, source_target_pairs={{0,64},{16,80},{32,96},{48,112},{64,128},{80,144},{96,160},{112,17... | collective-permute-start | bytes 196616 | tf_op jit(solution)/shard_map/ppermute | solution.py:12
  109.7 0.0 collective-permute-done.10
  109.7 0.0 collective-permute-done.11
  109.7 3.1 %collective-permute-done.14 = bf16[2,2,8192]{2,0,1:T(2,128)(2,1)S(1)} collective-permute-done((bf16[2,2,8192]{2,0,1:T(2,128)(2,1)S(1)}, bf16[2,2,8192]{2,0,1:T(2,128)(2,1)S(1)}, u32[]{:S(2)}, u32[]{:S(2)}) %collective-permute-start.14) | collective-permute-done | bytes 65568 | tf_op jit(solution)/shard_map/ppermute | solution.py:12
  112.8 9.4 %collective-permute-done.15 = bf16[2,2,8192]{2,0,1:T(2,128)(2,1)S(1)} collective-permute-done((bf16[2,2,8192]{2,0,1:T(2,128)(2,1)S(1)}, bf16[2,2,8192]{2,0,1:T(2,128)(2,1)S(1)}, u32[]{:S(2)}, u32[]{:S(2)}) %collective-permute-start.15) | collective-permute-done | bytes 65568 | tf_op jit(solution)/shard_map/ppermute | solution.py:12
  122.3 1.3 %fusion.55 = f32[2,1,8192]{2,1,0:T(1,128)} fusion(bf16[2,2,8192]{2,0,1:T(2,128)(2,1)S(1)} %collective-permute-done.15, bf16[2,2,8192]{2,0,1:T(2,128)(2,1)S(1)} %collective-permute-done.14, bf16[1,2,8192]{2,0,1:T(2,128)(2,1)S(1)} %collective-permute-done.13, f32[1,1,8192]{2,1,0:T(1,128)S(1)} %fusion.81, f32[1,1,8192]{2,1,0:T(1,128)S(1)} %bitcast.244, ...), kind=kLoop, calls=%fused_computation.108 | loop fusion | flops 622592 | bytes 950272 | tf_op jit(solution)/shard_map/add | solution.py:166
  (25 shorter events, 0.4 us)
Async XLA Ops:
  0.0 7.3 %collective-permute-start = (bf16[2,384,384]{2,1,0:T(8,128)(2,1)}, bf16[2,384,384]{2,1,0:T(8,128)(2,1)S(1)}, u32[]{:S(2)}, u32[]{:S(2)}) collective-permute-start(bf16[2,384,384]{2,1,0:T(8,128)(2,1)} %bitcast.234), channel_id=1, source_target_pairs={{0,1},{1,0},{2,3},{3,2},{4,5},{5,4},{6,7},{7,6},{8,9},{9,8},{10,11... | collective-permute-start | bytes 1769480 | tf_op jit(solution)/shard_map/ppermute | solution.py:64
  4.0 3.3 %collective-permute-start.1 = (bf16[384,128]{0,1:T(8,128)(2,1)S(1)}, bf16[384,128]{0,1:T(8,128)(2,1)S(1)}, u32[]{:S(2)}, u32[]{:S(2)}) collective-permute-start(bf16[384,128]{0,1:T(8,128)(2,1)S(1)} %broadcast_select_fusion), channel_id=1, source_target_pairs={{0,1},{1,0},{2,3},{3,2},{4,5},{5,4},{6,7},{7,6},{8,9},{9,8},{10,11... | collective-permute-start | bytes 294920 | tf_op jit(solution)/shard_map/ppermute | solution.py:64
  7.3 1.5 %copy-start.1 = (bf16[2,384,384]{2,1,0:T(8,128)(2,1)S(1)}, bf16[2,384,384]{2,1,0:T(8,128)(2,1)}, u32[]{:S(2)}) copy-start(bf16[2,384,384]{2,1,0:T(8,128)(2,1)} %get-tuple-element.59) | copy-start | bytes 1769476
  11.7 6.5 %collective-permute-start.3 = (bf16[768,64]{0,1:T(8,128)(2,1)S(1)}, bf16[768,64]{0,1:T(8,128)(2,1)S(1)}, u32[]{:S(2)}, u32[]{:S(2)}) collective-permute-start(bf16[768,64]{0,1:T(8,128)(2,1)S(1)} %pad_maximum_fusion.2), channel_id=1, source_target_pairs={{1,3},{3,5},{5,7},{7,9},{9,11},{11,13},{13,15},{2,0},{4,2},{6,4},{... | collective-permute-start | bytes 294920 | tf_op jit(solution)/shard_map/ppermute | solution.py:89
  14.1 11.8 %collective-permute-start.2 = (bf16[2,384,384]{2,1,0:T(8,128)(2,1)S(1)}, bf16[2,384,384]{2,1,0:T(8,128)(2,1)S(1)}, u32[]{:S(2)}, u32[]{:S(2)}) collective-permute-start(bf16[2,384,384]{2,1,0:T(8,128)(2,1)S(1)} %constant_dynamic-update-slice_fusion), channel_id=1, source_target_pairs={{1,3},{3,5},{5,7},{7,9},{9,11},{11,13},{13,15},{2,0},{4,2},{6,4},{... | collective-permute-start | bytes 1769480 | tf_op jit(solution)/shard_map/ppermute | solution.py:89
  18.6 10.6 %collective-permute-start.4 = (bf16[768,64]{0,1:T(8,128)(2,1)S(1)}, bf16[768,64]{0,1:T(8,128)(2,1)S(1)}, u32[]{:S(2)}, u32[]{:S(2)}) collective-permute-start(bf16[768,64]{0,1:T(8,128)(2,1)S(1)} %fusion.35), channel_id=1, source_target_pairs={{1,5},{3,7},{5,9},{7,11},{9,13},{11,15},{4,0},{6,2},{8,4},{10,6},{... | collective-permute-start | bytes 294920 | tf_op jit(solution)/shard_map/ppermute | solution.py:107
  29.5 11.0 %copy-start.4 = (s32[8192]{0:T(1024)S(1)}, s32[8192]{0:T(1024)}, u32[]{:S(2)}) copy-start(s32[8192]{0:T(1024)} %param.13) | copy-start | bytes 98308
  29.5 11.0 %copy-start.5 = (s32[8192]{0:T(1024)S(1)}, s32[8192]{0:T(1024)}, u32[]{:S(2)}) copy-start(s32[8192]{0:T(1024)} %param.12) | copy-start | bytes 98308
  29.5 8.8 %collective-permute-start.5 = (bf16[768,64]{0,1:T(8,128)(2,1)S(1)}, bf16[768,64]{0,1:T(8,128)(2,1)S(1)}, u32[]{:S(2)}, u32[]{:S(2)}) collective-permute-start(bf16[768,64]{0,1:T(8,128)(2,1)S(1)} %fusion.23), channel_id=1, source_target_pairs={{1,5},{3,7},{5,9},{7,11},{9,13},{11,15},{4,0},{6,2},{8,4},{10,6},{... | collective-permute-start | bytes 294920 | tf_op jit(solution)/shard_map/ppermute | solution.py:107
  38.6 8.7 %collective-permute-start.6 = (bf16[768,64]{0,1:T(8,128)(2,1)S(1)}, bf16[768,64]{0,1:T(8,128)(2,1)S(1)}, u32[]{:S(2)}, u32[]{:S(2)}) collective-permute-start(bf16[768,64]{0,1:T(8,128)(2,1)S(1)} %fusion.24), channel_id=1, source_target_pairs={{1,5},{3,7},{5,9},{7,11},{9,13},{11,15},{4,0},{6,2},{8,4},{10,6},{... | collective-permute-start | bytes 294920 | tf_op jit(solution)/shard_map/ppermute | solution.py:107
  40.6 9.2 %copy-start.6 = (s32[8]{0:T(128)S(1)}, s32[8]{0:T(128)}, u32[]{:S(2)}) copy-start(s32[8]{0:T(128)} %param.14) | copy-start | bytes 100
  40.6 13.1 %copy-start = (bf16[1,1,2,384,384]{4,3,2,1,0:T(8,128)(2,1)S(1)}, bf16[1,1,2,384,384]{4,3,2,1,0:T(8,128)(2,1)}, u32[]{:S(2)}) copy-start(bf16[1,1,2,384,384]{4,3,2,1,0:T(8,128)(2,1)} %param.9) | copy-start | bytes 1769476
  47.7 5.9 %collective-permute-start.7 = (bf16[384,128]{0,1:T(8,128)(2,1)S(1)}, bf16[384,128]{0,1:T(8,128)(2,1)S(1)}, u32[]{:S(2)}, u32[]{:S(2)}) collective-permute-start(bf16[384,128]{0,1:T(8,128)(2,1)S(1)} %pad_maximum_fusion.3), channel_id=1, source_target_pairs={{1,2},{3,4},{5,6},{7,8},{9,10},{11,12},{13,14},{2,1},{4,3},{6,5},{... | collective-permute-start | bytes 294920 | tf_op jit(solution)/shard_map/ppermute | solution.py:113
  60.0 28.3 %copy-start.3 = (f32[8,8192]{1,0:T(8,128)S(1)}, f32[8,8192]{1,0:T(8,128)}, u32[]{:S(2)}) copy-start(f32[8,8192]{1,0:T(8,128)} %param.15) | copy-start | bytes 786436
  61.1 28.3 %collective-permute-start.12 = (bf16[1,2,8192]{2,0,1:T(2,128)(2,1)S(1)}, bf16[1,2,8192]{2,0,1:T(2,128)(2,1)S(1)}, u32[]{:S(2)}, u32[]{:S(2)}) collective-permute-start(bf16[1,2,8192]{2,0,1:T(2,128)(2,1)S(1)} %copy.43), channel_id=1, source_target_pairs={{0,16},{16,32},{32,48},{48,64},{64,80},{80,96},{96,112},{112,128},... | collective-permute-start | bytes 98312 | tf_op jit(solution)/shard_map/ppermute | solution.py:12
  65.4 24.0 %collective-permute-start.13 = (bf16[1,2,8192]{2,0,1:T(2,128)(2,1)S(1)}, bf16[1,2,8192]{2,0,1:T(2,128)(2,1)S(1)}, u32[]{:S(2)}, u32[]{:S(2)}) collective-permute-start(bf16[1,2,8192]{2,0,1:T(2,128)(2,1)S(1)} %copy.43), channel_id=1, source_target_pairs={{0,32},{16,48},{32,64},{48,80},{64,96},{80,112},{96,128},{112,144}... | collective-permute-start | bytes 98312 | tf_op jit(solution)/shard_map/ppermute | solution.py:12
  71.5 18.0 %collective-permute-start.8 = (bf16[1,2,8192]{2,0,1:T(2,128)(2,1)S(1)}, bf16[1,2,8192]{2,0,1:T(2,128)(2,1)S(1)}, u32[]{:S(2)}, u32[]{:S(2)}) collective-permute-start(bf16[1,2,8192]{2,0,1:T(2,128)(2,1)S(1)} %copy.43), channel_id=1, source_target_pairs={{16,0},{32,16},{48,32},{64,48},{80,64},{96,80},{112,96},{128,112},... | collective-permute-start | bytes 98312 | tf_op jit(solution)/shard_map/ppermute | solution.py:12
  83.5 7.5 %collective-permute-start.9 = (bf16[1,2,8192]{2,0,1:T(2,128)(2,1)S(1)}, bf16[1,2,8192]{2,0,1:T(2,128)(2,1)S(1)}, u32[]{:S(2)}, u32[]{:S(2)}) collective-permute-start(bf16[1,2,8192]{2,0,1:T(2,128)(2,1)S(1)} %copy.43), channel_id=1, source_target_pairs={{32,0},{48,16},{64,32},{80,48},{96,64},{112,80},{128,96},{144,112}... | collective-permute-start | bytes 98312 | tf_op jit(solution)/shard_map/ppermute | solution.py:12
  91.5 18.2 %collective-permute-start.10 = (bf16[2,2,8192]{2,0,1:T(2,128)(2,1)S(1)}, bf16[2,2,8192]{2,0,1:T(2,128)(2,1)S(1)}, u32[]{:S(2)}, u32[]{:S(2)}) collective-permute-start(bf16[2,2,8192]{2,0,1:T(2,128)(2,1)S(1)} %get-tuple-element.141), channel_id=1, source_target_pairs={{64,0},{80,16},{96,32},{112,48},{128,64},{144,80},{160,96},{176,11... | collective-permute-start | bytes 196616 | tf_op jit(solution)/shard_map/ppermute | solution.py:12
  100.1 9.6 %collective-permute-start.11 = (bf16[2,2,8192]{2,0,1:T(2,128)(2,1)S(1)}, bf16[2,2,8192]{2,0,1:T(2,128)(2,1)S(1)}, u32[]{:S(2)}, u32[]{:S(2)}) collective-permute-start(bf16[2,2,8192]{2,0,1:T(2,128)(2,1)S(1)} %get-tuple-element.142), channel_id=1, source_target_pairs={{48,0},{64,16},{80,32},{96,48},{112,64},{128,80},{144,96},{160,112... | collective-permute-start | bytes 196616 | tf_op jit(solution)/shard_map/ppermute | solution.py:12
  102.0 10.8 %collective-permute-start.14 = (bf16[2,2,8192]{2,0,1:T(2,128)(2,1)S(1)}, bf16[2,2,8192]{2,0,1:T(2,128)(2,1)S(1)}, u32[]{:S(2)}, u32[]{:S(2)}) collective-permute-start(bf16[2,2,8192]{2,0,1:T(2,128)(2,1)S(1)} %get-tuple-element.143), channel_id=1, source_target_pairs={{0,48},{16,64},{32,80},{48,96},{64,112},{80,128},{96,144},{112,160... | collective-permute-start | bytes 196616 | tf_op jit(solution)/shard_map/ppermute | solution.py:12
  107.7 14.5 %collective-permute-start.15 = (bf16[2,2,8192]{2,0,1:T(2,128)(2,1)S(1)}, bf16[2,2,8192]{2,0,1:T(2,128)(2,1)S(1)}, u32[]{:S(2)}, u32[]{:S(2)}) collective-permute-start(bf16[2,2,8192]{2,0,1:T(2,128)(2,1)S(1)} %get-tuple-element.144), channel_id=1, source_target_pairs={{0,64},{16,80},{32,96},{48,112},{64,128},{80,144},{96,160},{112,17... | collective-permute-start | bytes 196616 | tf_op jit(solution)/shard_map/ppermute | solution.py:12

commit v11 on v10

--- a/solution.py
+++ b/solution.py
@@ -68,24 +68,20 @@
     def forward_pair():
         real_part, imag_part = matrix_product(blocks, other_blocks)
         source = complex_product(blocks, other_src, False) + forward_src
-        return real_part.astype(jnp.bfloat16), imag_part.astype(jnp.bfloat16), source.astype(
-            jnp.bfloat16
-        )
+        return jnp.stack([real_part, imag_part]).astype(jnp.bfloat16), source.astype(jnp.bfloat16)
 
     def backward_pair():
         real_part, imag_part = adjoint_product(other_blocks, blocks)
         source = complex_product(blocks, other_src, True) + backward_src
-        return real_part.astype(jnp.bfloat16), imag_part.astype(jnp.bfloat16), source.astype(
-            jnp.bfloat16
-        )
+        return jnp.stack([real_part, imag_part]).astype(jnp.bfloat16), source.astype(jnp.bfloat16)
 
-    real_part, imag_part, pair_src = lax.cond(odd, forward_pair, backward_pair)
+    own_map, pair_src = lax.cond(odd, forward_pair, backward_pair)
+    real_part, imag_part = own_map[0], own_map[1]
     chain_src = stacked(pair_src)
     chips = count // 2
     chip = lax.axis_index("section") // 2
     chain = [(2 * y + 1, 2 * y + 3) for y in range(chips - 1)]
     chain += [(2 * y, 2 * y - 2) for y in range(1, chips)]
-    own_map = jnp.stack([real_part, imag_part])
     upstream_map, upstream_src = lax.ppermute((own_map, chain_src), "section", chain)
     has_upstream = jnp.where(odd, chip >= 1, chip <= chips - 2)
     joint_real, joint_imag = matrix_product(own_map, upstream_map)

time: 124 us -> 132 us (1.065)
  the two profiles are of different devices: /device:TPU:22 before, /device:TPU:18 now
where the time goes in v11:
time: 132 us; the launch traced here: 131 us
  starting transfers between devices  61.7 us (47%)
  waiting for transfers between devices  40.3 us (31%)
  matrix products  12.4 us (9%)
  local copies, waits for them, and re-layouts  8.13 us (6%)
  other arithmetic  8 us (6%)
    ppermute x8, starting transfers between devices, passed_along(): lax.ppermute(value, axis, [(source, source + steps) for source in range(l...  44.4 us
    ppermute x3, waiting for transfers between devices, sweeps(): arrived = lax.ppermute(state, 'section', stride)  15.6 us
    ppermute x8, waiting for transfers between devices, passed_along(): lax.ppermute(value, axis, [(source, source + steps) for source in range(l...  13.1 us
    ppermute x2, waiting for transfers between devices, sweeps(): lax.ppermute((own_map, chain_src), 'section', chain)  6.97 us
    dot_general x2, matrix products, picked_rows(): jnp.einsum('ar,ap->rp', table, selector.astype(table.dtype), preferred_el...  6.68 us
    ppermute x3, starting transfers between devices, sweeps(): arrived = lax.ppermute(state, 'section', stride)  6.21 us
    ppermute x2, starting transfers between devices, sweeps(): lax.ppermute((own_map, chain_src), 'section', chain)  4.71 us
    ppermute x2, starting transfers between devices, sweeps(): lax.ppermute((blocks, jnp.where(odd, backward_src, forward_src)), 'sectio...  4.32 us
  transfers between devices with their start and end apart: 16, of which 10 were waited for; matrix products, arithmetic and copies ran while one was open for 5% of the time, Pallas kernels for 0%

profile of v11, /device:TPU:18, one launch (start us, length us, event | category | flops | bytes accessed | tf_op | source)
XLA Modules:
  0.0 131.1 jit_solution(17277038428227441654)
XLA Ops:
  0.0 1.9 %collective-permute-start = (bf16[2,384,384]{2,1,0:T(8,128)(2,1)}, bf16[2,384,384]{2,1,0:T(8,128)(2,1)S(1)}, u32[]{:S(2)}, u32[]{:S(2)}) collective-permute-start(bf16[2,384,384]{2,1,0:T(8,128)(2,1)} %bitcast.290), channel_id=1, source_target_pairs={{0,1},{1,0},{2,3},{3,2},{4,5},{5,4},{6,7},{7,6},{8,9},{9,8},{10,11... | collective-permute-start | bytes 1769480 | tf_op jit(solution)/shard_map/ppermute | solution.py:64
  1.9 1.6 %copy.16 = bf16[1,1,384,128]{2,3,1,0:T(8,128)(2,1)} copy(bf16[1,1,384,128]{3,2,1,0:T(8,128)(2,1)} %param.11) | data formatting | bytes 196608 | tf_op args[2]
  3.6 1.0 copy.17
  4.6 0.9 broadcast_select_fusion
  5.5 2.4 %collective-permute-start.1 = (bf16[384,128]{0,1:T(8,128)(2,1)S(1)}, bf16[384,128]{0,1:T(8,128)(2,1)S(1)}, u32[]{:S(2)}, u32[]{:S(2)}) collective-permute-start(bf16[384,128]{0,1:T(8,128)(2,1)S(1)} %broadcast_select_fusion), channel_id=1, source_target_pairs={{0,1},{1,0},{2,3},{3,2},{4,5},{5,4},{6,7},{7,6},{8,9},{9,8},{10,11... | collective-permute-start | bytes 294920 | tf_op jit(solution)/shard_map/ppermute | solution.py:64
  8.0 0.9 collective-permute-done.1
  8.9 0.0 collective-permute-done
  8.9 11.1 %conditional.1 = (bf16[2,384,384]{2,1,0:T(8,128)(2,1)S(1)}, bf16[384,128]{0,1:T(8,128)(2,1)S(1)}, bf16[2,384,384]{1,2,0:T(8,128)(2,1)}, bf16[384,384]{0,1:T(8,128)(2,1)}, bf16[384,384]{0,1:T(8,128)(2,1)}) conditional(s32[]{:T(128)} %convert_element_type.280, (bf16[2,384,384]{2,1,0:T(8,128)(2,1)}, bf16[2,384,384]{2,1,0:T(8,128)(2,1)S(1)}, ...), branch_computations={%region_1.2_spmd.clone, %region_2.3_spmd.clone} | conditional | flops 530497536 | bytes 17793204 | solution.py:78
  8.9 0.6 copy-done.7
  9.5 1.9 %convolution_bitcast_fusion = f32[2,2,384,384]{3,2,0,1:T(8,128)S(1)} fusion(bf16[2,384,384]{2,1,0:T(8,128)(2,1)} %get-tuple-element.113, bf16[2,384,384]{2,1,0:T(8,128)(2,1)S(1)} %get-tuple-element.114), kind=kOutput, calls=%fused_computation | convolution fusion | flops 452984832 | bytes 3538944 | tf_op jit(solution)/shard_map/cond/branch_0_fun/ckj,dji->cdik/dot_general | solution.py:36
  11.4 0.1 fusion.109
  11.5 0.1 fusion.110
  11.5 0.1 pad_maximum_fusion
  11.6 1.1 copy.32
  12.7 0.8 fusion.108
  13.4 1.8 %copy.34 = bf16[384,384]{0,1:T(8,128)(2,1)} copy(bf16[384,384]{1,0:T(8,128)(2,1)} %fusion.108) | data formatting | bytes 589824 | tf_op jit(solution)/shard_map/cond
  15.3 0.8 fusion.107
  16.0 1.8 %copy.36 = bf16[384,384]{0,1:T(8,128)(2,1)} copy(bf16[384,384]{1,0:T(8,128)(2,1)} %fusion.107) | data formatting | bytes 589824 | tf_op jit(solution)/shard_map/cond
  17.9 1.2 fusion.9
  19.1 0.9 fusion.6
  20.0 2.4 %collective-permute-start.3 = (bf16[768,64]{0,1:T(8,128)(2,1)S(1)}, bf16[768,64]{0,1:T(8,128)(2,1)S(1)}, u32[]{:S(2)}, u32[]{:S(2)}) collective-permute-start(bf16[768,64]{0,1:T(8,128)(2,1)S(1)} %pad_maximum_fusion.2), channel_id=1, source_target_pairs={{1,3},{3,5},{5,7},{7,9},{9,11},{11,13},{13,15},{2,0},{4,2},{6,4},{... | collective-permute-start | bytes 294920 | tf_op jit(solution)/shard_map/ppermute | solution.py:85
  22.4 2.4 %collective-permute-start.2 = (bf16[2,384,384]{1,2,0:T(8,128)(2,1)}, bf16[2,384,384]{1,2,0:T(8,128)(2,1)S(1)}, u32[]{:S(2)}, u32[]{:S(2)}) collective-permute-start(bf16[2,384,384]{1,2,0:T(8,128)(2,1)} %get-tuple-element.137), channel_id=1, source_target_pairs={{1,3},{3,5},{5,7},{7,9},{9,11},{11,13},{13,15},{2,0},{4,2},{6,4},{... | collective-permute-start | bytes 1769480 | tf_op jit(solution)/shard_map/ppermute | solution.py:85
  24.8 1.8 %collective-permute-done.3 = bf16[768,64]{0,1:T(8,128)(2,1)S(1)} collective-permute-done((bf16[768,64]{0,1:T(8,128)(2,1)S(1)}, bf16[768,64]{0,1:T(8,128)(2,1)S(1)}, u32[]{:S(2)}, u32[]{:S(2)}) %collective-permute-start.3) | collective-permute-done | bytes 98336 | tf_op jit(solution)/shard_map/ppermute | solution.py:85
  26.6 0.3 fusion.51
  26.9 2.2 %collective-permute-start.4 = (bf16[768,64]{0,1:T(8,128)(2,1)S(1)}, bf16[768,64]{0,1:T(8,128)(2,1)S(1)}, u32[]{:S(2)}, u32[]{:S(2)}) collective-permute-start(bf16[768,64]{0,1:T(8,128)(2,1)S(1)} %fusion.39), channel_id=1, source_target_pairs={{1,5},{3,7},{5,9},{7,11},{9,13},{11,15},{4,0},{6,2},{8,4},{10,6},{... | collective-permute-start | bytes 294920 | tf_op jit(solution)/shard_map/ppermute | solution.py:103
  29.2 5.2 %collective-permute-done.2 = bf16[2,384,384]{1,2,0:T(8,128)(2,1)S(1)} collective-permute-done((bf16[2,384,384]{1,2,0:T(8,128)(2,1)}, bf16[2,384,384]{1,2,0:T(8,128)(2,1)S(1)}, u32[]{:S(2)}, u32[]{:S(2)}) %collective-permute-start.2) | collective-permute-done | bytes 589856 | tf_op jit(solution)/shard_map/ppermute | solution.py:85
  34.4 0.8 convolution_bitcast_fusion.2
  35.2 0.3 fusion.92
  35.5 2.2 %collective-permute-done.4 = bf16[768,64]{0,1:T(8,128)(2,1)S(1)} collective-permute-done((bf16[768,64]{0,1:T(8,128)(2,1)S(1)}, bf16[768,64]{0,1:T(8,128)(2,1)S(1)}, u32[]{:S(2)}, u32[]{:S(2)}) %collective-permute-start.4) | collective-permute-done | bytes 98336 | tf_op jit(solution)/shard_map/ppermute | solution.py:103
  37.7 0.3 fusion.27
  38.0 0.0 copy-start.12
  38.1 2.1 %collective-permute-start.5 = (bf16[768,64]{0,1:T(8,128)(2,1)S(1)}, bf16[768,64]{0,1:T(8,128)(2,1)S(1)}, u32[]{:S(2)}, u32[]{:S(2)}) collective-permute-start(bf16[768,64]{0,1:T(8,128)(2,1)S(1)} %fusion.27), channel_id=1, source_target_pairs={{1,5},{3,7},{5,9},{7,11},{9,13},{11,15},{4,0},{6,2},{8,4},{10,6},{... | collective-permute-start | bytes 294920 | tf_op jit(solution)/shard_map/ppermute | solution.py:103
  40.1 6.7 %collective-permute-done.5 = bf16[768,64]{0,1:T(8,128)(2,1)S(1)} collective-permute-done((bf16[768,64]{0,1:T(8,128)(2,1)S(1)}, bf16[768,64]{0,1:T(8,128)(2,1)S(1)}, u32[]{:S(2)}, u32[]{:S(2)}) %collective-permute-start.5) | collective-permute-done | bytes 98336 | tf_op jit(solution)/shard_map/ppermute | solution.py:103
  46.8 0.3 fusion.28
  47.2 1.9 %collective-permute-start.6 = (bf16[768,64]{0,1:T(8,128)(2,1)S(1)}, bf16[768,64]{0,1:T(8,128)(2,1)S(1)}, u32[]{:S(2)}, u32[]{:S(2)}) collective-permute-start(bf16[768,64]{0,1:T(8,128)(2,1)S(1)} %fusion.28), channel_id=1, source_target_pairs={{1,5},{3,7},{5,9},{7,11},{9,13},{11,15},{4,0},{6,2},{8,4},{10,6},{... | collective-permute-start | bytes 294920 | tf_op jit(solution)/shard_map/ppermute | solution.py:103
  49.1 0.0 copy-start.13
  49.1 0.0 copy-start
  49.1 6.6 %collective-permute-done.6 = bf16[768,64]{0,1:T(8,128)(2,1)S(1)} collective-permute-done((bf16[768,64]{0,1:T(8,128)(2,1)S(1)}, bf16[768,64]{0,1:T(8,128)(2,1)S(1)}, u32[]{:S(2)}, u32[]{:S(2)}) %collective-permute-start.6) | collective-permute-done | bytes 98336 | tf_op jit(solution)/shard_map/ppermute | solution.py:103
  55.8 0.3 fusion.29
  56.1 2.1 %collective-permute-start.7 = (bf16[384,128]{0,1:T(8,128)(2,1)S(1)}, bf16[384,128]{0,1:T(8,128)(2,1)S(1)}, u32[]{:S(2)}, u32[]{:S(2)}) collective-permute-start(bf16[384,128]{0,1:T(8,128)(2,1)S(1)} %pad_maximum_fusion.3), channel_id=1, source_target_pairs={{1,2},{3,4},{5,6},{7,8},{9,10},{11,12},{13,14},{2,1},{4,3},{6,5},{... | collective-permute-start | bytes 294920 | tf_op jit(solution)/shard_map/ppermute | solution.py:109
  58.3 3.8 %collective-permute-done.7 = bf16[384,128]{0,1:T(8,128)(2,1)S(1)} collective-permute-done((bf16[384,128]{0,1:T(8,128)(2,1)S(1)}, bf16[384,128]{0,1:T(8,128)(2,1)S(1)}, u32[]{:S(2)}, u32[]{:S(2)}) %collective-permute-start.7) | collective-permute-done | bytes 98336 | tf_op jit(solution)/shard_map/ppermute | solution.py:109
  62.1 0.3 convolution_bitcast_fusion.3
  62.4 0.3 convolution_bitcast_fusion.4
  62.7 3.7 %fusion.22 = f32[128,8192]{1,0:T(8,128)S(1)} fusion(s32[8192]{0:T(1024)S(1)} %get-tuple-element.179, f32[384,64]{0,1:T(8,128)S(1)} %get-tuple-element.165, f32[384,64]{0,1:T(8,128)S(1)} %get-tuple-element.164, f32[384,64]{0,1:T(8,128)S(1)} %get-tuple-element.195, f32[384,64]{0,1:T(8,128)S(1)} %get-tuple-element.196, pred[]{:T(512)S(6)} %eq.63, ...), kind=kOutput, calls=%fused_computation.44 | convolution fusion | flops 808894464 | bytes 4816897 | tf_op jit(solution)/shard_map/ar,ap->rp/dot_general | solution.py:55
  66.5 3.0 %multiply_reduce_fusion = (f32[8192]{0:T(1024)S(1)}, f32[128,8192]{1,0:T(8,128)S(1)}) fusion(f32[128,8192]{1,0:T(8,128)S(1)} %fusion.22, s32[8192]{0:T(1024)S(1)} %get-tuple-element.178, bf16[384,64]{0,1:T(8,128)(2,1)S(1)} %get-tuple-element.169, bf16[384,64]{0,1:T(8,128)(2,1)S(1)} %get-tuple-element.168), kind=kOutput, calls=%fused_computation.47 | convolution fusion | flops 810737664 | bytes 8552448 | tf_op jit(solution)/shard_map/ar,ap->rp/dot_general | solution.py:55
  69.4 0.0 copy-start.10
  69.4 0.9 fusion.25
  70.4 0.1 maximum_multiply_fusion
  70.4 0.1 copy.45
  70.5 4.3 %collective-permute-start.12 = (bf16[1,2,8192]{2,0,1:T(2,128)(2,1)S(1)}, bf16[1,2,8192]{2,0,1:T(2,128)(2,1)S(1)}, u32[]{:S(2)}, u32[]{:S(2)}) collective-permute-start(bf16[1,2,8192]{2,0,1:T(2,128)(2,1)S(1)} %copy.45), channel_id=1, source_target_pairs={{0,16},{16,32},{32,48},{48,64},{64,80},{80,96},{96,112},{112,128},... | collective-permute-start | bytes 98312 | tf_op jit(solution)/shard_map/ppermute | solution.py:12
  74.8 6.1 %collective-permute-start.13 = (bf16[1,2,8192]{2,0,1:T(2,128)(2,1)S(1)}, bf16[1,2,8192]{2,0,1:T(2,128)(2,1)S(1)}, u32[]{:S(2)}, u32[]{:S(2)}) collective-permute-start(bf16[1,2,8192]{2,0,1:T(2,128)(2,1)S(1)} %copy.45), channel_id=1, source_target_pairs={{0,32},{16,48},{32,64},{48,80},{64,96},{80,112},{96,128},{112,144}... | collective-permute-start | bytes 98312 | tf_op jit(solution)/shard_map/ppermute | solution.py:12
  80.9 11.7 %collective-permute-start.8 = (bf16[1,2,8192]{2,0,1:T(2,128)(2,1)S(1)}, bf16[1,2,8192]{2,0,1:T(2,128)(2,1)S(1)}, u32[]{:S(2)}, u32[]{:S(2)}) collective-permute-start(bf16[1,2,8192]{2,0,1:T(2,128)(2,1)S(1)} %copy.45), channel_id=1, source_target_pairs={{16,0},{32,16},{48,32},{64,48},{80,64},{96,80},{112,96},{128,112},... | collective-permute-start | bytes 98312 | tf_op jit(solution)/shard_map/ppermute | solution.py:12
  92.6 4.8 %collective-permute-start.9 = (bf16[1,2,8192]{2,0,1:T(2,128)(2,1)S(1)}, bf16[1,2,8192]{2,0,1:T(2,128)(2,1)S(1)}, u32[]{:S(2)}, u32[]{:S(2)}) collective-permute-start(bf16[1,2,8192]{2,0,1:T(2,128)(2,1)S(1)} %copy.45), channel_id=1, source_target_pairs={{32,0},{48,16},{64,32},{80,48},{96,64},{112,80},{128,96},{144,112}... | collective-permute-start | bytes 98312 | tf_op jit(solution)/shard_map/ppermute | solution.py:12
  97.4 1.1 select_reduce_fusion.12
  98.5 0.0 collective-permute-done.12
  98.5 1.5 %collective-permute-done.9 = bf16[1,2,8192]{2,0,1:T(2,128)(2,1)S(1)} collective-permute-done((bf16[1,2,8192]{2,0,1:T(2,128)(2,1)S(1)}, bf16[1,2,8192]{2,0,1:T(2,128)(2,1)S(1)}, u32[]{:S(2)}, u32[]{:S(2)}) %collective-permute-start.9) | collective-permute-done | bytes 32800 | tf_op jit(solution)/shard_map/ppermute | solution.py:12
  100.0 0.5 pad_maximum_fusion.4
  100.6 7.9 %collective-permute-start.10 = (bf16[2,2,8192]{2,0,1:T(2,128)(2,1)S(1)}, bf16[2,2,8192]{2,0,1:T(2,128)(2,1)S(1)}, u32[]{:S(2)}, u32[]{:S(2)}) collective-permute-start(bf16[2,2,8192]{2,0,1:T(2,128)(2,1)S(1)} %get-tuple-element.174), channel_id=1, source_target_pairs={{64,0},{80,16},{96,32},{112,48},{128,64},{144,80},{160,96},{176,11... | collective-permute-start | bytes 196616 | tf_op jit(solution)/shard_map/ppermute | solution.py:12
  108.5 1.9 %collective-permute-start.11 = (bf16[2,2,8192]{2,0,1:T(2,128)(2,1)S(1)}, bf16[2,2,8192]{2,0,1:T(2,128)(2,1)S(1)}, u32[]{:S(2)}, u32[]{:S(2)}) collective-permute-start(bf16[2,2,8192]{2,0,1:T(2,128)(2,1)S(1)} %get-tuple-element.175), channel_id=1, source_target_pairs={{48,0},{64,16},{80,32},{96,48},{112,64},{128,80},{144,96},{160,112... | collective-permute-start | bytes 196616 | tf_op jit(solution)/shard_map/ppermute | solution.py:12
  110.4 5.7 %collective-permute-start.14 = (bf16[2,2,8192]{2,0,1:T(2,128)(2,1)S(1)}, bf16[2,2,8192]{2,0,1:T(2,128)(2,1)S(1)}, u32[]{:S(2)}, u32[]{:S(2)}) collective-permute-start(bf16[2,2,8192]{2,0,1:T(2,128)(2,1)S(1)} %get-tuple-element.176), channel_id=1, source_target_pairs={{0,48},{16,64},{32,80},{48,96},{64,112},{80,128},{96,144},{112,160... | collective-permute-start | bytes 196616 | tf_op jit(solution)/shard_map/ppermute | solution.py:12
  116.1 2.0 %collective-permute-start.15 = (bf16[2,2,8192]{2,0,1:T(2,128)(2,1)S(1)}, bf16[2,2,8192]{2,0,1:T(2,128)(2,1)S(1)}, u32[]{:S(2)}, u32[]{:S(2)}) collective-permute-start(bf16[2,2,8192]{2,0,1:T(2,128)(2,1)S(1)} %get-tuple-element.177), channel_id=1, source_target_pairs={{0,64},{16,80},{32,96},{48,112},{64,128},{80,144},{96,160},{112,17... | collective-permute-start | bytes 196616 | tf_op jit(solution)/shard_map/ppermute | solution.py:12
  118.2 3.3 %collective-permute-done.14 = bf16[2,2,8192]{2,0,1:T(2,128)(2,1)S(1)} collective-permute-done((bf16[2,2,8192]{2,0,1:T(2,128)(2,1)S(1)}, bf16[2,2,8192]{2,0,1:T(2,128)(2,1)S(1)}, u32[]{:S(2)}, u32[]{:S(2)}) %collective-permute-start.14) | collective-permute-done | bytes 65568 | tf_op jit(solution)/shard_map/ppermute | solution.py:12
  121.4 8.3 %collective-permute-done.15 = bf16[2,2,8192]{2,0,1:T(2,128)(2,1)S(1)} collective-permute-done((bf16[2,2,8192]{2,0,1:T(2,128)(2,1)S(1)}, bf16[2,2,8192]{2,0,1:T(2,128)(2,1)S(1)}, u32[]{:S(2)}, u32[]{:S(2)}) %collective-permute-start.15) | collective-permute-done | bytes 65568 | tf_op jit(solution)/shard_map/ppermute | solution.py:12
  129.7 1.3 %fusion.59 = f32[2,1,8192]{2,1,0:T(1,128)} fusion(bf16[2,2,8192]{2,0,1:T(2,128)(2,1)S(1)} %collective-permute-done.15, bf16[2,2,8192]{2,0,1:T(2,128)(2,1)S(1)} %collective-permute-done.14, bf16[1,2,8192]{2,0,1:T(2,128)(2,1)S(1)} %collective-permute-done.13, f32[1,1,8192]{2,1,0:T(1,128)S(1)} %fusion.85, f32[1,1,8192]{2,1,0:T(1,128)S(1)} %bitcast.295, ...), kind=kLoop, calls=%fused_computation.119 | loop fusion | flops 622592 | bytes 950272 | tf_op jit(solution)/shard_map/add | solution.py:162
  (31 shorter events, 0.3 us)
Async XLA Ops:
  0.0 8.9 %collective-permute-start = (bf16[2,384,384]{2,1,0:T(8,128)(2,1)}, bf16[2,384,384]{2,1,0:T(8,128)(2,1)S(1)}, u32[]{:S(2)}, u32[]{:S(2)}) collective-permute-start(bf16[2,384,384]{2,1,0:T(8,128)(2,1)} %bitcast.290), channel_id=1, source_target_pairs={{0,1},{1,0},{2,3},{3,2},{4,5},{5,4},{6,7},{7,6},{8,9},{9,8},{10,11... | collective-permute-start | bytes 1769480 | tf_op jit(solution)/shard_map/ppermute | solution.py:64
  4.6 4.3 %copy-start.3 = (bf16[1,1,384,128]{2,3,1,0:T(8,128)(2,1)}, bf16[1,1,384,128]{2,3,1,0:T(8,128)(2,1)S(1)}, u32[]{:S(2)}) copy-start(bf16[1,1,384,128]{2,3,1,0:T(8,128)(2,1)S(1)} %copy.17) | copy-start | bytes 294916
  5.5 3.3 %collective-permute-start.1 = (bf16[384,128]{0,1:T(8,128)(2,1)S(1)}, bf16[384,128]{0,1:T(8,128)(2,1)S(1)}, u32[]{:S(2)}, u32[]{:S(2)}) collective-permute-start(bf16[384,128]{0,1:T(8,128)(2,1)S(1)} %broadcast_select_fusion), channel_id=1, source_target_pairs={{0,1},{1,0},{2,3},{3,2},{4,5},{5,4},{6,7},{7,6},{8,9},{9,8},{10,11... | collective-permute-start | bytes 294920 | tf_op jit(solution)/shard_map/ppermute | solution.py:64
  8.9 0.6 copy-start.7
  12.7 5.2 %copy-start.1 = (bf16[2,384,384]{2,1,0:T(8,128)(2,1)S(1)}, bf16[2,384,384]{2,1,0:T(8,128)(2,1)}, u32[]{:S(2)}) copy-start(bf16[2,384,384]{2,1,0:T(8,128)(2,1)} %get-tuple-element.113) | copy-start | bytes 1769476 | tf_op jit(solution)/shard_map/cond
  20.0 6.5 %collective-permute-start.3 = (bf16[768,64]{0,1:T(8,128)(2,1)S(1)}, bf16[768,64]{0,1:T(8,128)(2,1)S(1)}, u32[]{:S(2)}, u32[]{:S(2)}) collective-permute-start(bf16[768,64]{0,1:T(8,128)(2,1)S(1)} %pad_maximum_fusion.2), channel_id=1, source_target_pairs={{1,3},{3,5},{5,7},{7,9},{9,11},{11,13},{13,15},{2,0},{4,2},{6,4},{... | collective-permute-start | bytes 294920 | tf_op jit(solution)/shard_map/ppermute | solution.py:85
  22.4 12.0 %collective-permute-start.2 = (bf16[2,384,384]{1,2,0:T(8,128)(2,1)}, bf16[2,384,384]{1,2,0:T(8,128)(2,1)S(1)}, u32[]{:S(2)}, u32[]{:S(2)}) collective-permute-start(bf16[2,384,384]{1,2,0:T(8,128)(2,1)} %get-tuple-element.137), channel_id=1, source_target_pairs={{1,3},{3,5},{5,7},{7,9},{9,11},{11,13},{13,15},{2,0},{4,2},{6,4},{... | collective-permute-start | bytes 1769480 | tf_op jit(solution)/shard_map/ppermute | solution.py:85
  26.9 10.8 %collective-permute-start.4 = (bf16[768,64]{0,1:T(8,128)(2,1)S(1)}, bf16[768,64]{0,1:T(8,128)(2,1)S(1)}, u32[]{:S(2)}, u32[]{:S(2)}) collective-permute-start(bf16[768,64]{0,1:T(8,128)(2,1)S(1)} %fusion.39), channel_id=1, source_target_pairs={{1,5},{3,7},{5,9},{7,11},{9,13},{11,15},{4,0},{6,2},{8,4},{10,6},{... | collective-permute-start | bytes 294920 | tf_op jit(solution)/shard_map/ppermute | solution.py:103
  38.0 11.0 %copy-start.11 = (s32[8192]{0:T(1024)S(1)}, s32[8192]{0:T(1024)}, u32[]{:S(2)}) copy-start(s32[8192]{0:T(1024)} %param.13) | copy-start | bytes 98308
  38.0 11.0 %copy-start.12 = (s32[8192]{0:T(1024)S(1)}, s32[8192]{0:T(1024)}, u32[]{:S(2)}) copy-start(s32[8192]{0:T(1024)} %param.12) | copy-start | bytes 98308
  38.1 8.8 %collective-permute-start.5 = (bf16[768,64]{0,1:T(8,128)(2,1)S(1)}, bf16[768,64]{0,1:T(8,128)(2,1)S(1)}, u32[]{:S(2)}, u32[]{:S(2)}) collective-permute-start(bf16[768,64]{0,1:T(8,128)(2,1)S(1)} %fusion.27), channel_id=1, source_target_pairs={{1,5},{3,7},{5,9},{7,11},{9,13},{11,15},{4,0},{6,2},{8,4},{10,6},{... | collective-permute-start | bytes 294920 | tf_op jit(solution)/shard_map/ppermute | solution.py:103
  47.2 8.6 %collective-permute-start.6 = (bf16[768,64]{0,1:T(8,128)(2,1)S(1)}, bf16[768,64]{0,1:T(8,128)(2,1)S(1)}, u32[]{:S(2)}, u32[]{:S(2)}) collective-permute-start(bf16[768,64]{0,1:T(8,128)(2,1)S(1)} %fusion.28), channel_id=1, source_target_pairs={{1,5},{3,7},{5,9},{7,11},{9,13},{11,15},{4,0},{6,2},{8,4},{10,6},{... | collective-permute-start | bytes 294920 | tf_op jit(solution)/shard_map/ppermute | solution.py:103
  49.1 9.1 %copy-start.13 = (s32[8]{0:T(128)S(1)}, s32[8]{0:T(128)}, u32[]{:S(2)}) copy-start(s32[8]{0:T(128)} %param.14) | copy-start | bytes 100
  49.1 13.0 %copy-start = (bf16[1,1,2,384,384]{4,3,2,1,0:T(8,128)(2,1)S(1)}, bf16[1,1,2,384,384]{4,3,2,1,0:T(8,128)(2,1)}, u32[]{:S(2)}) copy-start(bf16[1,1,2,384,384]{4,3,2,1,0:T(8,128)(2,1)} %param.9) | copy-start | bytes 1769476
  56.1 6.6 %copy-start.4 = (bf16[1,1,384,128]{2,3,1,0:T(8,128)(2,1)S(1)}, bf16[1,1,384,128]{2,3,1,0:T(8,128)(2,1)}, u32[]{:S(2)}) copy-start(bf16[1,1,384,128]{2,3,1,0:T(8,128)(2,1)} %copy-done.3) | copy-start | bytes 294916
  56.1 5.9 %collective-permute-start.7 = (bf16[384,128]{0,1:T(8,128)(2,1)S(1)}, bf16[384,128]{0,1:T(8,128)(2,1)S(1)}, u32[]{:S(2)}, u32[]{:S(2)}) collective-permute-start(bf16[384,128]{0,1:T(8,128)(2,1)S(1)} %pad_maximum_fusion.3), channel_id=1, source_target_pairs={{1,2},{3,4},{5,6},{7,8},{9,10},{11,12},{13,14},{2,1},{4,3},{6,5},{... | collective-permute-start | bytes 294920 | tf_op jit(solution)/shard_map/ppermute | solution.py:109
  69.4 28.0 %copy-start.10 = (f32[8,8192]{1,0:T(8,128)S(1)}, f32[8,8192]{1,0:T(8,128)}, u32[]{:S(2)}) copy-start(f32[8,8192]{1,0:T(8,128)} %param.15) | copy-start | bytes 786436
  70.5 28.0 %collective-permute-start.12 = (bf16[1,2,8192]{2,0,1:T(2,128)(2,1)S(1)}, bf16[1,2,8192]{2,0,1:T(2,128)(2,1)S(1)}, u32[]{:S(2)}, u32[]{:S(2)}) collective-permute-start(bf16[1,2,8192]{2,0,1:T(2,128)(2,1)S(1)} %copy.45), channel_id=1, source_target_pairs={{0,16},{16,32},{32,48},{48,64},{64,80},{80,96},{96,112},{112,128},... | collective-permute-start | bytes 98312 | tf_op jit(solution)/shard_map/ppermute | solution.py:12
  74.8 23.8 %collective-permute-start.13 = (bf16[1,2,8192]{2,0,1:T(2,128)(2,1)S(1)}, bf16[1,2,8192]{2,0,1:T(2,128)(2,1)S(1)}, u32[]{:S(2)}, u32[]{:S(2)}) collective-permute-start(bf16[1,2,8192]{2,0,1:T(2,128)(2,1)S(1)} %copy.45), channel_id=1, source_target_pairs={{0,32},{16,48},{32,64},{48,80},{64,96},{80,112},{96,128},{112,144}... | collective-permute-start | bytes 98312 | tf_op jit(solution)/shard_map/ppermute | solution.py:12
  80.9 17.7 %collective-permute-start.8 = (bf16[1,2,8192]{2,0,1:T(2,128)(2,1)S(1)}, bf16[1,2,8192]{2,0,1:T(2,128)(2,1)S(1)}, u32[]{:S(2)}, u32[]{:S(2)}) collective-permute-start(bf16[1,2,8192]{2,0,1:T(2,128)(2,1)S(1)} %copy.45), channel_id=1, source_target_pairs={{16,0},{32,16},{48,32},{64,48},{80,64},{96,80},{112,96},{128,112},... | collective-permute-start | bytes 98312 | tf_op jit(solution)/shard_map/ppermute | solution.py:12
  92.6 7.5 %collective-permute-start.9 = (bf16[1,2,8192]{2,0,1:T(2,128)(2,1)S(1)}, bf16[1,2,8192]{2,0,1:T(2,128)(2,1)S(1)}, u32[]{:S(2)}, u32[]{:S(2)}) collective-permute-start(bf16[1,2,8192]{2,0,1:T(2,128)(2,1)S(1)} %copy.45), channel_id=1, source_target_pairs={{32,0},{48,16},{64,32},{80,48},{96,64},{112,80},{128,96},{144,112}... | collective-permute-start | bytes 98312 | tf_op jit(solution)/shard_map/ppermute | solution.py:12
  100.6 17.6 %collective-permute-start.10 = (bf16[2,2,8192]{2,0,1:T(2,128)(2,1)S(1)}, bf16[2,2,8192]{2,0,1:T(2,128)(2,1)S(1)}, u32[]{:S(2)}, u32[]{:S(2)}) collective-permute-start(bf16[2,2,8192]{2,0,1:T(2,128)(2,1)S(1)} %get-tuple-element.174), channel_id=1, source_target_pairs={{64,0},{80,16},{96,32},{112,48},{128,64},{144,80},{160,96},{176,11... | collective-permute-start | bytes 196616 | tf_op jit(solution)/shard_map/ppermute | solution.py:12
  108.5 9.7 %collective-permute-start.11 = (bf16[2,2,8192]{2,0,1:T(2,128)(2,1)S(1)}, bf16[2,2,8192]{2,0,1:T(2,128)(2,1)S(1)}, u32[]{:S(2)}, u32[]{:S(2)}) collective-permute-start(bf16[2,2,8192]{2,0,1:T(2,128)(2,1)S(1)} %get-tuple-element.175), channel_id=1, source_target_pairs={{48,0},{64,16},{80,32},{96,48},{112,64},{128,80},{144,96},{160,112... | collective-permute-start | bytes 196616 | tf_op jit(solution)/shard_map/ppermute | solution.py:12
  110.4 11.0 %collective-permute-start.14 = (bf16[2,2,8192]{2,0,1:T(2,128)(2,1)S(1)}, bf16[2,2,8192]{2,0,1:T(2,128)(2,1)S(1)}, u32[]{:S(2)}, u32[]{:S(2)}) collective-permute-start(bf16[2,2,8192]{2,0,1:T(2,128)(2,1)S(1)} %get-tuple-element.176), channel_id=1, source_target_pairs={{0,48},{16,64},{32,80},{48,96},{64,112},{80,128},{96,144},{112,160... | collective-permute-start | bytes 196616 | tf_op jit(solution)/shard_map/ppermute | solution.py:12
  116.1 13.6 %collective-permute-start.15 = (bf16[2,2,8192]{2,0,1:T(2,128)(2,1)S(1)}, bf16[2,2,8192]{2,0,1:T(2,128)(2,1)S(1)}, u32[]{:S(2)}, u32[]{:S(2)}) collective-permute-start(bf16[2,2,8192]{2,0,1:T(2,128)(2,1)S(1)} %get-tuple-element.177), channel_id=1, source_target_pairs={{0,64},{16,80},{32,96},{48,112},{64,128},{80,144},{96,160},{112,17... | collective-permute-start | bytes 196616 | tf_op jit(solution)/shard_map/ppermute | solution.py:12

commit v12 on v10

--- a/solution.py
+++ b/solution.py
@@ -111,10 +111,10 @@
     hand_over = [(s, s + 1) for s in range(1, count - 1, 2)]
     hand_over += [(s, s - 1) for s in range(2, count, 2)]
     neighbour = lax.ppermute(state, "section", hand_over)
-    other = jnp.where(
+    other = lax.cond(
         odd,
-        (complex_product(blocks, neighbour, True) + backward_src).astype(jnp.bfloat16),
-        (complex_product(blocks, neighbour, False) + forward_src).astype(jnp.bfloat16),
+        lambda: (complex_product(blocks, neighbour, True) + backward_src).astype(jnp.bfloat16),
+        lambda: (complex_product(blocks, neighbour, False) + forward_src).astype(jnp.bfloat16),
     )
     return state, other
 

time: 124 us -> 124 us (level)
    unnamed x18 -> x21, local copies, waits for them, and re-layouts: 3.87 us -> 2.76 us
  transfers between devices with their start and end apart: 16 -> 16, of which waited for: 10 -> 11; matrix products, arithmetic and copies ran while one was open for 5% -> 4% of each run, Pallas kernels for 0% -> 0%
where the time goes in v12:
time: 124 us
  starting transfers between devices  62.5 us (50%)
  waiting for transfers between devices  39.5 us (32%)
  matrix products  10.3 us (8%)
  other arithmetic  7.35 us (6%)
  local copies, waits for them, and re-layouts  3.14 us (3%)
    ppermute x8, starting transfers between devices, passed_along(): lax.ppermute(value, axis, [(source, source + steps) for source in range(l...  45.3 us
    ppermute x8, waiting for transfers between devices, passed_along(): lax.ppermute(value, axis, [(source, source + steps) for source in range(l...  14.1 us
    ppermute x3, waiting for transfers between devices, sweeps(): arrived = lax.ppermute(state, 'section', stride)  13.8 us
    ppermute x2, waiting for transfers between devices, sweeps(): lax.ppermute((own_map, chain_src), 'section', chain)  6.75 us
    ppermute x3, starting transfers between devices, sweeps(): arrived = lax.ppermute(state, 'section', stride)  6.21 us
    dot_general x2, matrix products, picked_rows(): jnp.einsum('ar,ap->rp', table, selector.astype(table.dtype), preferred_el...  5.64 us
    ppermute x2, starting transfers between devices, sweeps(): lax.ppermute((own_map, chain_src), 'section', chain)  4.72 us
    ppermute x2, starting transfers between devices, sweeps(): lax.ppermute((blocks, jnp.where(odd, backward_src, forward_src)), 'sectio...  4.32 us
  transfers between devices with their start and end apart: 16, of which 11 were waited for; matrix products, arithmetic and copies ran while one was open for 4% of the time, Pallas kernels for 0%

profile of v12, /device:TPU:22, one launch (start us, length us, event | category | flops | bytes accessed | tf_op | source)
XLA Modules:
  0.0 123.5 jit_solution(729231608862832210)
XLA Ops:
  0.0 0.9 copy.65
  0.9 1.9 %collective-permute-start = (bf16[2,384,384]{2,1,0:T(8,128)(2,1)}, bf16[2,384,384]{2,1,0:T(8,128)(2,1)S(1)}, u32[]{:S(2)}, u32[]{:S(2)}) collective-permute-start(bf16[2,384,384]{2,1,0:T(8,128)(2,1)} %bitcast.221), channel_id=1, source_target_pairs={{0,1},{1,0},{2,3},{3,2},{4,5},{5,4},{6,7},{7,6},{8,9},{9,8},{10,11... | collective-permute-start | bytes 1769480 | tf_op jit(solution)/shard_map/ppermute | solution.py:64
  2.8 0.9 broadcast_select_fusion
  3.7 2.4 %collective-permute-start.1 = (bf16[384,128]{1,0:T(8,128)(2,1)S(1)}, bf16[384,128]{1,0:T(8,128)(2,1)S(1)}, u32[]{:S(2)}, u32[]{:S(2)}) collective-permute-start(bf16[384,128]{1,0:T(8,128)(2,1)S(1)} %broadcast_select_fusion), channel_id=1, source_target_pairs={{0,1},{1,0},{2,3},{3,2},{4,5},{5,4},{6,7},{7,6},{8,9},{9,8},{10,11... | collective-permute-start | bytes 294920 | tf_op jit(solution)/shard_map/ppermute | solution.py:64
  6.2 0.9 collective-permute-done.1
  7.1 0.0 collective-permute-done
  7.1 4.3 %conditional.6 = (bf16[1,384,384]{2,1,0:T(8,128)(2,1)S(1)}, bf16[1,384,384]{2,1,0:T(8,128)(2,1)S(1)}, f32[384,128]{0,1:T(8,128)S(1)}, bf16[384,128]{1,0:T(8,128)...) conditional(s32[]{:T(128)} %convert_element_type.303, (bf16[2,384,384]{2,1,0:T(8,128)(2,1)}, ...), branch_computations={%region_1.2_spmd, %region_2.3_spmd} | conditional | flops 529317888 | bytes 12681320
  7.1 1.4 %fusion.7 = f32[2,384,128]{1,2,0:T(8,128)S(1)} fusion(bf16[2,384,384]{2,1,0:T(8,128)(2,1)} %get-tuple-element.76, bf16[384,128]{1,0:T(8,128)(2,1)S(1)} %get-tuple-element.122), kind=kOutput, calls=%fused_computation.13 | convolution fusion | flops 75497472 | bytes 1081344 | tf_op jit(solution)/shard_map/cond/branch_0_fun/cji,jn->cin/dot_general | solution.py:18
  8.6 0.8 convolution_bitcast_fusion
  9.4 0.0 copy-start.4
  9.4 0.2 fusion.1
  9.6 0.9 copy.37
  10.5 0.9 copy.39
  11.4 0.1 copy.21
  11.6 2.4 %collective-permute-start.3 = (bf16[768,64]{0,1:T(8,128)(2,1)S(1)}, bf16[768,64]{0,1:T(8,128)(2,1)S(1)}, u32[]{:S(2)}, u32[]{:S(2)}) collective-permute-start(bf16[768,64]{0,1:T(8,128)(2,1)S(1)} %pad_maximum_fusion.4), channel_id=1, source_target_pairs={{1,3},{3,5},{5,7},{7,9},{9,11},{11,13},{13,15},{2,0},{4,2},{6,4},{... | collective-permute-start | bytes 294920 | tf_op jit(solution)/shard_map/ppermute | solution.py:89
  14.0 2.4 %collective-permute-start.2 = (bf16[2,384,384]{2,1,0:T(8,128)(2,1)S(1)}, bf16[2,384,384]{2,1,0:T(8,128)(2,1)S(1)}, u32[]{:S(2)}, u32[]{:S(2)}) collective-permute-start(bf16[2,384,384]{2,1,0:T(8,128)(2,1)S(1)} %constant_dynamic-update-slice_fusion), channel_id=1, source_target_pairs={{1,3},{3,5},{5,7},{7,9},{9,11},{11,13},{13,15},{2,0},{4,2},{6,4},{... | collective-permute-start | bytes 1769480 | tf_op jit(solution)/shard_map/ppermute | solution.py:89
  16.4 1.7 %collective-permute-done.3 = bf16[768,64]{0,1:T(8,128)(2,1)S(1)} collective-permute-done((bf16[768,64]{0,1:T(8,128)(2,1)S(1)}, bf16[768,64]{0,1:T(8,128)(2,1)S(1)}, u32[]{:S(2)}, u32[]{:S(2)}) %collective-permute-start.3) | collective-permute-done | bytes 98336 | tf_op jit(solution)/shard_map/ppermute | solution.py:89
  18.1 0.3 fusion.46
  18.5 2.2 %collective-permute-start.4 = (bf16[768,64]{0,1:T(8,128)(2,1)S(1)}, bf16[768,64]{0,1:T(8,128)(2,1)S(1)}, u32[]{:S(2)}, u32[]{:S(2)}) collective-permute-start(bf16[768,64]{0,1:T(8,128)(2,1)S(1)} %fusion.43), channel_id=1, source_target_pairs={{1,5},{3,7},{5,9},{7,11},{9,13},{11,15},{4,0},{6,2},{8,4},{10,6},{... | collective-permute-start | bytes 294920 | tf_op jit(solution)/shard_map/ppermute | solution.py:107
  20.8 5.0 %collective-permute-done.2 = bf16[2,384,384]{2,1,0:T(8,128)(2,1)S(1)} collective-permute-done((bf16[2,384,384]{2,1,0:T(8,128)(2,1)S(1)}, bf16[2,384,384]{2,1,0:T(8,128)(2,1)S(1)}, u32[]{:S(2)}, u32[]{:S(2)}) %collective-permute-start.2) | collective-permute-done | bytes 589856 | tf_op jit(solution)/shard_map/ppermute | solution.py:89
  25.8 0.8 convolution_bitcast_fusion.2
  26.6 1.1 fusion.79
  27.7 1.0 fusion.40
  28.8 0.3 collective-permute-done.4
  29.1 0.3 fusion.31
  29.4 0.0 copy-start.7
  29.5 2.1 %collective-permute-start.5 = (bf16[768,64]{0,1:T(8,128)(2,1)S(1)}, bf16[768,64]{0,1:T(8,128)(2,1)S(1)}, u32[]{:S(2)}, u32[]{:S(2)}) collective-permute-start(bf16[768,64]{0,1:T(8,128)(2,1)S(1)} %fusion.31), channel_id=1, source_target_pairs={{1,5},{3,7},{5,9},{7,11},{9,13},{11,15},{4,0},{6,2},{8,4},{10,6},{... | collective-permute-start | bytes 294920 | tf_op jit(solution)/shard_map/ppermute | solution.py:107
  31.5 6.7 %collective-permute-done.5 = bf16[768,64]{0,1:T(8,128)(2,1)S(1)} collective-permute-done((bf16[768,64]{0,1:T(8,128)(2,1)S(1)}, bf16[768,64]{0,1:T(8,128)(2,1)S(1)}, u32[]{:S(2)}, u32[]{:S(2)}) %collective-permute-start.5) | collective-permute-done | bytes 98336 | tf_op jit(solution)/shard_map/ppermute | solution.py:107
  38.2 0.3 fusion.32
  38.5 1.9 %collective-permute-start.6 = (bf16[768,64]{0,1:T(8,128)(2,1)S(1)}, bf16[768,64]{0,1:T(8,128)(2,1)S(1)}, u32[]{:S(2)}, u32[]{:S(2)}) collective-permute-start(bf16[768,64]{0,1:T(8,128)(2,1)S(1)} %fusion.32), channel_id=1, source_target_pairs={{1,5},{3,7},{5,9},{7,11},{9,13},{11,15},{4,0},{6,2},{8,4},{10,6},{... | collective-permute-start | bytes 294920 | tf_op jit(solution)/shard_map/ppermute | solution.py:107
  40.5 0.0 copy-start.8
  40.5 0.0 copy-start
  40.5 0.0 copy-start.3
  40.5 6.7 %collective-permute-done.6 = bf16[768,64]{0,1:T(8,128)(2,1)S(1)} collective-permute-done((bf16[768,64]{0,1:T(8,128)(2,1)S(1)}, bf16[768,64]{0,1:T(8,128)(2,1)S(1)}, u32[]{:S(2)}, u32[]{:S(2)}) %collective-permute-start.6) | collective-permute-done | bytes 98336 | tf_op jit(solution)/shard_map/ppermute | solution.py:107
  47.3 0.3 fusion.33
  47.6 1.9 %collective-permute-start.7 = (bf16[384,128]{0,1:T(8,128)(2,1)S(1)}, bf16[384,128]{0,1:T(8,128)(2,1)S(1)}, u32[]{:S(2)}, u32[]{:S(2)}) collective-permute-start(bf16[384,128]{0,1:T(8,128)(2,1)S(1)} %pad_maximum_fusion.5), channel_id=1, source_target_pairs={{1,2},{3,4},{5,6},{7,8},{9,10},{11,12},{13,14},{2,1},{4,3},{6,5},{... | collective-permute-start | bytes 294920 | tf_op jit(solution)/shard_map/ppermute | solution.py:113
  49.6 4.0 %collective-permute-done.7 = bf16[384,128]{0,1:T(8,128)(2,1)S(1)} collective-permute-done((bf16[384,128]{0,1:T(8,128)(2,1)S(1)}, bf16[384,128]{0,1:T(8,128)(2,1)S(1)}, u32[]{:S(2)}, u32[]{:S(2)}) %collective-permute-start.7) | collective-permute-done | bytes 98336 | tf_op jit(solution)/shard_map/ppermute | solution.py:113
  53.6 0.7 conditional.5
  53.6 0.3 fusion.19
  53.9 0.1 copy.41
  54.3 2.6 %fusion.26 = f32[128,8192]{1,0:T(8,128)S(1)} fusion(s32[8192]{0:T(1024)S(1)} %get-tuple-element.173, f32[384,128]{1,0:T(8,128)S(1)} %get-tuple-element.130, bf16[384,128]{1,0:T(8,128)(2,1)S(1)} %get-tuple-element.105), kind=kOutput, calls=%fused_computation.46 | convolution fusion | flops 808599552 | bytes 4521984 | tf_op jit(solution)/shard_map/ar,ap->rp/dot_general | solution.py:55
  56.9 3.0 %multiply_reduce_fusion = (f32[8192]{0:T(1024)S(1)}, f32[128,8192]{1,0:T(8,128)S(1)}) fusion(f32[128,8192]{1,0:T(8,128)S(1)} %fusion.26, s32[8192]{0:T(1024)S(1)} %get-tuple-element.172, bf16[384,64]{0,1:T(8,128)(2,1)S(1)} %get-tuple-element.163, bf16[384,64]{0,1:T(8,128)(2,1)S(1)} %get-tuple-element.162), kind=kOutput, calls=%fused_computation.49 | convolution fusion | flops 810737664 | bytes 8552448 | tf_op jit(solution)/shard_map/ar,ap->rp/dot_general | solution.py:55
  59.9 0.0 copy-start.5
  59.9 0.9 fusion.29
  60.8 0.1 maximum_multiply_fusion
  60.9 0.1 copy.46
  61.0 4.3 %collective-permute-start.12 = (bf16[1,2,8192]{2,0,1:T(2,128)(2,1)S(1)}, bf16[1,2,8192]{2,0,1:T(2,128)(2,1)S(1)}, u32[]{:S(2)}, u32[]{:S(2)}) collective-permute-start(bf16[1,2,8192]{2,0,1:T(2,128)(2,1)S(1)} %copy.46), channel_id=1, source_target_pairs={{0,16},{16,32},{32,48},{48,64},{64,80},{80,96},{96,112},{112,128},... | collective-permute-start | bytes 98312 | tf_op jit(solution)/shard_map/ppermute | solution.py:12
  65.3 6.1 %collective-permute-start.13 = (bf16[1,2,8192]{2,0,1:T(2,128)(2,1)S(1)}, bf16[1,2,8192]{2,0,1:T(2,128)(2,1)S(1)}, u32[]{:S(2)}, u32[]{:S(2)}) collective-permute-start(bf16[1,2,8192]{2,0,1:T(2,128)(2,1)S(1)} %copy.46), channel_id=1, source_target_pairs={{0,32},{16,48},{32,64},{48,80},{64,96},{80,112},{96,128},{112,144}... | collective-permute-start | bytes 98312 | tf_op jit(solution)/shard_map/ppermute | solution.py:12
  71.4 12.0 %collective-permute-start.8 = (bf16[1,2,8192]{2,0,1:T(2,128)(2,1)S(1)}, bf16[1,2,8192]{2,0,1:T(2,128)(2,1)S(1)}, u32[]{:S(2)}, u32[]{:S(2)}) collective-permute-start(bf16[1,2,8192]{2,0,1:T(2,128)(2,1)S(1)} %copy.46), channel_id=1, source_target_pairs={{16,0},{32,16},{48,32},{64,48},{80,64},{96,80},{112,96},{128,112},... | collective-permute-start | bytes 98312 | tf_op jit(solution)/shard_map/ppermute | solution.py:12
  83.3 4.8 %collective-permute-start.9 = (bf16[1,2,8192]{2,0,1:T(2,128)(2,1)S(1)}, bf16[1,2,8192]{2,0,1:T(2,128)(2,1)S(1)}, u32[]{:S(2)}, u32[]{:S(2)}) collective-permute-start(bf16[1,2,8192]{2,0,1:T(2,128)(2,1)S(1)} %copy.46), channel_id=1, source_target_pairs={{32,0},{48,16},{64,32},{80,48},{96,64},{112,80},{128,96},{144,112}... | collective-permute-start | bytes 98312 | tf_op jit(solution)/shard_map/ppermute | solution.py:12
  88.2 1.1 select_reduce_fusion.12
  89.3 0.0 collective-permute-done.12
  89.3 0.0 collective-permute-done.13
  89.3 0.0 collective-permute-done.8
  89.3 1.5 %collective-permute-done.9 = bf16[1,2,8192]{2,0,1:T(2,128)(2,1)S(1)} collective-permute-done((bf16[1,2,8192]{2,0,1:T(2,128)(2,1)S(1)}, bf16[1,2,8192]{2,0,1:T(2,128)(2,1)S(1)}, u32[]{:S(2)}, u32[]{:S(2)}) %collective-permute-start.9) | collective-permute-done | bytes 32800 | tf_op jit(solution)/shard_map/ppermute | solution.py:12
  90.8 0.5 pad_maximum_fusion.6
  91.3 8.6 %collective-permute-start.10 = (bf16[2,2,8192]{2,0,1:T(2,128)(2,1)S(1)}, bf16[2,2,8192]{2,0,1:T(2,128)(2,1)S(1)}, u32[]{:S(2)}, u32[]{:S(2)}) collective-permute-start(bf16[2,2,8192]{2,0,1:T(2,128)(2,1)S(1)} %get-tuple-element.168), channel_id=1, source_target_pairs={{64,0},{80,16},{96,32},{112,48},{128,64},{144,80},{160,96},{176,11... | collective-permute-start | bytes 196616 | tf_op jit(solution)/shard_map/ppermute | solution.py:12
  100.0 1.9 %collective-permute-start.11 = (bf16[2,2,8192]{2,0,1:T(2,128)(2,1)S(1)}, bf16[2,2,8192]{2,0,1:T(2,128)(2,1)S(1)}, u32[]{:S(2)}, u32[]{:S(2)}) collective-permute-start(bf16[2,2,8192]{2,0,1:T(2,128)(2,1)S(1)} %get-tuple-element.169), channel_id=1, source_target_pairs={{48,0},{64,16},{80,32},{96,48},{112,64},{128,80},{144,96},{160,112... | collective-permute-start | bytes 196616 | tf_op jit(solution)/shard_map/ppermute | solution.py:12
  101.9 5.7 %collective-permute-start.14 = (bf16[2,2,8192]{2,0,1:T(2,128)(2,1)S(1)}, bf16[2,2,8192]{2,0,1:T(2,128)(2,1)S(1)}, u32[]{:S(2)}, u32[]{:S(2)}) collective-permute-start(bf16[2,2,8192]{2,0,1:T(2,128)(2,1)S(1)} %get-tuple-element.170), channel_id=1, source_target_pairs={{0,48},{16,64},{32,80},{48,96},{64,112},{80,128},{96,144},{112,160... | collective-permute-start | bytes 196616 | tf_op jit(solution)/shard_map/ppermute | solution.py:12
  107.6 1.9 %collective-permute-start.15 = (bf16[2,2,8192]{2,0,1:T(2,128)(2,1)S(1)}, bf16[2,2,8192]{2,0,1:T(2,128)(2,1)S(1)}, u32[]{:S(2)}, u32[]{:S(2)}) collective-permute-start(bf16[2,2,8192]{2,0,1:T(2,128)(2,1)S(1)} %get-tuple-element.171), channel_id=1, source_target_pairs={{0,64},{16,80},{32,96},{48,112},{64,128},{80,144},{96,160},{112,17... | collective-permute-start | bytes 196616 | tf_op jit(solution)/shard_map/ppermute | solution.py:12
  109.6 0.1 collective-permute-done.11
  109.7 3.0 %collective-permute-done.14 = bf16[2,2,8192]{2,0,1:T(2,128)(2,1)S(1)} collective-permute-done((bf16[2,2,8192]{2,0,1:T(2,128)(2,1)S(1)}, bf16[2,2,8192]{2,0,1:T(2,128)(2,1)S(1)}, u32[]{:S(2)}, u32[]{:S(2)}) %collective-permute-start.14) | collective-permute-done | bytes 65568 | tf_op jit(solution)/shard_map/ppermute | solution.py:12
  112.7 9.5 %collective-permute-done.15 = bf16[2,2,8192]{2,0,1:T(2,128)(2,1)S(1)} collective-permute-done((bf16[2,2,8192]{2,0,1:T(2,128)(2,1)S(1)}, bf16[2,2,8192]{2,0,1:T(2,128)(2,1)S(1)}, u32[]{:S(2)}, u32[]{:S(2)}) %collective-permute-start.15) | collective-permute-done | bytes 65568 | tf_op jit(solution)/shard_map/ppermute | solution.py:12
  122.2 1.3 %fusion.51 = f32[2,1,8192]{2,1,0:T(1,128)} fusion(bf16[2,2,8192]{2,0,1:T(2,128)(2,1)S(1)} %collective-permute-done.15, bf16[2,2,8192]{2,0,1:T(2,128)(2,1)S(1)} %collective-permute-done.14, bf16[1,2,8192]{2,0,1:T(2,128)(2,1)S(1)} %collective-permute-done.13, f32[1,1,8192]{2,1,0:T(1,128)S(1)} %fusion.77, f32[1,1,8192]{2,1,0:T(1,128)S(1)} %bitcast.235, ...), kind=kLoop, calls=%fused_computation.105 | loop fusion | flops 622592 | bytes 950272 | tf_op jit(solution)/shard_map/add | solution.py:166
  (31 shorter events, 0.4 us)
Async XLA Ops:
  0.9 6.2 %collective-permute-start = (bf16[2,384,384]{2,1,0:T(8,128)(2,1)}, bf16[2,384,384]{2,1,0:T(8,128)(2,1)S(1)}, u32[]{:S(2)}, u32[]{:S(2)}) collective-permute-start(bf16[2,384,384]{2,1,0:T(8,128)(2,1)} %bitcast.221), channel_id=1, source_target_pairs={{0,1},{1,0},{2,3},{3,2},{4,5},{5,4},{6,7},{7,6},{8,9},{9,8},{10,11... | collective-permute-start | bytes 1769480 | tf_op jit(solution)/shard_map/ppermute | solution.py:64
  3.7 3.3 %collective-permute-start.1 = (bf16[384,128]{1,0:T(8,128)(2,1)S(1)}, bf16[384,128]{1,0:T(8,128)(2,1)S(1)}, u32[]{:S(2)}, u32[]{:S(2)}) collective-permute-start(bf16[384,128]{1,0:T(8,128)(2,1)S(1)} %broadcast_select_fusion), channel_id=1, source_target_pairs={{0,1},{1,0},{2,3},{3,2},{4,5},{5,4},{6,7},{7,6},{8,9},{9,8},{10,11... | collective-permute-start | bytes 294920 | tf_op jit(solution)/shard_map/ppermute | solution.py:64
  7.1 1.5 %copy-start.1 = (bf16[2,384,384]{2,1,0:T(8,128)(2,1)S(1)}, bf16[2,384,384]{2,1,0:T(8,128)(2,1)}, u32[]{:S(2)}) copy-start(bf16[2,384,384]{2,1,0:T(8,128)(2,1)} %get-tuple-element.76) | copy-start | bytes 1769476
  9.4 1.9 %copy-start.4 = (bf16[384,128]{1,0:T(8,128)(2,1)S(1)}, bf16[384,128]{1,0:T(8,128)(2,1)}, u32[]{:S(2)}) copy-start(bf16[384,128]{1,0:T(8,128)(2,1)} %get-tuple-element.192) | copy-start | bytes 294916
  11.6 6.5 %collective-permute-start.3 = (bf16[768,64]{0,1:T(8,128)(2,1)S(1)}, bf16[768,64]{0,1:T(8,128)(2,1)S(1)}, u32[]{:S(2)}, u32[]{:S(2)}) collective-permute-start(bf16[768,64]{0,1:T(8,128)(2,1)S(1)} %pad_maximum_fusion.4), channel_id=1, source_target_pairs={{1,3},{3,5},{5,7},{7,9},{9,11},{11,13},{13,15},{2,0},{4,2},{6,4},{... | collective-permute-start | bytes 294920 | tf_op jit(solution)/shard_map/ppermute | solution.py:89
  14.0 11.8 %collective-permute-start.2 = (bf16[2,384,384]{2,1,0:T(8,128)(2,1)S(1)}, bf16[2,384,384]{2,1,0:T(8,128)(2,1)S(1)}, u32[]{:S(2)}, u32[]{:S(2)}) collective-permute-start(bf16[2,384,384]{2,1,0:T(8,128)(2,1)S(1)} %constant_dynamic-update-slice_fusion), channel_id=1, source_target_pairs={{1,3},{3,5},{5,7},{7,9},{9,11},{11,13},{13,15},{2,0},{4,2},{6,4},{... | collective-permute-start | bytes 1769480 | tf_op jit(solution)/shard_map/ppermute | solution.py:89
  18.5 10.6 %collective-permute-start.4 = (bf16[768,64]{0,1:T(8,128)(2,1)S(1)}, bf16[768,64]{0,1:T(8,128)(2,1)S(1)}, u32[]{:S(2)}, u32[]{:S(2)}) collective-permute-start(bf16[768,64]{0,1:T(8,128)(2,1)S(1)} %fusion.43), channel_id=1, source_target_pairs={{1,5},{3,7},{5,9},{7,11},{9,13},{11,15},{4,0},{6,2},{8,4},{10,6},{... | collective-permute-start | bytes 294920 | tf_op jit(solution)/shard_map/ppermute | solution.py:107
  29.4 11.0 %copy-start.6 = (s32[8192]{0:T(1024)S(1)}, s32[8192]{0:T(1024)}, u32[]{:S(2)}) copy-start(s32[8192]{0:T(1024)} %param.15) | copy-start | bytes 98308
  29.4 11.0 %copy-start.7 = (s32[8192]{0:T(1024)S(1)}, s32[8192]{0:T(1024)}, u32[]{:S(2)}) copy-start(s32[8192]{0:T(1024)} %param.14) | copy-start | bytes 98308
  29.5 8.8 %collective-permute-start.5 = (bf16[768,64]{0,1:T(8,128)(2,1)S(1)}, bf16[768,64]{0,1:T(8,128)(2,1)S(1)}, u32[]{:S(2)}, u32[]{:S(2)}) collective-permute-start(bf16[768,64]{0,1:T(8,128)(2,1)S(1)} %fusion.31), channel_id=1, source_target_pairs={{1,5},{3,7},{5,9},{7,11},{9,13},{11,15},{4,0},{6,2},{8,4},{10,6},{... | collective-permute-start | bytes 294920 | tf_op jit(solution)/shard_map/ppermute | solution.py:107
  38.5 8.7 %collective-permute-start.6 = (bf16[768,64]{0,1:T(8,128)(2,1)S(1)}, bf16[768,64]{0,1:T(8,128)(2,1)S(1)}, u32[]{:S(2)}, u32[]{:S(2)}) collective-permute-start(bf16[768,64]{0,1:T(8,128)(2,1)S(1)} %fusion.32), channel_id=1, source_target_pairs={{1,5},{3,7},{5,9},{7,11},{9,13},{11,15},{4,0},{6,2},{8,4},{10,6},{... | collective-permute-start | bytes 294920 | tf_op jit(solution)/shard_map/ppermute | solution.py:107
  40.5 9.1 %copy-start.8 = (s32[8]{0:T(128)S(1)}, s32[8]{0:T(128)}, u32[]{:S(2)}) copy-start(s32[8]{0:T(128)} %param.16) | copy-start | bytes 100
  40.5 13.1 %copy-start = (bf16[1,1,2,384,384]{4,3,2,1,0:T(8,128)(2,1)S(1)}, bf16[1,1,2,384,384]{4,3,2,1,0:T(8,128)(2,1)}, u32[]{:S(2)}) copy-start(bf16[1,1,2,384,384]{4,3,2,1,0:T(8,128)(2,1)} %param.11) | copy-start | bytes 1769476
  40.5 13.0 %copy-start.3 = (bf16[1,1,384,128]{3,2,1,0:T(8,128)(2,1)S(1)}, bf16[1,1,384,128]{3,2,1,0:T(8,128)(2,1)}, u32[]{:S(2)}) copy-start(bf16[1,1,384,128]{3,2,1,0:T(8,128)(2,1)} %param.13) | copy-start | bytes 294916
  47.6 5.9 %collective-permute-start.7 = (bf16[384,128]{0,1:T(8,128)(2,1)S(1)}, bf16[384,128]{0,1:T(8,128)(2,1)S(1)}, u32[]{:S(2)}, u32[]{:S(2)}) collective-permute-start(bf16[384,128]{0,1:T(8,128)(2,1)S(1)} %pad_maximum_fusion.5), channel_id=1, source_target_pairs={{1,2},{3,4},{5,6},{7,8},{9,10},{11,12},{13,14},{2,1},{4,3},{6,5},{... | collective-permute-start | bytes 294920 | tf_op jit(solution)/shard_map/ppermute | solution.py:113
  59.9 28.3 %copy-start.5 = (f32[8,8192]{1,0:T(8,128)S(1)}, f32[8,8192]{1,0:T(8,128)}, u32[]{:S(2)}) copy-start(f32[8,8192]{1,0:T(8,128)} %param.17) | copy-start | bytes 786436
  61.0 28.3 %collective-permute-start.12 = (bf16[1,2,8192]{2,0,1:T(2,128)(2,1)S(1)}, bf16[1,2,8192]{2,0,1:T(2,128)(2,1)S(1)}, u32[]{:S(2)}, u32[]{:S(2)}) collective-permute-start(bf16[1,2,8192]{2,0,1:T(2,128)(2,1)S(1)} %copy.46), channel_id=1, source_target_pairs={{0,16},{16,32},{32,48},{48,64},{64,80},{80,96},{96,112},{112,128},... | collective-permute-start | bytes 98312 | tf_op jit(solution)/shard_map/ppermute | solution.py:12
  65.3 24.0 %collective-permute-start.13 = (bf16[1,2,8192]{2,0,1:T(2,128)(2,1)S(1)}, bf16[1,2,8192]{2,0,1:T(2,128)(2,1)S(1)}, u32[]{:S(2)}, u32[]{:S(2)}) collective-permute-start(bf16[1,2,8192]{2,0,1:T(2,128)(2,1)S(1)} %copy.46), channel_id=1, source_target_pairs={{0,32},{16,48},{32,64},{48,80},{64,96},{80,112},{96,128},{112,144}... | collective-permute-start | bytes 98312 | tf_op jit(solution)/shard_map/ppermute | solution.py:12
  71.4 18.0 %collective-permute-start.8 = (bf16[1,2,8192]{2,0,1:T(2,128)(2,1)S(1)}, bf16[1,2,8192]{2,0,1:T(2,128)(2,1)S(1)}, u32[]{:S(2)}, u32[]{:S(2)}) collective-permute-start(bf16[1,2,8192]{2,0,1:T(2,128)(2,1)S(1)} %copy.46), channel_id=1, source_target_pairs={{16,0},{32,16},{48,32},{64,48},{80,64},{96,80},{112,96},{128,112},... | collective-permute-start | bytes 98312 | tf_op jit(solution)/shard_map/ppermute | solution.py:12
  83.3 7.5 %collective-permute-start.9 = (bf16[1,2,8192]{2,0,1:T(2,128)(2,1)S(1)}, bf16[1,2,8192]{2,0,1:T(2,128)(2,1)S(1)}, u32[]{:S(2)}, u32[]{:S(2)}) collective-permute-start(bf16[1,2,8192]{2,0,1:T(2,128)(2,1)S(1)} %copy.46), channel_id=1, source_target_pairs={{32,0},{48,16},{64,32},{80,48},{96,64},{112,80},{128,96},{144,112}... | collective-permute-start | bytes 98312 | tf_op jit(solution)/shard_map/ppermute | solution.py:12
  91.3 18.2 %collective-permute-start.10 = (bf16[2,2,8192]{2,0,1:T(2,128)(2,1)S(1)}, bf16[2,2,8192]{2,0,1:T(2,128)(2,1)S(1)}, u32[]{:S(2)}, u32[]{:S(2)}) collective-permute-start(bf16[2,2,8192]{2,0,1:T(2,128)(2,1)S(1)} %get-tuple-element.168), channel_id=1, source_target_pairs={{64,0},{80,16},{96,32},{112,48},{128,64},{144,80},{160,96},{176,11... | collective-permute-start | bytes 196616 | tf_op jit(solution)/shard_map/ppermute | solution.py:12
  100.0 9.7 %collective-permute-start.11 = (bf16[2,2,8192]{2,0,1:T(2,128)(2,1)S(1)}, bf16[2,2,8192]{2,0,1:T(2,128)(2,1)S(1)}, u32[]{:S(2)}, u32[]{:S(2)}) collective-permute-start(bf16[2,2,8192]{2,0,1:T(2,128)(2,1)S(1)} %get-tuple-element.169), channel_id=1, source_target_pairs={{48,0},{64,16},{80,32},{96,48},{112,64},{128,80},{144,96},{160,112... | collective-permute-start | bytes 196616 | tf_op jit(solution)/shard_map/ppermute | solution.py:12
  101.9 10.8 %collective-permute-start.14 = (bf16[2,2,8192]{2,0,1:T(2,128)(2,1)S(1)}, bf16[2,2,8192]{2,0,1:T(2,128)(2,1)S(1)}, u32[]{:S(2)}, u32[]{:S(2)}) collective-permute-start(bf16[2,2,8192]{2,0,1:T(2,128)(2,1)S(1)} %get-tuple-element.170), channel_id=1, source_target_pairs={{0,48},{16,64},{32,80},{48,96},{64,112},{80,128},{96,144},{112,160... | collective-permute-start | bytes 196616 | tf_op jit(solution)/shard_map/ppermute | solution.py:12
  107.6 14.5 %collective-permute-start.15 = (bf16[2,2,8192]{2,0,1:T(2,128)(2,1)S(1)}, bf16[2,2,8192]{2,0,1:T(2,128)(2,1)S(1)}, u32[]{:S(2)}, u32[]{:S(2)}) collective-permute-start(bf16[2,2,8192]{2,0,1:T(2,128)(2,1)S(1)} %get-tuple-element.171), channel_id=1, source_target_pairs={{0,64},{16,80},{32,96},{48,112},{64,128},{80,144},{96,160},{112,17... | collective-permute-start | bytes 196616 | tf_op jit(solution)/shard_map/ppermute | solution.py:12

commit v13 on v10

--- a/solution.py
+++ b/solution.py
@@ -61,9 +61,13 @@
     count = lax.axis_size("section")
     odd = lax.axis_index("section") % 2 == 1
     swap = [(2 * y + side, 2 * y + 1 - side) for y in range(count // 2) for side in (0, 1)]
-    other_blocks, other_src = lax.ppermute(
-        (blocks, jnp.where(odd, backward_src, forward_src)), "section", swap
+    width = blocks.shape[1]
+    packed = jnp.concatenate(
+        [blocks[0], blocks[1], jnp.where(odd, backward_src, forward_src)], axis=1
     )
+    arrived = lax.ppermute(packed, "section", swap)
+    other_blocks = jnp.stack([arrived[:, :width], arrived[:, width:2 * width]])
+    other_src = arrived[:, 2 * width:]
 
     def forward_pair():
         real_part, imag_part = matrix_product(blocks, other_blocks)

time: 124 us -> 119 us (0.960)
  the two profiles are of different devices: /device:TPU:22 before, /device:TPU:149 now
where the time goes in v13:
time: 119 us
  starting transfers between devices  74.9 us (63%)
  waiting for transfers between devices  20.1 us (17%)
  matrix products  9.62 us (8%)
  other arithmetic  7.4 us (6%)
  local copies, waits for them, and re-layouts  6.18 us (5%)
    ppermute x8, starting transfers between devices, passed_along(): lax.ppermute(value, axis, [(source, source + steps) for source in range(l...  43.1 us
    ppermute x3, starting transfers between devices, sweeps(): arrived = lax.ppermute(state, 'section', stride)  14.9 us
    ppermute x8, waiting for transfers between devices, passed_along(): lax.ppermute(value, axis, [(source, source + steps) for source in range(l...  9.16 us
    ppermute x2, starting transfers between devices, sweeps(): lax.ppermute((own_map, chain_src), 'section', chain)  7.62 us
    ppermute x1, starting transfers between devices, sweeps(): neighbour = lax.ppermute(state, 'section', hand_over)  6.68 us
    dot_general x2, matrix products, picked_rows(): jnp.einsum('ar,ap->rp', table, selector.astype(table.dtype), preferred_el...  5.81 us
    unnamed x18, local copies, waits for them, and re-layouts  4.86 us
    ppermute x3, waiting for transfers between devices, sweeps(): arrived = lax.ppermute(state, 'section', stride)  4.25 us
  transfers between devices with their start and end apart: 15, of which 8 were waited for; matrix products, arithmetic and copies ran while one was open for 4% of the time, Pallas kernels for 0%

profile of v13, /device:TPU:149, one launch (start us, length us, event | category | flops | bytes accessed | tf_op | source)
XLA Modules:
  0.0 118.7 jit_solution(17935187228725981191)
XLA Ops:
  0.0 1.0 copy.15
  1.0 1.0 copy.16
  2.0 1.1 fusion.90
  3.1 0.2 copy.42
  3.4 0.0 copy-start
  3.4 0.2 copy.43
  3.6 0.1 pad_maximum_fusion.2
  3.7 2.6 %collective-permute-start = (bf16[384,896]{0,1:T(8,128)(2,1)S(1)}, bf16[384,896]{0,1:T(8,128)(2,1)S(1)}, u32[]{:S(2)}, u32[]{:S(2)}) collective-permute-start(bf16[384,896]{0,1:T(8,128)(2,1)S(1)} %pad_maximum_fusion.2), channel_id=1, source_target_pairs={{0,1},{1,0},{2,3},{3,2},{4,5},{5,4},{6,7},{7,6},{8,9},{9,8},{10,11... | collective-permute-start | bytes 2064392 | tf_op jit(solution)/shard_map/ppermute | solution.py:68
  6.3 1.7 %collective-permute-done = bf16[384,896]{0,1:T(8,128)(2,1)S(1)} collective-permute-done((bf16[384,896]{0,1:T(8,128)(2,1)S(1)}, bf16[384,896]{0,1:T(8,128)(2,1)S(1)}, u32[]{:S(2)}, u32[]{:S(2)}) %collective-permute-start) | collective-permute-done | bytes 688160 | tf_op jit(solution)/shard_map/ppermute | solution.py:68
  8.0 0.1 slice_bitcast_fusion.3
  8.1 0.1 pad_maximum_fusion.3
  8.2 4.5 %conditional.3 = (bf16[1,384,384]{2,1,0:T(8,128)(2,1)S(1)}, bf16[1,384,384]{2,1,0:T(8,128)(2,1)S(1)}, f32[384,128]{0,1:T(8,128)S(1)}, bf16[384,128]{0,1:T(8,128)...) conditional(s32[]{:T(128)} %convert_element_type.304, (bf16[2,384,384]{2,1,0:T(8,128)(2,1)S(1)}, ...), branch_computations={%region_1.2_spmd, %region_2.3_spmd} | conditional | flops 529317888 | bytes 9928752
  8.2 0.3 fusion.15
  8.6 0.8 convolution_bitcast_fusion.1
  9.4 0.9 fusion.9
  10.3 1.2 copy.11
  11.5 1.2 copy.12
  12.8 3.2 %collective-permute-start.2 = (bf16[768,64]{0,1:T(8,128)(2,1)S(1)}, bf16[768,64]{0,1:T(8,128)(2,1)S(1)}, u32[]{:S(2)}, u32[]{:S(2)}) collective-permute-start(bf16[768,64]{0,1:T(8,128)(2,1)S(1)} %pad_maximum_fusion.4), channel_id=1, source_target_pairs={{1,3},{3,5},{5,7},{7,9},{9,11},{11,13},{13,15},{2,0},{4,2},{6,4},{... | collective-permute-start | bytes 294920 | tf_op jit(solution)/shard_map/ppermute | solution.py:93
  16.1 4.4 %collective-permute-start.1 = (bf16[2,384,384]{2,1,0:T(8,128)(2,1)S(1)}, bf16[2,384,384]{2,1,0:T(8,128)(2,1)S(1)}, u32[]{:S(2)}, u32[]{:S(2)}) collective-permute-start(bf16[2,384,384]{2,1,0:T(8,128)(2,1)S(1)} %constant_dynamic-update-slice_fusion), channel_id=1, source_target_pairs={{1,3},{3,5},{5,7},{7,9},{9,11},{11,13},{13,15},{2,0},{4,2},{6,4},{... | collective-permute-start | bytes 1769480 | tf_op jit(solution)/shard_map/ppermute | solution.py:93
  20.5 0.0 collective-permute-done.2
  20.5 0.3 fusion.47
  20.9 4.3 %collective-permute-start.3 = (bf16[768,64]{0,1:T(8,128)(2,1)S(1)}, bf16[768,64]{0,1:T(8,128)(2,1)S(1)}, u32[]{:S(2)}, u32[]{:S(2)}) collective-permute-start(bf16[768,64]{0,1:T(8,128)(2,1)S(1)} %fusion.35), channel_id=1, source_target_pairs={{1,5},{3,7},{5,9},{7,11},{9,13},{11,15},{4,0},{6,2},{8,4},{10,6},{... | collective-permute-start | bytes 294920 | tf_op jit(solution)/shard_map/ppermute | solution.py:111
  25.2 2.8 %collective-permute-done.1 = bf16[2,384,384]{2,1,0:T(8,128)(2,1)S(1)} collective-permute-done((bf16[2,384,384]{2,1,0:T(8,128)(2,1)S(1)}, bf16[2,384,384]{2,1,0:T(8,128)(2,1)S(1)}, u32[]{:S(2)}, u32[]{:S(2)}) %collective-permute-start.1) | collective-permute-done | bytes 589856 | tf_op jit(solution)/shard_map/ppermute | solution.py:93
  28.1 0.8 convolution_bitcast_fusion.2
  28.9 1.1 fusion.88
  30.0 1.0 fusion.32
  31.0 0.0 collective-permute-done.3
  31.0 0.3 fusion.23
  31.4 0.0 copy-start.3
  31.4 4.7 %collective-permute-start.4 = (bf16[768,64]{0,1:T(8,128)(2,1)S(1)}, bf16[768,64]{0,1:T(8,128)(2,1)S(1)}, u32[]{:S(2)}, u32[]{:S(2)}) collective-permute-start(bf16[768,64]{0,1:T(8,128)(2,1)S(1)} %fusion.23), channel_id=1, source_target_pairs={{1,5},{3,7},{5,9},{7,11},{9,13},{11,15},{4,0},{6,2},{8,4},{10,6},{... | collective-permute-start | bytes 294920 | tf_op jit(solution)/shard_map/ppermute | solution.py:111
  36.0 2.6 %collective-permute-done.4 = bf16[768,64]{0,1:T(8,128)(2,1)S(1)} collective-permute-done((bf16[768,64]{0,1:T(8,128)(2,1)S(1)}, bf16[768,64]{0,1:T(8,128)(2,1)S(1)}, u32[]{:S(2)}, u32[]{:S(2)}) %collective-permute-start.4) | collective-permute-done | bytes 98336 | tf_op jit(solution)/shard_map/ppermute | solution.py:111
  38.6 0.3 fusion.24
  39.0 5.9 %collective-permute-start.5 = (bf16[768,64]{0,1:T(8,128)(2,1)S(1)}, bf16[768,64]{0,1:T(8,128)(2,1)S(1)}, u32[]{:S(2)}, u32[]{:S(2)}) collective-permute-start(bf16[768,64]{0,1:T(8,128)(2,1)S(1)} %fusion.24), channel_id=1, source_target_pairs={{1,5},{3,7},{5,9},{7,11},{9,13},{11,15},{4,0},{6,2},{8,4},{10,6},{... | collective-permute-start | bytes 294920 | tf_op jit(solution)/shard_map/ppermute | solution.py:111
  44.9 0.0 copy-start.4
  44.9 1.7 %collective-permute-done.5 = bf16[768,64]{0,1:T(8,128)(2,1)S(1)} collective-permute-done((bf16[768,64]{0,1:T(8,128)(2,1)S(1)}, bf16[768,64]{0,1:T(8,128)(2,1)S(1)}, u32[]{:S(2)}, u32[]{:S(2)}) %collective-permute-start.5) | collective-permute-done | bytes 98336 | tf_op jit(solution)/shard_map/ppermute | solution.py:111
  46.6 0.3 fusion.25
  47.0 6.7 %collective-permute-start.6 = (bf16[384,128]{0,1:T(8,128)(2,1)S(1)}, bf16[384,128]{0,1:T(8,128)(2,1)S(1)}, u32[]{:S(2)}, u32[]{:S(2)}) collective-permute-start(bf16[384,128]{0,1:T(8,128)(2,1)S(1)} %pad_maximum_fusion.5), channel_id=1, source_target_pairs={{1,2},{3,4},{5,6},{7,8},{9,10},{11,12},{13,14},{2,1},{4,3},{6,5},{... | collective-permute-start | bytes 294920 | tf_op jit(solution)/shard_map/ppermute | solution.py:117
  53.7 2.1 %collective-permute-done.6 = bf16[384,128]{0,1:T(8,128)(2,1)S(1)} collective-permute-done((bf16[384,128]{0,1:T(8,128)(2,1)S(1)}, bf16[384,128]{0,1:T(8,128)(2,1)S(1)}, u32[]{:S(2)}, u32[]{:S(2)}) %collective-permute-start.6) | collective-permute-done | bytes 98336 | tf_op jit(solution)/shard_map/ppermute | solution.py:117
  55.8 0.3 convolution_bitcast_fusion.3
  56.1 0.3 convolution_bitcast_fusion.4
  56.4 2.8 %fusion.18 = f32[128,8192]{1,0:T(8,128)S(1)} fusion(s32[8192]{0:T(1024)S(1)} %get-tuple-element.150, f32[384,64]{0,1:T(8,128)S(1)} %get-tuple-element.136, f32[384,64]{0,1:T(8,128)S(1)} %get-tuple-element.135, f32[384,64]{0,1:T(8,128)S(1)} %get-tuple-element.166, f32[384,64]{0,1:T(8,128)S(1)} %get-tuple-element.167, pred[]{:T(512)S(6)} %eq.63, ...), kind=kOutput, calls=%fused_computation.32 | convolution fusion | flops 808894464 | bytes 4816897 | tf_op jit(solution)/shard_map/ar,ap->rp/dot_general | solution.py:55
  59.2 3.0 %multiply_reduce_fusion = (f32[8192]{0:T(1024)S(1)}, f32[128,8192]{1,0:T(8,128)S(1)}) fusion(f32[128,8192]{1,0:T(8,128)S(1)} %fusion.18, s32[8192]{0:T(1024)S(1)} %get-tuple-element.149, bf16[384,64]{0,1:T(8,128)(2,1)S(1)} %get-tuple-element.140, bf16[384,64]{0,1:T(8,128)(2,1)S(1)} %get-tuple-element.139), kind=kOutput, calls=%fused_computation.35 | convolution fusion | flops 810737664 | bytes 8552448 | tf_op jit(solution)/shard_map/ar,ap->rp/dot_general | solution.py:55
  62.2 0.0 copy-start.1
  62.2 0.9 fusion.21
  63.2 0.1 maximum_multiply_fusion
  63.2 0.1 copy.47
  63.3 4.0 %collective-permute-start.11 = (bf16[1,2,8192]{2,0,1:T(2,128)(2,1)S(1)}, bf16[1,2,8192]{2,0,1:T(2,128)(2,1)S(1)}, u32[]{:S(2)}, u32[]{:S(2)}) collective-permute-start(bf16[1,2,8192]{2,0,1:T(2,128)(2,1)S(1)} %copy.47), channel_id=1, source_target_pairs={{0,16},{16,32},{32,48},{48,64},{64,80},{80,96},{96,112},{112,128},... | collective-permute-start | bytes 98312 | tf_op jit(solution)/shard_map/ppermute | solution.py:12
  67.3 7.0 %collective-permute-start.12 = (bf16[1,2,8192]{2,0,1:T(2,128)(2,1)S(1)}, bf16[1,2,8192]{2,0,1:T(2,128)(2,1)S(1)}, u32[]{:S(2)}, u32[]{:S(2)}) collective-permute-start(bf16[1,2,8192]{2,0,1:T(2,128)(2,1)S(1)} %copy.47), channel_id=1, source_target_pairs={{0,32},{16,48},{32,64},{48,80},{64,96},{80,112},{96,128},{112,144}... | collective-permute-start | bytes 98312 | tf_op jit(solution)/shard_map/ppermute | solution.py:12
  74.3 1.9 %collective-permute-start.7 = (bf16[1,2,8192]{2,0,1:T(2,128)(2,1)S(1)}, bf16[1,2,8192]{2,0,1:T(2,128)(2,1)S(1)}, u32[]{:S(2)}, u32[]{:S(2)}) collective-permute-start(bf16[1,2,8192]{2,0,1:T(2,128)(2,1)S(1)} %copy.47), channel_id=1, source_target_pairs={{16,0},{32,16},{48,32},{64,48},{80,64},{96,80},{112,96},{128,112},... | collective-permute-start | bytes 98312 | tf_op jit(solution)/shard_map/ppermute | solution.py:12
  76.3 9.2 %collective-permute-start.8 = (bf16[1,2,8192]{2,0,1:T(2,128)(2,1)S(1)}, bf16[1,2,8192]{2,0,1:T(2,128)(2,1)S(1)}, u32[]{:S(2)}, u32[]{:S(2)}) collective-permute-start(bf16[1,2,8192]{2,0,1:T(2,128)(2,1)S(1)} %copy.47), channel_id=1, source_target_pairs={{32,0},{48,16},{64,32},{80,48},{96,64},{112,80},{128,96},{144,112}... | collective-permute-start | bytes 98312 | tf_op jit(solution)/shard_map/ppermute | solution.py:12
  85.5 1.1 select_reduce_fusion.12
  86.6 0.0 collective-permute-done.11
  86.6 0.0 collective-permute-done.7
  86.6 0.1 collective-permute-done.8
  86.8 0.5 pad_maximum_fusion.6
  87.3 8.4 %collective-permute-start.10 = (bf16[2,2,8192]{2,0,1:T(2,128)(2,1)S(1)}, bf16[2,2,8192]{2,0,1:T(2,128)(2,1)S(1)}, u32[]{:S(2)}, u32[]{:S(2)}) collective-permute-start(bf16[2,2,8192]{2,0,1:T(2,128)(2,1)S(1)} %get-tuple-element.146), channel_id=1, source_target_pairs={{48,0},{64,16},{80,32},{96,48},{112,64},{128,80},{144,96},{160,112... | collective-permute-start | bytes 196616 | tf_op jit(solution)/shard_map/ppermute | solution.py:12
  95.7 1.9 %collective-permute-start.13 = (bf16[2,2,8192]{2,0,1:T(2,128)(2,1)S(1)}, bf16[2,2,8192]{2,0,1:T(2,128)(2,1)S(1)}, u32[]{:S(2)}, u32[]{:S(2)}) collective-permute-start(bf16[2,2,8192]{2,0,1:T(2,128)(2,1)S(1)} %get-tuple-element.147), channel_id=1, source_target_pairs={{0,48},{16,64},{32,80},{48,96},{64,112},{80,128},{96,144},{112,160... | collective-permute-start | bytes 196616 | tf_op jit(solution)/shard_map/ppermute | solution.py:12
  97.7 6.0 %collective-permute-start.14 = (bf16[2,2,8192]{2,0,1:T(2,128)(2,1)S(1)}, bf16[2,2,8192]{2,0,1:T(2,128)(2,1)S(1)}, u32[]{:S(2)}, u32[]{:S(2)}) collective-permute-start(bf16[2,2,8192]{2,0,1:T(2,128)(2,1)S(1)} %get-tuple-element.148), channel_id=1, source_target_pairs={{0,64},{16,80},{32,96},{48,112},{64,128},{80,144},{96,160},{112,17... | collective-permute-start | bytes 196616 | tf_op jit(solution)/shard_map/ppermute | solution.py:12
  103.6 4.7 %collective-permute-start.9 = (bf16[2,2,8192]{2,0,1:T(2,128)(2,1)S(1)}, bf16[2,2,8192]{2,0,1:T(2,128)(2,1)S(1)}, u32[]{:S(2)}, u32[]{:S(2)}) collective-permute-start(bf16[2,2,8192]{2,0,1:T(2,128)(2,1)S(1)} %get-tuple-element.145), channel_id=1, source_target_pairs={{64,0},{80,16},{96,32},{112,48},{128,64},{144,80},{160,96},{176,11... | collective-permute-start | bytes 196616 | tf_op jit(solution)/shard_map/ppermute | solution.py:12
  108.3 0.0 collective-permute-done.10
  108.3 0.0 collective-permute-done.13
  108.3 3.6 %collective-permute-done.14 = bf16[2,2,8192]{2,0,1:T(2,128)(2,1)S(1)} collective-permute-done((bf16[2,2,8192]{2,0,1:T(2,128)(2,1)S(1)}, bf16[2,2,8192]{2,0,1:T(2,128)(2,1)S(1)}, u32[]{:S(2)}, u32[]{:S(2)}) %collective-permute-start.14) | collective-permute-done | bytes 65568 | tf_op jit(solution)/shard_map/ppermute | solution.py:12
  111.9 5.5 %collective-permute-done.9 = bf16[2,2,8192]{2,0,1:T(2,128)(2,1)S(1)} collective-permute-done((bf16[2,2,8192]{2,0,1:T(2,128)(2,1)S(1)}, bf16[2,2,8192]{2,0,1:T(2,128)(2,1)S(1)}, u32[]{:S(2)}, u32[]{:S(2)}) %collective-permute-start.9) | collective-permute-done | bytes 65568 | tf_op jit(solution)/shard_map/ppermute | solution.py:12
  117.3 1.3 %fusion.55 = f32[2,1,8192]{2,1,0:T(1,128)} fusion(bf16[2,2,8192]{2,0,1:T(2,128)(2,1)S(1)} %collective-permute-done.14, bf16[2,2,8192]{2,0,1:T(2,128)(2,1)S(1)} %collective-permute-done.13, bf16[1,2,8192]{2,0,1:T(2,128)(2,1)S(1)} %collective-permute-done.12, f32[1,1,8192]{2,1,0:T(1,128)S(1)} %fusion.81, f32[1,1,8192]{2,1,0:T(1,128)S(1)} %bitcast.251, ...), kind=kLoop, calls=%fused_computation.112 | loop fusion | flops 622592 | bytes 950272 | tf_op jit(solution)/shard_map/add | solution.py:170
  (28 shorter events, 0.4 us)
Async XLA Ops:
  3.4 4.8 %copy-start = (bf16[1,1,2,384,384]{4,3,2,1,0:T(8,128)(2,1)S(1)}, bf16[1,1,2,384,384]{4,3,2,1,0:T(8,128)(2,1)}, u32[]{:S(2)}) copy-start(bf16[1,1,2,384,384]{4,3,2,1,0:T(8,128)(2,1)} %param.9) | copy-start | bytes 1769476
  3.7 4.3 %collective-permute-start = (bf16[384,896]{0,1:T(8,128)(2,1)S(1)}, bf16[384,896]{0,1:T(8,128)(2,1)S(1)}, u32[]{:S(2)}, u32[]{:S(2)}) collective-permute-start(bf16[384,896]{0,1:T(8,128)(2,1)S(1)} %pad_maximum_fusion.2), channel_id=1, source_target_pairs={{0,1},{1,0},{2,3},{3,2},{4,5},{5,4},{6,7},{7,6},{8,9},{9,8},{10,11... | collective-permute-start | bytes 2064392 | tf_op jit(solution)/shard_map/ppermute | solution.py:68
  12.8 7.7 %collective-permute-start.2 = (bf16[768,64]{0,1:T(8,128)(2,1)S(1)}, bf16[768,64]{0,1:T(8,128)(2,1)S(1)}, u32[]{:S(2)}, u32[]{:S(2)}) collective-permute-start(bf16[768,64]{0,1:T(8,128)(2,1)S(1)} %pad_maximum_fusion.4), channel_id=1, source_target_pairs={{1,3},{3,5},{5,7},{7,9},{9,11},{11,13},{13,15},{2,0},{4,2},{6,4},{... | collective-permute-start | bytes 294920 | tf_op jit(solution)/shard_map/ppermute | solution.py:93
  16.1 12.0 %collective-permute-start.1 = (bf16[2,384,384]{2,1,0:T(8,128)(2,1)S(1)}, bf16[2,384,384]{2,1,0:T(8,128)(2,1)S(1)}, u32[]{:S(2)}, u32[]{:S(2)}) collective-permute-start(bf16[2,384,384]{2,1,0:T(8,128)(2,1)S(1)} %constant_dynamic-update-slice_fusion), channel_id=1, source_target_pairs={{1,3},{3,5},{5,7},{7,9},{9,11},{11,13},{13,15},{2,0},{4,2},{6,4},{... | collective-permute-start | bytes 1769480 | tf_op jit(solution)/shard_map/ppermute | solution.py:93
  20.9 10.1 %collective-permute-start.3 = (bf16[768,64]{0,1:T(8,128)(2,1)S(1)}, bf16[768,64]{0,1:T(8,128)(2,1)S(1)}, u32[]{:S(2)}, u32[]{:S(2)}) collective-permute-start(bf16[768,64]{0,1:T(8,128)(2,1)S(1)} %fusion.35), channel_id=1, source_target_pairs={{1,5},{3,7},{5,9},{7,11},{9,13},{11,15},{4,0},{6,2},{8,4},{10,6},{... | collective-permute-start | bytes 294920 | tf_op jit(solution)/shard_map/ppermute | solution.py:111
  31.4 13.5 %copy-start.2 = (s32[8192]{0:T(1024)S(1)}, s32[8192]{0:T(1024)}, u32[]{:S(2)}) copy-start(s32[8192]{0:T(1024)} %param.13) | copy-start | bytes 98308
  31.4 13.5 %copy-start.3 = (s32[8192]{0:T(1024)S(1)}, s32[8192]{0:T(1024)}, u32[]{:S(2)}) copy-start(s32[8192]{0:T(1024)} %param.12) | copy-start | bytes 98308
  31.4 7.3 %collective-permute-start.4 = (bf16[768,64]{0,1:T(8,128)(2,1)S(1)}, bf16[768,64]{0,1:T(8,128)(2,1)S(1)}, u32[]{:S(2)}, u32[]{:S(2)}) collective-permute-start(bf16[768,64]{0,1:T(8,128)(2,1)S(1)} %fusion.23), channel_id=1, source_target_pairs={{1,5},{3,7},{5,9},{7,11},{9,13},{11,15},{4,0},{6,2},{8,4},{10,6},{... | collective-permute-start | bytes 294920 | tf_op jit(solution)/shard_map/ppermute | solution.py:111
  39.0 7.6 %collective-permute-start.5 = (bf16[768,64]{0,1:T(8,128)(2,1)S(1)}, bf16[768,64]{0,1:T(8,128)(2,1)S(1)}, u32[]{:S(2)}, u32[]{:S(2)}) collective-permute-start(bf16[768,64]{0,1:T(8,128)(2,1)S(1)} %fusion.24), channel_id=1, source_target_pairs={{1,5},{3,7},{5,9},{7,11},{9,13},{11,15},{4,0},{6,2},{8,4},{10,6},{... | collective-permute-start | bytes 294920 | tf_op jit(solution)/shard_map/ppermute | solution.py:111
  44.9 8.7 %copy-start.4 = (s32[8]{0:T(128)S(1)}, s32[8]{0:T(128)}, u32[]{:S(2)}) copy-start(s32[8]{0:T(128)} %param.14) | copy-start | bytes 100
  47.0 8.8 %collective-permute-start.6 = (bf16[384,128]{0,1:T(8,128)(2,1)S(1)}, bf16[384,128]{0,1:T(8,128)(2,1)S(1)}, u32[]{:S(2)}, u32[]{:S(2)}) collective-permute-start(bf16[384,128]{0,1:T(8,128)(2,1)S(1)} %pad_maximum_fusion.5), channel_id=1, source_target_pairs={{1,2},{3,4},{5,6},{7,8},{9,10},{11,12},{13,14},{2,1},{4,3},{6,5},{... | collective-permute-start | bytes 294920 | tf_op jit(solution)/shard_map/ppermute | solution.py:117
  62.2 23.2 %copy-start.1 = (f32[8,8192]{1,0:T(8,128)S(1)}, f32[8,8192]{1,0:T(8,128)}, u32[]{:S(2)}) copy-start(f32[8,8192]{1,0:T(8,128)} %param.15) | copy-start | bytes 786436
  63.3 23.3 %collective-permute-start.11 = (bf16[1,2,8192]{2,0,1:T(2,128)(2,1)S(1)}, bf16[1,2,8192]{2,0,1:T(2,128)(2,1)S(1)}, u32[]{:S(2)}, u32[]{:S(2)}) collective-permute-start(bf16[1,2,8192]{2,0,1:T(2,128)(2,1)S(1)} %copy.47), channel_id=1, source_target_pairs={{0,16},{16,32},{32,48},{48,64},{64,80},{80,96},{96,112},{112,128},... | collective-permute-start | bytes 98312 | tf_op jit(solution)/shard_map/ppermute | solution.py:12
  67.3 19.3 %collective-permute-start.12 = (bf16[1,2,8192]{2,0,1:T(2,128)(2,1)S(1)}, bf16[1,2,8192]{2,0,1:T(2,128)(2,1)S(1)}, u32[]{:S(2)}, u32[]{:S(2)}) collective-permute-start(bf16[1,2,8192]{2,0,1:T(2,128)(2,1)S(1)} %copy.47), channel_id=1, source_target_pairs={{0,32},{16,48},{32,64},{48,80},{64,96},{80,112},{96,128},{112,144}... | collective-permute-start | bytes 98312 | tf_op jit(solution)/shard_map/ppermute | solution.py:12
  74.3 12.3 %collective-permute-start.7 = (bf16[1,2,8192]{2,0,1:T(2,128)(2,1)S(1)}, bf16[1,2,8192]{2,0,1:T(2,128)(2,1)S(1)}, u32[]{:S(2)}, u32[]{:S(2)}) collective-permute-start(bf16[1,2,8192]{2,0,1:T(2,128)(2,1)S(1)} %copy.47), channel_id=1, source_target_pairs={{16,0},{32,16},{48,32},{64,48},{80,64},{96,80},{112,96},{128,112},... | collective-permute-start | bytes 98312 | tf_op jit(solution)/shard_map/ppermute | solution.py:12
  76.3 10.5 %collective-permute-start.8 = (bf16[1,2,8192]{2,0,1:T(2,128)(2,1)S(1)}, bf16[1,2,8192]{2,0,1:T(2,128)(2,1)S(1)}, u32[]{:S(2)}, u32[]{:S(2)}) collective-permute-start(bf16[1,2,8192]{2,0,1:T(2,128)(2,1)S(1)} %copy.47), channel_id=1, source_target_pairs={{32,0},{48,16},{64,32},{80,48},{96,64},{112,80},{128,96},{144,112}... | collective-permute-start | bytes 98312 | tf_op jit(solution)/shard_map/ppermute | solution.py:12
  87.3 21.0 %collective-permute-start.10 = (bf16[2,2,8192]{2,0,1:T(2,128)(2,1)S(1)}, bf16[2,2,8192]{2,0,1:T(2,128)(2,1)S(1)}, u32[]{:S(2)}, u32[]{:S(2)}) collective-permute-start(bf16[2,2,8192]{2,0,1:T(2,128)(2,1)S(1)} %get-tuple-element.146), channel_id=1, source_target_pairs={{48,0},{64,16},{80,32},{96,48},{112,64},{128,80},{144,96},{160,112... | collective-permute-start | bytes 196616 | tf_op jit(solution)/shard_map/ppermute | solution.py:12
  95.7 12.6 %collective-permute-start.13 = (bf16[2,2,8192]{2,0,1:T(2,128)(2,1)S(1)}, bf16[2,2,8192]{2,0,1:T(2,128)(2,1)S(1)}, u32[]{:S(2)}, u32[]{:S(2)}) collective-permute-start(bf16[2,2,8192]{2,0,1:T(2,128)(2,1)S(1)} %get-tuple-element.147), channel_id=1, source_target_pairs={{0,48},{16,64},{32,80},{48,96},{64,112},{80,128},{96,144},{112,160... | collective-permute-start | bytes 196616 | tf_op jit(solution)/shard_map/ppermute | solution.py:12
  97.7 14.2 %collective-permute-start.14 = (bf16[2,2,8192]{2,0,1:T(2,128)(2,1)S(1)}, bf16[2,2,8192]{2,0,1:T(2,128)(2,1)S(1)}, u32[]{:S(2)}, u32[]{:S(2)}) collective-permute-start(bf16[2,2,8192]{2,0,1:T(2,128)(2,1)S(1)} %get-tuple-element.148), channel_id=1, source_target_pairs={{0,64},{16,80},{32,96},{48,112},{64,128},{80,144},{96,160},{112,17... | collective-permute-start | bytes 196616 | tf_op jit(solution)/shard_map/ppermute | solution.py:12
  103.6 13.7 %collective-permute-start.9 = (bf16[2,2,8192]{2,0,1:T(2,128)(2,1)S(1)}, bf16[2,2,8192]{2,0,1:T(2,128)(2,1)S(1)}, u32[]{:S(2)}, u32[]{:S(2)}) collective-permute-start(bf16[2,2,8192]{2,0,1:T(2,128)(2,1)S(1)} %get-tuple-element.145), channel_id=1, source_target_pairs={{64,0},{80,16},{96,32},{112,48},{128,64},{144,80},{160,96},{176,11... | collective-permute-start | bytes 196616 | tf_op jit(solution)/shard_map/ppermute | solution.py:12

commit v14 on v13

--- a/solution.py
+++ b/solution.py
@@ -90,7 +90,11 @@
     chain = [(2 * y + 1, 2 * y + 3) for y in range(chips - 1)]
     chain += [(2 * y, 2 * y - 2) for y in range(1, chips)]
     own_map = jnp.stack([real_part, imag_part])
-    upstream_map, upstream_src = lax.ppermute((own_map, chain_src), "section", chain)
+    upstream = lax.ppermute(
+        jnp.concatenate([real_part, imag_part, joined(chain_src)], axis=1), "section", chain
+    )
+    upstream_map = jnp.stack([upstream[:, :width], upstream[:, width:2 * width]])
+    upstream_src = stacked(upstream[:, 2 * width:])
     has_upstream = jnp.where(odd, chip >= 1, chip <= chips - 2)
     joint_real, joint_imag = matrix_product(own_map, upstream_map)
     joint_real = jnp.where(has_upstream, joint_real, real_part).astype(jnp.bfloat16)

time: 119 us -> 127 us (1.067)
  the two profiles are of different devices: /device:TPU:149 before, /device:TPU:18 now
where the time goes in v14:
time: 127 us; the launch traced here: 126 us
  starting transfers between devices  59.5 us (47%)
  waiting for transfers between devices  42.6 us (34%)
  matrix products  9.55 us (8%)
  other arithmetic  7.71 us (6%)
  local copies, waits for them, and re-layouts  5.67 us (4%)
    ppermute x8, starting transfers between devices, passed_along(): lax.ppermute(value, axis, [(source, source + steps) for source in range(l...  46.9 us
    ppermute x3, waiting for transfers between devices, sweeps(): arrived = lax.ppermute(state, 'section', stride)  16.8 us
    ppermute x1, waiting for transfers between devices, sweeps(): lax.ppermute(jnp.concatenate([real_part, imag_part, joined(chain_src)], a...  10.3 us
    ppermute x8, waiting for transfers between devices, passed_along(): lax.ppermute(value, axis, [(source, source + steps) for source in range(l...  9.61 us
    ppermute x3, starting transfers between devices, sweeps(): arrived = lax.ppermute(state, 'section', stride)  6.21 us
    dot_general x2, matrix products, picked_rows(): jnp.einsum('ar,ap->rp', table, selector.astype(table.dtype), preferred_el...  5.81 us
    ppermute x1, waiting for transfers between devices, sweeps(): neighbour = lax.ppermute(state, 'section', hand_over)  3.79 us
  transfers between devices with their start and end apart: 14, of which 9 were waited for; matrix products, arithmetic and copies ran while one was open for 3% of the time, Pallas kernels for 0%

profile of v14, /device:TPU:18, one launch (start us, length us, event | category | flops | bytes accessed | tf_op | source)
XLA Modules:
  0.0 125.6 jit_solution(10918234452786812359)
XLA Ops:
  0.0 1.0 copy.15
  1.0 1.0 copy.16
  2.0 1.1 fusion.89
  3.1 0.2 copy.41
  3.4 0.0 copy-start
  3.4 0.2 copy.42
  3.6 0.1 pad_maximum_fusion.2
  3.7 1.9 %collective-permute-start = (bf16[384,896]{0,1:T(8,128)(2,1)S(1)}, bf16[384,896]{0,1:T(8,128)(2,1)S(1)}, u32[]{:S(2)}, u32[]{:S(2)}) collective-permute-start(bf16[384,896]{0,1:T(8,128)(2,1)S(1)} %pad_maximum_fusion.2), channel_id=1, source_target_pairs={{0,1},{1,0},{2,3},{3,2},{4,5},{5,4},{6,7},{7,6},{8,9},{9,8},{10,11... | collective-permute-start | bytes 2064392 | tf_op jit(solution)/shard_map/ppermute | solution.py:68
  5.6 2.1 %collective-permute-done = bf16[384,896]{0,1:T(8,128)(2,1)S(1)} collective-permute-done((bf16[384,896]{0,1:T(8,128)(2,1)S(1)}, bf16[384,896]{0,1:T(8,128)(2,1)S(1)}, u32[]{:S(2)}, u32[]{:S(2)}) %collective-permute-start) | collective-permute-done | bytes 688160 | tf_op jit(solution)/shard_map/ppermute | solution.py:68
  7.7 0.1 slice_bitcast_fusion.5
  7.8 0.1 pad_maximum_fusion.4
  7.9 3.1 %conditional.3 = (bf16[1,384,384]{2,1,0:T(8,128)(2,1)S(1)}, bf16[1,384,384]{2,1,0:T(8,128)(2,1)S(1)}, f32[384,128]{0,1:T(8,128)S(1)}, bf16[384,384]{0,1:T(8,128)...) conditional(s32[]{:T(128)} %convert_element_type.300, ...), branch_computations={%region_1.2_spmd.clone, %region_2.3_spmd.clone} | conditional | flops 529317888 | bytes 9928752
  7.9 0.3 fusion.7
  8.2 0.8 convolution_bitcast_fusion
  9.0 0.2 fusion.1
  9.2 0.9 copy.35
  10.1 0.9 copy.37
  11.0 1.1 pad_maximum_fusion.3
  12.2 2.4 %collective-permute-start.1 = (bf16[384,896]{0,1:T(8,128)(2,1)S(1)}, bf16[384,896]{0,1:T(8,128)(2,1)S(1)}, u32[]{:S(2)}, u32[]{:S(2)}) collective-permute-start(bf16[384,896]{0,1:T(8,128)(2,1)S(1)} %pad_maximum_fusion.3), channel_id=1, source_target_pairs={{1,3},{3,5},{5,7},{7,9},{9,11},{11,13},{13,15},{2,0},{4,2},{6,4},{... | collective-permute-start | bytes 2064392 | tf_op jit(solution)/shard_map/ppermute | solution.py:93
  14.7 10.3 %collective-permute-done.1 = bf16[384,896]{0,1:T(8,128)(2,1)S(1)} collective-permute-done((bf16[384,896]{0,1:T(8,128)(2,1)S(1)}, bf16[384,896]{0,1:T(8,128)(2,1)S(1)}, u32[]{:S(2)}, u32[]{:S(2)}) %collective-permute-start.1) | collective-permute-done | bytes 688160 | tf_op jit(solution)/shard_map/ppermute | solution.py:93
  25.0 0.3 fusion.48
  25.4 2.2 %collective-permute-start.2 = (bf16[768,64]{0,1:T(8,128)(2,1)S(1)}, bf16[768,64]{0,1:T(8,128)(2,1)S(1)}, u32[]{:S(2)}, u32[]{:S(2)}) collective-permute-start(bf16[768,64]{0,1:T(8,128)(2,1)S(1)} %fusion.36), channel_id=1, source_target_pairs={{1,5},{3,7},{5,9},{7,11},{9,13},{11,15},{4,0},{6,2},{8,4},{10,6},{... | collective-permute-start | bytes 294920 | tf_op jit(solution)/shard_map/ppermute | solution.py:115
  27.6 0.1 slice_bitcast_fusion.3
  27.7 0.8 convolution_bitcast_fusion.2
  28.5 1.1 fusion.87
  29.6 1.0 fusion.32
  30.6 3.4 %collective-permute-done.2 = bf16[768,64]{0,1:T(8,128)(2,1)S(1)} collective-permute-done((bf16[768,64]{0,1:T(8,128)(2,1)S(1)}, bf16[768,64]{0,1:T(8,128)(2,1)S(1)}, u32[]{:S(2)}, u32[]{:S(2)}) %collective-permute-start.2) | collective-permute-done | bytes 98336 | tf_op jit(solution)/shard_map/ppermute | solution.py:115
  34.0 0.3 fusion.23
  34.3 0.0 copy-start.3
  34.3 2.1 %collective-permute-start.3 = (bf16[768,64]{0,1:T(8,128)(2,1)S(1)}, bf16[768,64]{0,1:T(8,128)(2,1)S(1)}, u32[]{:S(2)}, u32[]{:S(2)}) collective-permute-start(bf16[768,64]{0,1:T(8,128)(2,1)S(1)} %fusion.23), channel_id=1, source_target_pairs={{1,5},{3,7},{5,9},{7,11},{9,13},{11,15},{4,0},{6,2},{8,4},{10,6},{... | collective-permute-start | bytes 294920 | tf_op jit(solution)/shard_map/ppermute | solution.py:115
  36.4 6.7 %collective-permute-done.3 = bf16[768,64]{0,1:T(8,128)(2,1)S(1)} collective-permute-done((bf16[768,64]{0,1:T(8,128)(2,1)S(1)}, bf16[768,64]{0,1:T(8,128)(2,1)S(1)}, u32[]{:S(2)}, u32[]{:S(2)}) %collective-permute-start.3) | collective-permute-done | bytes 98336 | tf_op jit(solution)/shard_map/ppermute | solution.py:115
  43.1 0.3 fusion.24
  43.4 1.9 %collective-permute-start.4 = (bf16[768,64]{0,1:T(8,128)(2,1)S(1)}, bf16[768,64]{0,1:T(8,128)(2,1)S(1)}, u32[]{:S(2)}, u32[]{:S(2)}) collective-permute-start(bf16[768,64]{0,1:T(8,128)(2,1)S(1)} %fusion.24), channel_id=1, source_target_pairs={{1,5},{3,7},{5,9},{7,11},{9,13},{11,15},{4,0},{6,2},{8,4},{10,6},{... | collective-permute-start | bytes 294920 | tf_op jit(solution)/shard_map/ppermute | solution.py:115
  45.4 0.0 copy-start.4
  45.4 6.7 %collective-permute-done.4 = bf16[768,64]{0,1:T(8,128)(2,1)S(1)} collective-permute-done((bf16[768,64]{0,1:T(8,128)(2,1)S(1)}, bf16[768,64]{0,1:T(8,128)(2,1)S(1)}, u32[]{:S(2)}, u32[]{:S(2)}) %collective-permute-start.4) | collective-permute-done | bytes 98336 | tf_op jit(solution)/shard_map/ppermute | solution.py:115
  52.1 0.3 fusion.25
  52.5 2.1 %collective-permute-start.5 = (bf16[384,128]{0,1:T(8,128)(2,1)S(1)}, bf16[384,128]{0,1:T(8,128)(2,1)S(1)}, u32[]{:S(2)}, u32[]{:S(2)}) collective-permute-start(bf16[384,128]{0,1:T(8,128)(2,1)S(1)} %pad_maximum_fusion.5), channel_id=1, source_target_pairs={{1,2},{3,4},{5,6},{7,8},{9,10},{11,12},{13,14},{2,1},{4,3},{6,5},{... | collective-permute-start | bytes 294920 | tf_op jit(solution)/shard_map/ppermute | solution.py:121
  54.7 3.8 %collective-permute-done.5 = bf16[384,128]{0,1:T(8,128)(2,1)S(1)} collective-permute-done((bf16[384,128]{0,1:T(8,128)(2,1)S(1)}, bf16[384,128]{0,1:T(8,128)(2,1)S(1)}, u32[]{:S(2)}, u32[]{:S(2)}) %collective-permute-start.5) | collective-permute-done | bytes 98336 | tf_op jit(solution)/shard_map/ppermute | solution.py:121
  58.5 0.3 convolution_bitcast_fusion.3
  58.8 0.3 convolution_bitcast_fusion.4
  59.1 2.8 %fusion.18 = f32[128,8192]{1,0:T(8,128)S(1)} fusion(s32[8192]{0:T(1024)S(1)} %get-tuple-element.184, f32[384,64]{0,1:T(8,128)S(1)} %get-tuple-element.172, f32[384,64]{0,1:T(8,128)S(1)} %get-tuple-element.171, f32[384,64]{0,1:T(8,128)S(1)} %get-tuple-element.200, f32[384,64]{0,1:T(8,128)S(1)} %get-tuple-element.201, pred[]{:T(512)S(6)} %eq.63, ...), kind=kOutput, calls=%fused_computation.32 | convolution fusion | flops 808894464 | bytes 4816897 | tf_op jit(solution)/shard_map/ar,ap->rp/dot_general | solution.py:55
  61.9 3.0 %multiply_reduce_fusion = (f32[8192]{0:T(1024)S(1)}, f32[128,8192]{1,0:T(8,128)S(1)}) fusion(f32[128,8192]{1,0:T(8,128)S(1)} %fusion.18, s32[8192]{0:T(1024)S(1)} %get-tuple-element.183, bf16[384,64]{0,1:T(8,128)(2,1)S(1)} %get-tuple-element.176, bf16[384,64]{0,1:T(8,128)(2,1)S(1)} %get-tuple-element.175), kind=kOutput, calls=%fused_computation.35 | convolution fusion | flops 810737664 | bytes 8552448 | tf_op jit(solution)/shard_map/ar,ap->rp/dot_general | solution.py:55
  64.9 0.0 copy-start.1
  64.9 0.9 fusion.21
  65.8 0.1 maximum_multiply_fusion
  65.9 0.1 copy.46
  66.0 4.3 %collective-permute-start.10 = (bf16[1,2,8192]{2,0,1:T(2,128)(2,1)S(1)}, bf16[1,2,8192]{2,0,1:T(2,128)(2,1)S(1)}, u32[]{:S(2)}, u32[]{:S(2)}) collective-permute-start(bf16[1,2,8192]{2,0,1:T(2,128)(2,1)S(1)} %copy.46), channel_id=1, source_target_pairs={{0,16},{16,32},{32,48},{48,64},{64,80},{80,96},{96,112},{112,128},... | collective-permute-start | bytes 98312 | tf_op jit(solution)/shard_map/ppermute | solution.py:12
  70.3 6.1 %collective-permute-start.11 = (bf16[1,2,8192]{2,0,1:T(2,128)(2,1)S(1)}, bf16[1,2,8192]{2,0,1:T(2,128)(2,1)S(1)}, u32[]{:S(2)}, u32[]{:S(2)}) collective-permute-start(bf16[1,2,8192]{2,0,1:T(2,128)(2,1)S(1)} %copy.46), channel_id=1, source_target_pairs={{0,32},{16,48},{32,64},{48,80},{64,96},{80,112},{96,128},{112,144}... | collective-permute-start | bytes 98312 | tf_op jit(solution)/shard_map/ppermute | solution.py:12
  76.4 11.7 %collective-permute-start.6 = (bf16[1,2,8192]{2,0,1:T(2,128)(2,1)S(1)}, bf16[1,2,8192]{2,0,1:T(2,128)(2,1)S(1)}, u32[]{:S(2)}, u32[]{:S(2)}) collective-permute-start(bf16[1,2,8192]{2,0,1:T(2,128)(2,1)S(1)} %copy.46), channel_id=1, source_target_pairs={{16,0},{32,16},{48,32},{64,48},{80,64},{96,80},{112,96},{128,112},... | collective-permute-start | bytes 98312 | tf_op jit(solution)/shard_map/ppermute | solution.py:12
  88.0 4.8 %collective-permute-start.7 = (bf16[1,2,8192]{2,0,1:T(2,128)(2,1)S(1)}, bf16[1,2,8192]{2,0,1:T(2,128)(2,1)S(1)}, u32[]{:S(2)}, u32[]{:S(2)}) collective-permute-start(bf16[1,2,8192]{2,0,1:T(2,128)(2,1)S(1)} %copy.46), channel_id=1, source_target_pairs={{32,0},{48,16},{64,32},{80,48},{96,64},{112,80},{128,96},{144,112}... | collective-permute-start | bytes 98312 | tf_op jit(solution)/shard_map/ppermute | solution.py:12
  92.9 1.1 select_reduce_fusion.12
  94.0 0.0 collective-permute-done.10
  94.0 0.0 collective-permute-done.6
  94.0 1.1 collective-permute-done.7
  95.1 0.5 pad_maximum_fusion.6
  95.6 1.9 %collective-permute-start.12 = (bf16[2,2,8192]{2,0,1:T(2,128)(2,1)S(1)}, bf16[2,2,8192]{2,0,1:T(2,128)(2,1)S(1)}, u32[]{:S(2)}, u32[]{:S(2)}) collective-permute-start(bf16[2,2,8192]{2,0,1:T(2,128)(2,1)S(1)} %get-tuple-element.181), channel_id=1, source_target_pairs={{0,48},{16,64},{32,80},{48,96},{64,112},{80,128},{96,144},{112,160... | collective-permute-start | bytes 196616 | tf_op jit(solution)/shard_map/ppermute | solution.py:12
  97.6 8.9 %collective-permute-start.13 = (bf16[2,2,8192]{2,0,1:T(2,128)(2,1)S(1)}, bf16[2,2,8192]{2,0,1:T(2,128)(2,1)S(1)}, u32[]{:S(2)}, u32[]{:S(2)}) collective-permute-start(bf16[2,2,8192]{2,0,1:T(2,128)(2,1)S(1)} %get-tuple-element.182), channel_id=1, source_target_pairs={{0,64},{16,80},{32,96},{48,112},{64,128},{80,144},{96,160},{112,17... | collective-permute-start | bytes 196616 | tf_op jit(solution)/shard_map/ppermute | solution.py:12
  106.5 3.8 %collective-permute-start.8 = (bf16[2,2,8192]{2,0,1:T(2,128)(2,1)S(1)}, bf16[2,2,8192]{2,0,1:T(2,128)(2,1)S(1)}, u32[]{:S(2)}, u32[]{:S(2)}) collective-permute-start(bf16[2,2,8192]{2,0,1:T(2,128)(2,1)S(1)} %get-tuple-element.179), channel_id=1, source_target_pairs={{64,0},{80,16},{96,32},{112,48},{128,64},{144,80},{160,96},{176,11... | collective-permute-start | bytes 196616 | tf_op jit(solution)/shard_map/ppermute | solution.py:12
  110.3 5.4 %collective-permute-start.9 = (bf16[2,2,8192]{2,0,1:T(2,128)(2,1)S(1)}, bf16[2,2,8192]{2,0,1:T(2,128)(2,1)S(1)}, u32[]{:S(2)}, u32[]{:S(2)}) collective-permute-start(bf16[2,2,8192]{2,0,1:T(2,128)(2,1)S(1)} %get-tuple-element.180), channel_id=1, source_target_pairs={{48,0},{64,16},{80,32},{96,48},{112,64},{128,80},{144,96},{160,112... | collective-permute-start | bytes 196616 | tf_op jit(solution)/shard_map/ppermute | solution.py:12
  115.7 0.0 collective-permute-done.12
  115.7 0.0 collective-permute-done.13
  115.7 3.4 %collective-permute-done.8 = bf16[2,2,8192]{2,0,1:T(2,128)(2,1)S(1)} collective-permute-done((bf16[2,2,8192]{2,0,1:T(2,128)(2,1)S(1)}, bf16[2,2,8192]{2,0,1:T(2,128)(2,1)S(1)}, u32[]{:S(2)}, u32[]{:S(2)}) %collective-permute-start.8) | collective-permute-done | bytes 65568 | tf_op jit(solution)/shard_map/ppermute | solution.py:12
  119.2 5.1 %collective-permute-done.9 = bf16[2,2,8192]{2,0,1:T(2,128)(2,1)S(1)} collective-permute-done((bf16[2,2,8192]{2,0,1:T(2,128)(2,1)S(1)}, bf16[2,2,8192]{2,0,1:T(2,128)(2,1)S(1)}, u32[]{:S(2)}, u32[]{:S(2)}) %collective-permute-start.9) | collective-permute-done | bytes 65568 | tf_op jit(solution)/shard_map/ppermute | solution.py:12
  124.3 1.3 %fusion.54 = f32[2,1,8192]{2,1,0:T(1,128)} fusion(bf16[2,2,8192]{2,0,1:T(2,128)(2,1)S(1)} %collective-permute-done.13, bf16[2,2,8192]{2,0,1:T(2,128)(2,1)S(1)} %collective-permute-done.12, bf16[1,2,8192]{2,0,1:T(2,128)(2,1)S(1)} %collective-permute-done.11, f32[1,1,8192]{2,1,0:T(1,128)S(1)} %fusion.80, f32[1,1,8192]{2,1,0:T(1,128)S(1)} %bitcast.255, ...), kind=kLoop, calls=%fused_computation.114 | loop fusion | flops 622592 | bytes 950272 | tf_op jit(solution)/shard_map/add | solution.py:174
  (26 shorter events, 0.4 us)
Async XLA Ops:
  3.4 4.5 %copy-start = (bf16[1,1,2,384,384]{4,3,2,1,0:T(8,128)(2,1)S(1)}, bf16[1,1,2,384,384]{4,3,2,1,0:T(8,128)(2,1)}, u32[]{:S(2)}) copy-start(bf16[1,1,2,384,384]{4,3,2,1,0:T(8,128)(2,1)} %param.9) | copy-start | bytes 1769476
  3.7 4.0 %collective-permute-start = (bf16[384,896]{0,1:T(8,128)(2,1)S(1)}, bf16[384,896]{0,1:T(8,128)(2,1)S(1)}, u32[]{:S(2)}, u32[]{:S(2)}) collective-permute-start(bf16[384,896]{0,1:T(8,128)(2,1)S(1)} %pad_maximum_fusion.2), channel_id=1, source_target_pairs={{0,1},{1,0},{2,3},{3,2},{4,5},{5,4},{6,7},{7,6},{8,9},{9,8},{10,11... | collective-permute-start | bytes 2064392 | tf_op jit(solution)/shard_map/ppermute | solution.py:68
  12.2 12.8 %collective-permute-start.1 = (bf16[384,896]{0,1:T(8,128)(2,1)S(1)}, bf16[384,896]{0,1:T(8,128)(2,1)S(1)}, u32[]{:S(2)}, u32[]{:S(2)}) collective-permute-start(bf16[384,896]{0,1:T(8,128)(2,1)S(1)} %pad_maximum_fusion.3), channel_id=1, source_target_pairs={{1,3},{3,5},{5,7},{7,9},{9,11},{11,13},{13,15},{2,0},{4,2},{6,4},{... | collective-permute-start | bytes 2064392 | tf_op jit(solution)/shard_map/ppermute | solution.py:93
  25.4 8.6 %collective-permute-start.2 = (bf16[768,64]{0,1:T(8,128)(2,1)S(1)}, bf16[768,64]{0,1:T(8,128)(2,1)S(1)}, u32[]{:S(2)}, u32[]{:S(2)}) collective-permute-start(bf16[768,64]{0,1:T(8,128)(2,1)S(1)} %fusion.36), channel_id=1, source_target_pairs={{1,5},{3,7},{5,9},{7,11},{9,13},{11,15},{4,0},{6,2},{8,4},{10,6},{... | collective-permute-start | bytes 294920 | tf_op jit(solution)/shard_map/ppermute | solution.py:115
  34.3 11.0 %copy-start.2 = (s32[8192]{0:T(1024)S(1)}, s32[8192]{0:T(1024)}, u32[]{:S(2)}) copy-start(s32[8192]{0:T(1024)} %param.13) | copy-start | bytes 98308
  34.3 11.0 %copy-start.3 = (s32[8192]{0:T(1024)S(1)}, s32[8192]{0:T(1024)}, u32[]{:S(2)}) copy-start(s32[8192]{0:T(1024)} %param.12) | copy-start | bytes 98308
  34.3 8.8 %collective-permute-start.3 = (bf16[768,64]{0,1:T(8,128)(2,1)S(1)}, bf16[768,64]{0,1:T(8,128)(2,1)S(1)}, u32[]{:S(2)}, u32[]{:S(2)}) collective-permute-start(bf16[768,64]{0,1:T(8,128)(2,1)S(1)} %fusion.23), channel_id=1, source_target_pairs={{1,5},{3,7},{5,9},{7,11},{9,13},{11,15},{4,0},{6,2},{8,4},{10,6},{... | collective-permute-start | bytes 294920 | tf_op jit(solution)/shard_map/ppermute | solution.py:115
  43.4 8.7 %collective-permute-start.4 = (bf16[768,64]{0,1:T(8,128)(2,1)S(1)}, bf16[768,64]{0,1:T(8,128)(2,1)S(1)}, u32[]{:S(2)}, u32[]{:S(2)}) collective-permute-start(bf16[768,64]{0,1:T(8,128)(2,1)S(1)} %fusion.24), channel_id=1, source_target_pairs={{1,5},{3,7},{5,9},{7,11},{9,13},{11,15},{4,0},{6,2},{8,4},{10,6},{... | collective-permute-start | bytes 294920 | tf_op jit(solution)/shard_map/ppermute | solution.py:115
  45.4 9.2 %copy-start.4 = (s32[8]{0:T(128)S(1)}, s32[8]{0:T(128)}, u32[]{:S(2)}) copy-start(s32[8]{0:T(128)} %param.14) | copy-start | bytes 100
  52.5 5.9 %collective-permute-start.5 = (bf16[384,128]{0,1:T(8,128)(2,1)S(1)}, bf16[384,128]{0,1:T(8,128)(2,1)S(1)}, u32[]{:S(2)}, u32[]{:S(2)}) collective-permute-start(bf16[384,128]{0,1:T(8,128)(2,1)S(1)} %pad_maximum_fusion.5), channel_id=1, source_target_pairs={{1,2},{3,4},{5,6},{7,8},{9,10},{11,12},{13,14},{2,1},{4,3},{6,5},{... | collective-permute-start | bytes 294920 | tf_op jit(solution)/shard_map/ppermute | solution.py:121
  64.9 28.0 %copy-start.1 = (f32[8,8192]{1,0:T(8,128)S(1)}, f32[8,8192]{1,0:T(8,128)}, u32[]{:S(2)}) copy-start(f32[8,8192]{1,0:T(8,128)} %param.15) | copy-start | bytes 786436
  66.0 28.0 %collective-permute-start.10 = (bf16[1,2,8192]{2,0,1:T(2,128)(2,1)S(1)}, bf16[1,2,8192]{2,0,1:T(2,128)(2,1)S(1)}, u32[]{:S(2)}, u32[]{:S(2)}) collective-permute-start(bf16[1,2,8192]{2,0,1:T(2,128)(2,1)S(1)} %copy.46), channel_id=1, source_target_pairs={{0,16},{16,32},{32,48},{48,64},{64,80},{80,96},{96,112},{112,128},... | collective-permute-start | bytes 98312 | tf_op jit(solution)/shard_map/ppermute | solution.py:12
  70.3 23.7 %collective-permute-start.11 = (bf16[1,2,8192]{2,0,1:T(2,128)(2,1)S(1)}, bf16[1,2,8192]{2,0,1:T(2,128)(2,1)S(1)}, u32[]{:S(2)}, u32[]{:S(2)}) collective-permute-start(bf16[1,2,8192]{2,0,1:T(2,128)(2,1)S(1)} %copy.46), channel_id=1, source_target_pairs={{0,32},{16,48},{32,64},{48,80},{64,96},{80,112},{96,128},{112,144}... | collective-permute-start | bytes 98312 | tf_op jit(solution)/shard_map/ppermute | solution.py:12
  76.4 17.7 %collective-permute-start.6 = (bf16[1,2,8192]{2,0,1:T(2,128)(2,1)S(1)}, bf16[1,2,8192]{2,0,1:T(2,128)(2,1)S(1)}, u32[]{:S(2)}, u32[]{:S(2)}) collective-permute-start(bf16[1,2,8192]{2,0,1:T(2,128)(2,1)S(1)} %copy.46), channel_id=1, source_target_pairs={{16,0},{32,16},{48,32},{64,48},{80,64},{96,80},{112,96},{128,112},... | collective-permute-start | bytes 98312 | tf_op jit(solution)/shard_map/ppermute | solution.py:12
  88.0 7.1 %collective-permute-start.7 = (bf16[1,2,8192]{2,0,1:T(2,128)(2,1)S(1)}, bf16[1,2,8192]{2,0,1:T(2,128)(2,1)S(1)}, u32[]{:S(2)}, u32[]{:S(2)}) collective-permute-start(bf16[1,2,8192]{2,0,1:T(2,128)(2,1)S(1)} %copy.46), channel_id=1, source_target_pairs={{32,0},{48,16},{64,32},{80,48},{96,64},{112,80},{128,96},{144,112}... | collective-permute-start | bytes 98312 | tf_op jit(solution)/shard_map/ppermute | solution.py:12
  95.6 20.1 %collective-permute-start.12 = (bf16[2,2,8192]{2,0,1:T(2,128)(2,1)S(1)}, bf16[2,2,8192]{2,0,1:T(2,128)(2,1)S(1)}, u32[]{:S(2)}, u32[]{:S(2)}) collective-permute-start(bf16[2,2,8192]{2,0,1:T(2,128)(2,1)S(1)} %get-tuple-element.181), channel_id=1, source_target_pairs={{0,48},{16,64},{32,80},{48,96},{64,112},{80,128},{96,144},{112,160... | collective-permute-start | bytes 196616 | tf_op jit(solution)/shard_map/ppermute | solution.py:12
  97.6 18.2 %collective-permute-start.13 = (bf16[2,2,8192]{2,0,1:T(2,128)(2,1)S(1)}, bf16[2,2,8192]{2,0,1:T(2,128)(2,1)S(1)}, u32[]{:S(2)}, u32[]{:S(2)}) collective-permute-start(bf16[2,2,8192]{2,0,1:T(2,128)(2,1)S(1)} %get-tuple-element.182), channel_id=1, source_target_pairs={{0,64},{16,80},{32,96},{48,112},{64,128},{80,144},{96,160},{112,17... | collective-permute-start | bytes 196616 | tf_op jit(solution)/shard_map/ppermute | solution.py:12
  106.5 12.7 %collective-permute-start.8 = (bf16[2,2,8192]{2,0,1:T(2,128)(2,1)S(1)}, bf16[2,2,8192]{2,0,1:T(2,128)(2,1)S(1)}, u32[]{:S(2)}, u32[]{:S(2)}) collective-permute-start(bf16[2,2,8192]{2,0,1:T(2,128)(2,1)S(1)} %get-tuple-element.179), channel_id=1, source_target_pairs={{64,0},{80,16},{96,32},{112,48},{128,64},{144,80},{160,96},{176,11... | collective-permute-start | bytes 196616 | tf_op jit(solution)/shard_map/ppermute | solution.py:12
  110.3 14.0 %collective-permute-start.9 = (bf16[2,2,8192]{2,0,1:T(2,128)(2,1)S(1)}, bf16[2,2,8192]{2,0,1:T(2,128)(2,1)S(1)}, u32[]{:S(2)}, u32[]{:S(2)}) collective-permute-start(bf16[2,2,8192]{2,0,1:T(2,128)(2,1)S(1)} %get-tuple-element.180), channel_id=1, source_target_pairs={{48,0},{64,16},{80,32},{96,48},{112,64},{128,80},{144,96},{160,112... | collective-permute-start | bytes 196616 | tf_op jit(solution)/shard_map/ppermute | solution.py:12

commit v15 on v13

--- a/solution.py
+++ b/solution.py
@@ -62,23 +62,23 @@
     odd = lax.axis_index("section") % 2 == 1
     swap = [(2 * y + side, 2 * y + 1 - side) for y in range(count // 2) for side in (0, 1)]
     width = blocks.shape[1]
-    packed = jnp.concatenate(
-        [blocks[0], blocks[1], jnp.where(odd, backward_src, forward_src)], axis=1
-    )
+    modes2 = forward_src.shape[1]
+    packed = jnp.concatenate([blocks[0], blocks[1], forward_src, backward_src], axis=1)
     arrived = lax.ppermute(packed, "section", swap)
     other_blocks = jnp.stack([arrived[:, :width], arrived[:, width:2 * width]])
-    other_src = arrived[:, 2 * width:]
+    other_forward = arrived[:, 2 * width:2 * width + modes2]
+    other_backward = arrived[:, 2 * width + modes2:]
 
     def forward_pair():
         real_part, imag_part = matrix_product(blocks, other_blocks)
-        source = complex_product(blocks, other_src, False) + forward_src
+        source = complex_product(blocks, other_forward, False) + forward_src
         return real_part.astype(jnp.bfloat16), imag_part.astype(jnp.bfloat16), source.astype(
             jnp.bfloat16
         )
 
     def backward_pair():
         real_part, imag_part = adjoint_product(other_blocks, blocks)
-        source = complex_product(blocks, other_src, True) + backward_src
+        source = complex_product(blocks, other_backward, True) + backward_src
         return real_part.astype(jnp.bfloat16), imag_part.astype(jnp.bfloat16), source.astype(
             jnp.bfloat16
         )

time: 119 us -> 120 us (level)
  no operation moved by 1% of the time
where the time goes in v15:
time: 120 us; the launch traced here: 119 us
  starting transfers between devices  74.9 us (62%)
  waiting for transfers between devices  20.2 us (17%)
  matrix products  9.63 us (8%)
  other arithmetic  7.39 us (6%)
  local copies, waits for them, and re-layouts  6.17 us (5%)
    ppermute x8, starting transfers between devices, passed_along(): lax.ppermute(value, axis, [(source, source + steps) for source in range(l...  43.1 us
    ppermute x3, starting transfers between devices, sweeps(): arrived = lax.ppermute(state, 'section', stride)  14.9 us
    ppermute x8, waiting for transfers between devices, passed_along(): lax.ppermute(value, axis, [(source, source + steps) for source in range(l...  9.18 us
    ppermute x2, starting transfers between devices, sweeps(): lax.ppermute((own_map, chain_src), 'section', chain)  7.62 us
    ppermute x1, starting transfers between devices, sweeps(): neighbour = lax.ppermute(state, 'section', hand_over)  6.68 us
    dot_general x2, matrix products, picked_rows(): jnp.einsum('ar,ap->rp', table, selector.astype(table.dtype), preferred_el...  5.81 us
    unnamed x18, local copies, waits for them, and re-layouts  4.86 us
    ppermute x3, waiting for transfers between devices, sweeps(): arrived = lax.ppermute(state, 'section', stride)  4.25 us
  transfers between devices with their start and end apart: 15, of which 8 were waited for; matrix products, arithmetic and copies ran while one was open for 4% of the time, Pallas kernels for 0%

profile of v15, /device:TPU:149, one launch (start us, length us, event | category | flops | bytes accessed | tf_op | source)
XLA Modules:
  0.0 118.8 jit_solution(15754857277787509418)
XLA Ops:
  0.0 1.0 copy.15
  1.0 1.0 copy.16
  2.0 1.1 fusion.92
  3.1 0.2 copy.42
  3.4 0.0 copy-start
  3.4 0.2 copy.43
  3.6 0.1 pad_maximum_fusion.2
  3.7 2.6 %collective-permute-start = (bf16[384,1024]{0,1:T(8,128)(2,1)S(1)}, bf16[384,1024]{0,1:T(8,128)(2,1)S(1)}, u32[]{:S(2)}, u32[]{:S(2)}) collective-permute-start(bf16[384,1024]{0,1:T(8,128)(2,1)S(1)} %pad_maximum_fusion.2), channel_id=1, source_target_pairs={{0,1},{1,0},{2,3},{3,2},{4,5},{5,4},{6,7},{7,6},{8,9},{9,8},{10,11... | collective-permute-start | bytes 2359304 | tf_op jit(solution)/shard_map/ppermute | solution.py:67
  6.3 1.9 %collective-permute-done = bf16[384,1024]{0,1:T(8,128)(2,1)S(1)} collective-permute-done((bf16[384,1024]{0,1:T(8,128)(2,1)S(1)}, bf16[384,1024]{0,1:T(8,128)(2,1)S(1)}, u32[]{:S(2)}, u32[]{:S(2)}) %collective-permute-start) | collective-permute-done | bytes 786464 | tf_op jit(solution)/shard_map/ppermute | solution.py:67
  8.2 0.1 slice_bitcast_fusion.3
  8.2 0.1 pad_maximum_fusion.3
  8.3 4.5 %conditional.3 = (bf16[1,384,384]{2,1,0:T(8,128)(2,1)S(1)}, bf16[1,384,384]{2,1,0:T(8,128)(2,1)S(1)}, f32[384,128]{0,1:T(8,128)S(1)}, bf16[384,128]{0,1:T(8,128)...) conditional(s32[]{:T(128)} %convert_element_type.304, (bf16[2,384,384]{2,1,0:T(8,128)(2,1)S(1)}, ...), branch_computations={%region_1.2_spmd, %region_2.3_spmd} | conditional | flops 529317888 | bytes 9928752
  8.3 0.3 fusion.16
  8.7 0.8 convolution_bitcast_fusion.1
  9.5 0.9 fusion.10
  10.5 1.2 copy.11
  11.6 1.2 copy.12
  12.9 3.2 %collective-permute-start.2 = (bf16[768,64]{0,1:T(8,128)(2,1)S(1)}, bf16[768,64]{0,1:T(8,128)(2,1)S(1)}, u32[]{:S(2)}, u32[]{:S(2)}) collective-permute-start(bf16[768,64]{0,1:T(8,128)(2,1)S(1)} %pad_maximum_fusion.4), channel_id=1, source_target_pairs={{1,3},{3,5},{5,7},{7,9},{9,11},{11,13},{13,15},{2,0},{4,2},{6,4},{... | collective-permute-start | bytes 294920 | tf_op jit(solution)/shard_map/ppermute | solution.py:93
  16.2 4.4 %collective-permute-start.1 = (bf16[2,384,384]{2,1,0:T(8,128)(2,1)S(1)}, bf16[2,384,384]{2,1,0:T(8,128)(2,1)S(1)}, u32[]{:S(2)}, u32[]{:S(2)}) collective-permute-start(bf16[2,384,384]{2,1,0:T(8,128)(2,1)S(1)} %constant_dynamic-update-slice_fusion), channel_id=1, source_target_pairs={{1,3},{3,5},{5,7},{7,9},{9,11},{11,13},{13,15},{2,0},{4,2},{6,4},{... | collective-permute-start | bytes 1769480 | tf_op jit(solution)/shard_map/ppermute | solution.py:93
  20.6 0.0 collective-permute-done.2
  20.7 0.3 fusion.49
  21.0 4.3 %collective-permute-start.3 = (bf16[768,64]{0,1:T(8,128)(2,1)S(1)}, bf16[768,64]{0,1:T(8,128)(2,1)S(1)}, u32[]{:S(2)}, u32[]{:S(2)}) collective-permute-start(bf16[768,64]{0,1:T(8,128)(2,1)S(1)} %fusion.37), channel_id=1, source_target_pairs={{1,5},{3,7},{5,9},{7,11},{9,13},{11,15},{4,0},{6,2},{8,4},{10,6},{... | collective-permute-start | bytes 294920 | tf_op jit(solution)/shard_map/ppermute | solution.py:111
  25.3 2.8 %collective-permute-done.1 = bf16[2,384,384]{2,1,0:T(8,128)(2,1)S(1)} collective-permute-done((bf16[2,384,384]{2,1,0:T(8,128)(2,1)S(1)}, bf16[2,384,384]{2,1,0:T(8,128)(2,1)S(1)}, u32[]{:S(2)}, u32[]{:S(2)}) %collective-permute-start.1) | collective-permute-done | bytes 589856 | tf_op jit(solution)/shard_map/ppermute | solution.py:93
  28.2 0.8 convolution_bitcast_fusion.2
  29.0 1.1 fusion.90
  30.1 1.0 fusion.34
  31.1 0.0 collective-permute-done.3
  31.1 0.3 fusion.25
  31.5 0.0 copy-start.3
  31.5 4.7 %collective-permute-start.4 = (bf16[768,64]{0,1:T(8,128)(2,1)S(1)}, bf16[768,64]{0,1:T(8,128)(2,1)S(1)}, u32[]{:S(2)}, u32[]{:S(2)}) collective-permute-start(bf16[768,64]{0,1:T(8,128)(2,1)S(1)} %fusion.25), channel_id=1, source_target_pairs={{1,5},{3,7},{5,9},{7,11},{9,13},{11,15},{4,0},{6,2},{8,4},{10,6},{... | collective-permute-start | bytes 294920 | tf_op jit(solution)/shard_map/ppermute | solution.py:111
  36.2 2.6 %collective-permute-done.4 = bf16[768,64]{0,1:T(8,128)(2,1)S(1)} collective-permute-done((bf16[768,64]{0,1:T(8,128)(2,1)S(1)}, bf16[768,64]{0,1:T(8,128)(2,1)S(1)}, u32[]{:S(2)}, u32[]{:S(2)}) %collective-permute-start.4) | collective-permute-done | bytes 98336 | tf_op jit(solution)/shard_map/ppermute | solution.py:111
  38.7 0.3 fusion.26
  39.1 5.9 %collective-permute-start.5 = (bf16[768,64]{0,1:T(8,128)(2,1)S(1)}, bf16[768,64]{0,1:T(8,128)(2,1)S(1)}, u32[]{:S(2)}, u32[]{:S(2)}) collective-permute-start(bf16[768,64]{0,1:T(8,128)(2,1)S(1)} %fusion.26), channel_id=1, source_target_pairs={{1,5},{3,7},{5,9},{7,11},{9,13},{11,15},{4,0},{6,2},{8,4},{10,6},{... | collective-permute-start | bytes 294920 | tf_op jit(solution)/shard_map/ppermute | solution.py:111
  45.0 0.0 copy-start.4
  45.1 1.7 %collective-permute-done.5 = bf16[768,64]{0,1:T(8,128)(2,1)S(1)} collective-permute-done((bf16[768,64]{0,1:T(8,128)(2,1)S(1)}, bf16[768,64]{0,1:T(8,128)(2,1)S(1)}, u32[]{:S(2)}, u32[]{:S(2)}) %collective-permute-start.5) | collective-permute-done | bytes 98336 | tf_op jit(solution)/shard_map/ppermute | solution.py:111
  46.7 0.3 fusion.27
  47.1 6.7 %collective-permute-start.6 = (bf16[384,128]{0,1:T(8,128)(2,1)S(1)}, bf16[384,128]{0,1:T(8,128)(2,1)S(1)}, u32[]{:S(2)}, u32[]{:S(2)}) collective-permute-start(bf16[384,128]{0,1:T(8,128)(2,1)S(1)} %pad_maximum_fusion.5), channel_id=1, source_target_pairs={{1,2},{3,4},{5,6},{7,8},{9,10},{11,12},{13,14},{2,1},{4,3},{6,5},{... | collective-permute-start | bytes 294920 | tf_op jit(solution)/shard_map/ppermute | solution.py:117
  53.8 2.1 %collective-permute-done.6 = bf16[384,128]{0,1:T(8,128)(2,1)S(1)} collective-permute-done((bf16[384,128]{0,1:T(8,128)(2,1)S(1)}, bf16[384,128]{0,1:T(8,128)(2,1)S(1)}, u32[]{:S(2)}, u32[]{:S(2)}) %collective-permute-start.6) | collective-permute-done | bytes 98336 | tf_op jit(solution)/shard_map/ppermute | solution.py:117
  55.9 0.3 convolution_bitcast_fusion.3
  56.2 0.3 convolution_bitcast_fusion.4
  56.5 2.8 %fusion.20 = f32[128,8192]{1,0:T(8,128)S(1)} fusion(s32[8192]{0:T(1024)S(1)} %get-tuple-element.152, f32[384,64]{0,1:T(8,128)S(1)} %get-tuple-element.138, f32[384,64]{0,1:T(8,128)S(1)} %get-tuple-element.137, f32[384,64]{0,1:T(8,128)S(1)} %get-tuple-element.168, f32[384,64]{0,1:T(8,128)S(1)} %get-tuple-element.169, pred[]{:T(512)S(6)} %eq.63, ...), kind=kOutput, calls=%fused_computation.34 | convolution fusion | flops 808894464 | bytes 4816897 | tf_op jit(solution)/shard_map/ar,ap->rp/dot_general | solution.py:55
  59.3 3.0 %multiply_reduce_fusion = (f32[8192]{0:T(1024)S(1)}, f32[128,8192]{1,0:T(8,128)S(1)}) fusion(f32[128,8192]{1,0:T(8,128)S(1)} %fusion.20, s32[8192]{0:T(1024)S(1)} %get-tuple-element.151, bf16[384,64]{0,1:T(8,128)(2,1)S(1)} %get-tuple-element.142, bf16[384,64]{0,1:T(8,128)(2,1)S(1)} %get-tuple-element.141), kind=kOutput, calls=%fused_computation.37 | convolution fusion | flops 810737664 | bytes 8552448 | tf_op jit(solution)/shard_map/ar,ap->rp/dot_general | solution.py:55
  62.3 0.0 copy-start.1
  62.4 0.9 fusion.23
  63.3 0.1 maximum_multiply_fusion
  63.4 0.1 copy.47
  63.4 4.0 %collective-permute-start.11 = (bf16[1,2,8192]{2,0,1:T(2,128)(2,1)S(1)}, bf16[1,2,8192]{2,0,1:T(2,128)(2,1)S(1)}, u32[]{:S(2)}, u32[]{:S(2)}) collective-permute-start(bf16[1,2,8192]{2,0,1:T(2,128)(2,1)S(1)} %copy.47), channel_id=1, source_target_pairs={{0,16},{16,32},{32,48},{48,64},{64,80},{80,96},{96,112},{112,128},... | collective-permute-start | bytes 98312 | tf_op jit(solution)/shard_map/ppermute | solution.py:12
  67.4 7.0 %collective-permute-start.12 = (bf16[1,2,8192]{2,0,1:T(2,128)(2,1)S(1)}, bf16[1,2,8192]{2,0,1:T(2,128)(2,1)S(1)}, u32[]{:S(2)}, u32[]{:S(2)}) collective-permute-start(bf16[1,2,8192]{2,0,1:T(2,128)(2,1)S(1)} %copy.47), channel_id=1, source_target_pairs={{0,32},{16,48},{32,64},{48,80},{64,96},{80,112},{96,128},{112,144}... | collective-permute-start | bytes 98312 | tf_op jit(solution)/shard_map/ppermute | solution.py:12
  74.4 1.9 %collective-permute-start.7 = (bf16[1,2,8192]{2,0,1:T(2,128)(2,1)S(1)}, bf16[1,2,8192]{2,0,1:T(2,128)(2,1)S(1)}, u32[]{:S(2)}, u32[]{:S(2)}) collective-permute-start(bf16[1,2,8192]{2,0,1:T(2,128)(2,1)S(1)} %copy.47), channel_id=1, source_target_pairs={{16,0},{32,16},{48,32},{64,48},{80,64},{96,80},{112,96},{128,112},... | collective-permute-start | bytes 98312 | tf_op jit(solution)/shard_map/ppermute | solution.py:12
  76.4 9.2 %collective-permute-start.8 = (bf16[1,2,8192]{2,0,1:T(2,128)(2,1)S(1)}, bf16[1,2,8192]{2,0,1:T(2,128)(2,1)S(1)}, u32[]{:S(2)}, u32[]{:S(2)}) collective-permute-start(bf16[1,2,8192]{2,0,1:T(2,128)(2,1)S(1)} %copy.47), channel_id=1, source_target_pairs={{32,0},{48,16},{64,32},{80,48},{96,64},{112,80},{128,96},{144,112}... | collective-permute-start | bytes 98312 | tf_op jit(solution)/shard_map/ppermute | solution.py:12
  85.6 1.1 select_reduce_fusion.12
  86.7 0.0 collective-permute-done.11
  86.7 0.0 collective-permute-done.12
  86.7 0.0 collective-permute-done.7
  86.7 0.1 collective-permute-done.8
  86.9 0.5 pad_maximum_fusion.6
  87.4 8.4 %collective-permute-start.10 = (bf16[2,2,8192]{2,0,1:T(2,128)(2,1)S(1)}, bf16[2,2,8192]{2,0,1:T(2,128)(2,1)S(1)}, u32[]{:S(2)}, u32[]{:S(2)}) collective-permute-start(bf16[2,2,8192]{2,0,1:T(2,128)(2,1)S(1)} %get-tuple-element.148), channel_id=1, source_target_pairs={{48,0},{64,16},{80,32},{96,48},{112,64},{128,80},{144,96},{160,112... | collective-permute-start | bytes 196616 | tf_op jit(solution)/shard_map/ppermute | solution.py:12
  95.8 1.9 %collective-permute-start.13 = (bf16[2,2,8192]{2,0,1:T(2,128)(2,1)S(1)}, bf16[2,2,8192]{2,0,1:T(2,128)(2,1)S(1)}, u32[]{:S(2)}, u32[]{:S(2)}) collective-permute-start(bf16[2,2,8192]{2,0,1:T(2,128)(2,1)S(1)} %get-tuple-element.149), channel_id=1, source_target_pairs={{0,48},{16,64},{32,80},{48,96},{64,112},{80,128},{96,144},{112,160... | collective-permute-start | bytes 196616 | tf_op jit(solution)/shard_map/ppermute | solution.py:12
  97.8 6.0 %collective-permute-start.14 = (bf16[2,2,8192]{2,0,1:T(2,128)(2,1)S(1)}, bf16[2,2,8192]{2,0,1:T(2,128)(2,1)S(1)}, u32[]{:S(2)}, u32[]{:S(2)}) collective-permute-start(bf16[2,2,8192]{2,0,1:T(2,128)(2,1)S(1)} %get-tuple-element.150), channel_id=1, source_target_pairs={{0,64},{16,80},{32,96},{48,112},{64,128},{80,144},{96,160},{112,17... | collective-permute-start | bytes 196616 | tf_op jit(solution)/shard_map/ppermute | solution.py:12
  103.7 4.7 %collective-permute-start.9 = (bf16[2,2,8192]{2,0,1:T(2,128)(2,1)S(1)}, bf16[2,2,8192]{2,0,1:T(2,128)(2,1)S(1)}, u32[]{:S(2)}, u32[]{:S(2)}) collective-permute-start(bf16[2,2,8192]{2,0,1:T(2,128)(2,1)S(1)} %get-tuple-element.147), channel_id=1, source_target_pairs={{64,0},{80,16},{96,32},{112,48},{128,64},{144,80},{160,96},{176,11... | collective-permute-start | bytes 196616 | tf_op jit(solution)/shard_map/ppermute | solution.py:12
  108.4 3.6 %collective-permute-done.13 = bf16[2,2,8192]{2,0,1:T(2,128)(2,1)S(1)} collective-permute-done((bf16[2,2,8192]{2,0,1:T(2,128)(2,1)S(1)}, bf16[2,2,8192]{2,0,1:T(2,128)(2,1)S(1)}, u32[]{:S(2)}, u32[]{:S(2)}) %collective-permute-start.13) | collective-permute-done | bytes 65568 | tf_op jit(solution)/shard_map/ppermute | solution.py:12
  112.1 0.0 collective-permute-done.14
  112.1 5.4 %collective-permute-done.9 = bf16[2,2,8192]{2,0,1:T(2,128)(2,1)S(1)} collective-permute-done((bf16[2,2,8192]{2,0,1:T(2,128)(2,1)S(1)}, bf16[2,2,8192]{2,0,1:T(2,128)(2,1)S(1)}, u32[]{:S(2)}, u32[]{:S(2)}) %collective-permute-start.9) | collective-permute-done | bytes 65568 | tf_op jit(solution)/shard_map/ppermute | solution.py:12
  117.5 1.3 %fusion.57 = f32[2,1,8192]{2,1,0:T(1,128)} fusion(bf16[2,2,8192]{2,0,1:T(2,128)(2,1)S(1)} %collective-permute-done.14, bf16[2,2,8192]{2,0,1:T(2,128)(2,1)S(1)} %collective-permute-done.13, bf16[1,2,8192]{2,0,1:T(2,128)(2,1)S(1)} %collective-permute-done.12, f32[1,1,8192]{2,1,0:T(1,128)S(1)} %fusion.83, f32[1,1,8192]{2,1,0:T(1,128)S(1)} %bitcast.251, ...), kind=kLoop, calls=%fused_computation.113 | loop fusion | flops 622592 | bytes 950272 | tf_op jit(solution)/shard_map/add | solution.py:170
  (26 shorter events, 0.4 us)
Async XLA Ops:
  3.4 4.9 %copy-start = (bf16[1,1,2,384,384]{4,3,2,1,0:T(8,128)(2,1)S(1)}, bf16[1,1,2,384,384]{4,3,2,1,0:T(8,128)(2,1)}, u32[]{:S(2)}) copy-start(bf16[1,1,2,384,384]{4,3,2,1,0:T(8,128)(2,1)} %param.9) | copy-start | bytes 1769476
  3.7 4.5 %collective-permute-start = (bf16[384,1024]{0,1:T(8,128)(2,1)S(1)}, bf16[384,1024]{0,1:T(8,128)(2,1)S(1)}, u32[]{:S(2)}, u32[]{:S(2)}) collective-permute-start(bf16[384,1024]{0,1:T(8,128)(2,1)S(1)} %pad_maximum_fusion.2), channel_id=1, source_target_pairs={{0,1},{1,0},{2,3},{3,2},{4,5},{5,4},{6,7},{7,6},{8,9},{9,8},{10,11... | collective-permute-start | bytes 2359304 | tf_op jit(solution)/shard_map/ppermute | solution.py:67
  12.9 7.7 %collective-permute-start.2 = (bf16[768,64]{0,1:T(8,128)(2,1)S(1)}, bf16[768,64]{0,1:T(8,128)(2,1)S(1)}, u32[]{:S(2)}, u32[]{:S(2)}) collective-permute-start(bf16[768,64]{0,1:T(8,128)(2,1)S(1)} %pad_maximum_fusion.4), channel_id=1, source_target_pairs={{1,3},{3,5},{5,7},{7,9},{9,11},{11,13},{13,15},{2,0},{4,2},{6,4},{... | collective-permute-start | bytes 294920 | tf_op jit(solution)/shard_map/ppermute | solution.py:93
  16.2 12.0 %collective-permute-start.1 = (bf16[2,384,384]{2,1,0:T(8,128)(2,1)S(1)}, bf16[2,384,384]{2,1,0:T(8,128)(2,1)S(1)}, u32[]{:S(2)}, u32[]{:S(2)}) collective-permute-start(bf16[2,384,384]{2,1,0:T(8,128)(2,1)S(1)} %constant_dynamic-update-slice_fusion), channel_id=1, source_target_pairs={{1,3},{3,5},{5,7},{7,9},{9,11},{11,13},{13,15},{2,0},{4,2},{6,4},{... | collective-permute-start | bytes 1769480 | tf_op jit(solution)/shard_map/ppermute | solution.py:93
  21.0 10.1 %collective-permute-start.3 = (bf16[768,64]{0,1:T(8,128)(2,1)S(1)}, bf16[768,64]{0,1:T(8,128)(2,1)S(1)}, u32[]{:S(2)}, u32[]{:S(2)}) collective-permute-start(bf16[768,64]{0,1:T(8,128)(2,1)S(1)} %fusion.37), channel_id=1, source_target_pairs={{1,5},{3,7},{5,9},{7,11},{9,13},{11,15},{4,0},{6,2},{8,4},{10,6},{... | collective-permute-start | bytes 294920 | tf_op jit(solution)/shard_map/ppermute | solution.py:111
  31.5 13.5 %copy-start.2 = (s32[8192]{0:T(1024)S(1)}, s32[8192]{0:T(1024)}, u32[]{:S(2)}) copy-start(s32[8192]{0:T(1024)} %param.13) | copy-start | bytes 98308
  31.5 13.5 %copy-start.3 = (s32[8192]{0:T(1024)S(1)}, s32[8192]{0:T(1024)}, u32[]{:S(2)}) copy-start(s32[8192]{0:T(1024)} %param.12) | copy-start | bytes 98308
  31.5 7.3 %collective-permute-start.4 = (bf16[768,64]{0,1:T(8,128)(2,1)S(1)}, bf16[768,64]{0,1:T(8,128)(2,1)S(1)}, u32[]{:S(2)}, u32[]{:S(2)}) collective-permute-start(bf16[768,64]{0,1:T(8,128)(2,1)S(1)} %fusion.25), channel_id=1, source_target_pairs={{1,5},{3,7},{5,9},{7,11},{9,13},{11,15},{4,0},{6,2},{8,4},{10,6},{... | collective-permute-start | bytes 294920 | tf_op jit(solution)/shard_map/ppermute | solution.py:111
  39.1 7.6 %collective-permute-start.5 = (bf16[768,64]{0,1:T(8,128)(2,1)S(1)}, bf16[768,64]{0,1:T(8,128)(2,1)S(1)}, u32[]{:S(2)}, u32[]{:S(2)}) collective-permute-start(bf16[768,64]{0,1:T(8,128)(2,1)S(1)} %fusion.26), channel_id=1, source_target_pairs={{1,5},{3,7},{5,9},{7,11},{9,13},{11,15},{4,0},{6,2},{8,4},{10,6},{... | collective-permute-start | bytes 294920 | tf_op jit(solution)/shard_map/ppermute | solution.py:111
  45.0 8.7 %copy-start.4 = (s32[8]{0:T(128)S(1)}, s32[8]{0:T(128)}, u32[]{:S(2)}) copy-start(s32[8]{0:T(128)} %param.14) | copy-start | bytes 100
  47.1 8.8 %collective-permute-start.6 = (bf16[384,128]{0,1:T(8,128)(2,1)S(1)}, bf16[384,128]{0,1:T(8,128)(2,1)S(1)}, u32[]{:S(2)}, u32[]{:S(2)}) collective-permute-start(bf16[384,128]{0,1:T(8,128)(2,1)S(1)} %pad_maximum_fusion.5), channel_id=1, source_target_pairs={{1,2},{3,4},{5,6},{7,8},{9,10},{11,12},{13,14},{2,1},{4,3},{6,5},{... | collective-permute-start | bytes 294920 | tf_op jit(solution)/shard_map/ppermute | solution.py:117
  62.3 23.2 %copy-start.1 = (f32[8,8192]{1,0:T(8,128)S(1)}, f32[8,8192]{1,0:T(8,128)}, u32[]{:S(2)}) copy-start(f32[8,8192]{1,0:T(8,128)} %param.15) | copy-start | bytes 786436
  63.4 23.3 %collective-permute-start.11 = (bf16[1,2,8192]{2,0,1:T(2,128)(2,1)S(1)}, bf16[1,2,8192]{2,0,1:T(2,128)(2,1)S(1)}, u32[]{:S(2)}, u32[]{:S(2)}) collective-permute-start(bf16[1,2,8192]{2,0,1:T(2,128)(2,1)S(1)} %copy.47), channel_id=1, source_target_pairs={{0,16},{16,32},{32,48},{48,64},{64,80},{80,96},{96,112},{112,128},... | collective-permute-start | bytes 98312 | tf_op jit(solution)/shard_map/ppermute | solution.py:12
  67.4 19.3 %collective-permute-start.12 = (bf16[1,2,8192]{2,0,1:T(2,128)(2,1)S(1)}, bf16[1,2,8192]{2,0,1:T(2,128)(2,1)S(1)}, u32[]{:S(2)}, u32[]{:S(2)}) collective-permute-start(bf16[1,2,8192]{2,0,1:T(2,128)(2,1)S(1)} %copy.47), channel_id=1, source_target_pairs={{0,32},{16,48},{32,64},{48,80},{64,96},{80,112},{96,128},{112,144}... | collective-permute-start | bytes 98312 | tf_op jit(solution)/shard_map/ppermute | solution.py:12
  74.4 12.3 %collective-permute-start.7 = (bf16[1,2,8192]{2,0,1:T(2,128)(2,1)S(1)}, bf16[1,2,8192]{2,0,1:T(2,128)(2,1)S(1)}, u32[]{:S(2)}, u32[]{:S(2)}) collective-permute-start(bf16[1,2,8192]{2,0,1:T(2,128)(2,1)S(1)} %copy.47), channel_id=1, source_target_pairs={{16,0},{32,16},{48,32},{64,48},{80,64},{96,80},{112,96},{128,112},... | collective-permute-start | bytes 98312 | tf_op jit(solution)/shard_map/ppermute | solution.py:12
  76.4 10.5 %collective-permute-start.8 = (bf16[1,2,8192]{2,0,1:T(2,128)(2,1)S(1)}, bf16[1,2,8192]{2,0,1:T(2,128)(2,1)S(1)}, u32[]{:S(2)}, u32[]{:S(2)}) collective-permute-start(bf16[1,2,8192]{2,0,1:T(2,128)(2,1)S(1)} %copy.47), channel_id=1, source_target_pairs={{32,0},{48,16},{64,32},{80,48},{96,64},{112,80},{128,96},{144,112}... | collective-permute-start | bytes 98312 | tf_op jit(solution)/shard_map/ppermute | solution.py:12
  87.4 21.0 %collective-permute-start.10 = (bf16[2,2,8192]{2,0,1:T(2,128)(2,1)S(1)}, bf16[2,2,8192]{2,0,1:T(2,128)(2,1)S(1)}, u32[]{:S(2)}, u32[]{:S(2)}) collective-permute-start(bf16[2,2,8192]{2,0,1:T(2,128)(2,1)S(1)} %get-tuple-element.148), channel_id=1, source_target_pairs={{48,0},{64,16},{80,32},{96,48},{112,64},{128,80},{144,96},{160,112... | collective-permute-start | bytes 196616 | tf_op jit(solution)/shard_map/ppermute | solution.py:12
  95.8 16.2 %collective-permute-start.13 = (bf16[2,2,8192]{2,0,1:T(2,128)(2,1)S(1)}, bf16[2,2,8192]{2,0,1:T(2,128)(2,1)S(1)}, u32[]{:S(2)}, u32[]{:S(2)}) collective-permute-start(bf16[2,2,8192]{2,0,1:T(2,128)(2,1)S(1)} %get-tuple-element.149), channel_id=1, source_target_pairs={{0,48},{16,64},{32,80},{48,96},{64,112},{80,128},{96,144},{112,160... | collective-permute-start | bytes 196616 | tf_op jit(solution)/shard_map/ppermute | solution.py:12
  97.8 14.3 %collective-permute-start.14 = (bf16[2,2,8192]{2,0,1:T(2,128)(2,1)S(1)}, bf16[2,2,8192]{2,0,1:T(2,128)(2,1)S(1)}, u32[]{:S(2)}, u32[]{:S(2)}) collective-permute-start(bf16[2,2,8192]{2,0,1:T(2,128)(2,1)S(1)} %get-tuple-element.150), channel_id=1, source_target_pairs={{0,64},{16,80},{32,96},{48,112},{64,128},{80,144},{96,160},{112,17... | collective-permute-start | bytes 196616 | tf_op jit(solution)/shard_map/ppermute | solution.py:12
  103.7 13.7 %collective-permute-start.9 = (bf16[2,2,8192]{2,0,1:T(2,128)(2,1)S(1)}, bf16[2,2,8192]{2,0,1:T(2,128)(2,1)S(1)}, u32[]{:S(2)}, u32[]{:S(2)}) collective-permute-start(bf16[2,2,8192]{2,0,1:T(2,128)(2,1)S(1)} %get-tuple-element.147), channel_id=1, source_target_pairs={{64,0},{80,16},{96,32},{112,48},{128,64},{144,80},{160,96},{176,11... | collective-permute-start | bytes 196616 | tf_op jit(solution)/shard_map/ppermute | solution.py:12
